TPU v7x, 32 devices: a whole 2x2x4 slice. The times are simulated.
32 devices in a mesh: grp: 2 (over y), outer: 4 (over x, core), inner: 4 (over z).
Axes of the slice: x: 2, y: 2, z: 4, core: 2. Of those that a mesh axis runs over, the one named last changes fastest.
Arguments:
- query: bfloat16 [4096, 1024], P(('grp', 'outer', 'inner')), parts along dimension 0, may hold values from -6 to 6
- key: bfloat16 [4096, 1024], P(('grp', 'outer', 'inner')), parts along dimension 0, may hold values from -6 to 6
- value: bfloat16 [4096, 1024], P(('grp', 'outer', 'inner')), parts along dimension 0, may hold values from -6 to 6
- grad_out: bfloat16 [4096, 1024], P(('grp', 'outer', 'inner')), parts along dimension 0, may hold values from -6 to 6
Outputs:
- normed_out: bfloat16 [4096, 1024], P(('grp', 'outer', 'inner')), parts along dimension 0
- grad_query: bfloat16 [4096, 1024], P(('grp', 'outer', 'inner')), parts along dimension 0
- grad_key: bfloat16 [4096, 1024], P(('grp', 'outer', 'inner')), parts along dimension 0
- grad_value: bfloat16 [4096, 1024], P(('grp', 'outer', 'inner')), parts along dimension 0
There are 2 independent parts, one for each index of `grp`. A program takes and returns all parts, laid end to end along the dimension named above; each array names one. Nothing has to cross between parts.
All inputs are finite; a program needn't handle non-finite values.
Results may differ from a plain program's by a relative error of at most 0.0059.
Values sent between devices are 32-bit elements; how exact they have to be, the bound alone decides.
No kernel may reach another device: no remote copies, remote signals or barrier semaphores. Data moves between devices by JAX's collectives and lax.ppermute only.
A program may use at most 64 MiB of HBM per device.

v0:
```python
import jax
import jax.numpy as jnp
from jax import lax
from jax.sharding import PartitionSpec as P

HEADS = 8
HEAD = 128


def carried_in(value, axis, join, neutral, backward):
    count, mine = (lax.axis_size(axis), lax.axis_index(axis))
    pieces = lax.all_gather(value, axis)
    if backward:
        pieces = pieces[::-1]
        mine = count - 1 - mine
    running = jnp.full_like(value, 0) + jnp.asarray(neutral, value.dtype)

    def lap(position, running):
        longer = join(running, pieces[position])
        return jnp.where(position < mine, longer, running)

    return lax.fori_loop(0, count - 1, lap, running)


def add_terms(earlier, later):
    return earlier + later


def forward_prefix(state):
    empty_state = jnp.zeros_like(state)
    inner_prior = carried_in(state, "inner", add_terms, empty_state, False)
    row_total = lax.psum(state, "inner")
    return carried_in(row_total, "outer", add_terms, empty_state, False) + inner_prior


def backward_suffix(state):
    empty_state = jnp.zeros_like(state)
    inner_later = carried_in(state, "inner", add_terms, empty_state, True)
    row_total = lax.psum(state, "inner")
    return carried_in(row_total, "outer", add_terms, empty_state, True) + inner_later


def per_device(query, key, value, grad_out):
    rows_dev = query.shape[0]
    scaling = HEAD ** (-0.5)
    queries = query.reshape(rows_dev, HEADS, HEAD)
    key_rows = key.reshape(rows_dev, HEADS, HEAD)
    value_rows = value.reshape(rows_dev, HEADS, HEAD)
    line = lax.broadcasted_iota(jnp.int32, (rows_dev, rows_dev), 0)
    column = lax.broadcasted_iota(jnp.int32, (rows_dev, rows_dev), 1)
    causal = (line >= column)[None]
    state = jnp.einsum("thi,thj->hij", key_rows, value_rows, preferred_element_type=jnp.float32)
    prior = forward_prefix(state)
    prior_half = prior.astype(jnp.bfloat16)
    scores = (
        jnp.einsum("thi,shi->hts", queries, key_rows, preferred_element_type=jnp.float32) * scaling
    )
    score_half = jnp.where(causal, scores, 0.0).astype(jnp.bfloat16)
    attended = jnp.einsum(
        "hts,shj->thj", score_half, value_rows, preferred_element_type=jnp.float32
    )
    attended = attended + scaling * jnp.einsum(
        "thi,hij->thj", queries, prior_half, preferred_element_type=jnp.float32
    )
    flat = attended.reshape(rows_dev, HEADS * HEAD)
    inverse = lax.rsqrt(jnp.mean(flat * flat, axis=-1, keepdims=True) + 1e-05)
    normed = flat * inverse
    grads_flat = grad_out.astype(jnp.float32)
    grad_pre = inverse * (
        grads_flat - normed * jnp.mean(grads_flat * normed, axis=-1, keepdims=True)
    )
    grad_half = grad_pre.astype(jnp.bfloat16).reshape(rows_dev, HEADS, HEAD)
    dscores = jnp.einsum("thj,shj->hts", grad_half, value_rows, preferred_element_type=jnp.float32)
    dscore_half = jnp.where(causal, dscores, 0.0).astype(jnp.bfloat16)
    grad_q = jnp.einsum("hts,shi->thi", dscore_half, key_rows, preferred_element_type=jnp.float32)
    grad_q = scaling * (
        grad_q
        + jnp.einsum("thj,hij->thi", grad_half, prior_half, preferred_element_type=jnp.float32)
    )
    grad_state = jnp.einsum("thi,thj->hij", queries, grad_half, preferred_element_type=jnp.float32)
    later = backward_suffix(grad_state)
    later_half = later.astype(jnp.bfloat16)
    grad_k = jnp.einsum("hts,thi->shi", dscore_half, queries, preferred_element_type=jnp.float32)
    grad_k = scaling * (
        grad_k
        + jnp.einsum("shj,hij->shi", value_rows, later_half, preferred_element_type=jnp.float32)
    )
    grad_v = jnp.einsum("hts,thj->shj", score_half, grad_half, preferred_element_type=jnp.float32)
    grad_v = grad_v + scaling * jnp.einsum(
        "shi,hij->shj", key_rows, later_half, preferred_element_type=jnp.float32
    )
    width = HEADS * HEAD
    return (
        normed.astype(jnp.bfloat16),
        grad_q.reshape(rows_dev, width).astype(jnp.bfloat16),
        grad_k.reshape(rows_dev, width).astype(jnp.bfloat16),
        grad_v.reshape(rows_dev, width).astype(jnp.bfloat16),
    )


def solution(mesh):
    placed = (
        P(("grp", "outer", "inner"), None),
        P(("grp", "outer", "inner"), None),
        P(("grp", "outer", "inner"), None),
        P(("grp", "outer", "inner"), None),
    )
    return jax.shard_map(
        per_device,
        mesh=mesh,
        in_specs=placed,
        out_specs=(
            P(("grp", "outer", "inner"), None),
            P(("grp", "outer", "inner"), None),
            P(("grp", "outer", "inner"), None),
            P(("grp", "outer", "inner"), None),
        ),
        check_vma=False,
    )
```

profile of v0, /device:TPU:0, one launch (start us, length us, event | category | flops | bytes accessed | tf_op | source)
XLA Modules:
  0.0 253.9 jit_solution(7140993363098596042)
XLA Ops:
  7.2 1.1 copy.62
  8.3 0.2 copy.35
  8.6 1.0 fusion.19
  9.6 48.5 %all-gather.11.cloned.1.call-done = f32[32,128,128]{2,1,0:T(8,128)} async-done(((f32[8,128,128]{2,1,0:T(8,128)}), f32[32,128,128]{2,1,0:T(8,128)}) %all-gather.11.cloned.1.call-update) | async-done | bytes 2097168 | tf_op jit(solution)/shard_map/all_gather | solution.py:12
  58.1 0.7 all-reduce.3.cloned.1.call-update
  58.9 39.7 %all-reduce.3.cloned.1.call-done = f32[1,8,128,128]{3,2,1,0:T(8,128)} async-done(((f32[1,8,128,128]{3,2,1,0:T(8,128)}), f32[1,8,128,128]{3,2,1,0:T(8,128)}) %all-reduce.3.cloned.1.call-update) | async-done | bytes 524304 | tf_op jit(solution)/shard_map/psum | solution.py:32
  98.7 0.3 fusion.8
  99.0 3.8 %while.57 = (s32[]{:T(128)}, f32[8,128,128]{2,1,0:T(8,128)S(1)}, s32[]{:T(128)}, f32[4,8,128,128]{3,2,1,0:T(8,128)}, s32[]{:T(128)}, /*index=5*/s32[]{:T(128)}) while((s32[]{:T(128)}, f32[8,128,128]{2,1,0:T(8,128)S(1)}, s32[]{:T(128)}, f32[4,8,128,128]{3,2,1,0:T(8,128)}, s32[]{:T(128)}, /*index=5*/s32[]{:T(128)}) %tuple.146), condition=%wide.region_4.5_spmd.clone, body=%wide.region_3.4_spmd.clone.sunk | while | flops 393220 | bytes 1572957 | solution.py:22
  99.1 1.2 add_select_fusion.9
  100.3 1.2 add_select_fusion.9
  101.6 1.2 add_select_fusion.9
  102.8 19.8 %all-gather.7.cloned.1.call-done = f32[4,8,128,128]{3,2,1,0:T(8,128)} async-done(((f32[1,8,128,128]{3,2,1,0:T(8,128)}), f32[4,8,128,128]{3,2,1,0:T(8,128)}) %all-gather.7.cloned.1.call-update) | async-done | bytes 2097168 | tf_op jit(solution)/shard_map/all_gather | solution.py:12
  122.6 3.7 %while.56 = (s32[]{:T(128)}, f32[8,128,128]{2,1,0:T(8,128)S(1)}, s32[]{:T(128)}, f32[4,8,128,128]{3,2,1,0:T(8,128)}, s32[]{:T(128)}, /*index=5*/s32[]{:T(128)}) while((s32[]{:T(128)}, f32[8,128,128]{2,1,0:T(8,128)S(1)}, s32[]{:T(128)}, f32[4,8,128,128]{3,2,1,0:T(8,128)}, s32[]{:T(128)}, /*index=5*/s32[]{:T(128)}) %tuple.122), condition=%wide.region_2.3_spmd.clone, body=%wide.region_1.2_spmd.clone.sunk | while | flops 393220 | bytes 1572957 | solution.py:22
  122.6 1.2 add_select_fusion.8
  123.9 1.2 add_select_fusion.8
  125.1 1.2 add_select_fusion.8
  126.4 0.3 fusion.6
  126.8 0.4 multiply_reduce_fusion
  127.1 0.2 copy.39
  127.4 0.2 fusion.13
  127.6 0.9 fusion.15
  128.6 0.2 fusion.24
  128.9 1.0 copy.48
  129.9 0.5 all-reduce.5.cloned.1.call-update
  130.5 0.5 all-gather.13.cloned.1.call-update
  131.1 40.3 %all-reduce.5.cloned.1.call-done = f32[1,8,128,128]{2,3,1,0:T(8,128)} async-done(((f32[1,8,128,128]{2,3,1,0:T(8,128)}), f32[1,8,128,128]{2,3,1,0:T(8,128)}) %all-reduce.5.cloned.1.call-update) | async-done | bytes 524304 | tf_op jit(solution)/shard_map/psum | solution.py:39
  171.4 2.0 copy.47
  173.5 0.3 fusion.12
  173.8 0.2 convolution_bitcast_fusion.2
  174.0 0.3 fusion.11
  174.3 0.9 copy.53
  175.2 1.0 fusion.38
  176.2 1.1 convolution_bitcast_fusion
  177.3 41.0 %all-gather.13.cloned.1.call-done = f32[32,128,128]{2,1,0:T(8,128)} async-done(((f32[8,128,128]{2,1,0:T(8,128)}), f32[32,128,128]{2,1,0:T(8,128)}) %all-gather.13.cloned.1.call-update) | async-done | bytes 2097168 | tf_op jit(solution)/shard_map/all_gather | solution.py:12
  218.3 1.7 rev.7
  220.0 0.6 while.59
  220.1 0.2 add_select_fusion.11
  220.3 0.2 add_select_fusion.11
  220.5 0.2 add_select_fusion.11
  220.6 20.5 %all-gather.9.cloned.1.call-done = f32[4,8,128,128]{3,2,1,0:T(8,128)} async-done(((f32[1,8,128,128]{3,2,1,0:T(8,128)}), f32[4,8,128,128]{3,2,1,0:T(8,128)}) %all-gather.9.cloned.1.call-update) | async-done | bytes 2097168 | tf_op jit(solution)/shard_map/all_gather | solution.py:12
  241.1 1.7 rev.6
  242.9 0.6 while.58
  242.9 0.2 add_select_fusion.10
  243.1 0.2 add_select_fusion.10
  243.5 1.5 fusion.9
  245.0 0.9 copy.55
  245.9 0.3 fusion.10
  246.2 0.9 copy.54
  (32 shorter events, 0.8 us)
Async XLA Ops:
  7.2 1.4 copy-start
  7.2 91.5 %copy-start.4 = (bf16[128,1024]{1,0:T(8,128)(2,1)S(1)}, bf16[128,1024]{1,0:T(8,128)(2,1)}, u32[]{:S(2)}) copy-start(bf16[128,1024]{1,0:T(8,128)(2,1)} %param.13) | copy-start | bytes 786436
  7.2 91.5 %copy-start.2 = (bf16[128,1024]{1,0:T(8,128)(2,1)S(1)}, bf16[128,1024]{1,0:T(8,128)(2,1)}, u32[]{:S(2)}) copy-start(bf16[128,1024]{1,0:T(8,128)(2,1)} %param.12) | copy-start | bytes 786436
  7.2 50.9 %all-gather.11.cloned.1.call-start = ((), (), s32[]{:S(2)}) async-start(), calls=%async_computation.4 | async-start | bytes 2621440 | tf_op jit(solution)/shard_map/all_gather | solution.py:12
  58.1 40.5 %all-reduce.3.cloned.1.call-start = ((), (), s32[]{:S(2)}) async-start(), calls=%async_computation | async-start | bytes 1048576 | tf_op jit(solution)/shard_map/psum | solution.py:32
  58.9 63.7 %all-gather.7.cloned.1.call-start = ((), (), s32[]{:S(2)}) async-start(), calls=%async_computation.1 | async-start | bytes 2621440 | tf_op jit(solution)/shard_map/all_gather | solution.py:12
  126.4 1.0 copy-start.5
  128.9 1.0 copy-start.1
  129.9 41.5 %all-reduce.5.cloned.1.call-start = ((), (), s32[]{:S(2)}) async-start(), calls=%async_computation.2 | async-start | bytes 1048576 | tf_op jit(solution)/shard_map/psum | solution.py:39
  130.5 87.9 %all-gather.13.cloned.1.call-start = ((), (), s32[]{:S(2)}) async-start(), calls=%async_computation.5 | async-start | bytes 2621440 | tf_op jit(solution)/shard_map/all_gather | solution.py:12
  131.0 110.1 %all-gather.9.cloned.1.call-start = ((), (), s32[]{:S(2)}) async-start(), calls=%async_computation.3 | async-start | bytes 2621440 | tf_op jit(solution)/shard_map/all_gather | solution.py:12
  243.5 2.4 copy-start.3
Sparse Core Ops, SparseCore 0:
  9.7 48.3 all-gather.10
  61.3 37.3 all-reduce.2
  100.2 22.3 all-gather.6
  132.7 38.6 all-reduce.4
  172.8 45.4 all-gather.12
  219.7 21.3 all-gather.8
where the time goes:
time: 254 us
  waiting for transfers between devices  212 us (83%)
  between operations  14.4 us (6%)
  local copies, waits for them, and re-layouts  10.8 us (4%)
  other arithmetic  9.62 us (4%)
  matrix products  6.99 us (3%)
    all_gather x4, waiting for transfers between devices, carried_in(): pieces = lax.all_gather(value, axis)  130 us
    psum x1, waiting for transfers between devices, backward_suffix(): row_total = lax.psum(state, 'inner')  40.3 us
    psum x1, waiting for transfers between devices, forward_prefix(): row_total = lax.psum(state, 'inner')  39.7 us
    select_n x12, other arithmetic, lap(): return jnp.where(position < mine, longer, running)  8.37 us
  transfers between devices with their start and end apart: 6, of which 6 were waited for; matrix products, arithmetic and copies ran while one was open for 5% of the time, Pallas kernels for 0%

commit v1 on v0

--- a/solution.py
+++ b/solution.py
@@ -7,37 +7,21 @@
 HEAD = 128
 
 
-def carried_in(value, axis, join, neutral, backward):
-    count, mine = (lax.axis_size(axis), lax.axis_index(axis))
-    pieces = lax.all_gather(value, axis)
-    if backward:
-        pieces = pieces[::-1]
-        mine = count - 1 - mine
-    running = jnp.full_like(value, 0) + jnp.asarray(neutral, value.dtype)
-
-    def lap(position, running):
-        longer = join(running, pieces[position])
-        return jnp.where(position < mine, longer, running)
-
-    return lax.fori_loop(0, count - 1, lap, running)
-
-
-def add_terms(earlier, later):
-    return earlier + later
-
-
-def forward_prefix(state):
-    empty_state = jnp.zeros_like(state)
-    inner_prior = carried_in(state, "inner", add_terms, empty_state, False)
-    row_total = lax.psum(state, "inner")
-    return carried_in(row_total, "outer", add_terms, empty_state, False) + inner_prior
-
-
-def backward_suffix(state):
-    empty_state = jnp.zeros_like(state)
-    inner_later = carried_in(state, "inner", add_terms, empty_state, True)
-    row_total = lax.psum(state, "inner")
-    return carried_in(row_total, "outer", add_terms, empty_state, True) + inner_later
+def hypercube_scan(value, backward):
+    earlier = jnp.zeros_like(value)
+    total = value
+    for axis in ("inner", "outer"):
+        count, mine = lax.axis_size(axis), lax.axis_index(axis)
+        bit = 1
+        while bit < count:
+            pairs = [(i, i ^ bit) for i in range(count)]
+            got = lax.ppermute(total, axis, pairs)
+            partner_lower = (mine & bit) != 0
+            take = jnp.logical_not(partner_lower) if backward else partner_lower
+            earlier = jnp.where(take, earlier + got, earlier)
+            total = total + got
+            bit *= 2
+    return earlier
 
 
 def per_device(query, key, value, grad_out):
@@ -50,7 +34,7 @@
     column = lax.broadcasted_iota(jnp.int32, (rows_dev, rows_dev), 1)
     causal = (line >= column)[None]
     state = jnp.einsum("thi,thj->hij", key_rows, value_rows, preferred_element_type=jnp.float32)
-    prior = forward_prefix(state)
+    prior = hypercube_scan(state, False)
     prior_half = prior.astype(jnp.bfloat16)
     scores = (
         jnp.einsum("thi,shi->hts", queries, key_rows, preferred_element_type=jnp.float32) * scaling
@@ -78,7 +62,7 @@
         + jnp.einsum("thj,hij->thi", grad_half, prior_half, preferred_element_type=jnp.float32)
     )
     grad_state = jnp.einsum("thi,thj->hij", queries, grad_half, preferred_element_type=jnp.float32)
-    later = backward_suffix(grad_state)
+    later = hypercube_scan(grad_state, True)
     later_half = later.astype(jnp.bfloat16)
     grad_k = jnp.einsum("hts,thi->shi", dscore_half, queries, preferred_element_type=jnp.float32)
     grad_k = scaling * (
@@ -99,21 +83,11 @@
 
 
 def solution(mesh):
-    placed = (
-        P(("grp", "outer", "inner"), None),
-        P(("grp", "outer", "inner"), None),
-        P(("grp", "outer", "inner"), None),
-        P(("grp", "outer", "inner"), None),
-    )
+    placed = P(("grp", "outer", "inner"), None)
     return jax.shard_map(
         per_device,
         mesh=mesh,
-        in_specs=placed,
-        out_specs=(
-            P(("grp", "outer", "inner"), None),
-            P(("grp", "outer", "inner"), None),
-            P(("grp", "outer", "inner"), None),
-            P(("grp", "outer", "inner"), None),
-        ),
+        in_specs=(placed, placed, placed, placed),
+        out_specs=(placed, placed, placed, placed),
         check_vma=False,
     )

time: 254 us -> 124 us (0.49)
  waiting for transfers between devices: 212 us -> 95 us
  between operations: 14.4 us -> 0.86 us
  starting transfers between devices: 0.16 us -> 11.7 us
  local copies, waits for them, and re-layouts: 10.8 us -> 6.17 us
  matrix products: 6.99 us -> 3.48 us
  other arithmetic: 9.62 us -> 6.74 us
    all_gather x4 -> x0, waiting for transfers between devices: 130 us -> none  [carried_in(): pieces = lax.all_gather(value, axis)]
    ppermute x0 -> x8, waiting for transfers between devices: none -> 95 us  [hypercube_scan(): got = lax.ppermute(total, axis, pairs)]
    psum x2 -> x0, waiting for transfers between devices: 80 us -> none  [the longest x1 40.3 us: backward_suffix(): row_total = lax.psum(state, 'inner')]
    ppermute x0 -> x8, starting transfers between devices: none -> 11.7 us  [hypercube_scan(): got = lax.ppermute(total, axis, pairs)]
    select_n x12 -> x0, other arithmetic: 8.37 us -> none  [lap(): return jnp.where(position < mine, longer, running)]
    rev x2 -> x0, local copies, waits for them, and re-layouts: 3.45 us -> none  [carried_in(): pieces = pieces[::-1]]
    add x0 -> x6, other arithmetic: none -> 3.07 us  [hypercube_scan(): total = total + got]
    unnamed x16 -> x20, local copies, waits for them, and re-layouts: 3.67 us -> 5.58 us
  transfers between devices with their start and end apart: 6 -> 8, of which waited for: 6 -> 8; matrix products, arithmetic and copies ran while one was open for 5% -> 2% of each run, Pallas kernels for 0% -> 0%
where the time goes in v1:
time: 124 us
  waiting for transfers between devices  95 us (77%)
  starting transfers between devices  11.7 us (9%)
  other arithmetic  6.74 us (5%)
  local copies, waits for them, and re-layouts  6.17 us (5%)
  matrix products  3.48 us (3%)
    ppermute x8, waiting for transfers between devices, hypercube_scan(): got = lax.ppermute(total, axis, pairs)  95 us
    ppermute x8, starting transfers between devices, hypercube_scan(): got = lax.ppermute(total, axis, pairs)  11.7 us
    unnamed x20, local copies, waits for them, and re-layouts  5.58 us
    add x6, other arithmetic, hypercube_scan(): total = total + got  3.07 us
  transfers between devices with their start and end apart: 8, of which 8 were waited for; matrix products, arithmetic and copies ran while one was open for 2% of the time, Pallas kernels for 0%

profile of v1, /device:TPU:0, one launch (start us, length us, event | category | flops | bytes accessed | tf_op | source)
XLA Modules:
  0.0 124.0 jit_solution(6710012333904236648)
XLA Ops:
  0.6 1.0 copy.38
  1.7 0.2 copy.11
  1.9 0.2 fusion.21
  2.1 3.1 %collective-permute-start = (f32[8,128,128]{2,1,0:T(8,128)S(1)}, f32[8,128,128]{2,1,0:T(8,128)S(1)}, u32[]{:S(2)}, u32[]{:S(2)}) collective-permute-start(f32[8,128,128]{2,1,0:T(8,128)S(1)} %fusion.21), channel_id=1, source_target_pairs={{0,1},{1,0},{2,3},{3,2},{4,5},{5,4},{6,7},{7,6},{8,9},{9,8},{10,11... | collective-permute-start | bytes 1572872 | tf_op jit(solution)/shard_map/ppermute | solution.py:18
  5.3 11.9 %collective-permute-done = f32[8,128,128]{2,1,0:T(8,128)S(1)} collective-permute-done((f32[8,128,128]{2,1,0:T(8,128)S(1)}, f32[8,128,128]{2,1,0:T(8,128)S(1)}, u32[]{:S(2)}, u32[]{:S(2)}) %collective-permute-start) | collective-permute-done | bytes 524320 | tf_op jit(solution)/shard_map/ppermute | solution.py:18
  17.2 0.1 add.60
  17.3 2.8 %collective-permute-start.1 = (f32[8,128,128]{2,1,0:T(8,128)S(1)}, f32[8,128,128]{2,1,0:T(8,128)S(1)}, u32[]{:S(2)}, u32[]{:S(2)}) collective-permute-start(f32[8,128,128]{2,1,0:T(8,128)S(1)} %add.60), channel_id=1, source_target_pairs={{0,2},{1,3},{2,0},{3,1},{4,6},{5,7},{6,4},{7,5},{8,10},{9,11},{10,... | collective-permute-start | bytes 1572872 | tf_op jit(solution)/shard_map/ppermute | solution.py:18
  20.1 22.5 %collective-permute-done.1 = f32[8,128,128]{2,1,0:T(8,128)S(1)} collective-permute-done((f32[8,128,128]{2,1,0:T(8,128)S(1)}, f32[8,128,128]{2,1,0:T(8,128)S(1)}, u32[]{:S(2)}, u32[]{:S(2)}) %collective-permute-start.1) | collective-permute-done | bytes 524320 | tf_op jit(solution)/shard_map/ppermute | solution.py:18
  42.6 0.1 collective-permute-start.2
  42.7 1.9 %collective-permute-done.2 = f32[8,128,128]{2,1,0:T(8,128)S(1)} collective-permute-done((f32[8,128,128]{2,1,0:T(8,128)S(1)}, f32[8,128,128]{2,1,0:T(8,128)S(1)}, u32[]{:S(2)}, u32[]{:S(2)}) %collective-permute-start.2) | collective-permute-done | bytes 524320 | tf_op jit(solution)/shard_map/ppermute | solution.py:18
  44.6 0.9 add.64
  45.5 1.4 %collective-permute-start.3 = (f32[8,128,128]{2,1,0:T(8,128)}, f32[8,128,128]{2,1,0:T(8,128)}, u32[]{:S(2)}, u32[]{:S(2)}) collective-permute-start(f32[8,128,128]{2,1,0:T(8,128)} %add.64), channel_id=1, source_target_pairs={{0,8},{4,12},{8,0},{12,4},{1,9},{5,13},{9,1},{13,5},{2,10},{6,14},... | collective-permute-start | bytes 1572872 | tf_op jit(solution)/shard_map/ppermute | solution.py:18
  46.9 0.3 fusion.8
  47.2 12.5 %collective-permute-done.3 = f32[8,128,128]{2,1,0:T(8,128)} collective-permute-done((f32[8,128,128]{2,1,0:T(8,128)}, f32[8,128,128]{2,1,0:T(8,128)}, u32[]{:S(2)}, u32[]{:S(2)}) %collective-permute-start.3) | collective-permute-done | bytes 524320 | tf_op jit(solution)/shard_map/ppermute | solution.py:18
  59.8 1.2 fusion.16
  61.0 0.3 fusion.6
  61.3 0.4 multiply_reduce_fusion
  61.7 0.2 copy.15
  61.9 0.7 copy-done.3
  62.6 0.2 fusion.13
  62.8 0.9 fusion.15
  63.7 0.2 copy.34
  63.9 0.3 convolution_bitcast_fusion.2
  64.2 0.6 collective-permute-start.4
  64.8 12.6 %collective-permute-done.4 = f32[8,128,128]{2,1,0:T(8,128)S(1)} collective-permute-done((f32[8,128,128]{2,1,0:T(8,128)S(1)}, f32[8,128,128]{2,1,0:T(8,128)S(1)}, u32[]{:S(2)}, u32[]{:S(2)}) %collective-permute-start.4) | collective-permute-done | bytes 524320 | tf_op jit(solution)/shard_map/ppermute | solution.py:18
  77.4 0.1 add.70
  77.5 2.3 %collective-permute-start.5 = (f32[8,128,128]{2,1,0:T(8,128)S(1)}, f32[8,128,128]{2,1,0:T(8,128)S(1)}, u32[]{:S(2)}, u32[]{:S(2)}) collective-permute-start(f32[8,128,128]{2,1,0:T(8,128)S(1)} %add.70), channel_id=1, source_target_pairs={{0,2},{1,3},{2,0},{3,1},{4,6},{5,7},{6,4},{7,5},{8,10},{9,11},{10,... | collective-permute-start | bytes 1572872 | tf_op jit(solution)/shard_map/ppermute | solution.py:18
  79.7 22.2 %collective-permute-done.5 = f32[8,128,128]{2,1,0:T(8,128)S(1)} collective-permute-done((f32[8,128,128]{2,1,0:T(8,128)S(1)}, f32[8,128,128]{2,1,0:T(8,128)S(1)}, u32[]{:S(2)}, u32[]{:S(2)}) %collective-permute-start.5) | collective-permute-done | bytes 524320 | tf_op jit(solution)/shard_map/ppermute | solution.py:18
  101.9 0.1 add.72
  102.0 0.1 collective-permute-start.6
  102.1 0.3 fusion.12
  102.5 0.3 convolution_bitcast_fusion.4
  102.7 0.4 copy-done.6
  103.2 1.0 collective-permute-done.6
  104.1 1.9 %add.74 = f32[8,128,128]{2,1,0:T(8,128)} add(f32[8,128,128]{2,1,0:T(8,128)S(1)} %add.72, f32[8,128,128]{2,1,0:T(8,128)} %collective-permute-done.6) | non-fusion elementwise | flops 131072 | bytes 1572864 | tf_op jit(solution)/shard_map/add | solution.py:22
  106.0 1.4 %collective-permute-start.7 = (f32[8,128,128]{2,1,0:T(8,128)}, f32[8,128,128]{2,1,0:T(8,128)}, u32[]{:S(2)}, u32[]{:S(2)}) collective-permute-start(f32[8,128,128]{2,1,0:T(8,128)} %add.74), channel_id=1, source_target_pairs={{0,8},{4,12},{8,0},{12,4},{1,9},{5,13},{9,1},{13,5},{2,10},{6,14},... | collective-permute-start | bytes 1572872 | tf_op jit(solution)/shard_map/ppermute | solution.py:18
  107.4 0.2 fusion.11
  107.6 0.9 copy.28
  108.5 0.1 copy-done.5
  108.6 0.2 fusion.39
  108.8 0.7 copy-done.7
  109.5 0.3 convolution_bitcast_fusion
  109.8 10.5 %collective-permute-done.7 = f32[8,128,128]{2,1,0:T(8,128)} collective-permute-done((f32[8,128,128]{2,1,0:T(8,128)}, f32[8,128,128]{2,1,0:T(8,128)}, u32[]{:S(2)}, u32[]{:S(2)}) %collective-permute-start.7) | collective-permute-done | bytes 524320 | tf_op jit(solution)/shard_map/ppermute | solution.py:18
  120.3 1.4 %fusion.17 = bf16[8,128,128]{2,1,0:T(8,128)(2,1)S(1)} fusion(f32[8,128,128]{2,1,0:T(8,128)} %collective-permute-done.7, f32[8,128,128]{2,1,0:T(8,128)} %collective-permute-done.6, f32[8,128,128]{2,1,0:T(8,128)S(1)} %collective-permute-done.5, f32[8,128,128]{2,1,0:T(8,128)S(1)} %collective-permute-done.4, pred[]{:T(512)S(6)} %not.15, pred[]{:T(512)S(6)} %not.14, ...), kind=kLoop, calls=%fused_computation.35 | loop fusion | flops 1048576 | bytes 2359300 | tf_op jit(solution)/shard_map/convert_element_type | solution.py:66
  121.7 0.3 fusion.9
  122.0 0.9 copy.30
  122.9 0.3 fusion.10
  123.2 0.9 copy.29
  (16 shorter events, 0.1 us)
Async XLA Ops:
  0.6 1.3 %copy-start = (bf16[128,1024]{1,0:T(8,128)(2,1)S(1)}, bf16[128,1024]{1,0:T(8,128)(2,1)}, u32[]{:S(2)}) copy-start(bf16[128,1024]{1,0:T(8,128)(2,1)} %param.6) | copy-start | bytes 786436
  2.1 15.0 %collective-permute-start = (f32[8,128,128]{2,1,0:T(8,128)S(1)}, f32[8,128,128]{2,1,0:T(8,128)S(1)}, u32[]{:S(2)}, u32[]{:S(2)}) collective-permute-start(f32[8,128,128]{2,1,0:T(8,128)S(1)} %fusion.21), channel_id=1, source_target_pairs={{0,1},{1,0},{2,3},{3,2},{4,5},{5,4},{6,7},{7,6},{8,9},{9,8},{10,11... | collective-permute-start | bytes 1572872 | tf_op jit(solution)/shard_map/ppermute | solution.py:18
  17.3 25.3 %collective-permute-start.1 = (f32[8,128,128]{2,1,0:T(8,128)S(1)}, f32[8,128,128]{2,1,0:T(8,128)S(1)}, u32[]{:S(2)}, u32[]{:S(2)}) collective-permute-start(f32[8,128,128]{2,1,0:T(8,128)S(1)} %add.60), channel_id=1, source_target_pairs={{0,2},{1,3},{2,0},{3,1},{4,6},{5,7},{6,4},{7,5},{8,10},{9,11},{10,... | collective-permute-start | bytes 1572872 | tf_op jit(solution)/shard_map/ppermute | solution.py:18
  42.6 4.3 %copy-start.1 = (bf16[128,1024]{1,0:T(8,128)(2,1)S(1)}, bf16[128,1024]{1,0:T(8,128)(2,1)}, u32[]{:S(2)}) copy-start(bf16[128,1024]{1,0:T(8,128)(2,1)} %param.4) | copy-start | bytes 786436
  42.6 4.3 %copy-start.2 = (bf16[128,1024]{1,0:T(8,128)(2,1)S(1)}, bf16[128,1024]{1,0:T(8,128)(2,1)}, u32[]{:S(2)}) copy-start(bf16[128,1024]{1,0:T(8,128)(2,1)} %param.5) | copy-start | bytes 786436
  42.6 2.0 %collective-permute-start.2 = (f32[8,128,128]{2,1,0:T(8,128)S(1)}, f32[8,128,128]{2,1,0:T(8,128)S(1)}, u32[]{:S(2)}, u32[]{:S(2)}) collective-permute-start(f32[8,128,128]{2,1,0:T(8,128)S(1)} %add.62), channel_id=1, source_target_pairs={{0,4},{4,0},{8,12},{12,8},{1,5},{5,1},{9,13},{13,9},{2,6},{6,2},{1... | collective-permute-start | bytes 1572872 | tf_op jit(solution)/shard_map/ppermute | solution.py:18
  45.5 14.3 %collective-permute-start.3 = (f32[8,128,128]{2,1,0:T(8,128)}, f32[8,128,128]{2,1,0:T(8,128)}, u32[]{:S(2)}, u32[]{:S(2)}) collective-permute-start(f32[8,128,128]{2,1,0:T(8,128)} %add.64), channel_id=1, source_target_pairs={{0,8},{4,12},{8,0},{12,4},{1,9},{5,13},{9,1},{13,5},{2,10},{6,14},... | collective-permute-start | bytes 1572872 | tf_op jit(solution)/shard_map/ppermute | solution.py:18
  47.2 14.1 %copy-start.4 = (bf16[8,128,128]{2,1,0:T(8,128)(2,1)}, bf16[8,128,128]{2,1,0:T(8,128)(2,1)S(1)}, u32[]{:S(2)}) copy-start(bf16[8,128,128]{2,1,0:T(8,128)(2,1)S(1)} %fusion.8) | copy-start | bytes 786436
  61.7 1.0 copy-start.3
  64.2 13.2 %collective-permute-start.4 = (f32[8,128,128]{2,1,0:T(8,128)S(1)}, f32[8,128,128]{2,1,0:T(8,128)S(1)}, u32[]{:S(2)}, u32[]{:S(2)}) collective-permute-start(f32[8,128,128]{2,1,0:T(8,128)S(1)} %convolution_bitcast_fusion.2), channel_id=1, source_target_pairs={{0,1},{1,0},{2,3},{3,2},{4,5},{5,4},{6,7},{7,6},{8,9},{9,8},{10,11... | collective-permute-start | bytes 1572872 | tf_op jit(solution)/shard_map/ppermute | solution.py:18
  77.5 24.5 %collective-permute-start.5 = (f32[8,128,128]{2,1,0:T(8,128)S(1)}, f32[8,128,128]{2,1,0:T(8,128)S(1)}, u32[]{:S(2)}, u32[]{:S(2)}) collective-permute-start(f32[8,128,128]{2,1,0:T(8,128)S(1)} %add.70), channel_id=1, source_target_pairs={{0,2},{1,3},{2,0},{3,1},{4,6},{5,7},{6,4},{7,5},{8,10},{9,11},{10,... | collective-permute-start | bytes 1572872 | tf_op jit(solution)/shard_map/ppermute | solution.py:18
  102.0 2.1 %collective-permute-start.6 = (f32[8,128,128]{2,1,0:T(8,128)S(1)}, f32[8,128,128]{2,1,0:T(8,128)}, u32[]{:S(2)}, u32[]{:S(2)}) collective-permute-start(f32[8,128,128]{2,1,0:T(8,128)S(1)} %add.72), channel_id=1, source_target_pairs={{0,4},{4,0},{8,12},{12,8},{1,5},{5,1},{9,13},{13,9},{2,6},{6,2},{1... | collective-permute-start | bytes 1572872 | tf_op jit(solution)/shard_map/ppermute | solution.py:18
  102.4 0.7 copy-start.6
  106.0 14.3 %collective-permute-start.7 = (f32[8,128,128]{2,1,0:T(8,128)}, f32[8,128,128]{2,1,0:T(8,128)}, u32[]{:S(2)}, u32[]{:S(2)}) collective-permute-start(f32[8,128,128]{2,1,0:T(8,128)} %add.74), channel_id=1, source_target_pairs={{0,8},{4,12},{8,0},{12,4},{1,9},{5,13},{9,1},{13,5},{2,10},{6,14},... | collective-permute-start | bytes 1572872 | tf_op jit(solution)/shard_map/ppermute | solution.py:18
  107.6 1.0 copy-start.5
  108.6 0.9 copy-start.7

commit v2 on v1

--- a/solution.py
+++ b/solution.py
@@ -7,21 +7,56 @@
 HEAD = 128
 
 
-def hypercube_scan(value, backward):
-    earlier = jnp.zeros_like(value)
-    total = value
+def axis_bits(axis):
+    count = lax.axis_size(axis)
+    return [1 << k for k in range(count.bit_length() - 1)]
+
+
+def swap(value, axis, bit):
+    count = lax.axis_size(axis)
+    return lax.ppermute(value, axis, [(i, i ^ bit) for i in range(count)])
+
+
+def partner_counts(axis, bit, backward):
+    partner_lower = (lax.axis_index(axis) & bit) != 0
+    return jnp.logical_not(partner_lower) if backward else partner_lower
+
+
+def subcube_step(earlier, total, axis, bit, backward):
+    got = swap(total, axis, bit)
+    earlier = jnp.where(partner_counts(axis, bit, backward), earlier + got, earlier)
+    return earlier, total + got
+
+
+def scan_inner_first(value, backward):
+    earlier, total = jnp.zeros_like(value), value
     for axis in ("inner", "outer"):
-        count, mine = lax.axis_size(axis), lax.axis_index(axis)
-        bit = 1
-        while bit < count:
-            pairs = [(i, i ^ bit) for i in range(count)]
-            got = lax.ppermute(total, axis, pairs)
-            partner_lower = (mine & bit) != 0
-            take = jnp.logical_not(partner_lower) if backward else partner_lower
-            earlier = jnp.where(take, earlier + got, earlier)
-            total = total + got
-            bit *= 2
+        for bit in axis_bits(axis):
+            earlier, total = subcube_step(earlier, total, axis, bit, backward)
     return earlier
+
+
+def scan_outer_middle(value, backward):
+    inner_bits = axis_bits("inner")
+    if not inner_bits:
+        return scan_inner_first(value, backward)
+    earlier, total = jnp.zeros_like(value), value
+    for bit in inner_bits[:-1]:
+        earlier, total = subcube_step(earlier, total, "inner", bit, backward)
+    rows_before, rows_total = jnp.zeros_like(value), total
+    for bit in axis_bits("outer"):
+        rows_before, rows_total = subcube_step(rows_before, rows_total, "outer", bit, backward)
+    top = inner_bits[-1]
+    counted = partner_counts("inner", top, backward)
+    sent = jnp.where(counted, rows_before, rows_before + total)
+    return rows_before + swap(sent, "inner", top) + earlier
+
+
+def chunked_scan(value, backward):
+    half = value.shape[0] // 2
+    first = scan_inner_first(value[:half], backward)
+    second = scan_outer_middle(value[half:], backward)
+    return jnp.concatenate([first, second], axis=0)
 
 
 def per_device(query, key, value, grad_out):
@@ -34,7 +69,7 @@
     column = lax.broadcasted_iota(jnp.int32, (rows_dev, rows_dev), 1)
     causal = (line >= column)[None]
     state = jnp.einsum("thi,thj->hij", key_rows, value_rows, preferred_element_type=jnp.float32)
-    prior = hypercube_scan(state, False)
+    prior = chunked_scan(state, False)
     prior_half = prior.astype(jnp.bfloat16)
     scores = (
         jnp.einsum("thi,shi->hts", queries, key_rows, preferred_element_type=jnp.float32) * scaling
@@ -62,7 +97,7 @@
         + jnp.einsum("thj,hij->thi", grad_half, prior_half, preferred_element_type=jnp.float32)
     )
     grad_state = jnp.einsum("thi,thj->hij", queries, grad_half, preferred_element_type=jnp.float32)
-    later = hypercube_scan(grad_state, True)
+    later = chunked_scan(grad_state, True)
     later_half = later.astype(jnp.bfloat16)
     grad_k = jnp.einsum("hts,thi->shi", dscore_half, queries, preferred_element_type=jnp.float32)
     grad_k = scaling * (

time: 124 us -> 108 us (0.87)
  waiting for transfers between devices: 95 us -> 75.5 us
  starting transfers between devices: 11.7 us -> 14.4 us
    ppermute x8 -> x16, waiting for transfers between devices: 95 us -> 75.5 us  [swap(): return lax.ppermute(value, axis, [(i, i ^ bit) for i in range(count)])]
    another operation x0 -> x4, other arithmetic: none -> 3.21 us
    ppermute x8 -> x16, starting transfers between devices: 11.7 us -> 14.4 us  [swap(): return lax.ppermute(value, axis, [(i, i ^ bit) for i in range(count)])]
    convert_element_type x2 -> x0, other arithmetic: 2.54 us -> none  [the longest x1 1.35 us: per_device(): later_half = later.astype(jnp.bfloat16)]
    add x6 -> x8, other arithmetic: 3.07 us -> 1.04 us  [subcube_step(): return (earlier, total + got)]
    unnamed x20 -> x22, local copies, waits for them, and re-layouts: 5.58 us -> 6.27 us
  transfers between devices with their start and end apart: 8 -> 16, of which waited for: 8 -> 11; matrix products, arithmetic and copies ran while one was open for 2% -> 5% of each run, Pallas kernels for 0% -> 0%
where the time goes in v2:
time: 108 us; the launch traced here: 107 us
  waiting for transfers between devices  75.5 us (70%)
  starting transfers between devices  14.4 us (13%)
  local copies, waits for them, and re-layouts  6.93 us (6%)
  other arithmetic  6.21 us (6%)
  matrix products  3.52 us (3%)
    ppermute x16, waiting for transfers between devices, swap(): return lax.ppermute(value, axis, [(i, i ^ bit) for i in range(count)])  75.5 us
    ppermute x16, starting transfers between devices, swap(): return lax.ppermute(value, axis, [(i, i ^ bit) for i in range(count)])  14.4 us
    unnamed x22, local copies, waits for them, and re-layouts  6.27 us
    another operation x4, other arithmetic  3.21 us
  transfers between devices with their start and end apart: 16, of which 11 were waited for; matrix products, arithmetic and copies ran while one was open for 5% of the time, Pallas kernels for 0%

profile of v2, /device:TPU:0, one launch (start us, length us, event | category | flops | bytes accessed | tf_op | source)
XLA Modules:
  0.0 107.5 jit_solution(16659450751666805465)
XLA Ops:
  0.6 1.0 copy.38
  1.7 0.2 copy.11
  1.9 0.2 fusion.21
  2.2 3.1 %collective-permute-start = (f32[4,128,128]{2,1,0:T(8,128)S(1)}, f32[4,128,128]{2,1,0:T(8,128)S(1)}, u32[]{:S(2)}, u32[]{:S(2)}) collective-permute-start(f32[4,128,128]{2,1,0:T(8,128)S(1)} %get-tuple-element.16), channel_id=1, source_target_pairs={{0,1},{1,0},{2,3},{3,2},{4,5},{5,4},{6,7},{7,6},{8,9},{9,8},{10,11... | collective-permute-start | bytes 786440 | tf_op jit(solution)/shard_map/ppermute | solution.py:17
  5.4 7.1 %collective-permute-done = f32[4,128,128]{2,1,0:T(8,128)S(1)} collective-permute-done((f32[4,128,128]{2,1,0:T(8,128)S(1)}, f32[4,128,128]{2,1,0:T(8,128)S(1)}, u32[]{:S(2)}, u32[]{:S(2)}) %collective-permute-start) | collective-permute-done | bytes 262176 | tf_op jit(solution)/shard_map/ppermute | solution.py:17
  12.5 4.8 %collective-permute-done.4 = f32[4,128,128]{2,1,0:T(8,128)S(1)} collective-permute-done((f32[4,128,128]{2,1,0:T(8,128)S(1)}, f32[4,128,128]{2,1,0:T(8,128)S(1)}, u32[]{:S(2)}, u32[]{:S(2)}) %collective-permute-start.4) | collective-permute-done | bytes 262176 | tf_op jit(solution)/shard_map/ppermute | solution.py:17
  17.4 2.8 %collective-permute-start.1 = (f32[4,128,128]{2,1,0:T(8,128)S(1)}, f32[4,128,128]{2,1,0:T(8,128)S(1)}, u32[]{:S(2)}, u32[]{:S(2)}) collective-permute-start(f32[4,128,128]{2,1,0:T(8,128)S(1)} %get-tuple-element.14), channel_id=1, source_target_pairs={{0,2},{1,3},{2,0},{3,1},{4,6},{5,7},{6,4},{7,5},{8,10},{9,11},{10,... | collective-permute-start | bytes 786440 | tf_op jit(solution)/shard_map/ppermute | solution.py:17
  20.2 1.6 %collective-permute-start.6 = (f32[4,128,128]{2,1,0:T(8,128)S(1)}, f32[4,128,128]{2,1,0:T(8,128)S(1)}, u32[]{:S(2)}, u32[]{:S(2)}) collective-permute-start(f32[4,128,128]{2,1,0:T(8,128)S(1)} %add.103), channel_id=1, source_target_pairs={{0,8},{4,12},{8,0},{12,4},{1,9},{5,13},{9,1},{13,5},{2,10},{6,14},... | collective-permute-start | bytes 786440 | tf_op jit(solution)/shard_map/ppermute | solution.py:17
  21.8 10.9 %collective-permute-done.1 = f32[4,128,128]{2,1,0:T(8,128)S(1)} collective-permute-done((f32[4,128,128]{2,1,0:T(8,128)S(1)}, f32[4,128,128]{2,1,0:T(8,128)S(1)}, u32[]{:S(2)}, u32[]{:S(2)}) %collective-permute-start.1) | collective-permute-done | bytes 262176 | tf_op jit(solution)/shard_map/ppermute | solution.py:17
  33.0 1.3 %collective-permute-done.2 = f32[4,128,128]{2,1,0:T(8,128)S(1)} collective-permute-done((f32[4,128,128]{2,1,0:T(8,128)S(1)}, f32[4,128,128]{2,1,0:T(8,128)S(1)}, u32[]{:S(2)}, u32[]{:S(2)}) %collective-permute-start.2) | collective-permute-done | bytes 262176 | tf_op jit(solution)/shard_map/ppermute | solution.py:17
  34.4 0.7 add.100
  35.1 1.5 %collective-permute-start.3 = (f32[4,128,128]{2,1,0:T(8,128)}, f32[4,128,128]{2,1,0:T(8,128)}, u32[]{:S(2)}, u32[]{:S(2)}) collective-permute-start(f32[4,128,128]{2,1,0:T(8,128)} %add.100), channel_id=1, source_target_pairs={{0,8},{4,12},{8,0},{12,4},{1,9},{5,13},{9,1},{13,5},{2,10},{6,14},... | collective-permute-start | bytes 786440 | tf_op jit(solution)/shard_map/ppermute | solution.py:17
  36.7 0.3 fusion.8
  37.0 11.2 %collective-permute-done.7 = f32[4,128,128]{2,1,0:T(8,128)S(1)} collective-permute-done((f32[4,128,128]{2,1,0:T(8,128)S(1)}, f32[4,128,128]{2,1,0:T(8,128)S(1)}, u32[]{:S(2)}, u32[]{:S(2)}) %collective-permute-start.7) | collective-permute-done | bytes 262176 | tf_op jit(solution)/shard_map/ppermute | solution.py:17
  48.3 1.0 fusion.16
  49.3 0.3 fusion.6
  49.6 0.4 multiply_reduce_fusion
  50.0 0.2 copy.15
  50.2 0.7 copy-done.5
  50.9 0.2 fusion.13
  51.2 0.9 fusion.15
  52.2 0.3 convolution_bitcast_fusion.2
  52.7 2.0 %collective-permute-start.8 = (f32[4,128,128]{2,1,0:T(8,128)S(1)}, f32[4,128,128]{2,1,0:T(8,128)S(1)}, u32[]{:S(2)}, u32[]{:S(2)}) collective-permute-start(f32[4,128,128]{2,1,0:T(8,128)S(1)} %get-tuple-element.12), channel_id=1, source_target_pairs={{0,1},{1,0},{2,3},{3,2},{4,5},{5,4},{6,7},{7,6},{8,9},{9,8},{10,11... | collective-permute-start | bytes 786440 | tf_op jit(solution)/shard_map/ppermute | solution.py:17
  54.7 7.2 %collective-permute-done.12 = f32[4,128,128]{2,1,0:T(8,128)S(1)} collective-permute-done((f32[4,128,128]{2,1,0:T(8,128)S(1)}, f32[4,128,128]{2,1,0:T(8,128)S(1)}, u32[]{:S(2)}, u32[]{:S(2)}) %collective-permute-start.12) | collective-permute-done | bytes 262176 | tf_op jit(solution)/shard_map/ppermute | solution.py:17
  61.8 4.3 %collective-permute-done.8 = f32[4,128,128]{2,1,0:T(8,128)S(1)} collective-permute-done((f32[4,128,128]{2,1,0:T(8,128)S(1)}, f32[4,128,128]{2,1,0:T(8,128)S(1)}, u32[]{:S(2)}, u32[]{:S(2)}) %collective-permute-start.8) | collective-permute-done | bytes 262176 | tf_op jit(solution)/shard_map/ppermute | solution.py:17
  66.2 0.6 copy-done.8
  66.8 0.5 collective-permute-start.9
  67.3 0.3 fusion.12
  67.6 0.6 copy-done.7
  68.2 0.2 fusion.45
  68.4 11.9 %collective-permute-done.9 = f32[4,128,128]{2,1,0:T(8,128)S(1)} collective-permute-done((f32[4,128,128]{2,1,0:T(8,128)S(1)}, f32[4,128,128]{2,1,0:T(8,128)S(1)}, u32[]{:S(2)}, u32[]{:S(2)}) %collective-permute-start.9) | collective-permute-done | bytes 262176 | tf_op jit(solution)/shard_map/ppermute | solution.py:17
  80.5 1.6 %collective-permute-start.14 = (f32[4,128,128]{2,1,0:T(8,128)S(1)}, f32[4,128,128]{2,1,0:T(8,128)S(1)}, u32[]{:S(2)}, u32[]{:S(2)}) collective-permute-start(f32[4,128,128]{2,1,0:T(8,128)S(1)} %add.119), channel_id=1, source_target_pairs={{0,8},{4,12},{8,0},{12,4},{1,9},{5,13},{9,1},{13,5},{2,10},{6,14},... | collective-permute-start | bytes 786440 | tf_op jit(solution)/shard_map/ppermute | solution.py:17
  82.1 0.2 convolution_bitcast_fusion.3
  82.3 0.3 fusion.11
  82.7 0.7 copy-done.3
  83.3 0.9 collective-permute-start.11
  84.2 5.5 %collective-permute-done.14 = f32[4,128,128]{2,1,0:T(8,128)S(1)} collective-permute-done((f32[4,128,128]{2,1,0:T(8,128)S(1)}, f32[4,128,128]{2,1,0:T(8,128)S(1)}, u32[]{:S(2)}, u32[]{:S(2)}) %collective-permute-start.14) | collective-permute-done | bytes 262176 | tf_op jit(solution)/shard_map/ppermute | solution.py:17
  89.7 0.8 add_select_fusion
  90.5 0.3 convolution_bitcast_fusion
  90.8 0.9 copy.28
  91.6 3.3 %collective-permute-done.11 = f32[4,128,128]{2,1,0:T(8,128)} collective-permute-done((f32[4,128,128]{2,1,0:T(8,128)S(1)}, f32[4,128,128]{2,1,0:T(8,128)}, u32[]{:S(2)}, u32[]{:S(2)}) %collective-permute-start.11) | collective-permute-done | bytes 262176 | tf_op jit(solution)/shard_map/ppermute | solution.py:17
  95.0 1.1 %fusion.17 = bf16[4,128,128]{2,1,0:T(8,128)(2,1)S(1)} fusion(f32[4,128,128]{2,1,0:T(8,128)} %collective-permute-done.11, f32[4,128,128]{2,1,0:T(8,128)S(1)} %copy-done.4, f32[4,128,128]{2,1,0:T(8,128)S(1)} %collective-permute-done.9, f32[4,128,128]{2,1,0:T(8,128)} %copy-done.8, pred[]{:T(512)S(6)} %not.19, pred[]{:T(512)S(6)} %not.18, pred[]{:T(512)S(6)} %not.17, ...), kind=kLoop, calls=%fused_computation.41 | loop fusion | flops 524288 | bytes 1179652 | tf_op jit(solution)/shard_map/convert
  96.1 8.0 %collective-permute-done.15 = f32[4,128,128]{2,1,0:T(8,128)} collective-permute-done((f32[4,128,128]{2,1,0:T(8,128)}, f32[4,128,128]{2,1,0:T(8,128)}, u32[]{:S(2)}, u32[]{:S(2)}) %collective-permute-start.15) | collective-permute-done | bytes 262176 | tf_op jit(solution)/shard_map/ppermute | solution.py:17
  104.1 1.0 add_convert_fusion
  105.1 0.3 fusion.9
  105.5 0.9 copy.30
  106.3 0.3 fusion.10
  106.6 0.9 copy.29
  (42 shorter events, 1.2 us)
Async XLA Ops:
  0.6 1.3 %copy-start = (bf16[128,1024]{1,0:T(8,128)(2,1)S(1)}, bf16[128,1024]{1,0:T(8,128)(2,1)}, u32[]{:S(2)}) copy-start(bf16[128,1024]{1,0:T(8,128)(2,1)} %param.6) | copy-start | bytes 786436
  2.2 10.3 %collective-permute-start = (f32[4,128,128]{2,1,0:T(8,128)S(1)}, f32[4,128,128]{2,1,0:T(8,128)S(1)}, u32[]{:S(2)}, u32[]{:S(2)}) collective-permute-start(f32[4,128,128]{2,1,0:T(8,128)S(1)} %get-tuple-element.16), channel_id=1, source_target_pairs={{0,1},{1,0},{2,3},{3,2},{4,5},{5,4},{6,7},{7,6},{8,9},{9,8},{10,11... | collective-permute-start | bytes 786440 | tf_op jit(solution)/shard_map/ppermute | solution.py:17
  5.3 11.9 %collective-permute-start.4 = (f32[4,128,128]{2,1,0:T(8,128)S(1)}, f32[4,128,128]{2,1,0:T(8,128)S(1)}, u32[]{:S(2)}, u32[]{:S(2)}) collective-permute-start(f32[4,128,128]{2,1,0:T(8,128)S(1)} %get-tuple-element.17), channel_id=1, source_target_pairs={{0,1},{1,0},{2,3},{3,2},{4,5},{5,4},{6,7},{7,6},{8,9},{9,8},{10,11... | collective-permute-start | bytes 786440 | tf_op jit(solution)/shard_map/ppermute | solution.py:17
  17.3 2.9 %collective-permute-start.5 = (f32[4,128,128]{2,1,0:T(8,128)S(1)}, f32[4,128,128]{2,1,0:T(8,128)S(1)}, u32[]{:S(2)}, u32[]{:S(2)}) collective-permute-start(f32[4,128,128]{2,1,0:T(8,128)S(1)} %get-tuple-element.15), channel_id=1, source_target_pairs={{0,4},{4,0},{8,12},{12,8},{1,5},{5,1},{9,13},{13,9},{2,6},{6,2},{1... | collective-permute-start | bytes 786440 | tf_op jit(solution)/shard_map/ppermute | solution.py:17
  17.4 15.3 %collective-permute-start.1 = (f32[4,128,128]{2,1,0:T(8,128)S(1)}, f32[4,128,128]{2,1,0:T(8,128)S(1)}, u32[]{:S(2)}, u32[]{:S(2)}) collective-permute-start(f32[4,128,128]{2,1,0:T(8,128)S(1)} %get-tuple-element.14), channel_id=1, source_target_pairs={{0,2},{1,3},{2,0},{3,1},{4,6},{5,7},{6,4},{7,5},{8,10},{9,11},{10,... | collective-permute-start | bytes 786440 | tf_op jit(solution)/shard_map/ppermute | solution.py:17
  20.2 12.6 %collective-permute-start.6 = (f32[4,128,128]{2,1,0:T(8,128)S(1)}, f32[4,128,128]{2,1,0:T(8,128)S(1)}, u32[]{:S(2)}, u32[]{:S(2)}) collective-permute-start(f32[4,128,128]{2,1,0:T(8,128)S(1)} %add.103), channel_id=1, source_target_pairs={{0,8},{4,12},{8,0},{12,4},{1,9},{5,13},{9,1},{13,5},{2,10},{6,14},... | collective-permute-start | bytes 786440 | tf_op jit(solution)/shard_map/ppermute | solution.py:17
  32.8 1.6 %collective-permute-start.2 = (f32[4,128,128]{2,1,0:T(8,128)S(1)}, f32[4,128,128]{2,1,0:T(8,128)S(1)}, u32[]{:S(2)}, u32[]{:S(2)}) collective-permute-start(f32[4,128,128]{2,1,0:T(8,128)S(1)} %add.98), channel_id=1, source_target_pairs={{0,4},{4,0},{8,12},{12,8},{1,5},{5,1},{9,13},{13,9},{2,6},{6,2},{1... | collective-permute-start | bytes 786440 | tf_op jit(solution)/shard_map/ppermute | solution.py:17
  32.9 15.3 %collective-permute-start.7 = (f32[4,128,128]{2,1,0:T(8,128)S(1)}, f32[4,128,128]{2,1,0:T(8,128)S(1)}, u32[]{:S(2)}, u32[]{:S(2)}) collective-permute-start(f32[4,128,128]{2,1,0:T(8,128)S(1)} %add_select_fusion.5), channel_id=1, source_target_pairs={{0,2},{1,3},{2,0},{3,1},{4,6},{5,7},{6,4},{7,5},{8,10},{9,11},{10,... | collective-permute-start | bytes 786440 | tf_op jit(solution)/shard_map/ppermute | solution.py:17
  33.0 3.6 %copy-start.1 = (bf16[128,1024]{1,0:T(8,128)(2,1)S(1)}, bf16[128,1024]{1,0:T(8,128)(2,1)}, u32[]{:S(2)}) copy-start(bf16[128,1024]{1,0:T(8,128)(2,1)} %param.4) | copy-start | bytes 786436
  33.0 3.6 %copy-start.2 = (bf16[128,1024]{1,0:T(8,128)(2,1)S(1)}, bf16[128,1024]{1,0:T(8,128)(2,1)}, u32[]{:S(2)}) copy-start(bf16[128,1024]{1,0:T(8,128)(2,1)} %param.5) | copy-start | bytes 786436
  35.1 13.2 %collective-permute-start.3 = (f32[4,128,128]{2,1,0:T(8,128)}, f32[4,128,128]{2,1,0:T(8,128)}, u32[]{:S(2)}, u32[]{:S(2)}) collective-permute-start(f32[4,128,128]{2,1,0:T(8,128)} %add.100), channel_id=1, source_target_pairs={{0,8},{4,12},{8,0},{12,4},{1,9},{5,13},{9,1},{13,5},{2,10},{6,14},... | collective-permute-start | bytes 786440 | tf_op jit(solution)/shard_map/ppermute | solution.py:17
  37.0 12.7 %copy-start.6 = (bf16[8,128,128]{2,1,0:T(8,128)(2,1)}, bf16[8,128,128]{2,1,0:T(8,128)(2,1)S(1)}, u32[]{:S(2)}) copy-start(bf16[8,128,128]{2,1,0:T(8,128)(2,1)S(1)} %fusion.8) | copy-start | bytes 786436
  50.0 1.0 copy-start.5
  52.6 9.2 %collective-permute-start.12 = (f32[4,128,128]{2,1,0:T(8,128)S(1)}, f32[4,128,128]{2,1,0:T(8,128)S(1)}, u32[]{:S(2)}, u32[]{:S(2)}) collective-permute-start(f32[4,128,128]{2,1,0:T(8,128)S(1)} %get-tuple-element.13), channel_id=1, source_target_pairs={{0,1},{1,0},{2,3},{3,2},{4,5},{5,4},{6,7},{7,6},{8,9},{9,8},{10,11... | collective-permute-start | bytes 786440 | tf_op jit(solution)/shard_map/ppermute | solution.py:17
  52.7 13.4 %collective-permute-start.8 = (f32[4,128,128]{2,1,0:T(8,128)S(1)}, f32[4,128,128]{2,1,0:T(8,128)S(1)}, u32[]{:S(2)}, u32[]{:S(2)}) collective-permute-start(f32[4,128,128]{2,1,0:T(8,128)S(1)} %get-tuple-element.12), channel_id=1, source_target_pairs={{0,1},{1,0},{2,3},{3,2},{4,5},{5,4},{6,7},{7,6},{8,9},{9,8},{10,11... | collective-permute-start | bytes 786440 | tf_op jit(solution)/shard_map/ppermute | solution.py:17
  66.1 0.7 copy-start.8
  66.8 13.5 %collective-permute-start.9 = (f32[4,128,128]{2,1,0:T(8,128)S(1)}, f32[4,128,128]{2,1,0:T(8,128)S(1)}, u32[]{:S(2)}, u32[]{:S(2)}) collective-permute-start(f32[4,128,128]{2,1,0:T(8,128)S(1)} %get-tuple-element.10), channel_id=1, source_target_pairs={{0,2},{1,3},{2,0},{3,1},{4,6},{5,7},{6,4},{7,5},{8,10},{9,11},{10,... | collective-permute-start | bytes 786440 | tf_op jit(solution)/shard_map/ppermute | solution.py:17
  67.3 0.9 copy-start.7
  67.3 13.2 %collective-permute-start.13 = (f32[4,128,128]{2,1,0:T(8,128)S(1)}, f32[4,128,128]{2,1,0:T(8,128)S(1)}, u32[]{:S(2)}, u32[]{:S(2)}) collective-permute-start(f32[4,128,128]{2,1,0:T(8,128)S(1)} %get-tuple-element.11), channel_id=1, source_target_pairs={{0,4},{4,0},{8,12},{12,8},{1,5},{5,1},{9,13},{13,9},{2,6},{6,2},{1... | collective-permute-start | bytes 786440 | tf_op jit(solution)/shard_map/ppermute | solution.py:17
  80.3 2.3 %collective-permute-start.10 = (f32[4,128,128]{2,1,0:T(8,128)S(1)}, f32[4,128,128]{2,1,0:T(8,128)S(1)}, u32[]{:S(2)}, u32[]{:S(2)}) collective-permute-start(f32[4,128,128]{2,1,0:T(8,128)S(1)} %add.114), channel_id=1, source_target_pairs={{0,4},{4,0},{8,12},{12,8},{1,5},{5,1},{9,13},{13,9},{2,6},{6,2},{1... | collective-permute-start | bytes 786440 | tf_op jit(solution)/shard_map/ppermute | solution.py:17
  80.5 9.2 %collective-permute-start.14 = (f32[4,128,128]{2,1,0:T(8,128)S(1)}, f32[4,128,128]{2,1,0:T(8,128)S(1)}, u32[]{:S(2)}, u32[]{:S(2)}) collective-permute-start(f32[4,128,128]{2,1,0:T(8,128)S(1)} %add.119), channel_id=1, source_target_pairs={{0,8},{4,12},{8,0},{12,4},{1,9},{5,13},{9,1},{13,5},{2,10},{6,14},... | collective-permute-start | bytes 786440 | tf_op jit(solution)/shard_map/ppermute | solution.py:17
  82.6 0.7 copy-start.3
  83.3 11.6 %collective-permute-start.11 = (f32[4,128,128]{2,1,0:T(8,128)S(1)}, f32[4,128,128]{2,1,0:T(8,128)}, u32[]{:S(2)}, u32[]{:S(2)}) collective-permute-start(f32[4,128,128]{2,1,0:T(8,128)S(1)} %add.116), channel_id=1, source_target_pairs={{0,8},{4,12},{8,0},{12,4},{1,9},{5,13},{9,1},{13,5},{2,10},{6,14},... | collective-permute-start | bytes 786440 | tf_op jit(solution)/shard_map/ppermute | solution.py:17
  90.5 13.6 %collective-permute-start.15 = (f32[4,128,128]{2,1,0:T(8,128)}, f32[4,128,128]{2,1,0:T(8,128)}, u32[]{:S(2)}, u32[]{:S(2)}) collective-permute-start(f32[4,128,128]{2,1,0:T(8,128)} %add_select_fusion), channel_id=1, source_target_pairs={{0,2},{1,3},{2,0},{3,1},{4,6},{5,7},{6,4},{7,5},{8,10},{9,11},{10,... | collective-permute-start | bytes 786440 | tf_op jit(solution)/shard_map/ppermute | solution.py:17
  90.8 4.2 %copy-start.4 = (f32[4,128,128]{2,1,0:T(8,128)S(1)}, f32[4,128,128]{2,1,0:T(8,128)}, u32[]{:S(2)}) copy-start(f32[4,128,128]{2,1,0:T(8,128)} %copy-done.3) | copy-start | bytes 786436

commit v3 on v2

--- a/solution.py
+++ b/solution.py
@@ -54,8 +54,12 @@
 
 def chunked_scan(value, backward):
     half = value.shape[0] // 2
-    first = scan_inner_first(value[:half], backward)
-    second = scan_outer_middle(value[half:], backward)
+    if backward:
+        first = scan_outer_middle(value[:half], backward)
+        second = scan_inner_first(value[half:], backward)
+    else:
+        first = scan_inner_first(value[:half], backward)
+        second = scan_outer_middle(value[half:], backward)
     return jnp.concatenate([first, second], axis=0)
 
 

time: 108 us -> 103 us (0.954)
  waiting for transfers between devices: 75.5 us -> 70 us
  local copies, waits for them, and re-layouts: 6.93 us -> 5.1 us
  other arithmetic: 6.21 us -> 7.58 us
    ppermute x16, waiting for transfers between devices: 75.5 us -> 70 us  [swap(): return lax.ppermute(value, axis, [(i, i ^ bit) for i in range(count)])]
    unnamed x22 -> x24, local copies, waits for them, and re-layouts: 6.27 us -> 4.43 us
  transfers between devices with their start and end apart: 16 -> 16, of which waited for: 11 -> 11; matrix products, arithmetic and copies ran while one was open for 5% -> 7% of each run, Pallas kernels for 0% -> 0%
where the time goes in v3:
time: 103 us; the launch traced here: 102 us
  waiting for transfers between devices  70 us (68%)
  starting transfers between devices  15.2 us (15%)
  other arithmetic  7.58 us (7%)
  local copies, waits for them, and re-layouts  5.1 us (5%)
  matrix products  3.52 us (3%)
    ppermute x16, waiting for transfers between devices, swap(): return lax.ppermute(value, axis, [(i, i ^ bit) for i in range(count)])  70 us
    ppermute x16, starting transfers between devices, swap(): return lax.ppermute(value, axis, [(i, i ^ bit) for i in range(count)])  15.2 us
    unnamed x24, local copies, waits for them, and re-layouts  4.43 us
    another operation x4, other arithmetic  3.15 us
  transfers between devices with their start and end apart: 16, of which 11 were waited for; matrix products, arithmetic and copies ran while one was open for 7% of the time, Pallas kernels for 0%

profile of v3, /device:TPU:0, one launch (start us, length us, event | category | flops | bytes accessed | tf_op | source)
XLA Modules:
  0.0 102.3 jit_solution(3370147203646421999)
XLA Ops:
  0.6 1.0 %copy.38 = bf16[16,8,8,128]{3,2,1,0:T(8,128)(2,1)S(1)} copy(bf16[16,8,8,128]{3,1,2,0:T(8,128)(2,1)} %bitcast.110) | data formatting | bytes 524288
  1.7 0.2 copy.11
  1.9 0.2 fusion.21
  2.2 3.1 %collective-permute-start = (f32[4,128,128]{2,1,0:T(8,128)S(1)}, f32[4,128,128]{2,1,0:T(8,128)S(1)}, u32[]{:S(2)}, u32[]{:S(2)}) collective-permute-start(f32[4,128,128]{2,1,0:T(8,128)S(1)} %get-tuple-element.16), channel_id=1, source_target_pairs={{0,1},{1,0},{2,3},{3,2},{4,5},{5,4},{6,7},{7,6},{8,9},{9,8},{10,11... | collective-permute-start | bytes 786440 | tf_op jit(solution)/shard_map/ppermute | solution.py:17
  5.4 7.1 %collective-permute-done = f32[4,128,128]{2,1,0:T(8,128)S(1)} collective-permute-done((f32[4,128,128]{2,1,0:T(8,128)S(1)}, f32[4,128,128]{2,1,0:T(8,128)S(1)}, u32[]{:S(2)}, u32[]{:S(2)}) %collective-permute-start) | collective-permute-done | bytes 262176 | tf_op jit(solution)/shard_map/ppermute | solution.py:17
  12.5 4.8 %collective-permute-done.4 = f32[4,128,128]{2,1,0:T(8,128)S(1)} collective-permute-done((f32[4,128,128]{2,1,0:T(8,128)S(1)}, f32[4,128,128]{2,1,0:T(8,128)S(1)}, u32[]{:S(2)}, u32[]{:S(2)}) %collective-permute-start.4) | collective-permute-done | bytes 262176 | tf_op jit(solution)/shard_map/ppermute | solution.py:17
  17.4 2.8 %collective-permute-start.1 = (f32[4,128,128]{2,1,0:T(8,128)S(1)}, f32[4,128,128]{2,1,0:T(8,128)S(1)}, u32[]{:S(2)}, u32[]{:S(2)}) collective-permute-start(f32[4,128,128]{2,1,0:T(8,128)S(1)} %get-tuple-element.14), channel_id=1, source_target_pairs={{0,2},{1,3},{2,0},{3,1},{4,6},{5,7},{6,4},{7,5},{8,10},{9,11},{10,... | collective-permute-start | bytes 786440 | tf_op jit(solution)/shard_map/ppermute | solution.py:17
  20.2 1.6 %collective-permute-start.6 = (f32[4,128,128]{2,1,0:T(8,128)S(1)}, f32[4,128,128]{2,1,0:T(8,128)S(1)}, u32[]{:S(2)}, u32[]{:S(2)}) collective-permute-start(f32[4,128,128]{2,1,0:T(8,128)S(1)} %add.103), channel_id=1, source_target_pairs={{0,8},{4,12},{8,0},{12,4},{1,9},{5,13},{9,1},{13,5},{2,10},{6,14},... | collective-permute-start | bytes 786440 | tf_op jit(solution)/shard_map/ppermute | solution.py:17
  21.8 10.9 %collective-permute-done.1 = f32[4,128,128]{2,1,0:T(8,128)S(1)} collective-permute-done((f32[4,128,128]{2,1,0:T(8,128)S(1)}, f32[4,128,128]{2,1,0:T(8,128)S(1)}, u32[]{:S(2)}, u32[]{:S(2)}) %collective-permute-start.1) | collective-permute-done | bytes 262176 | tf_op jit(solution)/shard_map/ppermute | solution.py:17
  32.8 0.8 add_select_fusion.5
  33.6 0.7 collective-permute-done.2
  34.4 0.7 add.100
  35.1 1.5 %collective-permute-start.3 = (f32[4,128,128]{2,1,0:T(8,128)}, f32[4,128,128]{2,1,0:T(8,128)}, u32[]{:S(2)}, u32[]{:S(2)}) collective-permute-start(f32[4,128,128]{2,1,0:T(8,128)} %add.100), channel_id=1, source_target_pairs={{0,8},{4,12},{8,0},{12,4},{1,9},{5,13},{9,1},{13,5},{2,10},{6,14},... | collective-permute-start | bytes 786440 | tf_op jit(solution)/shard_map/ppermute | solution.py:17
  36.7 0.3 fusion.8
  37.0 12.1 %collective-permute-done.7 = f32[4,128,128]{2,1,0:T(8,128)S(1)} collective-permute-done((f32[4,128,128]{2,1,0:T(8,128)}, f32[4,128,128]{2,1,0:T(8,128)S(1)}, u32[]{:S(2)}, u32[]{:S(2)}) %collective-permute-start.7) | collective-permute-done | bytes 262176 | tf_op jit(solution)/shard_map/ppermute | solution.py:17
  49.1 1.0 %fusion.16 = bf16[4,128,128]{2,1,0:T(8,128)(2,1)S(1)} fusion(f32[4,128,128]{2,1,0:T(8,128)} %collective-permute-done.3, f32[4,128,128]{2,1,0:T(8,128)S(1)} %collective-permute-done.2, f32[4,128,128]{2,1,0:T(8,128)S(1)} %collective-permute-done.1, f32[4,128,128]{2,1,0:T(8,128)S(1)} %collective-permute-done, pred[]{:T(512)S(6)} %ne.11, pred[]{:T(512)S(6)} %ne.10, ...), kind=kLoop, calls=%fused_computation.40 | loop fusion | flops 524288 | bytes 1179652 | tf_op jit(solution)/shard_map/convert.2
  50.1 0.3 fusion.6
  50.5 0.3 multiply_reduce_fusion
  50.8 0.2 copy.15
  51.1 0.7 copy-done.5
  51.8 0.2 fusion.13
  52.0 0.9 fusion.15
  52.9 0.2 copy.34
  53.1 0.3 convolution_bitcast_fusion.2
  53.5 2.0 %collective-permute-start.8 = (f32[4,128,128]{2,1,0:T(8,128)S(1)}, f32[4,128,128]{2,1,0:T(8,128)S(1)}, u32[]{:S(2)}, u32[]{:S(2)}) collective-permute-start(f32[4,128,128]{2,1,0:T(8,128)S(1)} %get-tuple-element.12), channel_id=1, source_target_pairs={{0,1},{1,0},{2,3},{3,2},{4,5},{5,4},{6,7},{7,6},{8,9},{9,8},{10,11... | collective-permute-start | bytes 786440 | tf_op jit(solution)/shard_map/ppermute | solution.py:17
  55.5 7.2 %collective-permute-done.12 = f32[4,128,128]{2,1,0:T(8,128)S(1)} collective-permute-done((f32[4,128,128]{2,1,0:T(8,128)S(1)}, f32[4,128,128]{2,1,0:T(8,128)S(1)}, u32[]{:S(2)}, u32[]{:S(2)}) %collective-permute-start.12) | collective-permute-done | bytes 262176 | tf_op jit(solution)/shard_map/ppermute | solution.py:17
  62.7 4.3 %collective-permute-done.8 = f32[4,128,128]{2,1,0:T(8,128)S(1)} collective-permute-done((f32[4,128,128]{2,1,0:T(8,128)S(1)}, f32[4,128,128]{2,1,0:T(8,128)S(1)}, u32[]{:S(2)}, u32[]{:S(2)}) %collective-permute-start.8) | collective-permute-done | bytes 262176 | tf_op jit(solution)/shard_map/ppermute | solution.py:17
  67.2 0.3 fusion.12
  67.5 0.5 collective-permute-start.13
  68.0 0.7 collective-permute-done.9
  68.7 1.6 %collective-permute-start.10 = (f32[4,128,128]{2,1,0:T(8,128)S(1)}, f32[4,128,128]{2,1,0:T(8,128)S(1)}, u32[]{:S(2)}, u32[]{:S(2)}) collective-permute-start(f32[4,128,128]{2,1,0:T(8,128)S(1)} %add.113), channel_id=1, source_target_pairs={{0,8},{4,12},{8,0},{12,4},{1,9},{5,13},{9,1},{13,5},{2,10},{6,14},... | collective-permute-start | bytes 786440 | tf_op jit(solution)/shard_map/ppermute | solution.py:17
  70.3 0.2 convolution_bitcast_fusion.3
  70.5 0.3 fusion.11
  70.8 11.6 %collective-permute-done.13 = f32[4,128,128]{2,1,0:T(8,128)S(1)} collective-permute-done((f32[4,128,128]{2,1,0:T(8,128)S(1)}, f32[4,128,128]{2,1,0:T(8,128)S(1)}, u32[]{:S(2)}, u32[]{:S(2)}) %collective-permute-start.13) | collective-permute-done | bytes 262176 | tf_op jit(solution)/shard_map/ppermute | solution.py:17
  82.7 0.7 add_select_fusion.3
  83.5 0.2 fusion.45
  83.7 0.4 collective-permute-done.14
  84.1 0.8 add.122
  84.9 1.5 %collective-permute-start.15 = (f32[4,128,128]{2,1,0:T(8,128)}, f32[4,128,128]{2,1,0:T(8,128)}, u32[]{:S(2)}, u32[]{:S(2)}) collective-permute-start(f32[4,128,128]{2,1,0:T(8,128)} %add.122), channel_id=1, source_target_pairs={{0,8},{4,12},{8,0},{12,4},{1,9},{5,13},{9,1},{13,5},{2,10},{6,14},... | collective-permute-start | bytes 786440 | tf_op jit(solution)/shard_map/ppermute | solution.py:17
  86.5 0.3 convolution_bitcast_fusion
  86.8 0.9 copy.28
  87.6 10.2 %collective-permute-done.11 = f32[4,128,128]{2,1,0:T(8,128)} collective-permute-done((f32[4,128,128]{2,1,0:T(8,128)}, f32[4,128,128]{2,1,0:T(8,128)}, u32[]{:S(2)}, u32[]{:S(2)}) %collective-permute-start.11) | collective-permute-done | bytes 262176 | tf_op jit(solution)/shard_map/ppermute | solution.py:17
  97.9 1.0 add_convert_fusion
  98.9 1.0 %fusion.17 = bf16[4,128,128]{2,1,0:T(8,128)(2,1)S(1)} fusion(f32[4,128,128]{2,1,0:T(8,128)} %collective-permute-done.15, f32[4,128,128]{2,1,0:T(8,128)S(1)} %copy-done.4, f32[4,128,128]{2,1,0:T(8,128)S(1)} %collective-permute-done.13, f32[4,128,128]{2,1,0:T(8,128)S(1)} %copy-done.9, pred[]{:T(512)S(6)} %not.19, pred[]{:T(512)S(6)} %not.18, pred[]{:T(512)S(6)} %not.17, ...), kind=kLoop, calls=%fused_computation.41 | loop fusion | flops 524288 | bytes 1179652 | tf_op jit(solution)/shard_map/convert.1
  99.9 0.3 fusion.9
  100.3 0.9 copy.30
  101.1 0.3 fusion.10
  101.4 0.9 copy.29
  (44 shorter events, 1.1 us)
Async XLA Ops:
  0.6 1.3 %copy-start = (bf16[128,1024]{1,0:T(8,128)(2,1)S(1)}, bf16[128,1024]{1,0:T(8,128)(2,1)}, u32[]{:S(2)}) copy-start(bf16[128,1024]{1,0:T(8,128)(2,1)} %param.6) | copy-start | bytes 786436
  2.2 10.3 %collective-permute-start = (f32[4,128,128]{2,1,0:T(8,128)S(1)}, f32[4,128,128]{2,1,0:T(8,128)S(1)}, u32[]{:S(2)}, u32[]{:S(2)}) collective-permute-start(f32[4,128,128]{2,1,0:T(8,128)S(1)} %get-tuple-element.16), channel_id=1, source_target_pairs={{0,1},{1,0},{2,3},{3,2},{4,5},{5,4},{6,7},{7,6},{8,9},{9,8},{10,11... | collective-permute-start | bytes 786440 | tf_op jit(solution)/shard_map/ppermute | solution.py:17
  5.3 11.9 %collective-permute-start.4 = (f32[4,128,128]{2,1,0:T(8,128)S(1)}, f32[4,128,128]{2,1,0:T(8,128)S(1)}, u32[]{:S(2)}, u32[]{:S(2)}) collective-permute-start(f32[4,128,128]{2,1,0:T(8,128)S(1)} %get-tuple-element.17), channel_id=1, source_target_pairs={{0,1},{1,0},{2,3},{3,2},{4,5},{5,4},{6,7},{7,6},{8,9},{9,8},{10,11... | collective-permute-start | bytes 786440 | tf_op jit(solution)/shard_map/ppermute | solution.py:17
  17.3 2.9 %collective-permute-start.5 = (f32[4,128,128]{2,1,0:T(8,128)S(1)}, f32[4,128,128]{2,1,0:T(8,128)S(1)}, u32[]{:S(2)}, u32[]{:S(2)}) collective-permute-start(f32[4,128,128]{2,1,0:T(8,128)S(1)} %get-tuple-element.15), channel_id=1, source_target_pairs={{0,4},{4,0},{8,12},{12,8},{1,5},{5,1},{9,13},{13,9},{2,6},{6,2},{1... | collective-permute-start | bytes 786440 | tf_op jit(solution)/shard_map/ppermute | solution.py:17
  17.4 15.3 %collective-permute-start.1 = (f32[4,128,128]{2,1,0:T(8,128)S(1)}, f32[4,128,128]{2,1,0:T(8,128)S(1)}, u32[]{:S(2)}, u32[]{:S(2)}) collective-permute-start(f32[4,128,128]{2,1,0:T(8,128)S(1)} %get-tuple-element.14), channel_id=1, source_target_pairs={{0,2},{1,3},{2,0},{3,1},{4,6},{5,7},{6,4},{7,5},{8,10},{9,11},{10,... | collective-permute-start | bytes 786440 | tf_op jit(solution)/shard_map/ppermute | solution.py:17
  20.2 12.6 %collective-permute-start.6 = (f32[4,128,128]{2,1,0:T(8,128)S(1)}, f32[4,128,128]{2,1,0:T(8,128)S(1)}, u32[]{:S(2)}, u32[]{:S(2)}) collective-permute-start(f32[4,128,128]{2,1,0:T(8,128)S(1)} %add.103), channel_id=1, source_target_pairs={{0,8},{4,12},{8,0},{12,4},{1,9},{5,13},{9,1},{13,5},{2,10},{6,14},... | collective-permute-start | bytes 786440 | tf_op jit(solution)/shard_map/ppermute | solution.py:17
  32.8 1.6 %collective-permute-start.2 = (f32[4,128,128]{2,1,0:T(8,128)S(1)}, f32[4,128,128]{2,1,0:T(8,128)S(1)}, u32[]{:S(2)}, u32[]{:S(2)}) collective-permute-start(f32[4,128,128]{2,1,0:T(8,128)S(1)} %add.98), channel_id=1, source_target_pairs={{0,4},{4,0},{8,12},{12,8},{1,5},{5,1},{9,13},{13,9},{2,6},{6,2},{1... | collective-permute-start | bytes 786440 | tf_op jit(solution)/shard_map/ppermute | solution.py:17
  33.6 15.4 %collective-permute-start.7 = (f32[4,128,128]{2,1,0:T(8,128)}, f32[4,128,128]{2,1,0:T(8,128)S(1)}, u32[]{:S(2)}, u32[]{:S(2)}) collective-permute-start(f32[4,128,128]{2,1,0:T(8,128)} %add_select_fusion.5), channel_id=1, source_target_pairs={{0,2},{1,3},{2,0},{3,1},{4,6},{5,7},{6,4},{7,5},{8,10},{9,11},{10,... | collective-permute-start | bytes 786440 | tf_op jit(solution)/shard_map/ppermute | solution.py:17
  33.6 3.0 %copy-start.1 = (bf16[128,1024]{1,0:T(8,128)(2,1)S(1)}, bf16[128,1024]{1,0:T(8,128)(2,1)}, u32[]{:S(2)}) copy-start(bf16[128,1024]{1,0:T(8,128)(2,1)} %param.4) | copy-start | bytes 786436
  33.6 3.0 %copy-start.2 = (bf16[128,1024]{1,0:T(8,128)(2,1)S(1)}, bf16[128,1024]{1,0:T(8,128)(2,1)}, u32[]{:S(2)}) copy-start(bf16[128,1024]{1,0:T(8,128)(2,1)} %param.5) | copy-start | bytes 786436
  35.1 14.0 %collective-permute-start.3 = (f32[4,128,128]{2,1,0:T(8,128)}, f32[4,128,128]{2,1,0:T(8,128)}, u32[]{:S(2)}, u32[]{:S(2)}) collective-permute-start(f32[4,128,128]{2,1,0:T(8,128)} %add.100), channel_id=1, source_target_pairs={{0,8},{4,12},{8,0},{12,4},{1,9},{5,13},{9,1},{13,5},{2,10},{6,14},... | collective-permute-start | bytes 786440 | tf_op jit(solution)/shard_map/ppermute | solution.py:17
  37.0 13.5 %copy-start.6 = (bf16[8,128,128]{2,1,0:T(8,128)(2,1)}, bf16[8,128,128]{2,1,0:T(8,128)(2,1)S(1)}, u32[]{:S(2)}) copy-start(bf16[8,128,128]{2,1,0:T(8,128)(2,1)S(1)} %fusion.8) | copy-start | bytes 786436
  50.8 1.0 copy-start.5
  53.4 9.2 %collective-permute-start.12 = (f32[4,128,128]{2,1,0:T(8,128)S(1)}, f32[4,128,128]{2,1,0:T(8,128)S(1)}, u32[]{:S(2)}, u32[]{:S(2)}) collective-permute-start(f32[4,128,128]{2,1,0:T(8,128)S(1)} %get-tuple-element.13), channel_id=1, source_target_pairs={{0,1},{1,0},{2,3},{3,2},{4,5},{5,4},{6,7},{7,6},{8,9},{9,8},{10,11... | collective-permute-start | bytes 786440 | tf_op jit(solution)/shard_map/ppermute | solution.py:17
  53.5 13.4 %collective-permute-start.8 = (f32[4,128,128]{2,1,0:T(8,128)S(1)}, f32[4,128,128]{2,1,0:T(8,128)S(1)}, u32[]{:S(2)}, u32[]{:S(2)}) collective-permute-start(f32[4,128,128]{2,1,0:T(8,128)S(1)} %get-tuple-element.12), channel_id=1, source_target_pairs={{0,1},{1,0},{2,3},{3,2},{4,5},{5,4},{6,7},{7,6},{8,9},{9,8},{10,11... | collective-permute-start | bytes 786440 | tf_op jit(solution)/shard_map/ppermute | solution.py:17
  62.7 4.4 %copy-start.8 = (f32[4,128,128]{2,1,0:T(8,128)}, f32[4,128,128]{2,1,0:T(8,128)S(1)}, u32[]{:S(2)}) copy-start(f32[4,128,128]{2,1,0:T(8,128)S(1)} %collective-permute-done.12) | copy-start | bytes 786436
  67.1 1.6 %collective-permute-start.9 = (f32[4,128,128]{2,1,0:T(8,128)S(1)}, f32[4,128,128]{2,1,0:T(8,128)S(1)}, u32[]{:S(2)}, u32[]{:S(2)}) collective-permute-start(f32[4,128,128]{2,1,0:T(8,128)S(1)} %get-tuple-element.10), channel_id=1, source_target_pairs={{0,4},{4,0},{8,12},{12,8},{1,5},{5,1},{9,13},{13,9},{2,6},{6,2},{1... | collective-permute-start | bytes 786440 | tf_op jit(solution)/shard_map/ppermute | solution.py:17
  67.5 15.0 %collective-permute-start.13 = (f32[4,128,128]{2,1,0:T(8,128)S(1)}, f32[4,128,128]{2,1,0:T(8,128)S(1)}, u32[]{:S(2)}, u32[]{:S(2)}) collective-permute-start(f32[4,128,128]{2,1,0:T(8,128)S(1)} %get-tuple-element.11), channel_id=1, source_target_pairs={{0,2},{1,3},{2,0},{3,1},{4,6},{5,7},{6,4},{7,5},{8,10},{9,11},{10,... | collective-permute-start | bytes 786440 | tf_op jit(solution)/shard_map/ppermute | solution.py:17
  68.7 14.0 %collective-permute-start.10 = (f32[4,128,128]{2,1,0:T(8,128)S(1)}, f32[4,128,128]{2,1,0:T(8,128)S(1)}, u32[]{:S(2)}, u32[]{:S(2)}) collective-permute-start(f32[4,128,128]{2,1,0:T(8,128)S(1)} %add.113), channel_id=1, source_target_pairs={{0,8},{4,12},{8,0},{12,4},{1,9},{5,13},{9,1},{13,5},{2,10},{6,14},... | collective-permute-start | bytes 786440 | tf_op jit(solution)/shard_map/ppermute | solution.py:17
  82.5 1.0 copy-start.7
  82.5 1.6 %collective-permute-start.14 = (f32[4,128,128]{2,1,0:T(8,128)S(1)}, f32[4,128,128]{2,1,0:T(8,128)S(1)}, u32[]{:S(2)}, u32[]{:S(2)}) collective-permute-start(f32[4,128,128]{2,1,0:T(8,128)S(1)} %add.120), channel_id=1, source_target_pairs={{0,4},{4,0},{8,12},{12,8},{1,5},{5,1},{9,13},{13,9},{2,6},{6,2},{1... | collective-permute-start | bytes 786440 | tf_op jit(solution)/shard_map/ppermute | solution.py:17
  83.4 14.5 %collective-permute-start.11 = (f32[4,128,128]{2,1,0:T(8,128)}, f32[4,128,128]{2,1,0:T(8,128)}, u32[]{:S(2)}, u32[]{:S(2)}) collective-permute-start(f32[4,128,128]{2,1,0:T(8,128)} %add_select_fusion.3), channel_id=1, source_target_pairs={{0,2},{1,3},{2,0},{3,1},{4,6},{5,7},{6,4},{7,5},{8,10},{9,11},{10,... | collective-permute-start | bytes 786440 | tf_op jit(solution)/shard_map/ppermute | solution.py:17
  84.1 0.8 copy-start.3
  84.9 14.0 %collective-permute-start.15 = (f32[4,128,128]{2,1,0:T(8,128)}, f32[4,128,128]{2,1,0:T(8,128)}, u32[]{:S(2)}, u32[]{:S(2)}) collective-permute-start(f32[4,128,128]{2,1,0:T(8,128)} %add.122), channel_id=1, source_target_pairs={{0,8},{4,12},{8,0},{12,4},{1,9},{5,13},{9,1},{13,5},{2,10},{6,14},... | collective-permute-start | bytes 786440 | tf_op jit(solution)/shard_map/ppermute | solution.py:17
  87.6 11.3 %copy-start.4 = (f32[4,128,128]{2,1,0:T(8,128)S(1)}, f32[4,128,128]{2,1,0:T(8,128)}, u32[]{:S(2)}) copy-start(f32[4,128,128]{2,1,0:T(8,128)} %copy-done.3) | copy-start | bytes 786436
  87.6 11.3 %copy-start.9 = (f32[4,128,128]{2,1,0:T(8,128)S(1)}, f32[4,128,128]{2,1,0:T(8,128)}, u32[]{:S(2)}) copy-start(f32[4,128,128]{2,1,0:T(8,128)} %copy-done.8) | copy-start | bytes 786436

commit v4 on v3

v4 whole, which is shorter than its diff:
```python
import jax
import jax.numpy as jnp
from jax import lax
from jax.sharding import PartitionSpec as P

HEADS = 8
HEAD = 128


def axis_bits(axis):
    count = lax.axis_size(axis)
    return [1 << k for k in range(count.bit_length() - 1)]


def swap(value, axis, bit):
    count = lax.axis_size(axis)
    return lax.ppermute(value, axis, [(i, i ^ bit) for i in range(count)])


def partner_counts(axis, bit, backward):
    partner_lower = (lax.axis_index(axis) & bit) != 0
    return jnp.logical_not(partner_lower) if backward else partner_lower


def subcube_step(earlier, total, axis, bit, backward):
    got = swap(total, axis, bit)
    earlier = jnp.where(partner_counts(axis, bit, backward), earlier + got, earlier)
    return lax.optimization_barrier(earlier), total + got


def chunked_scan(value, backward):
    half = value.shape[0] // 2
    group_a, group_b = value[:half], value[half:]
    if backward:
        group_a, group_b = group_b, group_a
    inner_bits, outer_bits = axis_bits("inner"), axis_bits("outer")
    earlier_a, total_a = jnp.zeros_like(group_a), group_a
    earlier_b, total_b = jnp.zeros_like(group_b), group_b
    for bit in inner_bits[:-1]:
        earlier_a, total_a = subcube_step(earlier_a, total_a, "inner", bit, backward)
        earlier_b, total_b = subcube_step(earlier_b, total_b, "inner", bit, backward)
    rows_before, rows_total = jnp.zeros_like(group_b), total_b
    for index, bit in enumerate(outer_bits):
        rows_before, rows_total = subcube_step(rows_before, rows_total, "outer", bit, backward)
        if index == 0 and not backward:
            (earlier_a, total_a), _ = lax.optimization_barrier(((earlier_a, total_a), rows_total))
    for bit in inner_bits[-1:]:
        earlier_a, total_a = subcube_step(earlier_a, total_a, "inner", bit, backward)
    for bit in outer_bits:
        earlier_a, total_a = subcube_step(earlier_a, total_a, "outer", bit, backward)
    if inner_bits:
        top = inner_bits[-1]
        counted = partner_counts("inner", top, backward)
        sent = jnp.where(counted, rows_before, rows_before + total_b)
        earlier_b = rows_before + swap(sent, "inner", top) + earlier_b
    else:
        earlier_b = rows_before
    if backward:
        earlier_a, earlier_b = earlier_b, earlier_a
    return jnp.concatenate([earlier_a, earlier_b], axis=0)


def dot(left, right, contract):
    return lax.dot_general(
        left, right, ((contract[0], contract[1]), ((), ())), preferred_element_type=jnp.float32
    )


def per_device(query, key, value, grad_out):
    rows_dev = query.shape[0]
    scaling = HEAD ** (-0.5)
    line = lax.broadcasted_iota(jnp.int32, (rows_dev, rows_dev), 0)
    column = lax.broadcasted_iota(jnp.int32, (rows_dev, rows_dev), 1)
    causal = line >= column
    heads = [slice(h * HEAD, (h + 1) * HEAD) for h in range(HEADS)]
    queries = [query[:, c] for c in heads]
    keys = [key[:, c] for c in heads]
    values = [value[:, c] for c in heads]
    state = jnp.stack([dot(k, v, ((0,), (0,))) for k, v in zip(keys, values)])
    prior = chunked_scan(state, False)
    prior_half = prior.astype(jnp.bfloat16)
    score_half = [
        jnp.where(causal, dot(q, k, ((1,), (1,))) * scaling, 0.0).astype(jnp.bfloat16)
        for q, k in zip(queries, keys)
    ]
    attended = jnp.concatenate(
        [
            dot(s, v, ((1,), (0,))) + scaling * dot(q, p, ((1,), (0,)))
            for s, v, q, p in zip(score_half, values, queries, prior_half)
        ],
        axis=1,
    )
    inverse = lax.rsqrt(jnp.mean(attended * attended, axis=-1, keepdims=True) + 1e-05)
    normed = attended * inverse
    grads_flat = grad_out.astype(jnp.float32)
    grad_pre = inverse * (
        grads_flat - normed * jnp.mean(grads_flat * normed, axis=-1, keepdims=True)
    )
    grad_half = grad_pre.astype(jnp.bfloat16)
    grads = [grad_half[:, c] for c in heads]
    dscore_half = [
        jnp.where(causal, dot(g, v, ((1,), (1,))), 0.0).astype(jnp.bfloat16)
        for g, v in zip(grads, values)
    ]
    grad_q = jnp.concatenate(
        [
            scaling * (dot(d, k, ((1,), (0,))) + dot(g, p, ((1,), (1,))))
            for d, k, g, p in zip(dscore_half, keys, grads, prior_half)
        ],
        axis=1,
    )
    grad_state = jnp.stack([dot(q, g, ((0,), (0,))) for q, g in zip(queries, grads)])
    later = chunked_scan(grad_state, True)
    later_half = later.astype(jnp.bfloat16)
    grad_k = jnp.concatenate(
        [
            scaling * (dot(d, q, ((0,), (0,))) + dot(v, l, ((1,), (1,))))
            for d, q, v, l in zip(dscore_half, queries, values, later_half)
        ],
        axis=1,
    )
    grad_v = jnp.concatenate(
        [
            dot(s, g, ((0,), (0,))) + scaling * dot(k, l, ((1,), (0,)))
            for s, g, k, l in zip(score_half, grads, keys, later_half)
        ],
        axis=1,
    )
    return (
        normed.astype(jnp.bfloat16),
        grad_q.astype(jnp.bfloat16),
        grad_k.astype(jnp.bfloat16),
        grad_v.astype(jnp.bfloat16),
    )


def solution(mesh):
    placed = P(("grp", "outer", "inner"), None)
    return jax.shard_map(
        per_device,
        mesh=mesh,
        in_specs=(placed, placed, placed, placed),
        out_specs=(placed, placed, placed, placed),
        check_vma=False,
    )
```

time: 103 us -> 109 us (1.058)
  matrix products: 3.52 us -> 20.8 us
  waiting for transfers between devices: 70 us -> 62.5 us
  other arithmetic: 7.58 us -> 2.68 us
    dot_general x12 -> x96, matrix products: 3.52 us -> 20.8 us  [dot(): lax.dot_general(left, right, ((contract[0], contract[1]), ((), ())), pref...]
    ppermute x16, waiting for transfers between devices: 70 us -> 62.5 us  [swap(): return lax.ppermute(value, axis, [(i, i ^ bit) for i in range(count)])]
    another operation x4 -> x6, other arithmetic: 3.15 us -> 0.17 us
    add x8, other arithmetic: 1.81 us -> 0.35 us  [subcube_step(): return (lax.optimization_barrier(earlier), total + got)]
    unnamed x24 -> x31, local copies, waits for them, and re-layouts: 4.43 us -> 5 us
  transfers between devices with their start and end apart: 16 -> 16, of which waited for: 11 -> 9; matrix products, arithmetic and copies ran while one was open for 7% -> 10% of each run, Pallas kernels for 0% -> 0%
where the time goes in v4:
time: 109 us; the launch traced here: 108 us
  waiting for transfers between devices  62.5 us (57%)
  matrix products  20.8 us (19%)
  starting transfers between devices  15.7 us (14%)
  local copies, waits for them, and re-layouts  5 us (5%)
  other arithmetic  2.68 us (2%)
  between operations  1.46 us (1%)
    ppermute x16, waiting for transfers between devices, swap(): return lax.ppermute(value, axis, [(i, i ^ bit) for i in range(count)])  62.5 us
    dot_general x96, matrix products, dot(): lax.dot_general(left, right, ((contract[0], contract[1]), ((), ())), pref...  20.8 us
    ppermute x16, starting transfers between devices, swap(): return lax.ppermute(value, axis, [(i, i ^ bit) for i in range(count)])  15.7 us
    unnamed x31, local copies, waits for them, and re-layouts  5 us
  transfers between devices with their start and end apart: 16, of which 9 were waited for; matrix products, arithmetic and copies ran while one was open for 10% of the time, Pallas kernels for 0%

profile of v4, /device:TPU:0, one launch (start us, length us, event | category | flops | bytes accessed | tf_op | source)
XLA Modules:
  0.0 108.2 jit_solution(3856398113102239413)
XLA Ops:
  0.6 1.0 convolution_bitcast_fusion.16
  1.6 1.0 convolution_bitcast_fusion.17
  2.6 1.0 convolution_bitcast_fusion.18
  3.6 0.9 convolution_bitcast_fusion.19
  4.6 3.1 %collective-permute-start.1 = (f32[4,128,128]{2,1,0:T(8,128)S(1)}, f32[4,128,128]{2,1,0:T(8,128)S(1)}, u32[]{:S(2)}, u32[]{:S(2)}) collective-permute-start(f32[4,128,128]{2,1,0:T(8,128)S(1)} %pad_maximum_fusion.1), channel_id=1, source_target_pairs={{0,1},{1,0},{2,3},{3,2},{4,5},{5,4},{6,7},{7,6},{8,9},{9,8},{10,11... | collective-permute-start | bytes 786440 | tf_op jit(solution)/shard_map/ppermute | solution.py:17
  8.5 0.9 collective-permute-start
  10.2 0.2 fusion.271
  10.4 0.2 fusion.260
  10.7 0.2 fusion.250
  10.9 0.2 fusion.240
  11.1 0.2 fusion.230
  11.5 0.2 fusion.220
  11.7 3.2 %collective-permute-done.1 = f32[4,128,128]{2,1,0:T(8,128)S(1)} collective-permute-done((f32[4,128,128]{2,1,0:T(8,128)S(1)}, f32[4,128,128]{2,1,0:T(8,128)S(1)}, u32[]{:S(2)}, u32[]{:S(2)}) %collective-permute-start.1) | collective-permute-done | bytes 262176 | tf_op jit(solution)/shard_map/ppermute | solution.py:17
  15.1 4.5 %collective-permute-done = f32[4,128,128]{2,1,0:T(8,128)S(1)} collective-permute-done((f32[4,128,128]{2,1,0:T(8,128)S(1)}, f32[4,128,128]{2,1,0:T(8,128)S(1)}, u32[]{:S(2)}, u32[]{:S(2)}) %collective-permute-start) | collective-permute-done | bytes 262176 | tf_op jit(solution)/shard_map/ppermute | solution.py:17
  19.7 2.8 %collective-permute-start.3 = (f32[4,128,128]{2,1,0:T(8,128)S(1)}, f32[4,128,128]{2,1,0:T(8,128)S(1)}, u32[]{:S(2)}, u32[]{:S(2)}) collective-permute-start(f32[4,128,128]{2,1,0:T(8,128)S(1)} %get-tuple-element.7), channel_id=1, source_target_pairs={{0,2},{1,3},{2,0},{3,1},{4,6},{5,7},{6,4},{7,5},{8,10},{9,11},{10,... | collective-permute-start | bytes 786440 | tf_op jit(solution)/shard_map/ppermute | solution.py:17
  22.5 0.2 fusion.210
  22.7 1.6 %collective-permute-start.6 = (f32[4,128,128]{2,1,0:T(8,128)S(1)}, f32[4,128,128]{2,1,0:T(8,128)S(1)}, u32[]{:S(2)}, u32[]{:S(2)}) collective-permute-start(f32[4,128,128]{2,1,0:T(8,128)S(1)} %get-tuple-element.25), channel_id=1, source_target_pairs={{0,8},{4,12},{8,0},{12,4},{1,9},{5,13},{9,1},{13,5},{2,10},{6,14},... | collective-permute-start | bytes 786440 | tf_op jit(solution)/shard_map/ppermute | solution.py:17
  24.3 0.8 fusion.71
  25.1 8.7 %collective-permute-done.3 = f32[4,128,128]{2,1,0:T(8,128)S(1)} collective-permute-done((f32[4,128,128]{2,1,0:T(8,128)S(1)}, f32[4,128,128]{2,1,0:T(8,128)S(1)}, u32[]{:S(2)}, u32[]{:S(2)}) %collective-permute-start.3) | collective-permute-done | bytes 262176 | tf_op jit(solution)/shard_map/ppermute | solution.py:17
  33.9 0.7 add_select_fusion.5
  34.7 0.7 collective-permute-done.4
  35.5 1.4 %collective-permute-start.5 = (f32[4,128,128]{2,1,0:T(8,128)S(1)}, f32[4,128,128]{2,1,0:T(8,128)S(1)}, u32[]{:S(2)}, u32[]{:S(2)}) collective-permute-start(f32[4,128,128]{2,1,0:T(8,128)S(1)} %get-tuple-element.28), channel_id=1, source_target_pairs={{0,8},{4,12},{8,0},{12,4},{1,9},{5,13},{9,1},{13,5},{2,10},{6,14},... | collective-permute-start | bytes 786440 | tf_op jit(solution)/shard_map/ppermute | solution.py:17
  37.3 12.8 %collective-permute-done.7 = f32[4,128,128]{2,1,0:T(8,128)S(1)} collective-permute-done((f32[4,128,128]{2,1,0:T(8,128)}, f32[4,128,128]{2,1,0:T(8,128)S(1)}, u32[]{:S(2)}, u32[]{:S(2)}) %collective-permute-start.7) | collective-permute-done | bytes 262176 | tf_op jit(solution)/shard_map/ppermute | solution.py:17
  52.2 0.2 convolution_bitcast_fusion.12
  52.4 0.2 convolution_bitcast_fusion.13
  52.6 0.2 convolution_bitcast_fusion.14
  52.8 0.2 convolution_bitcast_fusion.15
  53.1 0.2 convolution_bitcast_fusion.4
  53.3 0.2 convolution_bitcast_fusion.5
  53.5 0.2 convolution_bitcast_fusion.6
  53.7 0.2 convolution_bitcast_fusion.7
  57.2 2.1 %collective-permute-start.12 = (f32[4,128,128]{2,1,0:T(8,128)S(1)}, f32[4,128,128]{2,1,0:T(8,128)S(1)}, u32[]{:S(2)}, u32[]{:S(2)}) collective-permute-start(f32[4,128,128]{2,1,0:T(8,128)S(1)} %pad_maximum_fusion.3), channel_id=1, source_target_pairs={{0,1},{1,0},{2,3},{3,2},{4,5},{5,4},{6,7},{7,6},{8,9},{9,8},{10,11... | collective-permute-start | bytes 786440 | tf_op jit(solution)/shard_map/ppermute | solution.py:17
  59.8 0.2 fusion.77
  61.3 5.0 %collective-permute-done.8 = f32[4,128,128]{2,1,0:T(8,128)S(1)} collective-permute-done((f32[4,128,128]{2,1,0:T(8,128)S(1)}, f32[4,128,128]{2,1,0:T(8,128)S(1)}, u32[]{:S(2)}, u32[]{:S(2)}) %collective-permute-start.8) | collective-permute-done | bytes 262176 | tf_op jit(solution)/shard_map/ppermute | solution.py:17
  66.7 4.0 %collective-permute-done.12 = f32[4,128,128]{2,1,0:T(8,128)S(1)} collective-permute-done((f32[4,128,128]{2,1,0:T(8,128)S(1)}, f32[4,128,128]{2,1,0:T(8,128)S(1)}, u32[]{:S(2)}, u32[]{:S(2)}) %collective-permute-start.12) | collective-permute-done | bytes 262176 | tf_op jit(solution)/shard_map/ppermute | solution.py:17
  70.7 0.5 collective-permute-start.13
  71.2 1.4 %collective-permute-start.10 = (f32[4,128,128]{2,1,0:T(8,128)S(1)}, f32[4,128,128]{2,1,0:T(8,128)S(1)}, u32[]{:S(2)}, u32[]{:S(2)}) collective-permute-start(f32[4,128,128]{2,1,0:T(8,128)S(1)} %get-tuple-element.20), channel_id=1, source_target_pairs={{0,8},{4,12},{8,0},{12,4},{1,9},{5,13},{9,1},{13,5},{2,10},{6,14},... | collective-permute-start | bytes 786440 | tf_op jit(solution)/shard_map/ppermute | solution.py:17
  72.9 11.4 %collective-permute-done.13 = f32[4,128,128]{2,1,0:T(8,128)S(1)} collective-permute-done((f32[4,128,128]{2,1,0:T(8,128)S(1)}, f32[4,128,128]{2,1,0:T(8,128)S(1)}, u32[]{:S(2)}, u32[]{:S(2)}) %collective-permute-start.13) | collective-permute-done | bytes 262176 | tf_op jit(solution)/shard_map/ppermute | solution.py:17
  84.4 0.7 add_select_fusion.3
  85.4 0.8 copy.49
  86.3 1.4 %collective-permute-start.15 = (f32[4,128,128]{2,1,0:T(8,128)S(1)}, f32[4,128,128]{2,1,0:T(8,128)S(1)}, u32[]{:S(2)}, u32[]{:S(2)}) collective-permute-start(f32[4,128,128]{2,1,0:T(8,128)S(1)} %get-tuple-element.14), channel_id=1, source_target_pairs={{0,8},{4,12},{8,0},{12,4},{1,9},{5,13},{9,1},{13,5},{2,10},{6,14},... | collective-permute-start | bytes 786440 | tf_op jit(solution)/shard_map/ppermute | solution.py:17
  87.7 12.3 %collective-permute-done.11 = f32[4,128,128]{2,1,0:T(8,128)S(1)} collective-permute-done((f32[4,128,128]{2,1,0:T(8,128)}, f32[4,128,128]{2,1,0:T(8,128)S(1)}, u32[]{:S(2)}, u32[]{:S(2)}) %collective-permute-start.11) | collective-permute-done | bytes 262176 | tf_op jit(solution)/shard_map/ppermute | solution.py:17
  101.7 0.6 copy-done.7
  102.4 0.6 copy-done.5
  103.8 0.6 copy-done.9
  104.5 0.6 copy-done.11
  105.3 0.9 copy.50
  107.5 0.7 copy-done.13
  (138 shorter events, 14.6 us)
Async XLA Ops:
  0.6 2.9 %copy-start = (bf16[128,1024]{1,0:T(8,128)(2,1)S(1)}, bf16[128,1024]{1,0:T(8,128)(2,1)}, u32[]{:S(2)}) copy-start(bf16[128,1024]{1,0:T(8,128)(2,1)} %param.6) | copy-start | bytes 786436
  4.5 3.2 %copy-start.2 = (bf16[128,1024]{1,0:T(8,128)(2,1)S(1)}, bf16[128,1024]{1,0:T(8,128)(2,1)}, u32[]{:S(2)}) copy-start(bf16[128,1024]{1,0:T(8,128)(2,1)} %param.5) | copy-start | bytes 786436
  4.6 10.3 %collective-permute-start.1 = (f32[4,128,128]{2,1,0:T(8,128)S(1)}, f32[4,128,128]{2,1,0:T(8,128)S(1)}, u32[]{:S(2)}, u32[]{:S(2)}) collective-permute-start(f32[4,128,128]{2,1,0:T(8,128)S(1)} %pad_maximum_fusion.1), channel_id=1, source_target_pairs={{0,1},{1,0},{2,3},{3,2},{4,5},{5,4},{6,7},{7,6},{8,9},{9,8},{10,11... | collective-permute-start | bytes 786440 | tf_op jit(solution)/shard_map/ppermute | solution.py:17
  8.4 1.0 copy-start.1
  8.5 11.1 %collective-permute-start = (f32[4,128,128]{2,1,0:T(8,128)S(1)}, f32[4,128,128]{2,1,0:T(8,128)S(1)}, u32[]{:S(2)}, u32[]{:S(2)}) collective-permute-start(f32[4,128,128]{2,1,0:T(8,128)S(1)} %pad_maximum_fusion), channel_id=1, source_target_pairs={{0,1},{1,0},{2,3},{3,2},{4,5},{5,4},{6,7},{7,6},{8,9},{9,8},{10,11... | collective-permute-start | bytes 786440 | tf_op jit(solution)/shard_map/ppermute | solution.py:17
  9.5 0.7 copy-start.6
  9.7 0.7 copy-start.4
  14.9 4.8 %collective-permute-start.2 = (f32[4,128,128]{2,1,0:T(8,128)S(1)}, f32[4,128,128]{2,1,0:T(8,128)S(1)}, u32[]{:S(2)}, u32[]{:S(2)}) collective-permute-start(f32[4,128,128]{2,1,0:T(8,128)S(1)} %get-tuple-element.27), channel_id=1, source_target_pairs={{0,4},{4,0},{8,12},{12,8},{1,5},{5,1},{9,13},{13,9},{2,6},{6,2},{1... | collective-permute-start | bytes 786440 | tf_op jit(solution)/shard_map/ppermute | solution.py:17
  15.1 7.4 %copy-start.8 = (bf16[128,128]{1,0:T(8,128)(2,1)}, bf16[128,128]{1,0:T(8,128)(2,1)S(1)}, u32[]{:S(2)}) copy-start(bf16[128,128]{1,0:T(8,128)(2,1)S(1)} %fusion.70) | copy-start | bytes 98308
  19.7 14.1 %collective-permute-start.3 = (f32[4,128,128]{2,1,0:T(8,128)S(1)}, f32[4,128,128]{2,1,0:T(8,128)S(1)}, u32[]{:S(2)}, u32[]{:S(2)}) collective-permute-start(f32[4,128,128]{2,1,0:T(8,128)S(1)} %get-tuple-element.7), channel_id=1, source_target_pairs={{0,2},{1,3},{2,0},{3,1},{4,6},{5,7},{6,4},{7,5},{8,10},{9,11},{10,... | collective-permute-start | bytes 786440 | tf_op jit(solution)/shard_map/ppermute | solution.py:17
  22.7 11.2 %collective-permute-start.6 = (f32[4,128,128]{2,1,0:T(8,128)S(1)}, f32[4,128,128]{2,1,0:T(8,128)S(1)}, u32[]{:S(2)}, u32[]{:S(2)}) collective-permute-start(f32[4,128,128]{2,1,0:T(8,128)S(1)} %get-tuple-element.25), channel_id=1, source_target_pairs={{0,8},{4,12},{8,0},{12,4},{1,9},{5,13},{9,1},{13,5},{2,10},{6,14},... | collective-permute-start | bytes 786440 | tf_op jit(solution)/shard_map/ppermute | solution.py:17
  33.8 1.6 %collective-permute-start.4 = (f32[4,128,128]{2,1,0:T(8,128)S(1)}, f32[4,128,128]{2,1,0:T(8,128)S(1)}, u32[]{:S(2)}, u32[]{:S(2)}) collective-permute-start(f32[4,128,128]{2,1,0:T(8,128)S(1)} %get-tuple-element.30), channel_id=1, source_target_pairs={{0,4},{4,0},{8,12},{12,8},{1,5},{5,1},{9,13},{13,9},{2,6},{6,2},{1... | collective-permute-start | bytes 786440 | tf_op jit(solution)/shard_map/ppermute | solution.py:17
  34.7 2.2 %copy-start.10 = (bf16[128,128]{1,0:T(8,128)(2,1)S(1)}, bf16[128,128]{1,0:T(8,128)(2,1)}, u32[]{:S(2)}) copy-start(bf16[128,128]{1,0:T(8,128)(2,1)} %fusion.71) | copy-start | bytes 98308
  34.7 15.4 %collective-permute-start.7 = (f32[4,128,128]{2,1,0:T(8,128)}, f32[4,128,128]{2,1,0:T(8,128)S(1)}, u32[]{:S(2)}, u32[]{:S(2)}) collective-permute-start(f32[4,128,128]{2,1,0:T(8,128)} %add_select_fusion.5), channel_id=1, source_target_pairs={{0,2},{1,3},{2,0},{3,1},{4,6},{5,7},{6,4},{7,5},{8,10},{9,11},{10,... | collective-permute-start | bytes 786440 | tf_op jit(solution)/shard_map/ppermute | solution.py:17
  35.4 1.7 %copy-start.3 = (bf16[128,1024]{1,0:T(8,128)(2,1)S(1)}, bf16[128,1024]{1,0:T(8,128)(2,1)}, u32[]{:S(2)}) copy-start(bf16[128,1024]{1,0:T(8,128)(2,1)} %param.7) | copy-start | bytes 786436
  35.5 14.7 %collective-permute-start.5 = (f32[4,128,128]{2,1,0:T(8,128)S(1)}, f32[4,128,128]{2,1,0:T(8,128)S(1)}, u32[]{:S(2)}, u32[]{:S(2)}) collective-permute-start(f32[4,128,128]{2,1,0:T(8,128)S(1)} %get-tuple-element.28), channel_id=1, source_target_pairs={{0,8},{4,12},{8,0},{12,4},{1,9},{5,13},{9,1},{13,5},{2,10},{6,14},... | collective-permute-start | bytes 786440 | tf_op jit(solution)/shard_map/ppermute | solution.py:17
  57.1 9.2 %collective-permute-start.8 = (f32[4,128,128]{2,1,0:T(8,128)S(1)}, f32[4,128,128]{2,1,0:T(8,128)S(1)}, u32[]{:S(2)}, u32[]{:S(2)}) collective-permute-start(f32[4,128,128]{2,1,0:T(8,128)S(1)} %pad_maximum_fusion.2), channel_id=1, source_target_pairs={{0,1},{1,0},{2,3},{3,2},{4,5},{5,4},{6,7},{7,6},{8,9},{9,8},{10,11... | collective-permute-start | bytes 786440 | tf_op jit(solution)/shard_map/ppermute | solution.py:17
  57.2 13.4 %collective-permute-start.12 = (f32[4,128,128]{2,1,0:T(8,128)S(1)}, f32[4,128,128]{2,1,0:T(8,128)S(1)}, u32[]{:S(2)}, u32[]{:S(2)}) collective-permute-start(f32[4,128,128]{2,1,0:T(8,128)S(1)} %pad_maximum_fusion.3), channel_id=1, source_target_pairs={{0,1},{1,0},{2,3},{3,2},{4,5},{5,4},{6,7},{7,6},{8,9},{9,8},{10,11... | collective-permute-start | bytes 786440 | tf_op jit(solution)/shard_map/ppermute | solution.py:17
  61.3 5.1 %copy-start.12 = (bf16[128,1024]{1,0:T(8,128)(2,1)}, bf16[128,1024]{1,0:T(8,128)(2,1)S(1)}, u32[]{:S(2)}) copy-start(bf16[128,1024]{1,0:T(8,128)(2,1)S(1)} %fusion.95) | copy-start | bytes 786436
  66.4 4.8 %collective-permute-start.9 = (f32[4,128,128]{2,1,0:T(8,128)S(1)}, f32[4,128,128]{2,1,0:T(8,128)S(1)}, u32[]{:S(2)}, u32[]{:S(2)}) collective-permute-start(f32[4,128,128]{2,1,0:T(8,128)S(1)} %get-tuple-element.22), channel_id=1, source_target_pairs={{0,4},{4,0},{8,12},{12,8},{1,5},{5,1},{9,13},{13,9},{2,6},{6,2},{1... | collective-permute-start | bytes 786440 | tf_op jit(solution)/shard_map/ppermute | solution.py:17
  70.7 13.6 %collective-permute-start.13 = (f32[4,128,128]{2,1,0:T(8,128)S(1)}, f32[4,128,128]{2,1,0:T(8,128)S(1)}, u32[]{:S(2)}, u32[]{:S(2)}) collective-permute-start(f32[4,128,128]{2,1,0:T(8,128)S(1)} %get-tuple-element.18), channel_id=1, source_target_pairs={{0,2},{1,3},{2,0},{3,1},{4,6},{5,7},{6,4},{7,5},{8,10},{9,11},{10,... | collective-permute-start | bytes 786440 | tf_op jit(solution)/shard_map/ppermute | solution.py:17
  71.2 13.2 %collective-permute-start.10 = (f32[4,128,128]{2,1,0:T(8,128)S(1)}, f32[4,128,128]{2,1,0:T(8,128)S(1)}, u32[]{:S(2)}, u32[]{:S(2)}) collective-permute-start(f32[4,128,128]{2,1,0:T(8,128)S(1)} %get-tuple-element.20), channel_id=1, source_target_pairs={{0,8},{4,12},{8,0},{12,4},{1,9},{5,13},{9,1},{13,5},{2,10},{6,14},... | collective-permute-start | bytes 786440 | tf_op jit(solution)/shard_map/ppermute | solution.py:17
  84.3 1.9 %collective-permute-start.14 = (f32[4,128,128]{2,1,0:T(8,128)S(1)}, f32[4,128,128]{2,1,0:T(8,128)S(1)}, u32[]{:S(2)}, u32[]{:S(2)}) collective-permute-start(f32[4,128,128]{2,1,0:T(8,128)S(1)} %get-tuple-element.16), channel_id=1, source_target_pairs={{0,4},{4,0},{8,12},{12,8},{1,5},{5,1},{9,13},{13,9},{2,6},{6,2},{1... | collective-permute-start | bytes 786440 | tf_op jit(solution)/shard_map/ppermute | solution.py:17
  85.2 14.8 %collective-permute-start.11 = (f32[4,128,128]{2,1,0:T(8,128)}, f32[4,128,128]{2,1,0:T(8,128)S(1)}, u32[]{:S(2)}, u32[]{:S(2)}) collective-permute-start(f32[4,128,128]{2,1,0:T(8,128)} %add_select_fusion.3), channel_id=1, source_target_pairs={{0,2},{1,3},{2,0},{3,1},{4,6},{5,7},{6,4},{7,5},{8,10},{9,11},{10,... | collective-permute-start | bytes 786440 | tf_op jit(solution)/shard_map/ppermute | solution.py:17
  86.3 14.6 %collective-permute-start.15 = (f32[4,128,128]{2,1,0:T(8,128)S(1)}, f32[4,128,128]{2,1,0:T(8,128)S(1)}, u32[]{:S(2)}, u32[]{:S(2)}) collective-permute-start(f32[4,128,128]{2,1,0:T(8,128)S(1)} %get-tuple-element.14), channel_id=1, source_target_pairs={{0,8},{4,12},{8,0},{12,4},{1,9},{5,13},{9,1},{13,5},{2,10},{6,14},... | collective-permute-start | bytes 786440 | tf_op jit(solution)/shard_map/ppermute | solution.py:17
  101.5 0.8 copy-start.7
  102.2 0.8 copy-start.5
  103.6 0.8 copy-start.9
  104.4 0.8 copy-start.11
  107.5 0.7 copy-start.13

commit v5 on v3

--- a/solution.py
+++ b/solution.py
@@ -25,42 +25,39 @@
 def subcube_step(earlier, total, axis, bit, backward):
     got = swap(total, axis, bit)
     earlier = jnp.where(partner_counts(axis, bit, backward), earlier + got, earlier)
-    return earlier, total + got
-
-
-def scan_inner_first(value, backward):
-    earlier, total = jnp.zeros_like(value), value
-    for axis in ("inner", "outer"):
-        for bit in axis_bits(axis):
-            earlier, total = subcube_step(earlier, total, axis, bit, backward)
-    return earlier
-
-
-def scan_outer_middle(value, backward):
-    inner_bits = axis_bits("inner")
-    if not inner_bits:
-        return scan_inner_first(value, backward)
-    earlier, total = jnp.zeros_like(value), value
-    for bit in inner_bits[:-1]:
-        earlier, total = subcube_step(earlier, total, "inner", bit, backward)
-    rows_before, rows_total = jnp.zeros_like(value), total
-    for bit in axis_bits("outer"):
-        rows_before, rows_total = subcube_step(rows_before, rows_total, "outer", bit, backward)
-    top = inner_bits[-1]
-    counted = partner_counts("inner", top, backward)
-    sent = jnp.where(counted, rows_before, rows_before + total)
-    return rows_before + swap(sent, "inner", top) + earlier
+    return lax.optimization_barrier(earlier), total + got
 
 
 def chunked_scan(value, backward):
     half = value.shape[0] // 2
+    group_a, group_b = value[:half], value[half:]
     if backward:
-        first = scan_outer_middle(value[:half], backward)
-        second = scan_inner_first(value[half:], backward)
+        group_a, group_b = group_b, group_a
+    inner_bits, outer_bits = axis_bits("inner"), axis_bits("outer")
+    earlier_a, total_a = jnp.zeros_like(group_a), group_a
+    earlier_b, total_b = jnp.zeros_like(group_b), group_b
+    for bit in inner_bits[:-1]:
+        earlier_a, total_a = subcube_step(earlier_a, total_a, "inner", bit, backward)
+        earlier_b, total_b = subcube_step(earlier_b, total_b, "inner", bit, backward)
+    rows_before, rows_total = jnp.zeros_like(group_b), total_b
+    for index, bit in enumerate(outer_bits):
+        rows_before, rows_total = subcube_step(rows_before, rows_total, "outer", bit, backward)
+        if index == 0 and not backward:
+            (earlier_a, total_a), _ = lax.optimization_barrier(((earlier_a, total_a), rows_total))
+    for bit in inner_bits[-1:]:
+        earlier_a, total_a = subcube_step(earlier_a, total_a, "inner", bit, backward)
+    for bit in outer_bits:
+        earlier_a, total_a = subcube_step(earlier_a, total_a, "outer", bit, backward)
+    if inner_bits:
+        top = inner_bits[-1]
+        counted = partner_counts("inner", top, backward)
+        sent = jnp.where(counted, rows_before, rows_before + total_b)
+        earlier_b = rows_before + swap(sent, "inner", top) + earlier_b
     else:
-        first = scan_inner_first(value[:half], backward)
-        second = scan_outer_middle(value[half:], backward)
-    return jnp.concatenate([first, second], axis=0)
+        earlier_b = rows_before
+    if backward:
+        earlier_a, earlier_b = earlier_b, earlier_a
+    return jnp.concatenate([earlier_a, earlier_b], axis=0)
 
 
 def per_device(query, key, value, grad_out):

time: 103 us -> 104 us (level)
  waiting for transfers between devices: 70 us -> 74 us
  other arithmetic: 7.58 us -> 5.43 us
    ppermute x16, waiting for transfers between devices: 70 us -> 74 us  [swap(): return lax.ppermute(value, axis, [(i, i ^ bit) for i in range(count)])]
    another operation x4 -> x2, other arithmetic: 3.15 us -> 1.04 us
    unnamed x24 -> x12, local copies, waits for them, and re-layouts: 4.43 us -> 4.35 us
  transfers between devices with their start and end apart: 16 -> 16, of which waited for: 11 -> 13; matrix products, arithmetic and copies ran while one was open for 7% -> 4% of each run, Pallas kernels for 0% -> 0%
where the time goes in v5:
time: 104 us
  waiting for transfers between devices  74 us (71%)
  starting transfers between devices  15.3 us (15%)
  other arithmetic  5.43 us (5%)
  local copies, waits for them, and re-layouts  5.01 us (5%)
  matrix products  3.51 us (3%)
    ppermute x16, waiting for transfers between devices, swap(): return lax.ppermute(value, axis, [(i, i ^ bit) for i in range(count)])  74 us
    ppermute x16, starting transfers between devices, swap(): return lax.ppermute(value, axis, [(i, i ^ bit) for i in range(count)])  15.3 us
    unnamed x12, local copies, waits for them, and re-layouts  4.35 us
  transfers between devices with their start and end apart: 16, of which 13 were waited for; matrix products, arithmetic and copies ran while one was open for 4% of the time, Pallas kernels for 0%

profile of v5, /device:TPU:0, one launch (start us, length us, event | category | flops | bytes accessed | tf_op | source)
XLA Modules:
  0.0 104.2 jit_solution(15130802443381448453)
XLA Ops:
  0.6 1.0 copy.38
  1.7 0.2 copy.11
  1.9 0.2 fusion.19
  2.2 3.1 %collective-permute-start = (f32[4,128,128]{2,1,0:T(8,128)S(1)}, f32[4,128,128]{2,1,0:T(8,128)S(1)}, u32[]{:S(2)}, u32[]{:S(2)}) collective-permute-start(f32[4,128,128]{2,1,0:T(8,128)S(1)} %get-tuple-element.20), channel_id=1, source_target_pairs={{0,1},{1,0},{2,3},{3,2},{4,5},{5,4},{6,7},{7,6},{8,9},{9,8},{10,11... | collective-permute-start | bytes 786440 | tf_op jit(solution)/shard_map/ppermute | solution.py:17
  5.4 7.1 %collective-permute-done = f32[4,128,128]{2,1,0:T(8,128)S(1)} collective-permute-done((f32[4,128,128]{2,1,0:T(8,128)S(1)}, f32[4,128,128]{2,1,0:T(8,128)S(1)}, u32[]{:S(2)}, u32[]{:S(2)}) %collective-permute-start) | collective-permute-done | bytes 262176 | tf_op jit(solution)/shard_map/ppermute | solution.py:17
  12.5 4.8 %collective-permute-done.1 = f32[4,128,128]{2,1,0:T(8,128)S(1)} collective-permute-done((f32[4,128,128]{2,1,0:T(8,128)S(1)}, f32[4,128,128]{2,1,0:T(8,128)S(1)}, u32[]{:S(2)}, u32[]{:S(2)}) %collective-permute-start.1) | collective-permute-done | bytes 262176 | tf_op jit(solution)/shard_map/ppermute | solution.py:17
  17.4 1.5 %collective-permute-done.2 = f32[4,128,128]{2,1,0:T(8,128)S(1)} collective-permute-done((f32[4,128,128]{2,1,0:T(8,128)S(1)}, f32[4,128,128]{2,1,0:T(8,128)S(1)}, u32[]{:S(2)}, u32[]{:S(2)}) %collective-permute-start.2) | collective-permute-done | bytes 262176 | tf_op jit(solution)/shard_map/ppermute | solution.py:17
  19.0 2.8 %collective-permute-start.3 = (f32[4,128,128]{2,1,0:T(8,128)S(1)}, f32[4,128,128]{2,1,0:T(8,128)S(1)}, u32[]{:S(2)}, u32[]{:S(2)}) collective-permute-start(f32[4,128,128]{2,1,0:T(8,128)S(1)} %get-tuple-element.7), channel_id=1, source_target_pairs={{0,2},{1,3},{2,0},{3,1},{4,6},{5,7},{6,4},{7,5},{8,10},{9,11},{10,... | collective-permute-start | bytes 786440 | tf_op jit(solution)/shard_map/ppermute | solution.py:17
  21.8 1.5 %collective-permute-start.6 = (f32[4,128,128]{2,1,0:T(8,128)S(1)}, f32[4,128,128]{2,1,0:T(8,128)S(1)}, u32[]{:S(2)}, u32[]{:S(2)}) collective-permute-start(f32[4,128,128]{2,1,0:T(8,128)S(1)} %get-tuple-element.36), channel_id=1, source_target_pairs={{0,8},{4,12},{8,0},{12,4},{1,9},{5,13},{9,1},{13,5},{2,10},{6,14},... | collective-permute-start | bytes 786440 | tf_op jit(solution)/shard_map/ppermute | solution.py:17
  23.3 10.7 %collective-permute-done.3 = f32[4,128,128]{2,1,0:T(8,128)S(1)} collective-permute-done((f32[4,128,128]{2,1,0:T(8,128)S(1)}, f32[4,128,128]{2,1,0:T(8,128)S(1)}, u32[]{:S(2)}, u32[]{:S(2)}) %collective-permute-start.3) | collective-permute-done | bytes 262176 | tf_op jit(solution)/shard_map/ppermute | solution.py:17
  34.3 1.3 %collective-permute-done.4 = f32[4,128,128]{2,1,0:T(8,128)S(1)} collective-permute-done((f32[4,128,128]{2,1,0:T(8,128)S(1)}, f32[4,128,128]{2,1,0:T(8,128)S(1)}, u32[]{:S(2)}, u32[]{:S(2)}) %collective-permute-start.4) | collective-permute-done | bytes 262176 | tf_op jit(solution)/shard_map/ppermute | solution.py:17
  35.7 1.6 %collective-permute-start.5 = (f32[4,128,128]{2,1,0:T(8,128)S(1)}, f32[4,128,128]{2,1,0:T(8,128)S(1)}, u32[]{:S(2)}, u32[]{:S(2)}) collective-permute-start(f32[4,128,128]{2,1,0:T(8,128)S(1)} %get-tuple-element.31), channel_id=1, source_target_pairs={{0,8},{4,12},{8,0},{12,4},{1,9},{5,13},{9,1},{13,5},{2,10},{6,14},... | collective-permute-start | bytes 786440 | tf_op jit(solution)/shard_map/ppermute | solution.py:17
  37.3 0.3 fusion.8
  37.6 11.9 %collective-permute-done.7 = f32[4,128,128]{2,1,0:T(8,128)S(1)} collective-permute-done((f32[4,128,128]{2,1,0:T(8,128)S(1)}, f32[4,128,128]{2,1,0:T(8,128)S(1)}, u32[]{:S(2)}, u32[]{:S(2)}) %collective-permute-start.7) | collective-permute-done | bytes 262176 | tf_op jit(solution)/shard_map/ppermute | solution.py:17
  49.6 0.3 fusion.6
  50.0 0.4 multiply_reduce_fusion
  50.3 0.2 copy.15
  50.5 0.7 copy-done.3
  51.3 0.2 fusion.13
  51.5 0.9 fusion.15
  52.4 0.2 copy.34
  52.6 0.3 convolution_bitcast_fusion.2
  53.0 2.0 %collective-permute-start.8 = (f32[4,128,128]{2,1,0:T(8,128)S(1)}, f32[4,128,128]{2,1,0:T(8,128)}, u32[]{:S(2)}, u32[]{:S(2)}) collective-permute-start(f32[4,128,128]{2,1,0:T(8,128)S(1)} %get-tuple-element.16), channel_id=1, source_target_pairs={{0,1},{1,0},{2,3},{3,2},{4,5},{5,4},{6,7},{7,6},{8,9},{9,8},{10,11... | collective-permute-start | bytes 786440 | tf_op jit(solution)/shard_map/ppermute | solution.py:17
  55.0 0.3 fusion.12
  55.4 6.8 %collective-permute-done.12 = f32[4,128,128]{2,1,0:T(8,128)S(1)} collective-permute-done((f32[4,128,128]{2,1,0:T(8,128)S(1)}, f32[4,128,128]{2,1,0:T(8,128)S(1)}, u32[]{:S(2)}, u32[]{:S(2)}) %collective-permute-start.12) | collective-permute-done | bytes 262176 | tf_op jit(solution)/shard_map/ppermute | solution.py:17
  62.2 4.4 %collective-permute-done.8 = f32[4,128,128]{2,1,0:T(8,128)} collective-permute-done((f32[4,128,128]{2,1,0:T(8,128)S(1)}, f32[4,128,128]{2,1,0:T(8,128)}, u32[]{:S(2)}, u32[]{:S(2)}) %collective-permute-start.8) | collective-permute-done | bytes 262176 | tf_op jit(solution)/shard_map/ppermute | solution.py:17
  66.6 1.0 slice_add_fusion.1
  67.7 0.2 convolution_bitcast_fusion.3
  67.9 0.5 collective-permute-start.13
  68.4 0.3 fusion.11
  68.7 0.5 collective-permute-done.9
  69.2 1.6 %collective-permute-start.10 = (f32[4,128,128]{2,1,0:T(8,128)S(1)}, f32[4,128,128]{2,1,0:T(8,128)S(1)}, u32[]{:S(2)}, u32[]{:S(2)}) collective-permute-start(f32[4,128,128]{2,1,0:T(8,128)S(1)} %get-tuple-element.24), channel_id=1, source_target_pairs={{0,8},{4,12},{8,0},{12,4},{1,9},{5,13},{9,1},{13,5},{2,10},{6,14},... | collective-permute-start | bytes 786440 | tf_op jit(solution)/shard_map/ppermute | solution.py:17
  70.8 12.1 %collective-permute-done.13 = f32[4,128,128]{2,1,0:T(8,128)S(1)} collective-permute-done((f32[4,128,128]{2,1,0:T(8,128)S(1)}, f32[4,128,128]{2,1,0:T(8,128)S(1)}, u32[]{:S(2)}, u32[]{:S(2)}) %collective-permute-start.13) | collective-permute-done | bytes 262176 | tf_op jit(solution)/shard_map/ppermute | solution.py:17
  83.0 0.1 collective-permute-start.14
  83.1 0.2 fusion.49
  83.4 1.2 %collective-permute-done.14 = f32[4,128,128]{2,1,0:T(8,128)S(1)} collective-permute-done((f32[4,128,128]{2,1,0:T(8,128)S(1)}, f32[4,128,128]{2,1,0:T(8,128)S(1)}, u32[]{:S(2)}, u32[]{:S(2)}) %collective-permute-start.14) | collective-permute-done | bytes 262176 | tf_op jit(solution)/shard_map/ppermute | solution.py:17
  84.6 1.6 %collective-permute-start.15 = (f32[4,128,128]{2,1,0:T(8,128)S(1)}, f32[4,128,128]{2,1,0:T(8,128)}, u32[]{:S(2)}, u32[]{:S(2)}) collective-permute-start(f32[4,128,128]{2,1,0:T(8,128)S(1)} %get-tuple-element.27), channel_id=1, source_target_pairs={{0,8},{4,12},{8,0},{12,4},{1,9},{5,13},{9,1},{13,5},{2,10},{6,14},... | collective-permute-start | bytes 786440 | tf_op jit(solution)/shard_map/ppermute | solution.py:17
  86.2 0.7 add_select_fusion.3
  87.0 0.3 convolution_bitcast_fusion
  87.2 0.9 copy.28
  88.1 5.0 %collective-permute-done.15 = f32[4,128,128]{2,1,0:T(8,128)} collective-permute-done((f32[4,128,128]{2,1,0:T(8,128)S(1)}, f32[4,128,128]{2,1,0:T(8,128)}, u32[]{:S(2)}, u32[]{:S(2)}) %collective-permute-start.15) | collective-permute-done | bytes 262176 | tf_op jit(solution)/shard_map/ppermute | solution.py:17
  93.1 1.0 add_select_fusion
  94.1 6.7 %collective-permute-done.11 = f32[4,128,128]{2,1,0:T(8,128)} collective-permute-done((f32[4,128,128]{2,1,0:T(8,128)}, f32[4,128,128]{2,1,0:T(8,128)}, u32[]{:S(2)}, u32[]{:S(2)}) %collective-permute-start.11) | collective-permute-done | bytes 262176 | tf_op jit(solution)/shard_map/ppermute | solution.py:17
  100.9 1.0 add_convert_fusion
  101.9 0.3 fusion.9
  102.2 0.9 copy.30
  103.0 0.3 fusion.10
  103.4 0.9 copy.29
  (34 shorter events, 1.1 us)
Async XLA Ops:
  0.6 1.3 %copy-start = (bf16[128,1024]{1,0:T(8,128)(2,1)S(1)}, bf16[128,1024]{1,0:T(8,128)(2,1)}, u32[]{:S(2)}) copy-start(bf16[128,1024]{1,0:T(8,128)(2,1)} %param.6) | copy-start | bytes 786436
  2.2 10.3 %collective-permute-start = (f32[4,128,128]{2,1,0:T(8,128)S(1)}, f32[4,128,128]{2,1,0:T(8,128)S(1)}, u32[]{:S(2)}, u32[]{:S(2)}) collective-permute-start(f32[4,128,128]{2,1,0:T(8,128)S(1)} %get-tuple-element.20), channel_id=1, source_target_pairs={{0,1},{1,0},{2,3},{3,2},{4,5},{5,4},{6,7},{7,6},{8,9},{9,8},{10,11... | collective-permute-start | bytes 786440 | tf_op jit(solution)/shard_map/ppermute | solution.py:17
  5.3 11.9 %collective-permute-start.1 = (f32[4,128,128]{2,1,0:T(8,128)S(1)}, f32[4,128,128]{2,1,0:T(8,128)S(1)}, u32[]{:S(2)}, u32[]{:S(2)}) collective-permute-start(f32[4,128,128]{2,1,0:T(8,128)S(1)} %get-tuple-element.21), channel_id=1, source_target_pairs={{0,1},{1,0},{2,3},{3,2},{4,5},{5,4},{6,7},{7,6},{8,9},{9,8},{10,11... | collective-permute-start | bytes 786440 | tf_op jit(solution)/shard_map/ppermute | solution.py:17
  17.3 1.6 %collective-permute-start.2 = (f32[4,128,128]{2,1,0:T(8,128)S(1)}, f32[4,128,128]{2,1,0:T(8,128)S(1)}, u32[]{:S(2)}, u32[]{:S(2)}) collective-permute-start(f32[4,128,128]{2,1,0:T(8,128)S(1)} %get-tuple-element.19), channel_id=1, source_target_pairs={{0,4},{4,0},{8,12},{12,8},{1,5},{5,1},{9,13},{13,9},{2,6},{6,2},{1... | collective-permute-start | bytes 786440 | tf_op jit(solution)/shard_map/ppermute | solution.py:17
  19.0 15.0 %collective-permute-start.3 = (f32[4,128,128]{2,1,0:T(8,128)S(1)}, f32[4,128,128]{2,1,0:T(8,128)S(1)}, u32[]{:S(2)}, u32[]{:S(2)}) collective-permute-start(f32[4,128,128]{2,1,0:T(8,128)S(1)} %get-tuple-element.7), channel_id=1, source_target_pairs={{0,2},{1,3},{2,0},{3,1},{4,6},{5,7},{6,4},{7,5},{8,10},{9,11},{10,... | collective-permute-start | bytes 786440 | tf_op jit(solution)/shard_map/ppermute | solution.py:17
  21.8 12.4 %collective-permute-start.6 = (f32[4,128,128]{2,1,0:T(8,128)S(1)}, f32[4,128,128]{2,1,0:T(8,128)S(1)}, u32[]{:S(2)}, u32[]{:S(2)}) collective-permute-start(f32[4,128,128]{2,1,0:T(8,128)S(1)} %get-tuple-element.36), channel_id=1, source_target_pairs={{0,8},{4,12},{8,0},{12,4},{1,9},{5,13},{9,1},{13,5},{2,10},{6,14},... | collective-permute-start | bytes 786440 | tf_op jit(solution)/shard_map/ppermute | solution.py:17
  34.1 1.6 %collective-permute-start.4 = (f32[4,128,128]{2,1,0:T(8,128)S(1)}, f32[4,128,128]{2,1,0:T(8,128)S(1)}, u32[]{:S(2)}, u32[]{:S(2)}) collective-permute-start(f32[4,128,128]{2,1,0:T(8,128)S(1)} %get-tuple-element.33), channel_id=1, source_target_pairs={{0,4},{4,0},{8,12},{12,8},{1,5},{5,1},{9,13},{13,9},{2,6},{6,2},{1... | collective-permute-start | bytes 786440 | tf_op jit(solution)/shard_map/ppermute | solution.py:17
  34.2 3.1 %copy-start.1 = (bf16[128,1024]{1,0:T(8,128)(2,1)S(1)}, bf16[128,1024]{1,0:T(8,128)(2,1)}, u32[]{:S(2)}) copy-start(bf16[128,1024]{1,0:T(8,128)(2,1)} %param.4) | copy-start | bytes 786436
  34.2 3.1 %copy-start.2 = (bf16[128,1024]{1,0:T(8,128)(2,1)S(1)}, bf16[128,1024]{1,0:T(8,128)(2,1)}, u32[]{:S(2)}) copy-start(bf16[128,1024]{1,0:T(8,128)(2,1)} %param.5) | copy-start | bytes 786436
  34.2 15.3 %collective-permute-start.7 = (f32[4,128,128]{2,1,0:T(8,128)S(1)}, f32[4,128,128]{2,1,0:T(8,128)S(1)}, u32[]{:S(2)}, u32[]{:S(2)}) collective-permute-start(f32[4,128,128]{2,1,0:T(8,128)S(1)} %add_select_fusion.5), channel_id=1, source_target_pairs={{0,2},{1,3},{2,0},{3,1},{4,6},{5,7},{6,4},{7,5},{8,10},{9,11},{10,... | collective-permute-start | bytes 786440 | tf_op jit(solution)/shard_map/ppermute | solution.py:17
  35.7 13.8 %collective-permute-start.5 = (f32[4,128,128]{2,1,0:T(8,128)S(1)}, f32[4,128,128]{2,1,0:T(8,128)S(1)}, u32[]{:S(2)}, u32[]{:S(2)}) collective-permute-start(f32[4,128,128]{2,1,0:T(8,128)S(1)} %get-tuple-element.31), channel_id=1, source_target_pairs={{0,8},{4,12},{8,0},{12,4},{1,9},{5,13},{9,1},{13,5},{2,10},{6,14},... | collective-permute-start | bytes 786440 | tf_op jit(solution)/shard_map/ppermute | solution.py:17
  50.3 1.0 copy-start.3
  52.9 9.2 %collective-permute-start.12 = (f32[4,128,128]{2,1,0:T(8,128)S(1)}, f32[4,128,128]{2,1,0:T(8,128)S(1)}, u32[]{:S(2)}, u32[]{:S(2)}) collective-permute-start(f32[4,128,128]{2,1,0:T(8,128)S(1)} %get-tuple-element.17), channel_id=1, source_target_pairs={{0,1},{1,0},{2,3},{3,2},{4,5},{5,4},{6,7},{7,6},{8,9},{9,8},{10,11... | collective-permute-start | bytes 786440 | tf_op jit(solution)/shard_map/ppermute | solution.py:17
  53.0 13.5 %collective-permute-start.8 = (f32[4,128,128]{2,1,0:T(8,128)S(1)}, f32[4,128,128]{2,1,0:T(8,128)}, u32[]{:S(2)}, u32[]{:S(2)}) collective-permute-start(f32[4,128,128]{2,1,0:T(8,128)S(1)} %get-tuple-element.16), channel_id=1, source_target_pairs={{0,1},{1,0},{2,3},{3,2},{4,5},{5,4},{6,7},{7,6},{8,9},{9,8},{10,11... | collective-permute-start | bytes 786440 | tf_op jit(solution)/shard_map/ppermute | solution.py:17
  67.6 1.6 %collective-permute-start.9 = (f32[4,128,128]{2,1,0:T(8,128)S(1)}, f32[4,128,128]{2,1,0:T(8,128)S(1)}, u32[]{:S(2)}, u32[]{:S(2)}) collective-permute-start(f32[4,128,128]{2,1,0:T(8,128)S(1)} %get-tuple-element.14), channel_id=1, source_target_pairs={{0,4},{4,0},{8,12},{12,8},{1,5},{5,1},{9,13},{13,9},{2,6},{6,2},{1... | collective-permute-start | bytes 786440 | tf_op jit(solution)/shard_map/ppermute | solution.py:17
  67.9 15.0 %collective-permute-start.13 = (f32[4,128,128]{2,1,0:T(8,128)S(1)}, f32[4,128,128]{2,1,0:T(8,128)S(1)}, u32[]{:S(2)}, u32[]{:S(2)}) collective-permute-start(f32[4,128,128]{2,1,0:T(8,128)S(1)} %get-tuple-element.15), channel_id=1, source_target_pairs={{0,2},{1,3},{2,0},{3,1},{4,6},{5,7},{6,4},{7,5},{8,10},{9,11},{10,... | collective-permute-start | bytes 786440 | tf_op jit(solution)/shard_map/ppermute | solution.py:17
  69.2 14.1 %collective-permute-start.10 = (f32[4,128,128]{2,1,0:T(8,128)S(1)}, f32[4,128,128]{2,1,0:T(8,128)S(1)}, u32[]{:S(2)}, u32[]{:S(2)}) collective-permute-start(f32[4,128,128]{2,1,0:T(8,128)S(1)} %get-tuple-element.24), channel_id=1, source_target_pairs={{0,8},{4,12},{8,0},{12,4},{1,9},{5,13},{9,1},{13,5},{2,10},{6,14},... | collective-permute-start | bytes 786440 | tf_op jit(solution)/shard_map/ppermute | solution.py:17
  83.0 1.6 %collective-permute-start.14 = (f32[4,128,128]{2,1,0:T(8,128)S(1)}, f32[4,128,128]{2,1,0:T(8,128)S(1)}, u32[]{:S(2)}, u32[]{:S(2)}) collective-permute-start(f32[4,128,128]{2,1,0:T(8,128)S(1)} %get-tuple-element.29), channel_id=1, source_target_pairs={{0,4},{4,0},{8,12},{12,8},{1,5},{5,1},{9,13},{13,9},{2,6},{6,2},{1... | collective-permute-start | bytes 786440 | tf_op jit(solution)/shard_map/ppermute | solution.py:17
  84.6 8.5 %collective-permute-start.15 = (f32[4,128,128]{2,1,0:T(8,128)S(1)}, f32[4,128,128]{2,1,0:T(8,128)}, u32[]{:S(2)}, u32[]{:S(2)}) collective-permute-start(f32[4,128,128]{2,1,0:T(8,128)S(1)} %get-tuple-element.27), channel_id=1, source_target_pairs={{0,8},{4,12},{8,0},{12,4},{1,9},{5,13},{9,1},{13,5},{2,10},{6,14},... | collective-permute-start | bytes 786440 | tf_op jit(solution)/shard_map/ppermute | solution.py:17
  87.0 13.9 %collective-permute-start.11 = (f32[4,128,128]{2,1,0:T(8,128)}, f32[4,128,128]{2,1,0:T(8,128)}, u32[]{:S(2)}, u32[]{:S(2)}) collective-permute-start(f32[4,128,128]{2,1,0:T(8,128)} %add_select_fusion.3), channel_id=1, source_target_pairs={{0,2},{1,3},{2,0},{3,1},{4,6},{5,7},{6,4},{7,5},{8,10},{9,11},{10,... | collective-permute-start | bytes 786440 | tf_op jit(solution)/shard_map/ppermute | solution.py:17

commit v6 on v5

--- a/solution.py
+++ b/solution.py
@@ -25,7 +25,15 @@
 def subcube_step(earlier, total, axis, bit, backward):
     got = swap(total, axis, bit)
     earlier = jnp.where(partner_counts(axis, bit, backward), earlier + got, earlier)
-    return lax.optimization_barrier(earlier), total + got
+    return earlier, total + got
+
+
+def scan_inner_first(value, backward):
+    earlier, total = jnp.zeros_like(value), value
+    for axis in ("inner", "outer"):
+        for bit in axis_bits(axis):
+            earlier, total = subcube_step(earlier, total, axis, bit, backward)
+    return earlier
 
 
 def chunked_scan(value, backward):
@@ -34,27 +42,29 @@
     if backward:
         group_a, group_b = group_b, group_a
     inner_bits, outer_bits = axis_bits("inner"), axis_bits("outer")
-    earlier_a, total_a = jnp.zeros_like(group_a), group_a
+    if not inner_bits:
+        return scan_inner_first(value, backward)
+    earlier_a, total_a = subcube_step(
+        jnp.zeros_like(group_a), group_a, "inner", inner_bits[0], backward
+    )
     earlier_b, total_b = jnp.zeros_like(group_b), group_b
-    for bit in inner_bits[:-1]:
-        earlier_a, total_a = subcube_step(earlier_a, total_a, "inner", bit, backward)
+    for bit in inner_bits[1:]:
         earlier_b, total_b = subcube_step(earlier_b, total_b, "inner", bit, backward)
+    (earlier_b, total_b), _ = lax.optimization_barrier(((earlier_b, total_b), total_a))
     rows_before, rows_total = jnp.zeros_like(group_b), total_b
     for index, bit in enumerate(outer_bits):
         rows_before, rows_total = subcube_step(rows_before, rows_total, "outer", bit, backward)
-        if index == 0 and not backward:
+        if index == 0:
             (earlier_a, total_a), _ = lax.optimization_barrier(((earlier_a, total_a), rows_total))
-    for bit in inner_bits[-1:]:
+    for bit in inner_bits[1:]:
         earlier_a, total_a = subcube_step(earlier_a, total_a, "inner", bit, backward)
     for bit in outer_bits:
         earlier_a, total_a = subcube_step(earlier_a, total_a, "outer", bit, backward)
-    if inner_bits:
-        top = inner_bits[-1]
-        counted = partner_counts("inner", top, backward)
-        sent = jnp.where(counted, rows_before, rows_before + total_b)
-        earlier_b = rows_before + swap(sent, "inner", top) + earlier_b
-    else:
-        earlier_b = rows_before
+    low = inner_bits[0]
+    counted = partner_counts("inner", low, backward)
+    known = rows_before + earlier_b
+    sent = jnp.where(counted, known, known + group_b)
+    earlier_b = known + swap(sent, "inner", low)
     if backward:
         earlier_a, earlier_b = earlier_b, earlier_a
     return jnp.concatenate([earlier_a, earlier_b], axis=0)

time: 104 us -> 97.4 us (0.937)
  waiting for transfers between devices: 74 us -> 66.3 us
    ppermute x16, waiting for transfers between devices: 74 us -> 66.3 us  [swap(): return lax.ppermute(value, axis, [(i, i ^ bit) for i in range(count)])]
    add x8, other arithmetic: 1.41 us -> 2.83 us  [subcube_step(): return (earlier, total + got)]
    unnamed x12 -> x20, local copies, waits for them, and re-layouts: 4.35 us -> 5.21 us
  transfers between devices with their start and end apart: 16 -> 16, of which waited for: 13 -> 12; matrix products, arithmetic and copies ran while one was open for 4% -> 6% of each run, Pallas kernels for 0% -> 0%
where the time goes in v6:
time: 97.4 us; the launch traced here: 97.2 us
  waiting for transfers between devices  66.3 us (68%)
  starting transfers between devices  14.4 us (15%)
  other arithmetic  6.14 us (6%)
  local copies, waits for them, and re-layouts  5.87 us (6%)
  matrix products  3.51 us (4%)
    ppermute x16, waiting for transfers between devices, swap(): return lax.ppermute(value, axis, [(i, i ^ bit) for i in range(count)])  66.3 us
    ppermute x16, starting transfers between devices, swap(): return lax.ppermute(value, axis, [(i, i ^ bit) for i in range(count)])  14.4 us
    unnamed x20, local copies, waits for them, and re-layouts  5.21 us
    add x8, other arithmetic, subcube_step(): return (earlier, total + got)  2.83 us
  transfers between devices with their start and end apart: 16, of which 12 were waited for; matrix products, arithmetic and copies ran while one was open for 6% of the time, Pallas kernels for 0%

profile of v6, /device:TPU:0, one launch (start us, length us, event | category | flops | bytes accessed | tf_op | source)
XLA Modules:
  0.0 97.2 jit_solution(11807019389937659922)
XLA Ops:
  0.6 1.0 %copy.38 = bf16[16,8,8,128]{3,2,1,0:T(8,128)(2,1)S(1)} copy(bf16[16,8,8,128]{3,1,2,0:T(8,128)(2,1)} %bitcast.110) | data formatting | bytes 524288
  1.7 0.2 copy.11
  1.9 0.2 fusion.23
  2.2 3.1 %collective-permute-start = (f32[4,128,128]{2,1,0:T(8,128)S(1)}, f32[4,128,128]{2,1,0:T(8,128)S(1)}, u32[]{:S(2)}, u32[]{:S(2)}) collective-permute-start(f32[4,128,128]{2,1,0:T(8,128)S(1)} %get-tuple-element.36), channel_id=1, source_target_pairs={{0,1},{1,0},{2,3},{3,2},{4,5},{5,4},{6,7},{7,6},{8,9},{9,8},{10,11... | collective-permute-start | bytes 786440 | tf_op jit(solution)/shard_map/ppermute | solution.py:17
  5.3 2.6 %collective-permute-start.1 = (f32[4,128,128]{2,1,0:T(8,128)S(1)}, f32[4,128,128]{2,1,0:T(8,128)S(1)}, u32[]{:S(2)}, u32[]{:S(2)}) collective-permute-start(f32[4,128,128]{2,1,0:T(8,128)S(1)} %get-tuple-element.37), channel_id=1, source_target_pairs={{0,2},{1,3},{2,0},{3,1},{4,6},{5,7},{6,4},{7,5},{8,10},{9,11},{10,... | collective-permute-start | bytes 786440 | tf_op jit(solution)/shard_map/ppermute | solution.py:17
  7.9 9.2 %collective-permute-done = f32[4,128,128]{2,1,0:T(8,128)S(1)} collective-permute-done((f32[4,128,128]{2,1,0:T(8,128)S(1)}, f32[4,128,128]{2,1,0:T(8,128)S(1)}, u32[]{:S(2)}, u32[]{:S(2)}) %collective-permute-start) | collective-permute-done | bytes 262176 | tf_op jit(solution)/shard_map/ppermute | solution.py:17
  17.1 2.5 %collective-permute-done.1 = f32[4,128,128]{2,1,0:T(8,128)S(1)} collective-permute-done((f32[4,128,128]{2,1,0:T(8,128)S(1)}, f32[4,128,128]{2,1,0:T(8,128)S(1)}, u32[]{:S(2)}, u32[]{:S(2)}) %collective-permute-start.1) | collective-permute-done | bytes 262176 | tf_op jit(solution)/shard_map/ppermute | solution.py:17
  19.8 1.5 %collective-permute-done.2 = f32[4,128,128]{2,1,0:T(8,128)S(1)} collective-permute-done((f32[4,128,128]{2,1,0:T(8,128)S(1)}, f32[4,128,128]{2,1,0:T(8,128)S(1)}, u32[]{:S(2)}, u32[]{:S(2)}) %collective-permute-start.2) | collective-permute-done | bytes 262176 | tf_op jit(solution)/shard_map/ppermute | solution.py:17
  21.4 0.4 collective-permute-start.3
  21.8 1.5 %collective-permute-start.6 = (f32[4,128,128]{2,1,0:T(8,128)S(1)}, f32[4,128,128]{2,1,0:T(8,128)S(1)}, u32[]{:S(2)}, u32[]{:S(2)}) collective-permute-start(f32[4,128,128]{2,1,0:T(8,128)S(1)} %add.98), channel_id=1, source_target_pairs={{0,8},{4,12},{8,0},{12,4},{1,9},{5,13},{9,1},{13,5},{2,10},{6,14},... | collective-permute-start | bytes 786440 | tf_op jit(solution)/shard_map/ppermute | solution.py:17
  23.3 12.9 %collective-permute-done.3 = f32[4,128,128]{2,1,0:T(8,128)S(1)} collective-permute-done((f32[4,128,128]{2,1,0:T(8,128)S(1)}, f32[4,128,128]{2,1,0:T(8,128)S(1)}, u32[]{:S(2)}, u32[]{:S(2)}) %collective-permute-start.3) | collective-permute-done | bytes 262176 | tf_op jit(solution)/shard_map/ppermute | solution.py:17
  36.5 1.3 %collective-permute-done.4 = f32[4,128,128]{2,1,0:T(8,128)S(1)} collective-permute-done((f32[4,128,128]{2,1,0:T(8,128)S(1)}, f32[4,128,128]{2,1,0:T(8,128)S(1)}, u32[]{:S(2)}, u32[]{:S(2)}) %collective-permute-start.4) | collective-permute-done | bytes 262176 | tf_op jit(solution)/shard_map/ppermute | solution.py:17
  37.9 1.6 %collective-permute-start.5 = (f32[4,128,128]{2,1,0:T(8,128)S(1)}, f32[4,128,128]{2,1,0:T(8,128)S(1)}, u32[]{:S(2)}, u32[]{:S(2)}) collective-permute-start(f32[4,128,128]{2,1,0:T(8,128)S(1)} %add.102), channel_id=1, source_target_pairs={{0,8},{4,12},{8,0},{12,4},{1,9},{5,13},{9,1},{13,5},{2,10},{6,14},... | collective-permute-start | bytes 786440 | tf_op jit(solution)/shard_map/ppermute | solution.py:17
  39.4 0.3 fusion.8
  39.7 5.4 %collective-permute-done.7 = f32[4,128,128]{2,1,0:T(8,128)S(1)} collective-permute-done((f32[4,128,128]{2,1,0:T(8,128)S(1)}, f32[4,128,128]{2,1,0:T(8,128)S(1)}, u32[]{:S(2)}, u32[]{:S(2)}) %collective-permute-start.7) | collective-permute-done | bytes 262176 | tf_op jit(solution)/shard_map/ppermute | solution.py:17
  45.2 1.1 %collective-permute-done.5 = f32[4,128,128]{2,1,0:T(8,128)S(1)} collective-permute-done((f32[4,128,128]{2,1,0:T(8,128)S(1)}, f32[4,128,128]{2,1,0:T(8,128)S(1)}, u32[]{:S(2)}, u32[]{:S(2)}) %collective-permute-start.5) | collective-permute-done | bytes 262176 | tf_op jit(solution)/shard_map/ppermute | solution.py:17
  46.4 0.3 fusion.6
  46.7 0.4 multiply_reduce_fusion
  47.3 0.7 copy-done.5
  48.0 0.2 fusion.13
  48.2 0.9 fusion.15
  49.3 0.3 convolution_bitcast_fusion.2
  49.7 0.7 collective-permute-start.8
  50.4 1.3 %collective-permute-start.9 = (f32[4,128,128]{2,1,0:T(8,128)S(1)}, f32[4,128,128]{2,1,0:T(8,128)S(1)}, u32[]{:S(2)}, u32[]{:S(2)}) collective-permute-start(f32[4,128,128]{2,1,0:T(8,128)S(1)} %get-tuple-element.33), channel_id=1, source_target_pairs={{0,1},{1,0},{2,3},{3,2},{4,5},{5,4},{6,7},{7,6},{8,9},{9,8},{10,11... | collective-permute-start | bytes 786440 | tf_op jit(solution)/shard_map/ppermute | solution.py:17
  51.7 12.1 %collective-permute-done.8 = f32[4,128,128]{2,1,0:T(8,128)S(1)} collective-permute-done((f32[4,128,128]{2,1,0:T(8,128)S(1)}, f32[4,128,128]{2,1,0:T(8,128)S(1)}, u32[]{:S(2)}, u32[]{:S(2)}) %collective-permute-start.8) | collective-permute-done | bytes 262176 | tf_op jit(solution)/shard_map/ppermute | solution.py:17
  63.7 0.9 slice_add_fusion.2
  64.6 0.2 fusion.49
  64.9 1.3 %collective-permute-done.10 = f32[4,128,128]{2,1,0:T(8,128)S(1)} collective-permute-done((f32[4,128,128]{2,1,0:T(8,128)S(1)}, f32[4,128,128]{2,1,0:T(8,128)S(1)}, u32[]{:S(2)}, u32[]{:S(2)}) %collective-permute-start.10) | collective-permute-done | bytes 262176 | tf_op jit(solution)/shard_map/ppermute | solution.py:17
  66.2 1.6 %collective-permute-start.11 = (f32[4,128,128]{2,1,0:T(8,128)S(1)}, f32[4,128,128]{2,1,0:T(8,128)S(1)}, u32[]{:S(2)}, u32[]{:S(2)}) collective-permute-start(f32[4,128,128]{2,1,0:T(8,128)S(1)} %add.114), channel_id=1, source_target_pairs={{0,8},{4,12},{8,0},{12,4},{1,9},{5,13},{9,1},{13,5},{2,10},{6,14},... | collective-permute-start | bytes 786440 | tf_op jit(solution)/shard_map/ppermute | solution.py:17
  67.8 0.9 collective-permute-start.13
  68.7 0.3 fusion.12
  69.0 0.3 convolution_bitcast_fusion
  69.3 12.6 %collective-permute-done.13 = f32[4,128,128]{2,1,0:T(8,128)S(1)} collective-permute-done((f32[4,128,128]{2,1,0:T(8,128)}, f32[4,128,128]{2,1,0:T(8,128)S(1)}, u32[]{:S(2)}, u32[]{:S(2)}) %collective-permute-start.13) | collective-permute-done | bytes 262176 | tf_op jit(solution)/shard_map/ppermute | solution.py:17
  81.9 1.0 %add.120 = f32[4,128,128]{2,1,0:T(8,128)S(1)} add(f32[4,128,128]{2,1,0:T(8,128)} %get-tuple-element.19, f32[4,128,128]{2,1,0:T(8,128)S(1)} %collective-permute-done.13) | non-fusion elementwise | flops 65536 | bytes 786432 | tf_op jit(solution)/shard_map/add | solution.py:28
  82.9 0.9 add_select_fusion.3
  83.8 0.3 convolution_bitcast_fusion.4
  84.1 0.3 collective-permute-done.14
  84.4 0.7 add.122
  85.2 0.5 collective-permute-start.15
  85.7 0.2 fusion.11
  86.0 0.9 copy.28
  86.8 6.0 %collective-permute-done.12 = f32[4,128,128]{2,1,0:T(8,128)} collective-permute-done((f32[4,128,128]{2,1,0:T(8,128)}, f32[4,128,128]{2,1,0:T(8,128)}, u32[]{:S(2)}, u32[]{:S(2)}) %collective-permute-start.12) | collective-permute-done | bytes 262176 | tf_op jit(solution)/shard_map/ppermute | solution.py:17
  92.8 1.0 %add_convert_fusion = bf16[4,128,128]{2,1,0:T(8,128)(2,1)S(1)} fusion(f32[4,128,128]{2,1,0:T(8,128)S(1)} %copy-done.4, f32[4,128,128]{2,1,0:T(8,128)} %collective-permute-done.12), kind=kLoop, calls=%fused_computation.57 | loop fusion | flops 131072 | bytes 655360 | tf_op jit(solution)/shard_map/convert
  94.0 0.8 copy-done.3
  94.8 0.3 fusion.9
  95.2 0.9 copy.30
  96.0 0.3 fusion.10
  96.3 0.9 copy.29
  (40 shorter events, 1.3 us)
Async XLA Ops:
  0.6 1.3 %copy-start = (bf16[128,1024]{1,0:T(8,128)(2,1)S(1)}, bf16[128,1024]{1,0:T(8,128)(2,1)}, u32[]{:S(2)}) copy-start(bf16[128,1024]{1,0:T(8,128)(2,1)} %param.6) | copy-start | bytes 786436
  2.2 14.9 %collective-permute-start = (f32[4,128,128]{2,1,0:T(8,128)S(1)}, f32[4,128,128]{2,1,0:T(8,128)S(1)}, u32[]{:S(2)}, u32[]{:S(2)}) collective-permute-start(f32[4,128,128]{2,1,0:T(8,128)S(1)} %get-tuple-element.36), channel_id=1, source_target_pairs={{0,1},{1,0},{2,3},{3,2},{4,5},{5,4},{6,7},{7,6},{8,9},{9,8},{10,11... | collective-permute-start | bytes 786440 | tf_op jit(solution)/shard_map/ppermute | solution.py:17
  5.3 14.3 %collective-permute-start.1 = (f32[4,128,128]{2,1,0:T(8,128)S(1)}, f32[4,128,128]{2,1,0:T(8,128)S(1)}, u32[]{:S(2)}, u32[]{:S(2)}) collective-permute-start(f32[4,128,128]{2,1,0:T(8,128)S(1)} %get-tuple-element.37), channel_id=1, source_target_pairs={{0,2},{1,3},{2,0},{3,1},{4,6},{5,7},{6,4},{7,5},{8,10},{9,11},{10,... | collective-permute-start | bytes 786440 | tf_op jit(solution)/shard_map/ppermute | solution.py:17
  19.7 1.6 %collective-permute-start.2 = (f32[4,128,128]{2,1,0:T(8,128)S(1)}, f32[4,128,128]{2,1,0:T(8,128)S(1)}, u32[]{:S(2)}, u32[]{:S(2)}) collective-permute-start(f32[4,128,128]{2,1,0:T(8,128)S(1)} %get-tuple-element.12), channel_id=1, source_target_pairs={{0,4},{4,0},{8,12},{12,8},{1,5},{5,1},{9,13},{13,9},{2,6},{6,2},{1... | collective-permute-start | bytes 786440 | tf_op jit(solution)/shard_map/ppermute | solution.py:17
  21.4 14.8 %collective-permute-start.3 = (f32[4,128,128]{2,1,0:T(8,128)S(1)}, f32[4,128,128]{2,1,0:T(8,128)S(1)}, u32[]{:S(2)}, u32[]{:S(2)}) collective-permute-start(f32[4,128,128]{2,1,0:T(8,128)S(1)} %get-tuple-element.14), channel_id=1, source_target_pairs={{0,2},{1,3},{2,0},{3,1},{4,6},{5,7},{6,4},{7,5},{8,10},{9,11},{10,... | collective-permute-start | bytes 786440 | tf_op jit(solution)/shard_map/ppermute | solution.py:17
  21.8 14.6 %collective-permute-start.6 = (f32[4,128,128]{2,1,0:T(8,128)S(1)}, f32[4,128,128]{2,1,0:T(8,128)S(1)}, u32[]{:S(2)}, u32[]{:S(2)}) collective-permute-start(f32[4,128,128]{2,1,0:T(8,128)S(1)} %add.98), channel_id=1, source_target_pairs={{0,8},{4,12},{8,0},{12,4},{1,9},{5,13},{9,1},{13,5},{2,10},{6,14},... | collective-permute-start | bytes 786440 | tf_op jit(solution)/shard_map/ppermute | solution.py:17
  36.2 1.6 %collective-permute-start.4 = (f32[4,128,128]{2,1,0:T(8,128)S(1)}, f32[4,128,128]{2,1,0:T(8,128)S(1)}, u32[]{:S(2)}, u32[]{:S(2)}) collective-permute-start(f32[4,128,128]{2,1,0:T(8,128)S(1)} %add.100), channel_id=1, source_target_pairs={{0,4},{4,0},{8,12},{12,8},{1,5},{5,1},{9,13},{13,9},{2,6},{6,2},{1... | collective-permute-start | bytes 786440 | tf_op jit(solution)/shard_map/ppermute | solution.py:17
  36.4 8.8 %collective-permute-start.7 = (f32[4,128,128]{2,1,0:T(8,128)S(1)}, f32[4,128,128]{2,1,0:T(8,128)S(1)}, u32[]{:S(2)}, u32[]{:S(2)}) collective-permute-start(f32[4,128,128]{2,1,0:T(8,128)S(1)} %get-tuple-element.26), channel_id=1, source_target_pairs={{0,1},{1,0},{2,3},{3,2},{4,5},{5,4},{6,7},{7,6},{8,9},{9,8},{10,11... | collective-permute-start | bytes 786440 | tf_op jit(solution)/shard_map/ppermute | solution.py:17
  36.5 2.9 %copy-start.1 = (bf16[128,1024]{1,0:T(8,128)(2,1)S(1)}, bf16[128,1024]{1,0:T(8,128)(2,1)}, u32[]{:S(2)}) copy-start(bf16[128,1024]{1,0:T(8,128)(2,1)} %param.4) | copy-start | bytes 786436
  36.5 2.9 %copy-start.2 = (bf16[128,1024]{1,0:T(8,128)(2,1)S(1)}, bf16[128,1024]{1,0:T(8,128)(2,1)}, u32[]{:S(2)}) copy-start(bf16[128,1024]{1,0:T(8,128)(2,1)} %param.5) | copy-start | bytes 786436
  37.9 8.4 %collective-permute-start.5 = (f32[4,128,128]{2,1,0:T(8,128)S(1)}, f32[4,128,128]{2,1,0:T(8,128)S(1)}, u32[]{:S(2)}, u32[]{:S(2)}) collective-permute-start(f32[4,128,128]{2,1,0:T(8,128)S(1)} %add.102), channel_id=1, source_target_pairs={{0,8},{4,12},{8,0},{12,4},{1,9},{5,13},{9,1},{13,5},{2,10},{6,14},... | collective-permute-start | bytes 786440 | tf_op jit(solution)/shard_map/ppermute | solution.py:17
  47.1 1.0 copy-start.5
  49.7 14.1 %collective-permute-start.8 = (f32[4,128,128]{2,1,0:T(8,128)S(1)}, f32[4,128,128]{2,1,0:T(8,128)S(1)}, u32[]{:S(2)}, u32[]{:S(2)}) collective-permute-start(f32[4,128,128]{2,1,0:T(8,128)S(1)} %get-tuple-element.32), channel_id=1, source_target_pairs={{0,2},{1,3},{2,0},{3,1},{4,6},{5,7},{6,4},{7,5},{8,10},{9,11},{10,... | collective-permute-start | bytes 786440 | tf_op jit(solution)/shard_map/ppermute | solution.py:17
  50.4 13.4 %collective-permute-start.9 = (f32[4,128,128]{2,1,0:T(8,128)S(1)}, f32[4,128,128]{2,1,0:T(8,128)S(1)}, u32[]{:S(2)}, u32[]{:S(2)}) collective-permute-start(f32[4,128,128]{2,1,0:T(8,128)S(1)} %get-tuple-element.33), channel_id=1, source_target_pairs={{0,1},{1,0},{2,3},{3,2},{4,5},{5,4},{6,7},{7,6},{8,9},{9,8},{10,11... | collective-permute-start | bytes 786440 | tf_op jit(solution)/shard_map/ppermute | solution.py:17
  64.6 1.5 %collective-permute-start.10 = (f32[4,128,128]{2,1,0:T(8,128)S(1)}, f32[4,128,128]{2,1,0:T(8,128)S(1)}, u32[]{:S(2)}, u32[]{:S(2)}) collective-permute-start(f32[4,128,128]{2,1,0:T(8,128)S(1)} %get-tuple-element.16), channel_id=1, source_target_pairs={{0,4},{4,0},{8,12},{12,8},{1,5},{5,1},{9,13},{13,9},{2,6},{6,2},{1... | collective-permute-start | bytes 786440 | tf_op jit(solution)/shard_map/ppermute | solution.py:17
  66.2 16.7 %collective-permute-start.11 = (f32[4,128,128]{2,1,0:T(8,128)S(1)}, f32[4,128,128]{2,1,0:T(8,128)S(1)}, u32[]{:S(2)}, u32[]{:S(2)}) collective-permute-start(f32[4,128,128]{2,1,0:T(8,128)S(1)} %add.114), channel_id=1, source_target_pairs={{0,8},{4,12},{8,0},{12,4},{1,9},{5,13},{9,1},{13,5},{2,10},{6,14},... | collective-permute-start | bytes 786440 | tf_op jit(solution)/shard_map/ppermute | solution.py:17
  67.8 14.1 %collective-permute-start.13 = (f32[4,128,128]{2,1,0:T(8,128)}, f32[4,128,128]{2,1,0:T(8,128)S(1)}, u32[]{:S(2)}, u32[]{:S(2)}) collective-permute-start(f32[4,128,128]{2,1,0:T(8,128)} %get-tuple-element.19), channel_id=1, source_target_pairs={{0,2},{1,3},{2,0},{3,1},{4,6},{5,7},{6,4},{7,5},{8,10},{9,11},{10,... | collective-permute-start | bytes 786440 | tf_op jit(solution)/shard_map/ppermute | solution.py:17
  69.3 13.7 %copy-start.7 = (f32[4,128,128]{2,1,0:T(8,128)S(1)}, f32[4,128,128]{2,1,0:T(8,128)}, u32[]{:S(2)}) copy-start(f32[4,128,128]{2,1,0:T(8,128)} %get-tuple-element.17) | copy-start | bytes 786436
  82.8 1.6 %collective-permute-start.14 = (f32[4,128,128]{2,1,0:T(8,128)S(1)}, f32[4,128,128]{2,1,0:T(8,128)S(1)}, u32[]{:S(2)}, u32[]{:S(2)}) collective-permute-start(f32[4,128,128]{2,1,0:T(8,128)S(1)} %add.120), channel_id=1, source_target_pairs={{0,4},{4,0},{8,12},{12,8},{1,5},{5,1},{9,13},{13,9},{2,6},{6,2},{1... | collective-permute-start | bytes 786440 | tf_op jit(solution)/shard_map/ppermute | solution.py:17
  83.8 9.0 %collective-permute-start.12 = (f32[4,128,128]{2,1,0:T(8,128)}, f32[4,128,128]{2,1,0:T(8,128)}, u32[]{:S(2)}, u32[]{:S(2)}) collective-permute-start(f32[4,128,128]{2,1,0:T(8,128)} %get-tuple-element.24), channel_id=1, source_target_pairs={{0,1},{1,0},{2,3},{3,2},{4,5},{5,4},{6,7},{7,6},{8,9},{9,8},{10,11... | collective-permute-start | bytes 786440 | tf_op jit(solution)/shard_map/ppermute | solution.py:17
  85.2 8.7 %collective-permute-start.15 = (f32[4,128,128]{2,1,0:T(8,128)}, f32[4,128,128]{2,1,0:T(8,128)S(1)}, u32[]{:S(2)}, u32[]{:S(2)}) collective-permute-start(f32[4,128,128]{2,1,0:T(8,128)} %add.122), channel_id=1, source_target_pairs={{0,8},{4,12},{8,0},{12,4},{1,9},{5,13},{9,1},{13,5},{2,10},{6,14},... | collective-permute-start | bytes 786440 | tf_op jit(solution)/shard_map/ppermute | solution.py:17
  85.9 6.9 %copy-start.4 = (f32[4,128,128]{2,1,0:T(8,128)S(1)}, f32[4,128,128]{2,1,0:T(8,128)}, u32[]{:S(2)}) copy-start(f32[4,128,128]{2,1,0:T(8,128)} %get-tuple-element.25) | copy-start | bytes 786436
  92.8 1.1 %copy-start.6 = (f32[4,128,128]{2,1,0:T(8,128)S(1)}, f32[4,128,128]{2,1,0:T(8,128)}, u32[]{:S(2)}) copy-start(f32[4,128,128]{2,1,0:T(8,128)} %get-tuple-element.18) | copy-start | bytes 786436
  93.9 1.0 copy-start.3

commit v7 on v6

--- a/solution.py
+++ b/solution.py
@@ -50,12 +50,12 @@
     earlier_b, total_b = jnp.zeros_like(group_b), group_b
     for bit in inner_bits[1:]:
         earlier_b, total_b = subcube_step(earlier_b, total_b, "inner", bit, backward)
-    (earlier_b, total_b), _ = lax.optimization_barrier(((earlier_b, total_b), total_a))
+    total_b, _ = lax.optimization_barrier((total_b, total_a))
     rows_before, rows_total = jnp.zeros_like(group_b), total_b
     for index, bit in enumerate(outer_bits):
         rows_before, rows_total = subcube_step(rows_before, rows_total, "outer", bit, backward)
         if index == 0:
-            (earlier_a, total_a), _ = lax.optimization_barrier(((earlier_a, total_a), rows_total))
+            total_a, _ = lax.optimization_barrier((total_a, rows_total))
     for bit in inner_bits[1:]:
         earlier_a, total_a = subcube_step(earlier_a, total_a, "inner", bit, backward)
     for bit in outer_bits:

time: 97.4 us -> 98 us (level)
    unnamed x20 -> x30, local copies, waits for them, and re-layouts: 5.21 us -> 5.06 us
  transfers between devices with their start and end apart: 16 -> 16, of which waited for: 12 -> 13; matrix products, arithmetic and copies ran while one was open for 6% -> 6% of each run, Pallas kernels for 0% -> 0%
where the time goes in v7:
time: 98 us; the launch traced here: 97.8 us
  waiting for transfers between devices  66.3 us (68%)
  starting transfers between devices  14.3 us (15%)
  other arithmetic  7.03 us (7%)
  local copies, waits for them, and re-layouts  5.73 us (6%)
  matrix products  3.51 us (4%)
    ppermute x16, waiting for transfers between devices, swap(): return lax.ppermute(value, axis, [(i, i ^ bit) for i in range(count)])  66.3 us
    ppermute x16, starting transfers between devices, swap(): return lax.ppermute(value, axis, [(i, i ^ bit) for i in range(count)])  14.3 us
    unnamed x30, local copies, waits for them, and re-layouts  5.06 us
    add x8, other arithmetic, subcube_step(): return (earlier, total + got)  2.79 us
    another operation x4, other arithmetic  2.17 us
  transfers between devices with their start and end apart: 16, of which 13 were waited for; matrix products, arithmetic and copies ran while one was open for 6% of the time, Pallas kernels for 0%

profile of v7, /device:TPU:0, one launch (start us, length us, event | category | flops | bytes accessed | tf_op | source)
XLA Modules:
  0.0 97.8 jit_solution(8395804098978477813)
XLA Ops:
  0.6 1.0 %copy.38 = bf16[16,8,8,128]{3,2,1,0:T(8,128)(2,1)S(1)} copy(bf16[16,8,8,128]{3,1,2,0:T(8,128)(2,1)} %bitcast.110) | data formatting | bytes 524288
  1.7 0.2 copy.11
  2.2 3.1 %collective-permute-start = (f32[4,128,128]{2,1,0:T(8,128)S(1)}, f32[4,128,128]{2,1,0:T(8,128)S(1)}, u32[]{:S(2)}, u32[]{:S(2)}) collective-permute-start(f32[4,128,128]{2,1,0:T(8,128)S(1)} %get-tuple-element.28), channel_id=1, source_target_pairs={{0,1},{1,0},{2,3},{3,2},{4,5},{5,4},{6,7},{7,6},{8,9},{9,8},{10,11... | collective-permute-start | bytes 786440 | tf_op jit(solution)/shard_map/ppermute | solution.py:17
  5.3 2.6 %collective-permute-start.1 = (f32[4,128,128]{2,1,0:T(8,128)S(1)}, f32[4,128,128]{2,1,0:T(8,128)S(1)}, u32[]{:S(2)}, u32[]{:S(2)}) collective-permute-start(f32[4,128,128]{2,1,0:T(8,128)S(1)} %get-tuple-element.29), channel_id=1, source_target_pairs={{0,2},{1,3},{2,0},{3,1},{4,6},{5,7},{6,4},{7,5},{8,10},{9,11},{10,... | collective-permute-start | bytes 786440 | tf_op jit(solution)/shard_map/ppermute | solution.py:17
  7.9 9.2 %collective-permute-done = f32[4,128,128]{2,1,0:T(8,128)S(1)} collective-permute-done((f32[4,128,128]{2,1,0:T(8,128)S(1)}, f32[4,128,128]{2,1,0:T(8,128)S(1)}, u32[]{:S(2)}, u32[]{:S(2)}) %collective-permute-start) | collective-permute-done | bytes 262176 | tf_op jit(solution)/shard_map/ppermute | solution.py:17
  17.1 2.5 %collective-permute-done.1 = f32[4,128,128]{2,1,0:T(8,128)S(1)} collective-permute-done((f32[4,128,128]{2,1,0:T(8,128)S(1)}, f32[4,128,128]{2,1,0:T(8,128)S(1)}, u32[]{:S(2)}, u32[]{:S(2)}) %collective-permute-start.1) | collective-permute-done | bytes 262176 | tf_op jit(solution)/shard_map/ppermute | solution.py:17
  19.8 1.5 %collective-permute-done.2 = f32[4,128,128]{2,1,0:T(8,128)S(1)} collective-permute-done((f32[4,128,128]{2,1,0:T(8,128)S(1)}, f32[4,128,128]{2,1,0:T(8,128)S(1)}, u32[]{:S(2)}, u32[]{:S(2)}) %collective-permute-start.2) | collective-permute-done | bytes 262176 | tf_op jit(solution)/shard_map/ppermute | solution.py:17
  21.3 0.4 collective-permute-start.3
  21.7 1.5 %collective-permute-start.6 = (f32[4,128,128]{2,1,0:T(8,128)S(1)}, f32[4,128,128]{2,1,0:T(8,128)S(1)}, u32[]{:S(2)}, u32[]{:S(2)}) collective-permute-start(f32[4,128,128]{2,1,0:T(8,128)S(1)} %add.98), channel_id=1, source_target_pairs={{0,8},{4,12},{8,0},{12,4},{1,9},{5,13},{9,1},{13,5},{2,10},{6,14},... | collective-permute-start | bytes 786440 | tf_op jit(solution)/shard_map/ppermute | solution.py:17
  23.2 12.9 %collective-permute-done.3 = f32[4,128,128]{2,1,0:T(8,128)S(1)} collective-permute-done((f32[4,128,128]{2,1,0:T(8,128)S(1)}, f32[4,128,128]{2,1,0:T(8,128)S(1)}, u32[]{:S(2)}, u32[]{:S(2)}) %collective-permute-start.3) | collective-permute-done | bytes 262176 | tf_op jit(solution)/shard_map/ppermute | solution.py:17
  36.5 1.3 %collective-permute-done.4 = f32[4,128,128]{2,1,0:T(8,128)S(1)} collective-permute-done((f32[4,128,128]{2,1,0:T(8,128)S(1)}, f32[4,128,128]{2,1,0:T(8,128)S(1)}, u32[]{:S(2)}, u32[]{:S(2)}) %collective-permute-start.4) | collective-permute-done | bytes 262176 | tf_op jit(solution)/shard_map/ppermute | solution.py:17
  37.8 1.6 %collective-permute-start.5 = (f32[4,128,128]{2,1,0:T(8,128)S(1)}, f32[4,128,128]{2,1,0:T(8,128)S(1)}, u32[]{:S(2)}, u32[]{:S(2)}) collective-permute-start(f32[4,128,128]{2,1,0:T(8,128)S(1)} %add.102), channel_id=1, source_target_pairs={{0,8},{4,12},{8,0},{12,4},{1,9},{5,13},{9,1},{13,5},{2,10},{6,14},... | collective-permute-start | bytes 786440 | tf_op jit(solution)/shard_map/ppermute | solution.py:17
  39.4 0.3 fusion.8
  39.7 5.4 %collective-permute-done.7 = f32[4,128,128]{2,1,0:T(8,128)S(1)} collective-permute-done((f32[4,128,128]{2,1,0:T(8,128)S(1)}, f32[4,128,128]{2,1,0:T(8,128)S(1)}, u32[]{:S(2)}, u32[]{:S(2)}) %collective-permute-start.7) | collective-permute-done | bytes 262176 | tf_op jit(solution)/shard_map/ppermute | solution.py:17
  45.1 1.1 %collective-permute-done.5 = f32[4,128,128]{2,1,0:T(8,128)S(1)} collective-permute-done((f32[4,128,128]{2,1,0:T(8,128)S(1)}, f32[4,128,128]{2,1,0:T(8,128)S(1)}, u32[]{:S(2)}, u32[]{:S(2)}) %collective-permute-start.5) | collective-permute-done | bytes 262176 | tf_op jit(solution)/shard_map/ppermute | solution.py:17
  46.3 0.3 fusion.6
  46.6 0.4 multiply_reduce_fusion
  47.2 0.7 copy-done.7
  48.0 0.2 fusion.13
  48.2 0.9 fusion.15
  49.2 0.3 convolution_bitcast_fusion.2
  49.6 0.7 collective-permute-start.8
  50.3 1.2 %collective-permute-start.9 = (f32[4,128,128]{2,1,0:T(8,128)S(1)}, f32[4,128,128]{2,1,0:T(8,128)S(1)}, u32[]{:S(2)}, u32[]{:S(2)}) collective-permute-start(f32[4,128,128]{2,1,0:T(8,128)S(1)} %get-tuple-element.25), channel_id=1, source_target_pairs={{0,1},{1,0},{2,3},{3,2},{4,5},{5,4},{6,7},{7,6},{8,9},{9,8},{10,11... | collective-permute-start | bytes 786440 | tf_op jit(solution)/shard_map/ppermute | solution.py:17
  51.6 12.1 %collective-permute-done.8 = f32[4,128,128]{2,1,0:T(8,128)S(1)} collective-permute-done((f32[4,128,128]{2,1,0:T(8,128)S(1)}, f32[4,128,128]{2,1,0:T(8,128)S(1)}, u32[]{:S(2)}, u32[]{:S(2)}) %collective-permute-start.8) | collective-permute-done | bytes 262176 | tf_op jit(solution)/shard_map/ppermute | solution.py:17
  63.7 0.8 slice_add_fusion.2
  64.6 0.2 fusion.49
  64.8 1.3 %collective-permute-done.10 = f32[4,128,128]{2,1,0:T(8,128)S(1)} collective-permute-done((f32[4,128,128]{2,1,0:T(8,128)S(1)}, f32[4,128,128]{2,1,0:T(8,128)S(1)}, u32[]{:S(2)}, u32[]{:S(2)}) %collective-permute-start.10) | collective-permute-done | bytes 262176 | tf_op jit(solution)/shard_map/ppermute | solution.py:17
  66.1 0.7 copy-done.5
  66.8 1.5 %collective-permute-start.11 = (f32[4,128,128]{2,1,0:T(8,128)S(1)}, f32[4,128,128]{2,1,0:T(8,128)S(1)}, u32[]{:S(2)}, u32[]{:S(2)}) collective-permute-start(f32[4,128,128]{2,1,0:T(8,128)S(1)} %add.114), channel_id=1, source_target_pairs={{0,8},{4,12},{8,0},{12,4},{1,9},{5,13},{9,1},{13,5},{2,10},{6,14},... | collective-permute-start | bytes 786440 | tf_op jit(solution)/shard_map/ppermute | solution.py:17
  68.3 0.8 collective-permute-start.13
  69.1 0.3 fusion.12
  69.4 0.3 convolution_bitcast_fusion
  69.7 12.6 %collective-permute-done.13 = f32[4,128,128]{2,1,0:T(8,128)S(1)} collective-permute-done((f32[4,128,128]{2,1,0:T(8,128)}, f32[4,128,128]{2,1,0:T(8,128)S(1)}, u32[]{:S(2)}, u32[]{:S(2)}) %collective-permute-start.13) | collective-permute-done | bytes 262176 | tf_op jit(solution)/shard_map/ppermute | solution.py:17
  82.3 1.0 %add.120 = f32[4,128,128]{2,1,0:T(8,128)S(1)} add(f32[4,128,128]{2,1,0:T(8,128)} %get-tuple-element.11, f32[4,128,128]{2,1,0:T(8,128)S(1)} %collective-permute-done.13) | non-fusion elementwise | flops 65536 | bytes 786432 | tf_op jit(solution)/shard_map/add | solution.py:28
  83.4 0.9 add_select_fusion.3
  84.3 0.3 convolution_bitcast_fusion.4
  84.6 0.3 collective-permute-done.14
  84.9 0.8 add.122
  85.7 0.5 collective-permute-start.15
  86.2 0.2 fusion.11
  86.5 0.9 copy.28
  87.3 6.0 %collective-permute-done.12 = f32[4,128,128]{2,1,0:T(8,128)} collective-permute-done((f32[4,128,128]{2,1,0:T(8,128)}, f32[4,128,128]{2,1,0:T(8,128)}, u32[]{:S(2)}, u32[]{:S(2)}) %collective-permute-start.12) | collective-permute-done | bytes 262176 | tf_op jit(solution)/shard_map/ppermute | solution.py:17
  93.3 1.0 %add_convert_fusion = bf16[4,128,128]{2,1,0:T(8,128)(2,1)S(1)} fusion(f32[4,128,128]{2,1,0:T(8,128)S(1)} %copy-done.8, f32[4,128,128]{2,1,0:T(8,128)} %collective-permute-done.12), kind=kLoop, calls=%fused_computation.57 | loop fusion | flops 131072 | bytes 655360 | tf_op jit(solution)/shard_map/convert
  94.4 1.0 %fusion.19 = bf16[4,128,128]{2,1,0:T(8,128)(2,1)S(1)} fusion(f32[4,128,128]{2,1,0:T(8,128)} %collective-permute-done.15, f32[4,128,128]{2,1,0:T(8,128)S(1)} %copy-done.4, f32[4,128,128]{2,1,0:T(8,128)S(1)} %collective-permute-done.13, f32[4,128,128]{2,1,0:T(8,128)S(1)} %copy-done.10, pred[]{:T(512)S(6)} %not.19, pred[]{:T(512)S(6)} %not.18, pred[]{:T(512)S(6)} %not.17, ...), kind=kLoop, calls=%fused_computation.43 | loop fusion | flops 524288 | bytes 1179652 | tf_op jit(solution)/shard_map/convert.1
  95.4 0.3 fusion.9
  95.8 0.9 copy.30
  96.6 0.3 fusion.10
  96.9 0.9 copy.29
  (50 shorter events, 1.5 us)
Async XLA Ops:
  0.6 1.3 %copy-start = (bf16[128,1024]{1,0:T(8,128)(2,1)S(1)}, bf16[128,1024]{1,0:T(8,128)(2,1)}, u32[]{:S(2)}) copy-start(bf16[128,1024]{1,0:T(8,128)(2,1)} %param.6) | copy-start | bytes 786436
  2.2 14.9 %collective-permute-start = (f32[4,128,128]{2,1,0:T(8,128)S(1)}, f32[4,128,128]{2,1,0:T(8,128)S(1)}, u32[]{:S(2)}, u32[]{:S(2)}) collective-permute-start(f32[4,128,128]{2,1,0:T(8,128)S(1)} %get-tuple-element.28), channel_id=1, source_target_pairs={{0,1},{1,0},{2,3},{3,2},{4,5},{5,4},{6,7},{7,6},{8,9},{9,8},{10,11... | collective-permute-start | bytes 786440 | tf_op jit(solution)/shard_map/ppermute | solution.py:17
  5.3 14.3 %collective-permute-start.1 = (f32[4,128,128]{2,1,0:T(8,128)S(1)}, f32[4,128,128]{2,1,0:T(8,128)S(1)}, u32[]{:S(2)}, u32[]{:S(2)}) collective-permute-start(f32[4,128,128]{2,1,0:T(8,128)S(1)} %get-tuple-element.29), channel_id=1, source_target_pairs={{0,2},{1,3},{2,0},{3,1},{4,6},{5,7},{6,4},{7,5},{8,10},{9,11},{10,... | collective-permute-start | bytes 786440 | tf_op jit(solution)/shard_map/ppermute | solution.py:17
  19.7 1.6 %collective-permute-start.2 = (f32[4,128,128]{2,1,0:T(8,128)S(1)}, f32[4,128,128]{2,1,0:T(8,128)S(1)}, u32[]{:S(2)}, u32[]{:S(2)}) collective-permute-start(f32[4,128,128]{2,1,0:T(8,128)S(1)} %get-tuple-element.8), channel_id=1, source_target_pairs={{0,4},{4,0},{8,12},{12,8},{1,5},{5,1},{9,13},{13,9},{2,6},{6,2},{1... | collective-permute-start | bytes 786440 | tf_op jit(solution)/shard_map/ppermute | solution.py:17
  21.3 14.8 %collective-permute-start.3 = (f32[4,128,128]{2,1,0:T(8,128)S(1)}, f32[4,128,128]{2,1,0:T(8,128)S(1)}, u32[]{:S(2)}, u32[]{:S(2)}) collective-permute-start(f32[4,128,128]{2,1,0:T(8,128)S(1)} %get-tuple-element.9), channel_id=1, source_target_pairs={{0,2},{1,3},{2,0},{3,1},{4,6},{5,7},{6,4},{7,5},{8,10},{9,11},{10,... | collective-permute-start | bytes 786440 | tf_op jit(solution)/shard_map/ppermute | solution.py:17
  21.7 14.6 %collective-permute-start.6 = (f32[4,128,128]{2,1,0:T(8,128)S(1)}, f32[4,128,128]{2,1,0:T(8,128)S(1)}, u32[]{:S(2)}, u32[]{:S(2)}) collective-permute-start(f32[4,128,128]{2,1,0:T(8,128)S(1)} %add.98), channel_id=1, source_target_pairs={{0,8},{4,12},{8,0},{12,4},{1,9},{5,13},{9,1},{13,5},{2,10},{6,14},... | collective-permute-start | bytes 786440 | tf_op jit(solution)/shard_map/ppermute | solution.py:17
  36.2 1.6 %collective-permute-start.4 = (f32[4,128,128]{2,1,0:T(8,128)S(1)}, f32[4,128,128]{2,1,0:T(8,128)S(1)}, u32[]{:S(2)}, u32[]{:S(2)}) collective-permute-start(f32[4,128,128]{2,1,0:T(8,128)S(1)} %add.100), channel_id=1, source_target_pairs={{0,4},{4,0},{8,12},{12,8},{1,5},{5,1},{9,13},{13,9},{2,6},{6,2},{1... | collective-permute-start | bytes 786440 | tf_op jit(solution)/shard_map/ppermute | solution.py:17
  36.4 8.8 %collective-permute-start.7 = (f32[4,128,128]{2,1,0:T(8,128)S(1)}, f32[4,128,128]{2,1,0:T(8,128)S(1)}, u32[]{:S(2)}, u32[]{:S(2)}) collective-permute-start(f32[4,128,128]{2,1,0:T(8,128)S(1)} %get-tuple-element.18), channel_id=1, source_target_pairs={{0,1},{1,0},{2,3},{3,2},{4,5},{5,4},{6,7},{7,6},{8,9},{9,8},{10,11... | collective-permute-start | bytes 786440 | tf_op jit(solution)/shard_map/ppermute | solution.py:17
  36.5 2.9 %copy-start.1 = (bf16[128,1024]{1,0:T(8,128)(2,1)S(1)}, bf16[128,1024]{1,0:T(8,128)(2,1)}, u32[]{:S(2)}) copy-start(bf16[128,1024]{1,0:T(8,128)(2,1)} %param.4) | copy-start | bytes 786436
  36.5 2.9 %copy-start.2 = (bf16[128,1024]{1,0:T(8,128)(2,1)S(1)}, bf16[128,1024]{1,0:T(8,128)(2,1)}, u32[]{:S(2)}) copy-start(bf16[128,1024]{1,0:T(8,128)(2,1)} %param.5) | copy-start | bytes 786436
  37.8 8.4 %collective-permute-start.5 = (f32[4,128,128]{2,1,0:T(8,128)S(1)}, f32[4,128,128]{2,1,0:T(8,128)S(1)}, u32[]{:S(2)}, u32[]{:S(2)}) collective-permute-start(f32[4,128,128]{2,1,0:T(8,128)S(1)} %add.102), channel_id=1, source_target_pairs={{0,8},{4,12},{8,0},{12,4},{1,9},{5,13},{9,1},{13,5},{2,10},{6,14},... | collective-permute-start | bytes 786440 | tf_op jit(solution)/shard_map/ppermute | solution.py:17
  47.0 1.0 copy-start.7
  49.6 14.1 %collective-permute-start.8 = (f32[4,128,128]{2,1,0:T(8,128)S(1)}, f32[4,128,128]{2,1,0:T(8,128)S(1)}, u32[]{:S(2)}, u32[]{:S(2)}) collective-permute-start(f32[4,128,128]{2,1,0:T(8,128)S(1)} %get-tuple-element.24), channel_id=1, source_target_pairs={{0,2},{1,3},{2,0},{3,1},{4,6},{5,7},{6,4},{7,5},{8,10},{9,11},{10,... | collective-permute-start | bytes 786440 | tf_op jit(solution)/shard_map/ppermute | solution.py:17
  50.3 13.3 %collective-permute-start.9 = (f32[4,128,128]{2,1,0:T(8,128)S(1)}, f32[4,128,128]{2,1,0:T(8,128)S(1)}, u32[]{:S(2)}, u32[]{:S(2)}) collective-permute-start(f32[4,128,128]{2,1,0:T(8,128)S(1)} %get-tuple-element.25), channel_id=1, source_target_pairs={{0,1},{1,0},{2,3},{3,2},{4,5},{5,4},{6,7},{7,6},{8,9},{9,8},{10,11... | collective-permute-start | bytes 786440 | tf_op jit(solution)/shard_map/ppermute | solution.py:17
  63.7 0.9 copy-start.11
  63.7 0.9 copy-start.9
  64.6 1.5 %collective-permute-start.10 = (f32[4,128,128]{2,1,0:T(8,128)S(1)}, f32[4,128,128]{2,1,0:T(8,128)S(1)}, u32[]{:S(2)}, u32[]{:S(2)}) collective-permute-start(f32[4,128,128]{2,1,0:T(8,128)S(1)} %get-tuple-element.10), channel_id=1, source_target_pairs={{0,4},{4,0},{8,12},{12,8},{1,5},{5,1},{9,13},{13,9},{2,6},{6,2},{1... | collective-permute-start | bytes 786440 | tf_op jit(solution)/shard_map/ppermute | solution.py:17
  66.1 0.7 copy-start.5
  66.8 16.6 %collective-permute-start.11 = (f32[4,128,128]{2,1,0:T(8,128)S(1)}, f32[4,128,128]{2,1,0:T(8,128)S(1)}, u32[]{:S(2)}, u32[]{:S(2)}) collective-permute-start(f32[4,128,128]{2,1,0:T(8,128)S(1)} %add.114), channel_id=1, source_target_pairs={{0,8},{4,12},{8,0},{12,4},{1,9},{5,13},{9,1},{13,5},{2,10},{6,14},... | collective-permute-start | bytes 786440 | tf_op jit(solution)/shard_map/ppermute | solution.py:17
  68.3 14.0 %collective-permute-start.13 = (f32[4,128,128]{2,1,0:T(8,128)}, f32[4,128,128]{2,1,0:T(8,128)S(1)}, u32[]{:S(2)}, u32[]{:S(2)}) collective-permute-start(f32[4,128,128]{2,1,0:T(8,128)} %get-tuple-element.11), channel_id=1, source_target_pairs={{0,2},{1,3},{2,0},{3,1},{4,6},{5,7},{6,4},{7,5},{8,10},{9,11},{10,... | collective-permute-start | bytes 786440 | tf_op jit(solution)/shard_map/ppermute | solution.py:17
  69.7 13.7 %copy-start.6 = (f32[4,128,128]{2,1,0:T(8,128)S(1)}, f32[4,128,128]{2,1,0:T(8,128)}, u32[]{:S(2)}) copy-start(f32[4,128,128]{2,1,0:T(8,128)} %copy-done.5) | copy-start | bytes 786436
  69.7 13.7 %copy-start.12 = (f32[4,128,128]{2,1,0:T(8,128)S(1)}, f32[4,128,128]{2,1,0:T(8,128)}, u32[]{:S(2)}) copy-start(f32[4,128,128]{2,1,0:T(8,128)} %copy-done.11) | copy-start | bytes 786436
  83.3 1.6 %collective-permute-start.14 = (f32[4,128,128]{2,1,0:T(8,128)S(1)}, f32[4,128,128]{2,1,0:T(8,128)S(1)}, u32[]{:S(2)}, u32[]{:S(2)}) collective-permute-start(f32[4,128,128]{2,1,0:T(8,128)S(1)} %add.120), channel_id=1, source_target_pairs={{0,4},{4,0},{8,12},{12,8},{1,5},{5,1},{9,13},{13,9},{2,6},{6,2},{1... | collective-permute-start | bytes 786440 | tf_op jit(solution)/shard_map/ppermute | solution.py:17
  84.3 9.0 %collective-permute-start.12 = (f32[4,128,128]{2,1,0:T(8,128)}, f32[4,128,128]{2,1,0:T(8,128)}, u32[]{:S(2)}, u32[]{:S(2)}) collective-permute-start(f32[4,128,128]{2,1,0:T(8,128)} %get-tuple-element.16), channel_id=1, source_target_pairs={{0,1},{1,0},{2,3},{3,2},{4,5},{5,4},{6,7},{7,6},{8,9},{9,8},{10,11... | collective-permute-start | bytes 786440 | tf_op jit(solution)/shard_map/ppermute | solution.py:17
  84.9 0.8 copy-start.3
  85.7 8.7 %collective-permute-start.15 = (f32[4,128,128]{2,1,0:T(8,128)}, f32[4,128,128]{2,1,0:T(8,128)}, u32[]{:S(2)}, u32[]{:S(2)}) collective-permute-start(f32[4,128,128]{2,1,0:T(8,128)} %add.122), channel_id=1, source_target_pairs={{0,8},{4,12},{8,0},{12,4},{1,9},{5,13},{9,1},{13,5},{2,10},{6,14},... | collective-permute-start | bytes 786440 | tf_op jit(solution)/shard_map/ppermute | solution.py:17
  86.4 6.8 %copy-start.8 = (f32[4,128,128]{2,1,0:T(8,128)S(1)}, f32[4,128,128]{2,1,0:T(8,128)}, u32[]{:S(2)}) copy-start(f32[4,128,128]{2,1,0:T(8,128)} %get-tuple-element.17) | copy-start | bytes 786436
  93.3 1.1 %copy-start.4 = (f32[4,128,128]{2,1,0:T(8,128)S(1)}, f32[4,128,128]{2,1,0:T(8,128)}, u32[]{:S(2)}) copy-start(f32[4,128,128]{2,1,0:T(8,128)} %copy-done.3) | copy-start | bytes 786436
  93.3 1.1 %copy-start.10 = (f32[4,128,128]{2,1,0:T(8,128)S(1)}, f32[4,128,128]{2,1,0:T(8,128)}, u32[]{:S(2)}) copy-start(f32[4,128,128]{2,1,0:T(8,128)} %copy-done.9) | copy-start | bytes 786436

commit v8 on v6

--- a/solution.py
+++ b/solution.py
@@ -24,16 +24,23 @@
 
 def subcube_step(earlier, total, axis, bit, backward):
     got = swap(total, axis, bit)
-    earlier = jnp.where(partner_counts(axis, bit, backward), earlier + got, earlier)
-    return earlier, total + got
+    counted = partner_counts(axis, bit, backward)
+    return earlier + [jnp.where(counted, got, 0.0)], total + got
+
+
+def added(pieces, like):
+    total = jnp.zeros_like(like)
+    for piece in pieces:
+        total = total + piece
+    return total
 
 
 def scan_inner_first(value, backward):
-    earlier, total = jnp.zeros_like(value), value
+    earlier, total = [], value
     for axis in ("inner", "outer"):
         for bit in axis_bits(axis):
             earlier, total = subcube_step(earlier, total, axis, bit, backward)
-    return earlier
+    return added(earlier, value)
 
 
 def chunked_scan(value, backward):
@@ -44,14 +51,12 @@
     inner_bits, outer_bits = axis_bits("inner"), axis_bits("outer")
     if not inner_bits:
         return scan_inner_first(value, backward)
-    earlier_a, total_a = subcube_step(
-        jnp.zeros_like(group_a), group_a, "inner", inner_bits[0], backward
-    )
-    earlier_b, total_b = jnp.zeros_like(group_b), group_b
+    earlier_a, total_a = subcube_step([], group_a, "inner", inner_bits[0], backward)
+    earlier_b, total_b = [], group_b
     for bit in inner_bits[1:]:
         earlier_b, total_b = subcube_step(earlier_b, total_b, "inner", bit, backward)
     (earlier_b, total_b), _ = lax.optimization_barrier(((earlier_b, total_b), total_a))
-    rows_before, rows_total = jnp.zeros_like(group_b), total_b
+    rows_before, rows_total = [], total_b
     for index, bit in enumerate(outer_bits):
         rows_before, rows_total = subcube_step(rows_before, rows_total, "outer", bit, backward)
         if index == 0:
@@ -62,8 +67,9 @@
         earlier_a, total_a = subcube_step(earlier_a, total_a, "outer", bit, backward)
     low = inner_bits[0]
     counted = partner_counts("inner", low, backward)
-    known = rows_before + earlier_b
+    known = added(rows_before + earlier_b, group_b)
     sent = jnp.where(counted, known, known + group_b)
+    earlier_a = added(earlier_a, group_a)
     earlier_b = known + swap(sent, "inner", low)
     if backward:
         earlier_a, earlier_b = earlier_b, earlier_a

time: 97.4 us -> 97.4 us (level)
  no operation moved by 1% of the time
where the time goes in v8:
time: 97.4 us; the launch traced here: 97.2 us
  waiting for transfers between devices  66.4 us (68%)
  starting transfers between devices  14.4 us (15%)
  other arithmetic  6.12 us (6%)
  local copies, waits for them, and re-layouts  5.87 us (6%)
  matrix products  3.49 us (4%)
    ppermute x16, waiting for transfers between devices, swap(): return lax.ppermute(value, axis, [(i, i ^ bit) for i in range(count)])  66.4 us
    ppermute x16, starting transfers between devices, swap(): return lax.ppermute(value, axis, [(i, i ^ bit) for i in range(count)])  14.4 us
    unnamed x20, local copies, waits for them, and re-layouts  5.21 us
    add x8, other arithmetic, subcube_step(): return (earlier + [jnp.where(counted, got, 0.0)], total + got)  2.83 us
  transfers between devices with their start and end apart: 16, of which 12 were waited for; matrix products, arithmetic and copies ran while one was open for 6% of the time, Pallas kernels for 0%

profile of v8, /device:TPU:0, one launch (start us, length us, event | category | flops | bytes accessed | tf_op | source)
XLA Modules:
  0.0 97.2 jit_solution(1150850025129445541)
XLA Ops:
  0.6 1.0 %copy.38 = bf16[16,8,8,128]{3,2,1,0:T(8,128)(2,1)S(1)} copy(bf16[16,8,8,128]{3,1,2,0:T(8,128)(2,1)} %bitcast.110) | data formatting | bytes 524288
  1.7 0.2 copy.11
  1.9 0.2 fusion.19
  2.2 3.1 %collective-permute-start = (f32[4,128,128]{2,1,0:T(8,128)S(1)}, f32[4,128,128]{2,1,0:T(8,128)S(1)}, u32[]{:S(2)}, u32[]{:S(2)}) collective-permute-start(f32[4,128,128]{2,1,0:T(8,128)S(1)} %get-tuple-element.36), channel_id=1, source_target_pairs={{0,1},{1,0},{2,3},{3,2},{4,5},{5,4},{6,7},{7,6},{8,9},{9,8},{10,11... | collective-permute-start | bytes 786440 | tf_op jit(solution)/shard_map/ppermute | solution.py:17
  5.3 2.6 %collective-permute-start.1 = (f32[4,128,128]{2,1,0:T(8,128)S(1)}, f32[4,128,128]{2,1,0:T(8,128)S(1)}, u32[]{:S(2)}, u32[]{:S(2)}) collective-permute-start(f32[4,128,128]{2,1,0:T(8,128)S(1)} %get-tuple-element.37), channel_id=1, source_target_pairs={{0,2},{1,3},{2,0},{3,1},{4,6},{5,7},{6,4},{7,5},{8,10},{9,11},{10,... | collective-permute-start | bytes 786440 | tf_op jit(solution)/shard_map/ppermute | solution.py:17
  7.9 9.2 %collective-permute-done = f32[4,128,128]{2,1,0:T(8,128)S(1)} collective-permute-done((f32[4,128,128]{2,1,0:T(8,128)S(1)}, f32[4,128,128]{2,1,0:T(8,128)S(1)}, u32[]{:S(2)}, u32[]{:S(2)}) %collective-permute-start) | collective-permute-done | bytes 262176 | tf_op jit(solution)/shard_map/ppermute | solution.py:17
  17.1 2.5 %collective-permute-done.1 = f32[4,128,128]{2,1,0:T(8,128)S(1)} collective-permute-done((f32[4,128,128]{2,1,0:T(8,128)S(1)}, f32[4,128,128]{2,1,0:T(8,128)S(1)}, u32[]{:S(2)}, u32[]{:S(2)}) %collective-permute-start.1) | collective-permute-done | bytes 262176 | tf_op jit(solution)/shard_map/ppermute | solution.py:17
  19.8 1.5 %collective-permute-done.2 = f32[4,128,128]{2,1,0:T(8,128)S(1)} collective-permute-done((f32[4,128,128]{2,1,0:T(8,128)S(1)}, f32[4,128,128]{2,1,0:T(8,128)S(1)}, u32[]{:S(2)}, u32[]{:S(2)}) %collective-permute-start.2) | collective-permute-done | bytes 262176 | tf_op jit(solution)/shard_map/ppermute | solution.py:17
  21.4 0.4 collective-permute-start.3
  21.8 1.5 %collective-permute-start.6 = (f32[4,128,128]{2,1,0:T(8,128)S(1)}, f32[4,128,128]{2,1,0:T(8,128)S(1)}, u32[]{:S(2)}, u32[]{:S(2)}) collective-permute-start(f32[4,128,128]{2,1,0:T(8,128)S(1)} %add.98), channel_id=1, source_target_pairs={{0,8},{4,12},{8,0},{12,4},{1,9},{5,13},{9,1},{13,5},{2,10},{6,14},... | collective-permute-start | bytes 786440 | tf_op jit(solution)/shard_map/ppermute | solution.py:17
  23.3 12.9 %collective-permute-done.3 = f32[4,128,128]{2,1,0:T(8,128)S(1)} collective-permute-done((f32[4,128,128]{2,1,0:T(8,128)S(1)}, f32[4,128,128]{2,1,0:T(8,128)S(1)}, u32[]{:S(2)}, u32[]{:S(2)}) %collective-permute-start.3) | collective-permute-done | bytes 262176 | tf_op jit(solution)/shard_map/ppermute | solution.py:17
  36.5 1.3 %collective-permute-done.4 = f32[4,128,128]{2,1,0:T(8,128)S(1)} collective-permute-done((f32[4,128,128]{2,1,0:T(8,128)S(1)}, f32[4,128,128]{2,1,0:T(8,128)S(1)}, u32[]{:S(2)}, u32[]{:S(2)}) %collective-permute-start.4) | collective-permute-done | bytes 262176 | tf_op jit(solution)/shard_map/ppermute | solution.py:17
  37.9 1.6 %collective-permute-start.5 = (f32[4,128,128]{2,1,0:T(8,128)S(1)}, f32[4,128,128]{2,1,0:T(8,128)S(1)}, u32[]{:S(2)}, u32[]{:S(2)}) collective-permute-start(f32[4,128,128]{2,1,0:T(8,128)S(1)} %add.102), channel_id=1, source_target_pairs={{0,8},{4,12},{8,0},{12,4},{1,9},{5,13},{9,1},{13,5},{2,10},{6,14},... | collective-permute-start | bytes 786440 | tf_op jit(solution)/shard_map/ppermute | solution.py:17
  39.4 0.3 fusion.8
  39.7 5.4 %collective-permute-done.7 = f32[4,128,128]{2,1,0:T(8,128)S(1)} collective-permute-done((f32[4,128,128]{2,1,0:T(8,128)S(1)}, f32[4,128,128]{2,1,0:T(8,128)S(1)}, u32[]{:S(2)}, u32[]{:S(2)}) %collective-permute-start.7) | collective-permute-done | bytes 262176 | tf_op jit(solution)/shard_map/ppermute | solution.py:17
  45.2 1.1 %collective-permute-done.5 = f32[4,128,128]{2,1,0:T(8,128)S(1)} collective-permute-done((f32[4,128,128]{2,1,0:T(8,128)S(1)}, f32[4,128,128]{2,1,0:T(8,128)S(1)}, u32[]{:S(2)}, u32[]{:S(2)}) %collective-permute-start.5) | collective-permute-done | bytes 262176 | tf_op jit(solution)/shard_map/ppermute | solution.py:17
  46.4 0.3 fusion.6
  46.7 0.4 multiply_reduce_fusion
  47.3 0.7 copy-done.5
  48.0 0.2 fusion.13
  48.2 0.9 fusion.15
  49.3 0.3 convolution_bitcast_fusion.2
  49.7 0.7 collective-permute-start.8
  50.4 1.3 %collective-permute-start.9 = (f32[4,128,128]{2,1,0:T(8,128)S(1)}, f32[4,128,128]{2,1,0:T(8,128)S(1)}, u32[]{:S(2)}, u32[]{:S(2)}) collective-permute-start(f32[4,128,128]{2,1,0:T(8,128)S(1)} %get-tuple-element.33), channel_id=1, source_target_pairs={{0,1},{1,0},{2,3},{3,2},{4,5},{5,4},{6,7},{7,6},{8,9},{9,8},{10,11... | collective-permute-start | bytes 786440 | tf_op jit(solution)/shard_map/ppermute | solution.py:17
  51.6 12.1 %collective-permute-done.8 = f32[4,128,128]{2,1,0:T(8,128)S(1)} collective-permute-done((f32[4,128,128]{2,1,0:T(8,128)S(1)}, f32[4,128,128]{2,1,0:T(8,128)S(1)}, u32[]{:S(2)}, u32[]{:S(2)}) %collective-permute-start.8) | collective-permute-done | bytes 262176 | tf_op jit(solution)/shard_map/ppermute | solution.py:17
  63.7 0.9 slice_add_fusion.2
  64.6 0.2 fusion.43
  64.8 1.3 %collective-permute-done.10 = f32[4,128,128]{2,1,0:T(8,128)S(1)} collective-permute-done((f32[4,128,128]{2,1,0:T(8,128)S(1)}, f32[4,128,128]{2,1,0:T(8,128)S(1)}, u32[]{:S(2)}, u32[]{:S(2)}) %collective-permute-start.10) | collective-permute-done | bytes 262176 | tf_op jit(solution)/shard_map/ppermute | solution.py:17
  66.2 1.6 %collective-permute-start.11 = (f32[4,128,128]{2,1,0:T(8,128)S(1)}, f32[4,128,128]{2,1,0:T(8,128)S(1)}, u32[]{:S(2)}, u32[]{:S(2)}) collective-permute-start(f32[4,128,128]{2,1,0:T(8,128)S(1)} %add.114), channel_id=1, source_target_pairs={{0,8},{4,12},{8,0},{12,4},{1,9},{5,13},{9,1},{13,5},{2,10},{6,14},... | collective-permute-start | bytes 786440 | tf_op jit(solution)/shard_map/ppermute | solution.py:17
  67.8 0.9 collective-permute-start.13
  68.6 0.3 fusion.12
  69.0 0.3 convolution_bitcast_fusion
  69.3 12.6 %collective-permute-done.13 = f32[4,128,128]{2,1,0:T(8,128)S(1)} collective-permute-done((f32[4,128,128]{2,1,0:T(8,128)}, f32[4,128,128]{2,1,0:T(8,128)S(1)}, u32[]{:S(2)}, u32[]{:S(2)}) %collective-permute-start.13) | collective-permute-done | bytes 262176 | tf_op jit(solution)/shard_map/ppermute | solution.py:17
  81.9 1.0 %add.120 = f32[4,128,128]{2,1,0:T(8,128)S(1)} add(f32[4,128,128]{2,1,0:T(8,128)} %get-tuple-element.19, f32[4,128,128]{2,1,0:T(8,128)S(1)} %collective-permute-done.13) | non-fusion elementwise | flops 65536 | bytes 786432 | tf_op jit(solution)/shard_map/add | solution.py:28
  82.9 0.9 add_select_fusion
  83.8 0.3 convolution_bitcast_fusion.4
  84.1 0.3 collective-permute-done.14
  84.4 0.7 add.122
  85.2 0.5 collective-permute-start.15
  85.7 0.2 fusion.11
  85.9 0.9 copy.28
  86.8 6.0 %collective-permute-done.12 = f32[4,128,128]{2,1,0:T(8,128)} collective-permute-done((f32[4,128,128]{2,1,0:T(8,128)}, f32[4,128,128]{2,1,0:T(8,128)}, u32[]{:S(2)}, u32[]{:S(2)}) %collective-permute-start.12) | collective-permute-done | bytes 262176 | tf_op jit(solution)/shard_map/ppermute | solution.py:17
  92.8 1.0 %add_convert_fusion.1 = bf16[4,128,128]{2,1,0:T(8,128)(2,1)S(1)} fusion(f32[4,128,128]{2,1,0:T(8,128)S(1)} %copy-done.4, f32[4,128,128]{2,1,0:T(8,128)} %collective-permute-done.12), kind=kLoop, calls=%fused_computation.46 | loop fusion | flops 131072 | bytes 655360 | tf_op jit(solution)/shard_map/convert
  94.0 0.8 copy-done.3
  94.8 0.3 fusion.9
  95.1 0.9 copy.30
  96.0 0.3 fusion.10
  96.3 0.9 copy.29
  (40 shorter events, 1.3 us)
Async XLA Ops:
  0.6 1.3 %copy-start = (bf16[128,1024]{1,0:T(8,128)(2,1)S(1)}, bf16[128,1024]{1,0:T(8,128)(2,1)}, u32[]{:S(2)}) copy-start(bf16[128,1024]{1,0:T(8,128)(2,1)} %param.6) | copy-start | bytes 786436
  2.2 14.9 %collective-permute-start = (f32[4,128,128]{2,1,0:T(8,128)S(1)}, f32[4,128,128]{2,1,0:T(8,128)S(1)}, u32[]{:S(2)}, u32[]{:S(2)}) collective-permute-start(f32[4,128,128]{2,1,0:T(8,128)S(1)} %get-tuple-element.36), channel_id=1, source_target_pairs={{0,1},{1,0},{2,3},{3,2},{4,5},{5,4},{6,7},{7,6},{8,9},{9,8},{10,11... | collective-permute-start | bytes 786440 | tf_op jit(solution)/shard_map/ppermute | solution.py:17
  5.3 14.3 %collective-permute-start.1 = (f32[4,128,128]{2,1,0:T(8,128)S(1)}, f32[4,128,128]{2,1,0:T(8,128)S(1)}, u32[]{:S(2)}, u32[]{:S(2)}) collective-permute-start(f32[4,128,128]{2,1,0:T(8,128)S(1)} %get-tuple-element.37), channel_id=1, source_target_pairs={{0,2},{1,3},{2,0},{3,1},{4,6},{5,7},{6,4},{7,5},{8,10},{9,11},{10,... | collective-permute-start | bytes 786440 | tf_op jit(solution)/shard_map/ppermute | solution.py:17
  19.7 1.6 %collective-permute-start.2 = (f32[4,128,128]{2,1,0:T(8,128)S(1)}, f32[4,128,128]{2,1,0:T(8,128)S(1)}, u32[]{:S(2)}, u32[]{:S(2)}) collective-permute-start(f32[4,128,128]{2,1,0:T(8,128)S(1)} %get-tuple-element.12), channel_id=1, source_target_pairs={{0,4},{4,0},{8,12},{12,8},{1,5},{5,1},{9,13},{13,9},{2,6},{6,2},{1... | collective-permute-start | bytes 786440 | tf_op jit(solution)/shard_map/ppermute | solution.py:17
  21.4 14.8 %collective-permute-start.3 = (f32[4,128,128]{2,1,0:T(8,128)S(1)}, f32[4,128,128]{2,1,0:T(8,128)S(1)}, u32[]{:S(2)}, u32[]{:S(2)}) collective-permute-start(f32[4,128,128]{2,1,0:T(8,128)S(1)} %get-tuple-element.14), channel_id=1, source_target_pairs={{0,2},{1,3},{2,0},{3,1},{4,6},{5,7},{6,4},{7,5},{8,10},{9,11},{10,... | collective-permute-start | bytes 786440 | tf_op jit(solution)/shard_map/ppermute | solution.py:17
  21.8 14.6 %collective-permute-start.6 = (f32[4,128,128]{2,1,0:T(8,128)S(1)}, f32[4,128,128]{2,1,0:T(8,128)S(1)}, u32[]{:S(2)}, u32[]{:S(2)}) collective-permute-start(f32[4,128,128]{2,1,0:T(8,128)S(1)} %add.98), channel_id=1, source_target_pairs={{0,8},{4,12},{8,0},{12,4},{1,9},{5,13},{9,1},{13,5},{2,10},{6,14},... | collective-permute-start | bytes 786440 | tf_op jit(solution)/shard_map/ppermute | solution.py:17
  36.2 1.6 %collective-permute-start.4 = (f32[4,128,128]{2,1,0:T(8,128)S(1)}, f32[4,128,128]{2,1,0:T(8,128)S(1)}, u32[]{:S(2)}, u32[]{:S(2)}) collective-permute-start(f32[4,128,128]{2,1,0:T(8,128)S(1)} %add.100), channel_id=1, source_target_pairs={{0,4},{4,0},{8,12},{12,8},{1,5},{5,1},{9,13},{13,9},{2,6},{6,2},{1... | collective-permute-start | bytes 786440 | tf_op jit(solution)/shard_map/ppermute | solution.py:17
  36.4 8.8 %collective-permute-start.7 = (f32[4,128,128]{2,1,0:T(8,128)S(1)}, f32[4,128,128]{2,1,0:T(8,128)S(1)}, u32[]{:S(2)}, u32[]{:S(2)}) collective-permute-start(f32[4,128,128]{2,1,0:T(8,128)S(1)} %get-tuple-element.26), channel_id=1, source_target_pairs={{0,1},{1,0},{2,3},{3,2},{4,5},{5,4},{6,7},{7,6},{8,9},{9,8},{10,11... | collective-permute-start | bytes 786440 | tf_op jit(solution)/shard_map/ppermute | solution.py:17
  36.5 2.9 %copy-start.1 = (bf16[128,1024]{1,0:T(8,128)(2,1)S(1)}, bf16[128,1024]{1,0:T(8,128)(2,1)}, u32[]{:S(2)}) copy-start(bf16[128,1024]{1,0:T(8,128)(2,1)} %param.4) | copy-start | bytes 786436
  36.5 2.9 %copy-start.2 = (bf16[128,1024]{1,0:T(8,128)(2,1)S(1)}, bf16[128,1024]{1,0:T(8,128)(2,1)}, u32[]{:S(2)}) copy-start(bf16[128,1024]{1,0:T(8,128)(2,1)} %param.5) | copy-start | bytes 786436
  37.9 8.4 %collective-permute-start.5 = (f32[4,128,128]{2,1,0:T(8,128)S(1)}, f32[4,128,128]{2,1,0:T(8,128)S(1)}, u32[]{:S(2)}, u32[]{:S(2)}) collective-permute-start(f32[4,128,128]{2,1,0:T(8,128)S(1)} %add.102), channel_id=1, source_target_pairs={{0,8},{4,12},{8,0},{12,4},{1,9},{5,13},{9,1},{13,5},{2,10},{6,14},... | collective-permute-start | bytes 786440 | tf_op jit(solution)/shard_map/ppermute | solution.py:17
  47.0 1.0 copy-start.5
  49.7 14.1 %collective-permute-start.8 = (f32[4,128,128]{2,1,0:T(8,128)S(1)}, f32[4,128,128]{2,1,0:T(8,128)S(1)}, u32[]{:S(2)}, u32[]{:S(2)}) collective-permute-start(f32[4,128,128]{2,1,0:T(8,128)S(1)} %get-tuple-element.32), channel_id=1, source_target_pairs={{0,2},{1,3},{2,0},{3,1},{4,6},{5,7},{6,4},{7,5},{8,10},{9,11},{10,... | collective-permute-start | bytes 786440 | tf_op jit(solution)/shard_map/ppermute | solution.py:17
  50.4 13.4 %collective-permute-start.9 = (f32[4,128,128]{2,1,0:T(8,128)S(1)}, f32[4,128,128]{2,1,0:T(8,128)S(1)}, u32[]{:S(2)}, u32[]{:S(2)}) collective-permute-start(f32[4,128,128]{2,1,0:T(8,128)S(1)} %get-tuple-element.33), channel_id=1, source_target_pairs={{0,1},{1,0},{2,3},{3,2},{4,5},{5,4},{6,7},{7,6},{8,9},{9,8},{10,11... | collective-permute-start | bytes 786440 | tf_op jit(solution)/shard_map/ppermute | solution.py:17
  64.6 1.5 %collective-permute-start.10 = (f32[4,128,128]{2,1,0:T(8,128)S(1)}, f32[4,128,128]{2,1,0:T(8,128)S(1)}, u32[]{:S(2)}, u32[]{:S(2)}) collective-permute-start(f32[4,128,128]{2,1,0:T(8,128)S(1)} %get-tuple-element.16), channel_id=1, source_target_pairs={{0,4},{4,0},{8,12},{12,8},{1,5},{5,1},{9,13},{13,9},{2,6},{6,2},{1... | collective-permute-start | bytes 786440 | tf_op jit(solution)/shard_map/ppermute | solution.py:17
  66.2 16.7 %collective-permute-start.11 = (f32[4,128,128]{2,1,0:T(8,128)S(1)}, f32[4,128,128]{2,1,0:T(8,128)S(1)}, u32[]{:S(2)}, u32[]{:S(2)}) collective-permute-start(f32[4,128,128]{2,1,0:T(8,128)S(1)} %add.114), channel_id=1, source_target_pairs={{0,8},{4,12},{8,0},{12,4},{1,9},{5,13},{9,1},{13,5},{2,10},{6,14},... | collective-permute-start | bytes 786440 | tf_op jit(solution)/shard_map/ppermute | solution.py:17
  67.8 14.1 %collective-permute-start.13 = (f32[4,128,128]{2,1,0:T(8,128)}, f32[4,128,128]{2,1,0:T(8,128)S(1)}, u32[]{:S(2)}, u32[]{:S(2)}) collective-permute-start(f32[4,128,128]{2,1,0:T(8,128)} %get-tuple-element.19), channel_id=1, source_target_pairs={{0,2},{1,3},{2,0},{3,1},{4,6},{5,7},{6,4},{7,5},{8,10},{9,11},{10,... | collective-permute-start | bytes 786440 | tf_op jit(solution)/shard_map/ppermute | solution.py:17
  69.2 13.7 %copy-start.7 = (f32[4,128,128]{2,1,0:T(8,128)S(1)}, f32[4,128,128]{2,1,0:T(8,128)}, u32[]{:S(2)}) copy-start(f32[4,128,128]{2,1,0:T(8,128)} %get-tuple-element.17) | copy-start | bytes 786436
  82.8 1.6 %collective-permute-start.14 = (f32[4,128,128]{2,1,0:T(8,128)S(1)}, f32[4,128,128]{2,1,0:T(8,128)S(1)}, u32[]{:S(2)}, u32[]{:S(2)}) collective-permute-start(f32[4,128,128]{2,1,0:T(8,128)S(1)} %add.120), channel_id=1, source_target_pairs={{0,4},{4,0},{8,12},{12,8},{1,5},{5,1},{9,13},{13,9},{2,6},{6,2},{1... | collective-permute-start | bytes 786440 | tf_op jit(solution)/shard_map/ppermute | solution.py:17
  83.8 9.0 %collective-permute-start.12 = (f32[4,128,128]{2,1,0:T(8,128)}, f32[4,128,128]{2,1,0:T(8,128)}, u32[]{:S(2)}, u32[]{:S(2)}) collective-permute-start(f32[4,128,128]{2,1,0:T(8,128)} %get-tuple-element.24), channel_id=1, source_target_pairs={{0,1},{1,0},{2,3},{3,2},{4,5},{5,4},{6,7},{7,6},{8,9},{9,8},{10,11... | collective-permute-start | bytes 786440 | tf_op jit(solution)/shard_map/ppermute | solution.py:17
  85.2 8.7 %collective-permute-start.15 = (f32[4,128,128]{2,1,0:T(8,128)}, f32[4,128,128]{2,1,0:T(8,128)S(1)}, u32[]{:S(2)}, u32[]{:S(2)}) collective-permute-start(f32[4,128,128]{2,1,0:T(8,128)} %add.122), channel_id=1, source_target_pairs={{0,8},{4,12},{8,0},{12,4},{1,9},{5,13},{9,1},{13,5},{2,10},{6,14},... | collective-permute-start | bytes 786440 | tf_op jit(solution)/shard_map/ppermute | solution.py:17
  85.9 6.9 %copy-start.4 = (f32[4,128,128]{2,1,0:T(8,128)S(1)}, f32[4,128,128]{2,1,0:T(8,128)}, u32[]{:S(2)}) copy-start(f32[4,128,128]{2,1,0:T(8,128)} %get-tuple-element.25) | copy-start | bytes 786436
  92.8 1.1 %copy-start.6 = (f32[4,128,128]{2,1,0:T(8,128)S(1)}, f32[4,128,128]{2,1,0:T(8,128)}, u32[]{:S(2)}) copy-start(f32[4,128,128]{2,1,0:T(8,128)} %get-tuple-element.18) | copy-start | bytes 786436
  93.9 1.0 copy-start.3

commit v9 on v8

--- a/solution.py
+++ b/solution.py
@@ -26,6 +26,10 @@
     got = swap(total, axis, bit)
     counted = partner_counts(axis, bit, backward)
     return earlier + [jnp.where(counted, got, 0.0)], total + got
+
+
+def after(value, other):
+    return value + 0.0 * other[:1, :1, :1]
 
 
 def added(pieces, like):
@@ -60,7 +64,7 @@
     for index, bit in enumerate(outer_bits):
         rows_before, rows_total = subcube_step(rows_before, rows_total, "outer", bit, backward)
         if index == 0:
-            (earlier_a, total_a), _ = lax.optimization_barrier(((earlier_a, total_a), rows_total))
+            total_a = after(total_a, rows_total)
     for bit in inner_bits[1:]:
         earlier_a, total_a = subcube_step(earlier_a, total_a, "inner", bit, backward)
     for bit in outer_bits:

time: 97.4 us -> 98 us (level)
  waiting for transfers between devices: 66.4 us -> 63 us
  local copies, waits for them, and re-layouts: 5.87 us -> 7.42 us
  between operations: 0.9 us -> 2.22 us
  starting transfers between devices: 14.4 us -> 15.4 us
    ppermute x16, waiting for transfers between devices: 66.4 us -> 63 us  [swap(): return lax.ppermute(value, axis, [(i, i ^ bit) for i in range(count)])]
    add x8, other arithmetic: 2.83 us -> 1.05 us  [subcube_step(): return (earlier + [jnp.where(counted, got, 0.0)], total + got)]
    slice x0 -> x2, local copies, waits for them, and re-layouts: none -> 1.03 us  [after(): return value + 0.0 * other[:1, :1, :1]]
    another operation x4, other arithmetic: 1.21 us -> 2.2 us
    unnamed x20 -> x30, local copies, waits for them, and re-layouts: 5.21 us -> 5.73 us
where the time goes in v9:
time: 98 us; the launch traced here: 97.8 us
  waiting for transfers between devices  63 us (64%)
  starting transfers between devices  15.4 us (16%)
  local copies, waits for them, and re-layouts  7.42 us (8%)
  other arithmetic  5.28 us (5%)
  matrix products  4.46 us (5%)
  between operations  2.22 us (2%)
    ppermute x16, waiting for transfers between devices, swap(): return lax.ppermute(value, axis, [(i, i ^ bit) for i in range(count)])  63 us
    ppermute x16, starting transfers between devices, swap(): return lax.ppermute(value, axis, [(i, i ^ bit) for i in range(count)])  15.4 us
    unnamed x30, local copies, waits for them, and re-layouts  5.73 us
    another operation x4, other arithmetic  2.2 us
  transfers between devices with their start and end apart: 16, of which 12 were waited for; matrix products, arithmetic and copies ran while one was open for 6% of the time, Pallas kernels for 0%

profile of v9, /device:TPU:0, one launch (start us, length us, event | category | flops | bytes accessed | tf_op | source)
XLA Modules:
  0.0 97.8 jit_solution(16478565675592725770)
XLA Ops:
  0.6 1.0 %copy.38 = bf16[16,8,8,128]{3,2,1,0:T(8,128)(2,1)S(1)} copy(bf16[16,8,8,128]{3,1,2,0:T(8,128)(2,1)} %bitcast.112) | data formatting | bytes 524288
  1.7 0.2 copy.11
  2.2 3.1 %collective-permute-start = (f32[4,128,128]{2,1,0:T(8,128)S(1)}, f32[4,128,128]{2,1,0:T(8,128)S(1)}, u32[]{:S(2)}, u32[]{:S(2)}) collective-permute-start(f32[4,128,128]{2,1,0:T(8,128)S(1)} %get-tuple-element.28), channel_id=1, source_target_pairs={{0,1},{1,0},{2,3},{3,2},{4,5},{5,4},{6,7},{7,6},{8,9},{9,8},{10,11... | collective-permute-start | bytes 786440 | tf_op jit(solution)/shard_map/ppermute | solution.py:17
  5.3 2.6 %collective-permute-start.1 = (f32[4,128,128]{2,1,0:T(8,128)S(1)}, f32[4,128,128]{2,1,0:T(8,128)S(1)}, u32[]{:S(2)}, u32[]{:S(2)}) collective-permute-start(f32[4,128,128]{2,1,0:T(8,128)S(1)} %get-tuple-element.29), channel_id=1, source_target_pairs={{0,2},{1,3},{2,0},{3,1},{4,6},{5,7},{6,4},{7,5},{8,10},{9,11},{10,... | collective-permute-start | bytes 786440 | tf_op jit(solution)/shard_map/ppermute | solution.py:17
  7.9 9.2 %collective-permute-done = f32[4,128,128]{2,1,0:T(8,128)S(1)} collective-permute-done((f32[4,128,128]{2,1,0:T(8,128)S(1)}, f32[4,128,128]{2,1,0:T(8,128)S(1)}, u32[]{:S(2)}, u32[]{:S(2)}) %collective-permute-start) | collective-permute-done | bytes 262176 | tf_op jit(solution)/shard_map/ppermute | solution.py:17
  17.1 2.5 %collective-permute-done.1 = f32[4,128,128]{2,1,0:T(8,128)S(1)} collective-permute-done((f32[4,128,128]{2,1,0:T(8,128)S(1)}, f32[4,128,128]{2,1,0:T(8,128)S(1)}, u32[]{:S(2)}, u32[]{:S(2)}) %collective-permute-start.1) | collective-permute-done | bytes 262176 | tf_op jit(solution)/shard_map/ppermute | solution.py:17
  19.8 1.5 %collective-permute-done.2 = f32[4,128,128]{2,1,0:T(8,128)S(1)} collective-permute-done((f32[4,128,128]{2,1,0:T(8,128)S(1)}, f32[4,128,128]{2,1,0:T(8,128)S(1)}, u32[]{:S(2)}, u32[]{:S(2)}) %collective-permute-start.2) | collective-permute-done | bytes 262176 | tf_op jit(solution)/shard_map/ppermute | solution.py:17
  21.3 0.5 slice.26
  22.5 0.4 collective-permute-start.3
  22.9 1.5 %collective-permute-start.6 = (f32[4,128,128]{2,1,0:T(8,128)S(1)}, f32[4,128,128]{2,1,0:T(8,128)S(1)}, u32[]{:S(2)}, u32[]{:S(2)}) collective-permute-start(f32[4,128,128]{2,1,0:T(8,128)S(1)} %add.118), channel_id=1, source_target_pairs={{0,8},{4,12},{8,0},{12,4},{1,9},{5,13},{9,1},{13,5},{2,10},{6,14},... | collective-permute-start | bytes 786440 | tf_op jit(solution)/shard_map/ppermute | solution.py:17
  24.4 12.9 %collective-permute-done.3 = f32[4,128,128]{2,1,0:T(8,128)S(1)} collective-permute-done((f32[4,128,128]{2,1,0:T(8,128)S(1)}, f32[4,128,128]{2,1,0:T(8,128)S(1)}, u32[]{:S(2)}, u32[]{:S(2)}) %collective-permute-start.3) | collective-permute-done | bytes 262176 | tf_op jit(solution)/shard_map/ppermute | solution.py:17
  37.7 1.3 %collective-permute-done.4 = f32[4,128,128]{2,1,0:T(8,128)S(1)} collective-permute-done((f32[4,128,128]{2,1,0:T(8,128)S(1)}, f32[4,128,128]{2,1,0:T(8,128)S(1)}, u32[]{:S(2)}, u32[]{:S(2)}) %collective-permute-start.4) | collective-permute-done | bytes 262176 | tf_op jit(solution)/shard_map/ppermute | solution.py:17
  39.0 1.6 %collective-permute-start.5 = (f32[4,128,128]{2,1,0:T(8,128)S(1)}, f32[4,128,128]{2,1,0:T(8,128)S(1)}, u32[]{:S(2)}, u32[]{:S(2)}) collective-permute-start(f32[4,128,128]{2,1,0:T(8,128)S(1)} %add.125), channel_id=1, source_target_pairs={{0,8},{4,12},{8,0},{12,4},{1,9},{5,13},{9,1},{13,5},{2,10},{6,14},... | collective-permute-start | bytes 786440 | tf_op jit(solution)/shard_map/ppermute | solution.py:17
  40.6 0.3 fusion.8
  40.9 5.4 %collective-permute-done.7 = f32[4,128,128]{2,1,0:T(8,128)S(1)} collective-permute-done((f32[4,128,128]{2,1,0:T(8,128)S(1)}, f32[4,128,128]{2,1,0:T(8,128)S(1)}, u32[]{:S(2)}, u32[]{:S(2)}) %collective-permute-start.7) | collective-permute-done | bytes 262176 | tf_op jit(solution)/shard_map/ppermute | solution.py:17
  46.3 1.1 %collective-permute-done.5 = f32[4,128,128]{2,1,0:T(8,128)S(1)} collective-permute-done((f32[4,128,128]{2,1,0:T(8,128)S(1)}, f32[4,128,128]{2,1,0:T(8,128)S(1)}, u32[]{:S(2)}, u32[]{:S(2)}) %collective-permute-start.5) | collective-permute-done | bytes 262176 | tf_op jit(solution)/shard_map/ppermute | solution.py:17
  47.5 0.3 fusion.6
  47.9 0.4 multiply_reduce_fusion
  48.4 0.7 copy-done.7
  49.2 0.2 fusion.13
  49.4 0.9 fusion.15
  50.5 0.3 convolution_bitcast_fusion.2
  50.8 0.7 collective-permute-start.8
  51.5 1.3 %collective-permute-start.9 = (f32[4,128,128]{2,1,0:T(8,128)S(1)}, f32[4,128,128]{2,1,0:T(8,128)S(1)}, u32[]{:S(2)}, u32[]{:S(2)}) collective-permute-start(f32[4,128,128]{2,1,0:T(8,128)S(1)} %get-tuple-element.25), channel_id=1, source_target_pairs={{0,1},{1,0},{2,3},{3,2},{4,5},{5,4},{6,7},{7,6},{8,9},{9,8},{10,11... | collective-permute-start | bytes 786440 | tf_op jit(solution)/shard_map/ppermute | solution.py:17
  52.8 12.1 %collective-permute-done.8 = f32[4,128,128]{2,1,0:T(8,128)S(1)} collective-permute-done((f32[4,128,128]{2,1,0:T(8,128)S(1)}, f32[4,128,128]{2,1,0:T(8,128)S(1)}, u32[]{:S(2)}, u32[]{:S(2)}) %collective-permute-start.8) | collective-permute-done | bytes 262176 | tf_op jit(solution)/shard_map/ppermute | solution.py:17
  64.9 0.8 slice_add_fusion.2
  65.7 1.2 %fusion.43 = f32[8,128,128]{2,1,0:T(8,128)S(1)} fusion(bf16[128,8,128]{0,2,1:T(8,128)(2,1)S(1)} %bitcast.108, bf16[8,128,128]{2,1,0:T(8,128)(2,1)} %copy-done.10), kind=kOutput, calls=%fused_computation.78 | convolution fusion | flops 33554432 | bytes 1048576 | tf_op jit(solution)/shard_map/hts,thj->shj/dot_general | solution.py:128
  66.9 0.4 collective-permute-done.10
  67.3 0.5 slice.29
  68.5 0.9 collective-permute-start.13
  69.4 0.3 fusion.12
  69.7 1.5 %collective-permute-start.11 = (f32[4,128,128]{2,1,0:T(8,128)S(1)}, f32[4,128,128]{2,1,0:T(8,128)S(1)}, u32[]{:S(2)}, u32[]{:S(2)}) collective-permute-start(f32[4,128,128]{2,1,0:T(8,128)S(1)} %add.137), channel_id=1, source_target_pairs={{0,8},{4,12},{8,0},{12,4},{1,9},{5,13},{9,1},{13,5},{2,10},{6,14},... | collective-permute-start | bytes 786440 | tf_op jit(solution)/shard_map/ppermute | solution.py:17
  71.3 0.3 convolution_bitcast_fusion
  71.6 11.1 %collective-permute-done.13 = f32[4,128,128]{2,1,0:T(8,128)S(1)} collective-permute-done((f32[4,128,128]{2,1,0:T(8,128)S(1)}, f32[4,128,128]{2,1,0:T(8,128)S(1)}, u32[]{:S(2)}, u32[]{:S(2)}) %collective-permute-start.13) | collective-permute-done | bytes 262176 | tf_op jit(solution)/shard_map/ppermute | solution.py:17
  82.7 0.7 copy-done.11
  83.5 0.8 add_select_fusion
  84.3 0.3 convolution_bitcast_fusion.4
  84.6 0.4 collective-permute-done.14
  85.0 0.7 copy-done.5
  85.7 1.5 %collective-permute-start.15 = (f32[4,128,128]{2,1,0:T(8,128)S(1)}, f32[4,128,128]{2,1,0:T(8,128)}, u32[]{:S(2)}, u32[]{:S(2)}) collective-permute-start(f32[4,128,128]{2,1,0:T(8,128)S(1)} %add.148), channel_id=1, source_target_pairs={{0,8},{4,12},{8,0},{12,4},{1,9},{5,13},{9,1},{13,5},{2,10},{6,14},... | collective-permute-start | bytes 786440 | tf_op jit(solution)/shard_map/ppermute | solution.py:17
  87.4 0.8 copy.28
  88.2 5.0 %collective-permute-done.12 = f32[4,128,128]{2,1,0:T(8,128)} collective-permute-done((f32[4,128,128]{2,1,0:T(8,128)}, f32[4,128,128]{2,1,0:T(8,128)}, u32[]{:S(2)}, u32[]{:S(2)}) %collective-permute-start.12) | collective-permute-done | bytes 262176 | tf_op jit(solution)/shard_map/ppermute | solution.py:17
  93.3 1.0 %add_convert_fusion.1 = bf16[4,128,128]{2,1,0:T(8,128)(2,1)S(1)} fusion(f32[4,128,128]{2,1,0:T(8,128)S(1)} %get-tuple-element.17, f32[4,128,128]{2,1,0:T(8,128)} %collective-permute-done.12), kind=kLoop, calls=%fused_computation.46 | loop fusion | flops 131072 | bytes 655360 | tf_op jit(solution)/shard_map/convert
  94.4 1.1 %add_convert_fusion = bf16[4,128,128]{2,1,0:T(8,128)(2,1)S(1)} fusion(f32[4,128,128]{2,1,0:T(8,128)} %collective-permute-done.15, f32[4,128,128]{2,1,0:T(8,128)S(1)} %copy-done.6, f32[4,128,128]{2,1,0:T(8,128)S(1)} %copy-done.12, f32[4,128,128]{2,1,0:T(8,128)S(1)} %copy-done.9, pred[]{:T(512)S(6)} %not.19, pred[]{:T(512)S(6)} %not.18, pred[]{:T(512)S(6)} %not.17, ...), kind=kLoop, calls=%fused_computation.45 | loop fusion | flops 524288 | bytes 1179652 | tf_op jit(solution)/shard_map/convert.1
  95.4 0.3 fusion.9
  95.8 0.9 copy.30
  96.6 0.3 fusion.10
  96.9 0.9 copy.29
  (54 shorter events, 1.7 us)
Async XLA Ops:
  0.6 1.3 %copy-start = (bf16[128,1024]{1,0:T(8,128)(2,1)S(1)}, bf16[128,1024]{1,0:T(8,128)(2,1)}, u32[]{:S(2)}) copy-start(bf16[128,1024]{1,0:T(8,128)(2,1)} %param.6) | copy-start | bytes 786436
  2.2 14.9 %collective-permute-start = (f32[4,128,128]{2,1,0:T(8,128)S(1)}, f32[4,128,128]{2,1,0:T(8,128)S(1)}, u32[]{:S(2)}, u32[]{:S(2)}) collective-permute-start(f32[4,128,128]{2,1,0:T(8,128)S(1)} %get-tuple-element.28), channel_id=1, source_target_pairs={{0,1},{1,0},{2,3},{3,2},{4,5},{5,4},{6,7},{7,6},{8,9},{9,8},{10,11... | collective-permute-start | bytes 786440 | tf_op jit(solution)/shard_map/ppermute | solution.py:17
  5.3 14.3 %collective-permute-start.1 = (f32[4,128,128]{2,1,0:T(8,128)S(1)}, f32[4,128,128]{2,1,0:T(8,128)S(1)}, u32[]{:S(2)}, u32[]{:S(2)}) collective-permute-start(f32[4,128,128]{2,1,0:T(8,128)S(1)} %get-tuple-element.29), channel_id=1, source_target_pairs={{0,2},{1,3},{2,0},{3,1},{4,6},{5,7},{6,4},{7,5},{8,10},{9,11},{10,... | collective-permute-start | bytes 786440 | tf_op jit(solution)/shard_map/ppermute | solution.py:17
  19.7 1.6 %collective-permute-start.2 = (f32[4,128,128]{2,1,0:T(8,128)S(1)}, f32[4,128,128]{2,1,0:T(8,128)S(1)}, u32[]{:S(2)}, u32[]{:S(2)}) collective-permute-start(f32[4,128,128]{2,1,0:T(8,128)S(1)} %get-tuple-element.8), channel_id=1, source_target_pairs={{0,4},{4,0},{8,12},{12,8},{1,5},{5,1},{9,13},{13,9},{2,6},{6,2},{1... | collective-permute-start | bytes 786440 | tf_op jit(solution)/shard_map/ppermute | solution.py:17
  22.5 14.8 %collective-permute-start.3 = (f32[4,128,128]{2,1,0:T(8,128)S(1)}, f32[4,128,128]{2,1,0:T(8,128)S(1)}, u32[]{:S(2)}, u32[]{:S(2)}) collective-permute-start(f32[4,128,128]{2,1,0:T(8,128)S(1)} %broadcast_add_fusion.1), channel_id=1, source_target_pairs={{0,2},{1,3},{2,0},{3,1},{4,6},{5,7},{6,4},{7,5},{8,10},{9,11},{10,... | collective-permute-start | bytes 786440 | tf_op jit(solution)/shard_map/ppermute | solution.py:17
  22.9 14.6 %collective-permute-start.6 = (f32[4,128,128]{2,1,0:T(8,128)S(1)}, f32[4,128,128]{2,1,0:T(8,128)S(1)}, u32[]{:S(2)}, u32[]{:S(2)}) collective-permute-start(f32[4,128,128]{2,1,0:T(8,128)S(1)} %add.118), channel_id=1, source_target_pairs={{0,8},{4,12},{8,0},{12,4},{1,9},{5,13},{9,1},{13,5},{2,10},{6,14},... | collective-permute-start | bytes 786440 | tf_op jit(solution)/shard_map/ppermute | solution.py:17
  37.4 1.6 %collective-permute-start.4 = (f32[4,128,128]{2,1,0:T(8,128)S(1)}, f32[4,128,128]{2,1,0:T(8,128)S(1)}, u32[]{:S(2)}, u32[]{:S(2)}) collective-permute-start(f32[4,128,128]{2,1,0:T(8,128)S(1)} %fusion.55), channel_id=1, source_target_pairs={{0,4},{4,0},{8,12},{12,8},{1,5},{5,1},{9,13},{13,9},{2,6},{6,2},{1... | collective-permute-start | bytes 786440 | tf_op jit(solution)/shard_map/ppermute | solution.py:17
  37.5 8.8 %collective-permute-start.7 = (f32[4,128,128]{2,1,0:T(8,128)S(1)}, f32[4,128,128]{2,1,0:T(8,128)S(1)}, u32[]{:S(2)}, u32[]{:S(2)}) collective-permute-start(f32[4,128,128]{2,1,0:T(8,128)S(1)} %get-tuple-element.18), channel_id=1, source_target_pairs={{0,1},{1,0},{2,3},{3,2},{4,5},{5,4},{6,7},{7,6},{8,9},{9,8},{10,11... | collective-permute-start | bytes 786440 | tf_op jit(solution)/shard_map/ppermute | solution.py:17
  37.7 2.9 %copy-start.1 = (bf16[128,1024]{1,0:T(8,128)(2,1)S(1)}, bf16[128,1024]{1,0:T(8,128)(2,1)}, u32[]{:S(2)}) copy-start(bf16[128,1024]{1,0:T(8,128)(2,1)} %param.4) | copy-start | bytes 786436
  37.7 2.9 %copy-start.2 = (bf16[128,1024]{1,0:T(8,128)(2,1)S(1)}, bf16[128,1024]{1,0:T(8,128)(2,1)}, u32[]{:S(2)}) copy-start(bf16[128,1024]{1,0:T(8,128)(2,1)} %param.5) | copy-start | bytes 786436
  39.0 8.4 %collective-permute-start.5 = (f32[4,128,128]{2,1,0:T(8,128)S(1)}, f32[4,128,128]{2,1,0:T(8,128)S(1)}, u32[]{:S(2)}, u32[]{:S(2)}) collective-permute-start(f32[4,128,128]{2,1,0:T(8,128)S(1)} %add.125), channel_id=1, source_target_pairs={{0,8},{4,12},{8,0},{12,4},{1,9},{5,13},{9,1},{13,5},{2,10},{6,14},... | collective-permute-start | bytes 786440 | tf_op jit(solution)/shard_map/ppermute | solution.py:17
  40.9 7.0 %copy-start.10 = (bf16[8,128,128]{2,1,0:T(8,128)(2,1)}, bf16[8,128,128]{2,1,0:T(8,128)(2,1)S(1)}, u32[]{:S(2)}) copy-start(bf16[8,128,128]{2,1,0:T(8,128)(2,1)S(1)} %fusion.8) | copy-start | bytes 786436
  48.2 1.0 copy-start.7
  50.8 14.1 %collective-permute-start.8 = (f32[4,128,128]{2,1,0:T(8,128)S(1)}, f32[4,128,128]{2,1,0:T(8,128)S(1)}, u32[]{:S(2)}, u32[]{:S(2)}) collective-permute-start(f32[4,128,128]{2,1,0:T(8,128)S(1)} %get-tuple-element.24), channel_id=1, source_target_pairs={{0,2},{1,3},{2,0},{3,1},{4,6},{5,7},{6,4},{7,5},{8,10},{9,11},{10,... | collective-permute-start | bytes 786440 | tf_op jit(solution)/shard_map/ppermute | solution.py:17
  51.5 13.4 %collective-permute-start.9 = (f32[4,128,128]{2,1,0:T(8,128)S(1)}, f32[4,128,128]{2,1,0:T(8,128)S(1)}, u32[]{:S(2)}, u32[]{:S(2)}) collective-permute-start(f32[4,128,128]{2,1,0:T(8,128)S(1)} %get-tuple-element.25), channel_id=1, source_target_pairs={{0,1},{1,0},{2,3},{3,2},{4,5},{5,4},{6,7},{7,6},{8,9},{9,8},{10,11... | collective-permute-start | bytes 786440 | tf_op jit(solution)/shard_map/ppermute | solution.py:17
  64.9 0.8 copy-start.8
  65.7 1.5 %collective-permute-start.10 = (f32[4,128,128]{2,1,0:T(8,128)S(1)}, f32[4,128,128]{2,1,0:T(8,128)S(1)}, u32[]{:S(2)}, u32[]{:S(2)}) collective-permute-start(f32[4,128,128]{2,1,0:T(8,128)S(1)} %get-tuple-element.10), channel_id=1, source_target_pairs={{0,4},{4,0},{8,12},{12,8},{1,5},{5,1},{9,13},{13,9},{2,6},{6,2},{1... | collective-permute-start | bytes 786440 | tf_op jit(solution)/shard_map/ppermute | solution.py:17
  68.5 14.2 %collective-permute-start.13 = (f32[4,128,128]{2,1,0:T(8,128)S(1)}, f32[4,128,128]{2,1,0:T(8,128)S(1)}, u32[]{:S(2)}, u32[]{:S(2)}) collective-permute-start(f32[4,128,128]{2,1,0:T(8,128)S(1)} %broadcast_add_fusion), channel_id=1, source_target_pairs={{0,2},{1,3},{2,0},{3,1},{4,6},{5,7},{6,4},{7,5},{8,10},{9,11},{10,... | collective-permute-start | bytes 786440 | tf_op jit(solution)/shard_map/ppermute | solution.py:17
  69.7 13.7 %collective-permute-start.11 = (f32[4,128,128]{2,1,0:T(8,128)S(1)}, f32[4,128,128]{2,1,0:T(8,128)S(1)}, u32[]{:S(2)}, u32[]{:S(2)}) collective-permute-start(f32[4,128,128]{2,1,0:T(8,128)S(1)} %add.137), channel_id=1, source_target_pairs={{0,8},{4,12},{8,0},{12,4},{1,9},{5,13},{9,1},{13,5},{2,10},{6,14},... | collective-permute-start | bytes 786440 | tf_op jit(solution)/shard_map/ppermute | solution.py:17
  71.6 11.9 %copy-start.4 = (f32[4,128,128]{2,1,0:T(8,128)S(1)}, f32[4,128,128]{2,1,0:T(8,128)}, u32[]{:S(2)}) copy-start(f32[4,128,128]{2,1,0:T(8,128)} %get-tuple-element.11) | copy-start | bytes 786436
  82.7 0.7 copy-start.11
  83.4 1.5 %collective-permute-start.14 = (f32[4,128,128]{2,1,0:T(8,128)S(1)}, f32[4,128,128]{2,1,0:T(8,128)S(1)}, u32[]{:S(2)}, u32[]{:S(2)}) collective-permute-start(f32[4,128,128]{2,1,0:T(8,128)S(1)} %fusion.54), channel_id=1, source_target_pairs={{0,4},{4,0},{8,12},{12,8},{1,5},{5,1},{9,13},{13,9},{2,6},{6,2},{1... | collective-permute-start | bytes 786440 | tf_op jit(solution)/shard_map/ppermute | solution.py:17
  84.3 9.0 %collective-permute-start.12 = (f32[4,128,128]{2,1,0:T(8,128)}, f32[4,128,128]{2,1,0:T(8,128)}, u32[]{:S(2)}, u32[]{:S(2)}) collective-permute-start(f32[4,128,128]{2,1,0:T(8,128)} %get-tuple-element.16), channel_id=1, source_target_pairs={{0,1},{1,0},{2,3},{3,2},{4,5},{5,4},{6,7},{7,6},{8,9},{9,8},{10,11... | collective-permute-start | bytes 786440 | tf_op jit(solution)/shard_map/ppermute | solution.py:17
  85.0 0.7 copy-start.5
  85.7 8.7 %collective-permute-start.15 = (f32[4,128,128]{2,1,0:T(8,128)S(1)}, f32[4,128,128]{2,1,0:T(8,128)}, u32[]{:S(2)}, u32[]{:S(2)}) collective-permute-start(f32[4,128,128]{2,1,0:T(8,128)S(1)} %add.148), channel_id=1, source_target_pairs={{0,8},{4,12},{8,0},{12,4},{1,9},{5,13},{9,1},{13,5},{2,10},{6,14},... | collective-permute-start | bytes 786440 | tf_op jit(solution)/shard_map/ppermute | solution.py:17
  87.4 7.0 %copy-start.12 = (f32[4,128,128]{2,1,0:T(8,128)S(1)}, f32[4,128,128]{2,1,0:T(8,128)}, u32[]{:S(2)}) copy-start(f32[4,128,128]{2,1,0:T(8,128)} %copy-done.11) | copy-start | bytes 786436
  93.3 1.1 %copy-start.6 = (f32[4,128,128]{2,1,0:T(8,128)S(1)}, f32[4,128,128]{2,1,0:T(8,128)}, u32[]{:S(2)}) copy-start(f32[4,128,128]{2,1,0:T(8,128)} %copy-done.5) | copy-start | bytes 786436
  93.3 1.1 %copy-start.9 = (f32[4,128,128]{2,1,0:T(8,128)S(1)}, f32[4,128,128]{2,1,0:T(8,128)}, u32[]{:S(2)}) copy-start(f32[4,128,128]{2,1,0:T(8,128)} %copy-done.8) | copy-start | bytes 786436
  94.3 1.1 %copy-start.3 = (bf16[128,1024]{1,0:T(8,128)(2,1)S(1)}, bf16[128,1024]{1,0:T(8,128)(2,1)}, u32[]{:S(2)}) copy-start(bf16[128,1024]{1,0:T(8,128)(2,1)} %param.5) | copy-start | bytes 786436

commit v10 on v8

--- a/solution.py
+++ b/solution.py
@@ -59,7 +59,7 @@
     rows_before, rows_total = [], total_b
     for index, bit in enumerate(outer_bits):
         rows_before, rows_total = subcube_step(rows_before, rows_total, "outer", bit, backward)
-        if index == 0:
+        if index == 0 and not backward:
             (earlier_a, total_a), _ = lax.optimization_barrier(((earlier_a, total_a), rows_total))
     for bit in inner_bits[1:]:
         earlier_a, total_a = subcube_step(earlier_a, total_a, "inner", bit, backward)

time: 97.4 us -> 94.4 us (0.969)
  waiting for transfers between devices: 66.4 us -> 62.9 us
  starting transfers between devices: 14.4 us -> 15.4 us
    ppermute x16, waiting for transfers between devices: 66.4 us -> 62.9 us  [swap(): return lax.ppermute(value, axis, [(i, i ^ bit) for i in range(count)])]
    add x8, other arithmetic: 2.83 us -> 1.13 us  [subcube_step(): return (earlier + [jnp.where(counted, got, 0.0)], total + got)]
    unnamed x20 -> x24, local copies, waits for them, and re-layouts: 5.21 us -> 5.61 us
  transfers between devices with their start and end apart: 16 -> 16, of which waited for: 12 -> 13; matrix products, arithmetic and copies ran while one was open for 6% -> 6% of each run, Pallas kernels for 0% -> 0%
where the time goes in v10:
time: 94.4 us; the launch traced here: 94.1 us
  waiting for transfers between devices  62.9 us (67%)
  starting transfers between devices  15.4 us (16%)
  local copies, waits for them, and re-layouts  6.27 us (7%)
  other arithmetic  5.21 us (6%)
  matrix products  3.54 us (4%)
    ppermute x16, waiting for transfers between devices, swap(): return lax.ppermute(value, axis, [(i, i ^ bit) for i in range(count)])  62.9 us
    ppermute x16, starting transfers between devices, swap(): return lax.ppermute(value, axis, [(i, i ^ bit) for i in range(count)])  15.4 us
    unnamed x24, local copies, waits for them, and re-layouts  5.61 us
    another operation x4, other arithmetic  2.12 us
  transfers between devices with their start and end apart: 16, of which 13 were waited for; matrix products, arithmetic and copies ran while one was open for 6% of the time, Pallas kernels for 0%

profile of v10, /device:TPU:0, one launch (start us, length us, event | category | flops | bytes accessed | tf_op | source)
XLA Modules:
  0.0 94.1 jit_solution(15918756875969988170)
XLA Ops:
  0.6 1.0 %copy.38 = bf16[16,8,8,128]{3,2,1,0:T(8,128)(2,1)S(1)} copy(bf16[16,8,8,128]{3,1,2,0:T(8,128)(2,1)} %bitcast.110) | data formatting | bytes 524288
  1.7 0.2 copy.11
  2.2 3.1 %collective-permute-start = (f32[4,128,128]{2,1,0:T(8,128)S(1)}, f32[4,128,128]{2,1,0:T(8,128)S(1)}, u32[]{:S(2)}, u32[]{:S(2)}) collective-permute-start(f32[4,128,128]{2,1,0:T(8,128)S(1)} %get-tuple-element.32), channel_id=1, source_target_pairs={{0,1},{1,0},{2,3},{3,2},{4,5},{5,4},{6,7},{7,6},{8,9},{9,8},{10,11... | collective-permute-start | bytes 786440 | tf_op jit(solution)/shard_map/ppermute | solution.py:17
  5.3 2.6 %collective-permute-start.1 = (f32[4,128,128]{2,1,0:T(8,128)S(1)}, f32[4,128,128]{2,1,0:T(8,128)S(1)}, u32[]{:S(2)}, u32[]{:S(2)}) collective-permute-start(f32[4,128,128]{2,1,0:T(8,128)S(1)} %get-tuple-element.33), channel_id=1, source_target_pairs={{0,2},{1,3},{2,0},{3,1},{4,6},{5,7},{6,4},{7,5},{8,10},{9,11},{10,... | collective-permute-start | bytes 786440 | tf_op jit(solution)/shard_map/ppermute | solution.py:17
  7.9 9.2 %collective-permute-done = f32[4,128,128]{2,1,0:T(8,128)S(1)} collective-permute-done((f32[4,128,128]{2,1,0:T(8,128)S(1)}, f32[4,128,128]{2,1,0:T(8,128)S(1)}, u32[]{:S(2)}, u32[]{:S(2)}) %collective-permute-start) | collective-permute-done | bytes 262176 | tf_op jit(solution)/shard_map/ppermute | solution.py:17
  17.1 2.5 %collective-permute-done.1 = f32[4,128,128]{2,1,0:T(8,128)S(1)} collective-permute-done((f32[4,128,128]{2,1,0:T(8,128)S(1)}, f32[4,128,128]{2,1,0:T(8,128)S(1)}, u32[]{:S(2)}, u32[]{:S(2)}) %collective-permute-start.1) | collective-permute-done | bytes 262176 | tf_op jit(solution)/shard_map/ppermute | solution.py:17
  19.8 1.5 %collective-permute-done.2 = f32[4,128,128]{2,1,0:T(8,128)S(1)} collective-permute-done((f32[4,128,128]{2,1,0:T(8,128)S(1)}, f32[4,128,128]{2,1,0:T(8,128)S(1)}, u32[]{:S(2)}, u32[]{:S(2)}) %collective-permute-start.2) | collective-permute-done | bytes 262176 | tf_op jit(solution)/shard_map/ppermute | solution.py:17
  21.4 0.4 collective-permute-start.3
  21.8 1.5 %collective-permute-start.6 = (f32[4,128,128]{2,1,0:T(8,128)S(1)}, f32[4,128,128]{2,1,0:T(8,128)S(1)}, u32[]{:S(2)}, u32[]{:S(2)}) collective-permute-start(f32[4,128,128]{2,1,0:T(8,128)S(1)} %add.98), channel_id=1, source_target_pairs={{0,8},{4,12},{8,0},{12,4},{1,9},{5,13},{9,1},{13,5},{2,10},{6,14},... | collective-permute-start | bytes 786440 | tf_op jit(solution)/shard_map/ppermute | solution.py:17
  23.3 12.9 %collective-permute-done.3 = f32[4,128,128]{2,1,0:T(8,128)S(1)} collective-permute-done((f32[4,128,128]{2,1,0:T(8,128)S(1)}, f32[4,128,128]{2,1,0:T(8,128)S(1)}, u32[]{:S(2)}, u32[]{:S(2)}) %collective-permute-start.3) | collective-permute-done | bytes 262176 | tf_op jit(solution)/shard_map/ppermute | solution.py:17
  36.5 1.3 %collective-permute-done.4 = f32[4,128,128]{2,1,0:T(8,128)S(1)} collective-permute-done((f32[4,128,128]{2,1,0:T(8,128)S(1)}, f32[4,128,128]{2,1,0:T(8,128)S(1)}, u32[]{:S(2)}, u32[]{:S(2)}) %collective-permute-start.4) | collective-permute-done | bytes 262176 | tf_op jit(solution)/shard_map/ppermute | solution.py:17
  37.9 1.6 %collective-permute-start.5 = (f32[4,128,128]{2,1,0:T(8,128)S(1)}, f32[4,128,128]{2,1,0:T(8,128)S(1)}, u32[]{:S(2)}, u32[]{:S(2)}) collective-permute-start(f32[4,128,128]{2,1,0:T(8,128)S(1)} %add.102), channel_id=1, source_target_pairs={{0,8},{4,12},{8,0},{12,4},{1,9},{5,13},{9,1},{13,5},{2,10},{6,14},... | collective-permute-start | bytes 786440 | tf_op jit(solution)/shard_map/ppermute | solution.py:17
  39.4 0.3 fusion.8
  39.7 5.4 %collective-permute-done.7 = f32[4,128,128]{2,1,0:T(8,128)S(1)} collective-permute-done((f32[4,128,128]{2,1,0:T(8,128)S(1)}, f32[4,128,128]{2,1,0:T(8,128)S(1)}, u32[]{:S(2)}, u32[]{:S(2)}) %collective-permute-start.7) | collective-permute-done | bytes 262176 | tf_op jit(solution)/shard_map/ppermute | solution.py:17
  45.2 1.1 %collective-permute-done.5 = f32[4,128,128]{2,1,0:T(8,128)S(1)} collective-permute-done((f32[4,128,128]{2,1,0:T(8,128)S(1)}, f32[4,128,128]{2,1,0:T(8,128)S(1)}, u32[]{:S(2)}, u32[]{:S(2)}) %collective-permute-start.5) | collective-permute-done | bytes 262176 | tf_op jit(solution)/shard_map/ppermute | solution.py:17
  46.4 0.3 fusion.6
  46.7 0.3 multiply_reduce_fusion
  47.3 0.7 copy-done.5
  48.0 0.2 fusion.13
  48.2 0.9 fusion.15
  49.3 0.3 convolution_bitcast_fusion.2
  49.7 0.7 collective-permute-start.8
  50.4 1.3 %collective-permute-start.9 = (f32[4,128,128]{2,1,0:T(8,128)S(1)}, f32[4,128,128]{2,1,0:T(8,128)S(1)}, u32[]{:S(2)}, u32[]{:S(2)}) collective-permute-start(f32[4,128,128]{2,1,0:T(8,128)S(1)} %get-tuple-element.29), channel_id=1, source_target_pairs={{0,1},{1,0},{2,3},{3,2},{4,5},{5,4},{6,7},{7,6},{8,9},{9,8},{10,11... | collective-permute-start | bytes 786440 | tf_op jit(solution)/shard_map/ppermute | solution.py:17
  51.6 12.1 %collective-permute-done.8 = f32[4,128,128]{2,1,0:T(8,128)S(1)} collective-permute-done((f32[4,128,128]{2,1,0:T(8,128)S(1)}, f32[4,128,128]{2,1,0:T(8,128)S(1)}, u32[]{:S(2)}, u32[]{:S(2)}) %collective-permute-start.8) | collective-permute-done | bytes 262176 | tf_op jit(solution)/shard_map/ppermute | solution.py:17
  63.8 0.6 copy-done.6
  64.4 0.9 collective-permute-start.13
  65.3 0.3 fusion.12
  65.6 0.6 copy-done.9
  66.3 0.2 fusion.43
  66.5 0.4 collective-permute-done.10
  66.9 1.6 %collective-permute-start.11 = (f32[4,128,128]{2,1,0:T(8,128)S(1)}, f32[4,128,128]{2,1,0:T(8,128)S(1)}, u32[]{:S(2)}, u32[]{:S(2)}) collective-permute-start(f32[4,128,128]{2,1,0:T(8,128)S(1)} %add.114), channel_id=1, source_target_pairs={{0,8},{4,12},{8,0},{12,4},{1,9},{5,13},{9,1},{13,5},{2,10},{6,14},... | collective-permute-start | bytes 786440 | tf_op jit(solution)/shard_map/ppermute | solution.py:17
  68.4 9.2 %collective-permute-done.13 = f32[4,128,128]{2,1,0:T(8,128)S(1)} collective-permute-done((f32[4,128,128]{2,1,0:T(8,128)S(1)}, f32[4,128,128]{2,1,0:T(8,128)S(1)}, u32[]{:S(2)}, u32[]{:S(2)}) %collective-permute-start.13) | collective-permute-done | bytes 262176 | tf_op jit(solution)/shard_map/ppermute | solution.py:17
  77.8 0.3 convolution_bitcast_fusion
  78.1 0.3 convolution_bitcast_fusion.4
  78.4 0.9 collective-permute-done.14
  79.3 0.8 add.122
  80.1 1.5 %collective-permute-start.15 = (f32[4,128,128]{2,1,0:T(8,128)}, f32[4,128,128]{2,1,0:T(8,128)}, u32[]{:S(2)}, u32[]{:S(2)}) collective-permute-start(f32[4,128,128]{2,1,0:T(8,128)} %add.122), channel_id=1, source_target_pairs={{0,8},{4,12},{8,0},{12,4},{1,9},{5,13},{9,1},{13,5},{2,10},{6,14},... | collective-permute-start | bytes 786440 | tf_op jit(solution)/shard_map/ppermute | solution.py:17
  81.6 0.8 add_select_fusion
  82.4 0.2 fusion.11
  82.6 0.9 copy.28
  83.5 5.3 %collective-permute-done.15 = f32[4,128,128]{2,1,0:T(8,128)} collective-permute-done((f32[4,128,128]{2,1,0:T(8,128)}, f32[4,128,128]{2,1,0:T(8,128)}, u32[]{:S(2)}, u32[]{:S(2)}) %collective-permute-start.15) | collective-permute-done | bytes 262176 | tf_op jit(solution)/shard_map/ppermute | solution.py:17
  88.8 1.0 %add_convert_fusion = bf16[4,128,128]{2,1,0:T(8,128)(2,1)S(1)} fusion(f32[4,128,128]{2,1,0:T(8,128)} %collective-permute-done.15, f32[4,128,128]{2,1,0:T(8,128)S(1)} %copy-done.4, f32[4,128,128]{2,1,0:T(8,128)S(1)} %collective-permute-done.13, f32[4,128,128]{2,1,0:T(8,128)S(1)} %copy-done.7, pred[]{:T(512)S(6)} %not.19, pred[]{:T(512)S(6)} %not.18, ...), kind=kLoop, calls=%fused_computation.45 | loop fusion | flops 524288 | bytes 1179652 | tf_op jit(solution)/shard_map/convert.1
  89.8 1.0 %collective-permute-done.12 = f32[4,128,128]{2,1,0:T(8,128)} collective-permute-done((f32[4,128,128]{2,1,0:T(8,128)}, f32[4,128,128]{2,1,0:T(8,128)}, u32[]{:S(2)}, u32[]{:S(2)}) %collective-permute-start.12) | collective-permute-done | bytes 262176 | tf_op jit(solution)/shard_map/ppermute | solution.py:17
  90.8 1.0 %add_convert_fusion.1 = bf16[4,128,128]{2,1,0:T(8,128)(2,1)S(1)} fusion(f32[4,128,128]{2,1,0:T(8,128)S(1)} %get-tuple-element.21, f32[4,128,128]{2,1,0:T(8,128)} %collective-permute-done.12), kind=kLoop, calls=%fused_computation.46 | loop fusion | flops 131072 | bytes 655360 | tf_op jit(solution)/shard_map/convert
  91.7 0.3 fusion.9
  92.1 0.9 copy.30
  92.9 0.3 fusion.10
  93.2 0.9 copy.29
  (44 shorter events, 1.6 us)
Async XLA Ops:
  0.6 1.3 %copy-start = (bf16[128,1024]{1,0:T(8,128)(2,1)S(1)}, bf16[128,1024]{1,0:T(8,128)(2,1)}, u32[]{:S(2)}) copy-start(bf16[128,1024]{1,0:T(8,128)(2,1)} %param.6) | copy-start | bytes 786436
  2.2 14.9 %collective-permute-start = (f32[4,128,128]{2,1,0:T(8,128)S(1)}, f32[4,128,128]{2,1,0:T(8,128)S(1)}, u32[]{:S(2)}, u32[]{:S(2)}) collective-permute-start(f32[4,128,128]{2,1,0:T(8,128)S(1)} %get-tuple-element.32), channel_id=1, source_target_pairs={{0,1},{1,0},{2,3},{3,2},{4,5},{5,4},{6,7},{7,6},{8,9},{9,8},{10,11... | collective-permute-start | bytes 786440 | tf_op jit(solution)/shard_map/ppermute | solution.py:17
  5.3 14.3 %collective-permute-start.1 = (f32[4,128,128]{2,1,0:T(8,128)S(1)}, f32[4,128,128]{2,1,0:T(8,128)S(1)}, u32[]{:S(2)}, u32[]{:S(2)}) collective-permute-start(f32[4,128,128]{2,1,0:T(8,128)S(1)} %get-tuple-element.33), channel_id=1, source_target_pairs={{0,2},{1,3},{2,0},{3,1},{4,6},{5,7},{6,4},{7,5},{8,10},{9,11},{10,... | collective-permute-start | bytes 786440 | tf_op jit(solution)/shard_map/ppermute | solution.py:17
  19.7 1.6 %collective-permute-start.2 = (f32[4,128,128]{2,1,0:T(8,128)S(1)}, f32[4,128,128]{2,1,0:T(8,128)S(1)}, u32[]{:S(2)}, u32[]{:S(2)}) collective-permute-start(f32[4,128,128]{2,1,0:T(8,128)S(1)} %get-tuple-element.10), channel_id=1, source_target_pairs={{0,4},{4,0},{8,12},{12,8},{1,5},{5,1},{9,13},{13,9},{2,6},{6,2},{1... | collective-permute-start | bytes 786440 | tf_op jit(solution)/shard_map/ppermute | solution.py:17
  21.4 14.8 %collective-permute-start.3 = (f32[4,128,128]{2,1,0:T(8,128)S(1)}, f32[4,128,128]{2,1,0:T(8,128)S(1)}, u32[]{:S(2)}, u32[]{:S(2)}) collective-permute-start(f32[4,128,128]{2,1,0:T(8,128)S(1)} %get-tuple-element.12), channel_id=1, source_target_pairs={{0,2},{1,3},{2,0},{3,1},{4,6},{5,7},{6,4},{7,5},{8,10},{9,11},{10,... | collective-permute-start | bytes 786440 | tf_op jit(solution)/shard_map/ppermute | solution.py:17
  21.8 14.6 %collective-permute-start.6 = (f32[4,128,128]{2,1,0:T(8,128)S(1)}, f32[4,128,128]{2,1,0:T(8,128)S(1)}, u32[]{:S(2)}, u32[]{:S(2)}) collective-permute-start(f32[4,128,128]{2,1,0:T(8,128)S(1)} %add.98), channel_id=1, source_target_pairs={{0,8},{4,12},{8,0},{12,4},{1,9},{5,13},{9,1},{13,5},{2,10},{6,14},... | collective-permute-start | bytes 786440 | tf_op jit(solution)/shard_map/ppermute | solution.py:17
  36.2 1.6 %collective-permute-start.4 = (f32[4,128,128]{2,1,0:T(8,128)S(1)}, f32[4,128,128]{2,1,0:T(8,128)S(1)}, u32[]{:S(2)}, u32[]{:S(2)}) collective-permute-start(f32[4,128,128]{2,1,0:T(8,128)S(1)} %add.100), channel_id=1, source_target_pairs={{0,4},{4,0},{8,12},{12,8},{1,5},{5,1},{9,13},{13,9},{2,6},{6,2},{1... | collective-permute-start | bytes 786440 | tf_op jit(solution)/shard_map/ppermute | solution.py:17
  36.4 8.8 %collective-permute-start.7 = (f32[4,128,128]{2,1,0:T(8,128)S(1)}, f32[4,128,128]{2,1,0:T(8,128)S(1)}, u32[]{:S(2)}, u32[]{:S(2)}) collective-permute-start(f32[4,128,128]{2,1,0:T(8,128)S(1)} %get-tuple-element.22), channel_id=1, source_target_pairs={{0,1},{1,0},{2,3},{3,2},{4,5},{5,4},{6,7},{7,6},{8,9},{9,8},{10,11... | collective-permute-start | bytes 786440 | tf_op jit(solution)/shard_map/ppermute | solution.py:17
  36.5 2.9 %copy-start.1 = (bf16[128,1024]{1,0:T(8,128)(2,1)S(1)}, bf16[128,1024]{1,0:T(8,128)(2,1)}, u32[]{:S(2)}) copy-start(bf16[128,1024]{1,0:T(8,128)(2,1)} %param.4) | copy-start | bytes 786436
  36.5 2.9 %copy-start.2 = (bf16[128,1024]{1,0:T(8,128)(2,1)S(1)}, bf16[128,1024]{1,0:T(8,128)(2,1)}, u32[]{:S(2)}) copy-start(bf16[128,1024]{1,0:T(8,128)(2,1)} %param.5) | copy-start | bytes 786436
  37.9 8.4 %collective-permute-start.5 = (f32[4,128,128]{2,1,0:T(8,128)S(1)}, f32[4,128,128]{2,1,0:T(8,128)S(1)}, u32[]{:S(2)}, u32[]{:S(2)}) collective-permute-start(f32[4,128,128]{2,1,0:T(8,128)S(1)} %add.102), channel_id=1, source_target_pairs={{0,8},{4,12},{8,0},{12,4},{1,9},{5,13},{9,1},{13,5},{2,10},{6,14},... | collective-permute-start | bytes 786440 | tf_op jit(solution)/shard_map/ppermute | solution.py:17
  39.7 7.0 %copy-start.8 = (bf16[8,128,128]{2,1,0:T(8,128)(2,1)}, bf16[8,128,128]{2,1,0:T(8,128)(2,1)S(1)}, u32[]{:S(2)}) copy-start(bf16[8,128,128]{2,1,0:T(8,128)(2,1)S(1)} %fusion.8) | copy-start | bytes 786436
  47.0 1.0 %copy-start.5 = (bf16[128,1024]{1,0:T(8,128)(2,1)S(1)}, bf16[128,1024]{1,0:T(8,128)(2,1)}, u32[]{:S(2)}) copy-start(bf16[128,1024]{1,0:T(8,128)(2,1)} %param.7) | copy-start | bytes 786436
  49.7 14.1 %collective-permute-start.8 = (f32[4,128,128]{2,1,0:T(8,128)S(1)}, f32[4,128,128]{2,1,0:T(8,128)S(1)}, u32[]{:S(2)}, u32[]{:S(2)}) collective-permute-start(f32[4,128,128]{2,1,0:T(8,128)S(1)} %get-tuple-element.28), channel_id=1, source_target_pairs={{0,2},{1,3},{2,0},{3,1},{4,6},{5,7},{6,4},{7,5},{8,10},{9,11},{10,... | collective-permute-start | bytes 786440 | tf_op jit(solution)/shard_map/ppermute | solution.py:17
  50.4 13.4 %collective-permute-start.9 = (f32[4,128,128]{2,1,0:T(8,128)S(1)}, f32[4,128,128]{2,1,0:T(8,128)S(1)}, u32[]{:S(2)}, u32[]{:S(2)}) collective-permute-start(f32[4,128,128]{2,1,0:T(8,128)S(1)} %get-tuple-element.29), channel_id=1, source_target_pairs={{0,1},{1,0},{2,3},{3,2},{4,5},{5,4},{6,7},{7,6},{8,9},{9,8},{10,11... | collective-permute-start | bytes 786440 | tf_op jit(solution)/shard_map/ppermute | solution.py:17
  63.7 0.7 copy-start.6
  64.4 13.2 %collective-permute-start.13 = (f32[4,128,128]{2,1,0:T(8,128)S(1)}, f32[4,128,128]{2,1,0:T(8,128)S(1)}, u32[]{:S(2)}, u32[]{:S(2)}) collective-permute-start(f32[4,128,128]{2,1,0:T(8,128)S(1)} %get-tuple-element.27), channel_id=1, source_target_pairs={{0,2},{1,3},{2,0},{3,1},{4,6},{5,7},{6,4},{7,5},{8,10},{9,11},{10,... | collective-permute-start | bytes 786440 | tf_op jit(solution)/shard_map/ppermute | solution.py:17
  65.3 0.9 %copy-start.9 = (bf16[8,128,128]{2,1,0:T(8,128)(2,1)S(1)}, bf16[8,128,128]{2,1,0:T(8,128)(2,1)}, u32[]{:S(2)}) copy-start(bf16[8,128,128]{2,1,0:T(8,128)(2,1)} %copy-done.8) | copy-start | bytes 786436
  65.3 1.5 %collective-permute-start.10 = (f32[4,128,128]{2,1,0:T(8,128)S(1)}, f32[4,128,128]{2,1,0:T(8,128)S(1)}, u32[]{:S(2)}, u32[]{:S(2)}) collective-permute-start(f32[4,128,128]{2,1,0:T(8,128)S(1)} %get-tuple-element.14), channel_id=1, source_target_pairs={{0,4},{4,0},{8,12},{12,8},{1,5},{5,1},{9,13},{13,9},{2,6},{6,2},{1... | collective-permute-start | bytes 786440 | tf_op jit(solution)/shard_map/ppermute | solution.py:17
  66.9 14.7 %collective-permute-start.11 = (f32[4,128,128]{2,1,0:T(8,128)S(1)}, f32[4,128,128]{2,1,0:T(8,128)S(1)}, u32[]{:S(2)}, u32[]{:S(2)}) collective-permute-start(f32[4,128,128]{2,1,0:T(8,128)S(1)} %add.114), channel_id=1, source_target_pairs={{0,8},{4,12},{8,0},{12,4},{1,9},{5,13},{9,1},{13,5},{2,10},{6,14},... | collective-permute-start | bytes 786440 | tf_op jit(solution)/shard_map/ppermute | solution.py:17
  77.7 1.6 %collective-permute-start.14 = (f32[4,128,128]{2,1,0:T(8,128)S(1)}, f32[4,128,128]{2,1,0:T(8,128)S(1)}, u32[]{:S(2)}, u32[]{:S(2)}) collective-permute-start(f32[4,128,128]{2,1,0:T(8,128)S(1)} %add.120), channel_id=1, source_target_pairs={{0,4},{4,0},{8,12},{12,8},{1,5},{5,1},{9,13},{13,9},{2,6},{6,2},{1... | collective-permute-start | bytes 786440 | tf_op jit(solution)/shard_map/ppermute | solution.py:17
  79.3 0.8 copy-start.3
  80.1 8.7 %collective-permute-start.15 = (f32[4,128,128]{2,1,0:T(8,128)}, f32[4,128,128]{2,1,0:T(8,128)}, u32[]{:S(2)}, u32[]{:S(2)}) collective-permute-start(f32[4,128,128]{2,1,0:T(8,128)} %add.122), channel_id=1, source_target_pairs={{0,8},{4,12},{8,0},{12,4},{1,9},{5,13},{9,1},{13,5},{2,10},{6,14},... | collective-permute-start | bytes 786440 | tf_op jit(solution)/shard_map/ppermute | solution.py:17
  82.4 8.4 %collective-permute-start.12 = (f32[4,128,128]{2,1,0:T(8,128)}, f32[4,128,128]{2,1,0:T(8,128)}, u32[]{:S(2)}, u32[]{:S(2)}) collective-permute-start(f32[4,128,128]{2,1,0:T(8,128)} %get-tuple-element.20), channel_id=1, source_target_pairs={{0,1},{1,0},{2,3},{3,2},{4,5},{5,4},{6,7},{7,6},{8,9},{9,8},{10,11... | collective-permute-start | bytes 786440 | tf_op jit(solution)/shard_map/ppermute | solution.py:17
  82.6 6.2 %copy-start.4 = (f32[4,128,128]{2,1,0:T(8,128)S(1)}, f32[4,128,128]{2,1,0:T(8,128)}, u32[]{:S(2)}) copy-start(f32[4,128,128]{2,1,0:T(8,128)} %copy-done.3) | copy-start | bytes 786436
  82.6 6.2 %copy-start.7 = (f32[4,128,128]{2,1,0:T(8,128)S(1)}, f32[4,128,128]{2,1,0:T(8,128)}, u32[]{:S(2)}) copy-start(f32[4,128,128]{2,1,0:T(8,128)} %copy-done.6) | copy-start | bytes 786436

commit v11 on v10

--- a/solution.py
+++ b/solution.py
@@ -73,7 +73,7 @@
     earlier_b = known + swap(sent, "inner", low)
     if backward:
         earlier_a, earlier_b = earlier_b, earlier_a
-    return jnp.concatenate([earlier_a, earlier_b], axis=0)
+    return earlier_a, earlier_b
 
 
 def per_device(query, key, value, grad_out):
@@ -86,7 +86,7 @@
     column = lax.broadcasted_iota(jnp.int32, (rows_dev, rows_dev), 1)
     causal = (line >= column)[None]
     state = jnp.einsum("thi,thj->hij", key_rows, value_rows, preferred_element_type=jnp.float32)
-    prior = chunked_scan(state, False)
+    prior = jnp.concatenate(chunked_scan(state, False), axis=0)
     prior_half = prior.astype(jnp.bfloat16)
     scores = (
         jnp.einsum("thi,shi->hts", queries, key_rows, preferred_element_type=jnp.float32) * scaling
@@ -114,17 +114,33 @@
         + jnp.einsum("thj,hij->thi", grad_half, prior_half, preferred_element_type=jnp.float32)
     )
     grad_state = jnp.einsum("thi,thj->hij", queries, grad_half, preferred_element_type=jnp.float32)
-    later = chunked_scan(grad_state, True)
-    later_half = later.astype(jnp.bfloat16)
-    grad_k = jnp.einsum("hts,thi->shi", dscore_half, queries, preferred_element_type=jnp.float32)
-    grad_k = scaling * (
-        grad_k
-        + jnp.einsum("shj,hij->shi", value_rows, later_half, preferred_element_type=jnp.float32)
-    )
-    grad_v = jnp.einsum("hts,thj->shj", score_half, grad_half, preferred_element_type=jnp.float32)
-    grad_v = grad_v + scaling * jnp.einsum(
-        "shi,hij->shj", key_rows, later_half, preferred_element_type=jnp.float32
-    )
+    half = HEADS // 2
+    grad_k, grad_v = [], []
+    for heads, later in zip((slice(0, half), slice(half, HEADS)), chunked_scan(grad_state, True)):
+        later_half = later.astype(jnp.bfloat16)
+        queries_part, key_part, value_part = queries[:, heads], key_rows[:, heads], value_rows[:, heads]
+        part_k = jnp.einsum(
+            "hts,thi->shi", dscore_half[heads], queries_part, preferred_element_type=jnp.float32
+        )
+        grad_k.append(
+            scaling
+            * (
+                part_k
+                + jnp.einsum(
+                    "shj,hij->shi", value_part, later_half, preferred_element_type=jnp.float32
+                )
+            )
+        )
+        part_v = jnp.einsum(
+            "hts,thj->shj", score_half[heads], grad_half[:, heads], preferred_element_type=jnp.float32
+        )
+        grad_v.append(
+            part_v
+            + scaling
+            * jnp.einsum("shi,hij->shj", key_part, later_half, preferred_element_type=jnp.float32)
+        )
+    grad_k = jnp.concatenate(grad_k, axis=1)
+    grad_v = jnp.concatenate(grad_v, axis=1)
     width = HEADS * HEAD
     return (
         normed.astype(jnp.bfloat16),

time: 94.4 us -> 97.4 us (1.032)
  other arithmetic: 5.21 us -> 7.1 us
    convert_element_type x0 -> x2, other arithmetic: none -> 2.05 us  [per_device(): later_half = later.astype(jnp.bfloat16)]
    another operation x4 -> x2, other arithmetic: 2.12 us -> 1.05 us
    dot_general x4 -> x8, matrix products: 1.15 us -> 2.21 us  [the longest x2 1.05 us: per_device(): jnp.einsum('hts,thj->shj', score_half[heads], grad_half[:, heads], prefer...]
    unnamed x24 -> x20, local copies, waits for them, and re-layouts: 5.61 us -> 6.22 us
  transfers between devices with their start and end apart: 16 -> 16, of which waited for: 13 -> 10; matrix products, arithmetic and copies ran while one was open for 6% -> 9% of each run, Pallas kernels for 0% -> 0%
where the time goes in v11:
time: 97.4 us; the launch traced here: 97.1 us
  waiting for transfers between devices  62.7 us (64%)
  starting transfers between devices  15.2 us (16%)
  other arithmetic  7.1 us (7%)
  local copies, waits for them, and re-layouts  6.66 us (7%)
  matrix products  4.51 us (5%)
    ppermute x16, waiting for transfers between devices, swap(): return lax.ppermute(value, axis, [(i, i ^ bit) for i in range(count)])  62.7 us
    ppermute x16, starting transfers between devices, swap(): return lax.ppermute(value, axis, [(i, i ^ bit) for i in range(count)])  15.2 us
    unnamed x20, local copies, waits for them, and re-layouts  6.22 us
    convert_element_type x2, other arithmetic, per_device(): later_half = later.astype(jnp.bfloat16)  2.05 us
  transfers between devices with their start and end apart: 16, of which 10 were waited for; matrix products, arithmetic and copies ran while one was open for 9% of the time, Pallas kernels for 0%

profile of v11, /device:TPU:0, one launch (start us, length us, event | category | flops | bytes accessed | tf_op | source)
XLA Modules:
  0.0 97.1 jit_solution(11639394448174604289)
XLA Ops:
  0.6 1.2 %copy.27 = bf16[128,1024]{0,1:T(8,128)(2,1)S(1)} copy(bf16[128,1024]{1,0:T(8,128)(2,1)} %param.5) | data formatting | bytes 524288 | tf_op args[1]
  2.0 0.3 fusion.39
  2.3 3.1 %collective-permute-start = (f32[4,128,128]{2,1,0:T(8,128)S(1)}, f32[4,128,128]{2,1,0:T(8,128)S(1)}, u32[]{:S(2)}, u32[]{:S(2)}) collective-permute-start(f32[4,128,128]{2,1,0:T(8,128)S(1)} %get-tuple-element.36), channel_id=1, source_target_pairs={{0,1},{1,0},{2,3},{3,2},{4,5},{5,4},{6,7},{7,6},{8,9},{9,8},{10,11... | collective-permute-start | bytes 786440 | tf_op jit(solution)/shard_map/ppermute | solution.py:17
  5.5 2.6 %collective-permute-start.1 = (f32[4,128,128]{2,1,0:T(8,128)S(1)}, f32[4,128,128]{2,1,0:T(8,128)S(1)}, u32[]{:S(2)}, u32[]{:S(2)}) collective-permute-start(f32[4,128,128]{2,1,0:T(8,128)S(1)} %get-tuple-element.37), channel_id=1, source_target_pairs={{0,2},{1,3},{2,0},{3,1},{4,6},{5,7},{6,4},{7,5},{8,10},{9,11},{10,... | collective-permute-start | bytes 786440 | tf_op jit(solution)/shard_map/ppermute | solution.py:17
  8.0 9.2 %collective-permute-done = f32[4,128,128]{2,1,0:T(8,128)S(1)} collective-permute-done((f32[4,128,128]{2,1,0:T(8,128)S(1)}, f32[4,128,128]{2,1,0:T(8,128)S(1)}, u32[]{:S(2)}, u32[]{:S(2)}) %collective-permute-start) | collective-permute-done | bytes 262176 | tf_op jit(solution)/shard_map/ppermute | solution.py:17
  17.3 2.5 %collective-permute-done.1 = f32[4,128,128]{2,1,0:T(8,128)S(1)} collective-permute-done((f32[4,128,128]{2,1,0:T(8,128)S(1)}, f32[4,128,128]{2,1,0:T(8,128)S(1)}, u32[]{:S(2)}, u32[]{:S(2)}) %collective-permute-start.1) | collective-permute-done | bytes 262176 | tf_op jit(solution)/shard_map/ppermute | solution.py:17
  20.0 1.5 %collective-permute-done.2 = f32[4,128,128]{2,1,0:T(8,128)S(1)} collective-permute-done((f32[4,128,128]{2,1,0:T(8,128)S(1)}, f32[4,128,128]{2,1,0:T(8,128)S(1)}, u32[]{:S(2)}, u32[]{:S(2)}) %collective-permute-start.2) | collective-permute-done | bytes 262176 | tf_op jit(solution)/shard_map/ppermute | solution.py:17
  21.5 0.4 collective-permute-start.3
  21.9 1.5 %collective-permute-start.6 = (f32[4,128,128]{2,1,0:T(8,128)S(1)}, f32[4,128,128]{2,1,0:T(8,128)S(1)}, u32[]{:S(2)}, u32[]{:S(2)}) collective-permute-start(f32[4,128,128]{2,1,0:T(8,128)S(1)} %add.109), channel_id=1, source_target_pairs={{0,8},{4,12},{8,0},{12,4},{1,9},{5,13},{9,1},{13,5},{2,10},{6,14},... | collective-permute-start | bytes 786440 | tf_op jit(solution)/shard_map/ppermute | solution.py:17
  23.4 12.9 %collective-permute-done.3 = f32[4,128,128]{2,1,0:T(8,128)S(1)} collective-permute-done((f32[4,128,128]{2,1,0:T(8,128)S(1)}, f32[4,128,128]{2,1,0:T(8,128)S(1)}, u32[]{:S(2)}, u32[]{:S(2)}) %collective-permute-start.3) | collective-permute-done | bytes 262176 | tf_op jit(solution)/shard_map/ppermute | solution.py:17
  36.5 0.8 add_select_fusion.1
  37.5 0.5 collective-permute-done.4
  38.0 1.6 %collective-permute-start.5 = (f32[4,128,128]{2,1,0:T(8,128)S(1)}, f32[4,128,128]{2,1,0:T(8,128)S(1)}, u32[]{:S(2)}, u32[]{:S(2)}) collective-permute-start(f32[4,128,128]{2,1,0:T(8,128)S(1)} %add.113), channel_id=1, source_target_pairs={{0,8},{4,12},{8,0},{12,4},{1,9},{5,13},{9,1},{13,5},{2,10},{6,14},... | collective-permute-start | bytes 786440 | tf_op jit(solution)/shard_map/ppermute | solution.py:17
  39.6 0.3 fusion.5
  39.9 6.3 %collective-permute-done.7 = f32[4,128,128]{2,1,0:T(8,128)S(1)} collective-permute-done((f32[4,128,128]{2,1,0:T(8,128)}, f32[4,128,128]{2,1,0:T(8,128)S(1)}, u32[]{:S(2)}, u32[]{:S(2)}) %collective-permute-start.7) | collective-permute-done | bytes 262176 | tf_op jit(solution)/shard_map/ppermute | solution.py:17
  46.1 0.7 copy-done.6
  46.8 1.0 %add_convert_fusion.2 = bf16[4,128,128]{2,1,0:T(8,128)(2,1)S(1)} fusion(f32[4,128,128]{2,1,0:T(8,128)S(1)} %get-tuple-element.27, f32[4,128,128]{2,1,0:T(8,128)} %copy-done.6), kind=kLoop, calls=%fused_computation.48 | loop fusion | flops 131072 | bytes 655360 | tf_op jit(solution)/shard_map/convert.7
  47.9 0.3 fusion.3
  48.2 0.3 multiply_reduce_fusion
  48.5 0.2 copy.34
  48.8 0.7 copy-done.1
  49.5 0.2 fusion.20
  49.7 0.9 fusion.22
  50.8 0.3 convolution_bitcast_fusion
  51.1 0.2 collective-permute-start.8
  51.4 1.7 %collective-permute-start.9 = (f32[4,128,128]{2,1,0:T(8,128)S(1)}, f32[4,128,128]{2,1,0:T(8,128)S(1)}, u32[]{:S(2)}, u32[]{:S(2)}) collective-permute-start(f32[4,128,128]{2,1,0:T(8,128)S(1)} %get-tuple-element.33), channel_id=1, source_target_pairs={{0,1},{1,0},{2,3},{3,2},{4,5},{5,4},{6,7},{7,6},{8,9},{9,8},{10,11... | collective-permute-start | bytes 786440 | tf_op jit(solution)/shard_map/ppermute | solution.py:17
  53.1 0.3 fusion.7
  53.4 12.2 %collective-permute-done.8 = f32[4,128,128]{2,1,0:T(8,128)S(1)} collective-permute-done((f32[4,128,128]{2,1,0:T(8,128)S(1)}, f32[4,128,128]{2,1,0:T(8,128)S(1)}, u32[]{:S(2)}, u32[]{:S(2)}) %collective-permute-start.8) | collective-permute-done | bytes 262176 | tf_op jit(solution)/shard_map/ppermute | solution.py:17
  65.6 0.6 copy-done.2
  66.3 0.9 fusion.27
  67.1 0.3 convolution_bitcast_fusion.2
  67.4 0.6 collective-permute-start.13
  68.1 1.6 %collective-permute-start.11 = (f32[4,128,128]{2,1,0:T(8,128)S(1)}, f32[4,128,128]{2,1,0:T(8,128)S(1)}, u32[]{:S(2)}, u32[]{:S(2)}) collective-permute-start(f32[4,128,128]{2,1,0:T(8,128)S(1)} %add.125), channel_id=1, source_target_pairs={{0,8},{4,12},{8,0},{12,4},{1,9},{5,13},{9,1},{13,5},{2,10},{6,14},... | collective-permute-start | bytes 786440 | tf_op jit(solution)/shard_map/ppermute | solution.py:17
  69.9 0.2 fusion.6
  70.1 11.7 %collective-permute-done.13 = f32[4,128,128]{2,1,0:T(8,128)S(1)} collective-permute-done((f32[4,128,128]{2,1,0:T(8,128)S(1)}, f32[4,128,128]{2,1,0:T(8,128)S(1)}, u32[]{:S(2)}, u32[]{:S(2)}) %collective-permute-start.13) | collective-permute-done | bytes 262176 | tf_op jit(solution)/shard_map/ppermute | solution.py:17
  82.0 0.8 add_select_fusion
  82.9 0.9 copy.47
  83.9 1.0 %add.134 = f32[4,128,128]{2,1,0:T(8,128)S(1)} add(f32[4,128,128]{2,1,0:T(8,128)S(1)} %add.132, f32[4,128,128]{2,1,0:T(8,128)} %collective-permute-done.14) | non-fusion elementwise | flops 65536 | bytes 786432 | tf_op jit(solution)/shard_map/add | solution.py:28
  84.9 1.6 %collective-permute-start.15 = (f32[4,128,128]{2,1,0:T(8,128)S(1)}, f32[4,128,128]{2,1,0:T(8,128)S(1)}, u32[]{:S(2)}, u32[]{:S(2)}) collective-permute-start(f32[4,128,128]{2,1,0:T(8,128)S(1)} %add.134), channel_id=1, source_target_pairs={{0,8},{4,12},{8,0},{12,4},{1,9},{5,13},{9,1},{13,5},{2,10},{6,14},... | collective-permute-start | bytes 786440 | tf_op jit(solution)/shard_map/ppermute | solution.py:17
  86.5 5.2 %collective-permute-done.12 = f32[4,128,128]{2,1,0:T(8,128)} collective-permute-done((f32[4,128,128]{2,1,0:T(8,128)}, f32[4,128,128]{2,1,0:T(8,128)}, u32[]{:S(2)}, u32[]{:S(2)}) %collective-permute-start.12) | collective-permute-done | bytes 262176 | tf_op jit(solution)/shard_map/ppermute | solution.py:17
  91.7 1.0 %add_convert_fusion.1 = bf16[4,128,128]{2,1,0:T(8,128)(2,1)S(1)} fusion(f32[4,128,128]{2,1,0:T(8,128)S(1)} %get-tuple-element.25, f32[4,128,128]{2,1,0:T(8,128)} %collective-permute-done.12), kind=kLoop, calls=%fused_computation.46 | loop fusion | flops 131072 | bytes 655360 | tf_op jit(solution)/shard_map/convert_element_type | solution.py:120
  92.7 0.2 fusion.19
  93.0 0.7 collective-permute-done.15
  93.7 1.0 %add_convert_fusion = bf16[4,128,128]{2,1,0:T(8,128)(2,1)S(1)} fusion(f32[4,128,128]{2,1,0:T(8,128)S(1)} %collective-permute-done.15, f32[4,128,128]{2,1,0:T(8,128)} %collective-permute-done.14, f32[4,128,128]{2,1,0:T(8,128)S(1)} %collective-permute-done.13, f32[4,128,128]{2,1,0:T(8,128)S(1)} %copy-done.3, pred[]{:T(512)S(6)} %not.19, pred[]{:T(512)S(6)} %not.18, ...), kind=kLoop, calls=%fused_computation.45 | loop fusion | flops 524288 | bytes 1179652 | tf_op jit(solution)/shard_map/convert_element_type | solution.py:120
  94.7 0.2 fusion.18
  95.0 0.8 copy.49
  96.0 0.2 fusion.15
  96.2 0.8 copy.48
  (45 shorter events, 2.2 us)
Async XLA Ops:
  0.6 1.2 %copy-start.4 = (bf16[128,1024]{1,0:T(8,128)(2,1)S(1)}, bf16[128,1024]{1,0:T(8,128)(2,1)}, u32[]{:S(2)}) copy-start(bf16[128,1024]{1,0:T(8,128)(2,1)} %param.6) | copy-start | bytes 786436
  2.3 14.9 %collective-permute-start = (f32[4,128,128]{2,1,0:T(8,128)S(1)}, f32[4,128,128]{2,1,0:T(8,128)S(1)}, u32[]{:S(2)}, u32[]{:S(2)}) collective-permute-start(f32[4,128,128]{2,1,0:T(8,128)S(1)} %get-tuple-element.36), channel_id=1, source_target_pairs={{0,1},{1,0},{2,3},{3,2},{4,5},{5,4},{6,7},{7,6},{8,9},{9,8},{10,11... | collective-permute-start | bytes 786440 | tf_op jit(solution)/shard_map/ppermute | solution.py:17
  5.5 14.3 %collective-permute-start.1 = (f32[4,128,128]{2,1,0:T(8,128)S(1)}, f32[4,128,128]{2,1,0:T(8,128)S(1)}, u32[]{:S(2)}, u32[]{:S(2)}) collective-permute-start(f32[4,128,128]{2,1,0:T(8,128)S(1)} %get-tuple-element.37), channel_id=1, source_target_pairs={{0,2},{1,3},{2,0},{3,1},{4,6},{5,7},{6,4},{7,5},{8,10},{9,11},{10,... | collective-permute-start | bytes 786440 | tf_op jit(solution)/shard_map/ppermute | solution.py:17
  19.9 1.6 %collective-permute-start.2 = (f32[4,128,128]{2,1,0:T(8,128)S(1)}, f32[4,128,128]{2,1,0:T(8,128)S(1)}, u32[]{:S(2)}, u32[]{:S(2)}) collective-permute-start(f32[4,128,128]{2,1,0:T(8,128)S(1)} %get-tuple-element.10), channel_id=1, source_target_pairs={{0,4},{4,0},{8,12},{12,8},{1,5},{5,1},{9,13},{13,9},{2,6},{6,2},{1... | collective-permute-start | bytes 786440 | tf_op jit(solution)/shard_map/ppermute | solution.py:17
  21.5 14.8 %collective-permute-start.3 = (f32[4,128,128]{2,1,0:T(8,128)S(1)}, f32[4,128,128]{2,1,0:T(8,128)S(1)}, u32[]{:S(2)}, u32[]{:S(2)}) collective-permute-start(f32[4,128,128]{2,1,0:T(8,128)S(1)} %get-tuple-element.12), channel_id=1, source_target_pairs={{0,2},{1,3},{2,0},{3,1},{4,6},{5,7},{6,4},{7,5},{8,10},{9,11},{10,... | collective-permute-start | bytes 786440 | tf_op jit(solution)/shard_map/ppermute | solution.py:17
  21.9 14.6 %collective-permute-start.6 = (f32[4,128,128]{2,1,0:T(8,128)S(1)}, f32[4,128,128]{2,1,0:T(8,128)S(1)}, u32[]{:S(2)}, u32[]{:S(2)}) collective-permute-start(f32[4,128,128]{2,1,0:T(8,128)S(1)} %add.109), channel_id=1, source_target_pairs={{0,8},{4,12},{8,0},{12,4},{1,9},{5,13},{9,1},{13,5},{2,10},{6,14},... | collective-permute-start | bytes 786440 | tf_op jit(solution)/shard_map/ppermute | solution.py:17
  36.4 1.0 copy-start.5
  36.4 1.6 %collective-permute-start.4 = (f32[4,128,128]{2,1,0:T(8,128)S(1)}, f32[4,128,128]{2,1,0:T(8,128)S(1)}, u32[]{:S(2)}, u32[]{:S(2)}) collective-permute-start(f32[4,128,128]{2,1,0:T(8,128)S(1)} %add.111), channel_id=1, source_target_pairs={{0,4},{4,0},{8,12},{12,8},{1,5},{5,1},{9,13},{13,9},{2,6},{6,2},{1... | collective-permute-start | bytes 786440 | tf_op jit(solution)/shard_map/ppermute | solution.py:17
  37.2 8.9 %collective-permute-start.7 = (f32[4,128,128]{2,1,0:T(8,128)}, f32[4,128,128]{2,1,0:T(8,128)S(1)}, u32[]{:S(2)}, u32[]{:S(2)}) collective-permute-start(f32[4,128,128]{2,1,0:T(8,128)} %get-tuple-element.26), channel_id=1, source_target_pairs={{0,1},{1,0},{2,3},{3,2},{4,5},{5,4},{6,7},{7,6},{8,9},{9,8},{10,11... | collective-permute-start | bytes 786440 | tf_op jit(solution)/shard_map/ppermute | solution.py:17
  38.0 9.8 %collective-permute-start.5 = (f32[4,128,128]{2,1,0:T(8,128)S(1)}, f32[4,128,128]{2,1,0:T(8,128)S(1)}, u32[]{:S(2)}, u32[]{:S(2)}) collective-permute-start(f32[4,128,128]{2,1,0:T(8,128)S(1)} %add.113), channel_id=1, source_target_pairs={{0,8},{4,12},{8,0},{12,4},{1,9},{5,13},{9,1},{13,5},{2,10},{6,14},... | collective-permute-start | bytes 786440 | tf_op jit(solution)/shard_map/ppermute | solution.py:17
  46.1 0.7 copy-start.6
  48.5 1.0 copy-start.1
  51.1 14.4 %collective-permute-start.8 = (f32[4,128,128]{2,1,0:T(8,128)S(1)}, f32[4,128,128]{2,1,0:T(8,128)S(1)}, u32[]{:S(2)}, u32[]{:S(2)}) collective-permute-start(f32[4,128,128]{2,1,0:T(8,128)S(1)} %get-tuple-element.32), channel_id=1, source_target_pairs={{0,2},{1,3},{2,0},{3,1},{4,6},{5,7},{6,4},{7,5},{8,10},{9,11},{10,... | collective-permute-start | bytes 786440 | tf_op jit(solution)/shard_map/ppermute | solution.py:17
  51.4 14.2 %collective-permute-start.9 = (f32[4,128,128]{2,1,0:T(8,128)S(1)}, f32[4,128,128]{2,1,0:T(8,128)S(1)}, u32[]{:S(2)}, u32[]{:S(2)}) collective-permute-start(f32[4,128,128]{2,1,0:T(8,128)S(1)} %get-tuple-element.33), channel_id=1, source_target_pairs={{0,1},{1,0},{2,3},{3,2},{4,5},{5,4},{6,7},{7,6},{8,9},{9,8},{10,11... | collective-permute-start | bytes 786440 | tf_op jit(solution)/shard_map/ppermute | solution.py:17
  65.5 0.7 copy-start.2
  66.2 1.9 %collective-permute-start.10 = (f32[4,128,128]{2,1,0:T(8,128)S(1)}, f32[4,128,128]{2,1,0:T(8,128)S(1)}, u32[]{:S(2)}, u32[]{:S(2)}) collective-permute-start(f32[4,128,128]{2,1,0:T(8,128)S(1)} %get-tuple-element.14), channel_id=1, source_target_pairs={{0,4},{4,0},{8,12},{12,8},{1,5},{5,1},{9,13},{13,9},{2,6},{6,2},{1... | collective-permute-start | bytes 786440 | tf_op jit(solution)/shard_map/ppermute | solution.py:17
  67.4 14.3 %collective-permute-start.13 = (f32[4,128,128]{2,1,0:T(8,128)S(1)}, f32[4,128,128]{2,1,0:T(8,128)S(1)}, u32[]{:S(2)}, u32[]{:S(2)}) collective-permute-start(f32[4,128,128]{2,1,0:T(8,128)S(1)} %get-tuple-element.31), channel_id=1, source_target_pairs={{0,2},{1,3},{2,0},{3,1},{4,6},{5,7},{6,4},{7,5},{8,10},{9,11},{10,... | collective-permute-start | bytes 786440 | tf_op jit(solution)/shard_map/ppermute | solution.py:17
  68.1 13.8 %collective-permute-start.11 = (f32[4,128,128]{2,1,0:T(8,128)S(1)}, f32[4,128,128]{2,1,0:T(8,128)S(1)}, u32[]{:S(2)}, u32[]{:S(2)}) collective-permute-start(f32[4,128,128]{2,1,0:T(8,128)S(1)} %add.125), channel_id=1, source_target_pairs={{0,8},{4,12},{8,0},{12,4},{1,9},{5,13},{9,1},{13,5},{2,10},{6,14},... | collective-permute-start | bytes 786440 | tf_op jit(solution)/shard_map/ppermute | solution.py:17
  81.8 2.1 %collective-permute-start.14 = (f32[4,128,128]{2,1,0:T(8,128)S(1)}, f32[4,128,128]{2,1,0:T(8,128)}, u32[]{:S(2)}, u32[]{:S(2)}) collective-permute-start(f32[4,128,128]{2,1,0:T(8,128)S(1)} %add.132), channel_id=1, source_target_pairs={{0,4},{4,0},{8,12},{12,8},{1,5},{5,1},{9,13},{13,9},{2,6},{6,2},{1... | collective-permute-start | bytes 786440 | tf_op jit(solution)/shard_map/ppermute | solution.py:17
  82.7 9.0 %collective-permute-start.12 = (f32[4,128,128]{2,1,0:T(8,128)}, f32[4,128,128]{2,1,0:T(8,128)}, u32[]{:S(2)}, u32[]{:S(2)}) collective-permute-start(f32[4,128,128]{2,1,0:T(8,128)} %get-tuple-element.24), channel_id=1, source_target_pairs={{0,1},{1,0},{2,3},{3,2},{4,5},{5,4},{6,7},{7,6},{8,9},{9,8},{10,11... | collective-permute-start | bytes 786440 | tf_op jit(solution)/shard_map/ppermute | solution.py:17
  84.9 8.7 %collective-permute-start.15 = (f32[4,128,128]{2,1,0:T(8,128)S(1)}, f32[4,128,128]{2,1,0:T(8,128)S(1)}, u32[]{:S(2)}, u32[]{:S(2)}) collective-permute-start(f32[4,128,128]{2,1,0:T(8,128)S(1)} %add.134), channel_id=1, source_target_pairs={{0,8},{4,12},{8,0},{12,4},{1,9},{5,13},{9,1},{13,5},{2,10},{6,14},... | collective-permute-start | bytes 786440 | tf_op jit(solution)/shard_map/ppermute | solution.py:17
  91.7 1.0 %copy-start = (f32[4,128,128]{2,1,0:T(8,128)S(1)}, f32[4,128,128]{2,1,0:T(8,128)}, u32[]{:S(2)}) copy-start(f32[4,128,128]{2,1,0:T(8,128)} %fusion.27) | copy-start | bytes 786436
  92.7 1.0 copy-start.3

commit v12 on v10

--- a/solution.py
+++ b/solution.py
@@ -1,6 +1,10 @@
+import functools
+
 import jax
 import jax.numpy as jnp
 from jax import lax
+from jax.experimental import pallas as pl
+from jax.experimental.pallas import tpu as pltpu
 from jax.sharding import PartitionSpec as P
 
 HEADS = 8
@@ -50,7 +54,10 @@
         group_a, group_b = group_b, group_a
     inner_bits, outer_bits = axis_bits("inner"), axis_bits("outer")
     if not inner_bits:
-        return scan_inner_first(value, backward)
+        result = scan_inner_first(value, backward)
+        if backward:
+            return result[:half], jnp.zeros_like(result[:half]), result[half:]
+        return result
     earlier_a, total_a = subcube_step([], group_a, "inner", inner_bits[0], backward)
     earlier_b, total_b = [], group_b
     for bit in inner_bits[1:]:
@@ -70,10 +77,43 @@
     known = added(rows_before + earlier_b, group_b)
     sent = jnp.where(counted, known, known + group_b)
     earlier_a = added(earlier_a, group_a)
-    earlier_b = known + swap(sent, "inner", low)
+    got_b = swap(sent, "inner", low)
     if backward:
-        earlier_a, earlier_b = earlier_b, earlier_a
-    return jnp.concatenate([earlier_a, earlier_b], axis=0)
+        return known, got_b, earlier_a
+    return jnp.concatenate([earlier_a, known + got_b], axis=0)
+
+
+def tail_kernel(
+    scaling, lower_known, lower_got, upper_later, local_k, local_v, value, key, out_k, out_v
+):
+    half = HEADS // 2
+    for h in range(HEADS):
+        later = lower_known[h] + lower_got[h] if h < half else upper_later[h - half]
+        later_half = later.astype(jnp.bfloat16)
+        cols = slice(h * HEAD, (h + 1) * HEAD)
+        from_later_k = lax.dot_general(
+            value[:, cols], later_half, (((1,), (1,)), ((), ())), preferred_element_type=jnp.float32
+        )
+        out_k[:, cols] = (scaling * (local_k[h] + from_later_k)).astype(out_k.dtype)
+        from_later_v = lax.dot_general(
+            key[:, cols], later_half, (((1,), (0,)), ((), ())), preferred_element_type=jnp.float32
+        )
+        out_v[:, cols] = (local_v[h] + scaling * from_later_v).astype(out_v.dtype)
+
+
+def tail(lower_known, lower_got, upper_later, local_k, local_v, value, key):
+    rows = value.shape[0]
+    vmem = pl.BlockSpec(memory_space=pltpu.VMEM)
+    out = jax.ShapeDtypeStruct((rows, HEADS * HEAD), jnp.bfloat16)
+    return pl.pallas_call(
+        functools.partial(tail_kernel, HEAD ** (-0.5)),
+        out_shape=(out, out),
+        in_specs=[vmem] * 7,
+        out_specs=(vmem, vmem),
+        cost_estimate=pl.CostEstimate(
+            flops=4 * HEADS * rows * HEAD * HEAD, transcendentals=0, bytes_accessed=12 * rows * 1024 * 4
+        ),
+    )(lower_known, lower_got, upper_later, local_k, local_v, value, key)
 
 
 def per_device(query, key, value, grad_out):
@@ -114,23 +154,16 @@
         + jnp.einsum("thj,hij->thi", grad_half, prior_half, preferred_element_type=jnp.float32)
     )
     grad_state = jnp.einsum("thi,thj->hij", queries, grad_half, preferred_element_type=jnp.float32)
-    later = chunked_scan(grad_state, True)
-    later_half = later.astype(jnp.bfloat16)
-    grad_k = jnp.einsum("hts,thi->shi", dscore_half, queries, preferred_element_type=jnp.float32)
-    grad_k = scaling * (
-        grad_k
-        + jnp.einsum("shj,hij->shi", value_rows, later_half, preferred_element_type=jnp.float32)
-    )
-    grad_v = jnp.einsum("hts,thj->shj", score_half, grad_half, preferred_element_type=jnp.float32)
-    grad_v = grad_v + scaling * jnp.einsum(
-        "shi,hij->shj", key_rows, later_half, preferred_element_type=jnp.float32
-    )
+    lower_known, lower_got, upper_later = chunked_scan(grad_state, True)
+    local_k = jnp.einsum("hts,thi->hsi", dscore_half, queries, preferred_element_type=jnp.float32)
+    local_v = jnp.einsum("hts,thj->hsj", score_half, grad_half, preferred_element_type=jnp.float32)
+    grad_k, grad_v = tail(lower_known, lower_got, upper_later, local_k, local_v, value, key)
     width = HEADS * HEAD
     return (
         normed.astype(jnp.bfloat16),
         grad_q.reshape(rows_dev, width).astype(jnp.bfloat16),
-        grad_k.reshape(rows_dev, width).astype(jnp.bfloat16),
-        grad_v.reshape(rows_dev, width).astype(jnp.bfloat16),
+        grad_k,
+        grad_v,
     )
 
 

time: 94.4 us -> 91.9 us (0.974)
  Pallas kernels: 0 us -> 2.73 us
  local copies, waits for them, and re-layouts: 6.27 us -> 3.73 us
  other arithmetic: 5.21 us -> 3.18 us
    unnamed x24 -> x9, local copies, waits for them, and re-layouts: 5.61 us -> 2.29 us
    pallas_call x0 -> x1, Pallas kernels: none -> 2.73 us  [tail(): pl.pallas_call(functools.partial(tail_kernel, HEAD ** (-0.5)), out_shape=...]
    another operation x4 -> x2, other arithmetic: 2.12 us -> 0.12 us
    dot_general x4 -> x2, matrix products: 1.15 us -> 2.16 us  [the longest x1 1.09 us: per_device(): jnp.einsum('hts,thi->hsi', dscore_half, queries, preferred_element_type=j...]
    reshape x1, local copies, waits for them, and re-layouts: 0.23 us -> 1.17 us  [per_device(): key_rows = key.reshape(rows_dev, HEADS, HEAD)]
where the time goes in v12:
time: 91.9 us; the launch traced here: 91.7 us
  waiting for transfers between devices  62.1 us (68%)
  starting transfers between devices  14.7 us (16%)
  matrix products  4.42 us (5%)
  local copies, waits for them, and re-layouts  3.73 us (4%)
  other arithmetic  3.18 us (3%)
  Pallas kernels  2.73 us (3%)
    ppermute x16, waiting for transfers between devices, swap(): return lax.ppermute(value, axis, [(i, i ^ bit) for i in range(count)])  62.1 us
    ppermute x16, starting transfers between devices, swap(): return lax.ppermute(value, axis, [(i, i ^ bit) for i in range(count)])  14.7 us
    pallas_call x1, Pallas kernels, tail(): pl.pallas_call(functools.partial(tail_kernel, HEAD ** (-0.5)), out_shape=...  2.73 us
    unnamed x9, local copies, waits for them, and re-layouts  2.29 us
  transfers between devices with their start and end apart: 16, of which 13 were waited for; matrix products, arithmetic and copies ran while one was open for 6% of the time, Pallas kernels for 0%

profile of v12, /device:TPU:0, one launch (start us, length us, event | category | flops | bytes accessed | tf_op | source)
XLA Modules:
  0.0 91.7 jit_solution(3163040902084757033)
XLA Ops:
  0.7 1.2 %copy.32 = bf16[128,1024]{0,1:T(8,128)(2,1)S(1)} copy(bf16[128,1024]{1,0:T(8,128)(2,1)} %key.1) | data formatting | bytes 524288 | tf_op jit(solution)/shard_map/reshape | solution.py:123
  1.8 0.2 fusion.19
  2.1 3.1 %collective-permute-start = (f32[4,128,128]{2,1,0:T(8,128)S(1)}, f32[4,128,128]{2,1,0:T(8,128)S(1)}, u32[]{:S(2)}, u32[]{:S(2)}) collective-permute-start(f32[4,128,128]{2,1,0:T(8,128)S(1)} %get-tuple-element.36), channel_id=1, source_target_pairs={{0,1},{1,0},{2,3},{3,2},{4,5},{5,4},{6,7},{7,6},{8,9},{9,8},{10,11... | collective-permute-start | bytes 786440 | tf_op jit(solution)/shard_map/ppermute | solution.py:21
  5.2 2.6 %collective-permute-start.1 = (f32[4,128,128]{2,1,0:T(8,128)S(1)}, f32[4,128,128]{2,1,0:T(8,128)S(1)}, u32[]{:S(2)}, u32[]{:S(2)}) collective-permute-start(f32[4,128,128]{2,1,0:T(8,128)S(1)} %get-tuple-element.37), channel_id=1, source_target_pairs={{0,2},{1,3},{2,0},{3,1},{4,6},{5,7},{6,4},{7,5},{8,10},{9,11},{10,... | collective-permute-start | bytes 786440 | tf_op jit(solution)/shard_map/ppermute | solution.py:21
  7.8 9.2 %collective-permute-done = f32[4,128,128]{2,1,0:T(8,128)S(1)} collective-permute-done((f32[4,128,128]{2,1,0:T(8,128)S(1)}, f32[4,128,128]{2,1,0:T(8,128)S(1)}, u32[]{:S(2)}, u32[]{:S(2)}) %collective-permute-start) | collective-permute-done | bytes 262176 | tf_op jit(solution)/shard_map/ppermute | solution.py:21
  17.0 2.5 %collective-permute-done.1 = f32[4,128,128]{2,1,0:T(8,128)S(1)} collective-permute-done((f32[4,128,128]{2,1,0:T(8,128)S(1)}, f32[4,128,128]{2,1,0:T(8,128)S(1)}, u32[]{:S(2)}, u32[]{:S(2)}) %collective-permute-start.1) | collective-permute-done | bytes 262176 | tf_op jit(solution)/shard_map/ppermute | solution.py:21
  19.6 0.1 slice_add_fusion.1
  19.7 0.1 collective-permute-start.2
  19.7 1.5 %collective-permute-done.2 = f32[4,128,128]{2,1,0:T(8,128)S(1)} collective-permute-done((f32[4,128,128]{2,1,0:T(8,128)S(1)}, f32[4,128,128]{2,1,0:T(8,128)S(1)}, u32[]{:S(2)}, u32[]{:S(2)}) %collective-permute-start.2) | collective-permute-done | bytes 262176 | tf_op jit(solution)/shard_map/ppermute | solution.py:21
  21.3 0.4 collective-permute-start.3
  21.7 1.5 %collective-permute-start.6 = (f32[4,128,128]{2,1,0:T(8,128)S(1)}, f32[4,128,128]{2,1,0:T(8,128)S(1)}, u32[]{:S(2)}, u32[]{:S(2)}) collective-permute-start(f32[4,128,128]{2,1,0:T(8,128)S(1)} %add.88), channel_id=1, source_target_pairs={{0,8},{4,12},{8,0},{12,4},{1,9},{5,13},{9,1},{13,5},{2,10},{6,14},... | collective-permute-start | bytes 786440 | tf_op jit(solution)/shard_map/ppermute | solution.py:21
  23.2 12.9 %collective-permute-done.3 = f32[4,128,128]{2,1,0:T(8,128)S(1)} collective-permute-done((f32[4,128,128]{2,1,0:T(8,128)S(1)}, f32[4,128,128]{2,1,0:T(8,128)S(1)}, u32[]{:S(2)}, u32[]{:S(2)}) %collective-permute-start.3) | collective-permute-done | bytes 262176 | tf_op jit(solution)/shard_map/ppermute | solution.py:21
  36.1 0.1 collective-permute-start.4
  36.3 0.1 collective-permute-start.7
  36.4 1.3 %collective-permute-done.4 = f32[4,128,128]{2,1,0:T(8,128)S(1)} collective-permute-done((f32[4,128,128]{2,1,0:T(8,128)S(1)}, f32[4,128,128]{2,1,0:T(8,128)S(1)}, u32[]{:S(2)}, u32[]{:S(2)}) %collective-permute-start.4) | collective-permute-done | bytes 262176 | tf_op jit(solution)/shard_map/ppermute | solution.py:21
  37.8 1.6 %collective-permute-start.5 = (f32[4,128,128]{2,1,0:T(8,128)S(1)}, f32[4,128,128]{2,1,0:T(8,128)S(1)}, u32[]{:S(2)}, u32[]{:S(2)}) collective-permute-start(f32[4,128,128]{2,1,0:T(8,128)S(1)} %add.92), channel_id=1, source_target_pairs={{0,8},{4,12},{8,0},{12,4},{1,9},{5,13},{9,1},{13,5},{2,10},{6,14},... | collective-permute-start | bytes 786440 | tf_op jit(solution)/shard_map/ppermute | solution.py:21
  39.3 0.2 fusion.5
  39.6 5.5 %collective-permute-done.7 = f32[4,128,128]{2,1,0:T(8,128)S(1)} collective-permute-done((f32[4,128,128]{2,1,0:T(8,128)S(1)}, f32[4,128,128]{2,1,0:T(8,128)S(1)}, u32[]{:S(2)}, u32[]{:S(2)}) %collective-permute-start.7) | collective-permute-done | bytes 262176 | tf_op jit(solution)/shard_map/ppermute | solution.py:21
  45.1 1.1 %collective-permute-done.5 = f32[4,128,128]{2,1,0:T(8,128)S(1)} collective-permute-done((f32[4,128,128]{2,1,0:T(8,128)S(1)}, f32[4,128,128]{2,1,0:T(8,128)S(1)}, u32[]{:S(2)}, u32[]{:S(2)}) %collective-permute-start.5) | collective-permute-done | bytes 262176 | tf_op jit(solution)/shard_map/ppermute | solution.py:21
  46.2 0.1 add_convert_fusion.1
  46.3 0.3 fusion.3
  46.6 0.3 multiply_reduce_fusion
  47.0 0.2 copy.15
  47.2 0.7 copy-done.2
  47.9 0.2 fusion.8
  48.1 0.9 fusion.11
  49.0 0.3 convolution_bitcast_fusion
  49.3 0.8 collective-permute-start.9
  50.2 1.2 %collective-permute-start.8 = (f32[4,128,128]{2,1,0:T(8,128)S(1)}, f32[4,128,128]{2,1,0:T(8,128)S(1)}, u32[]{:S(2)}, u32[]{:S(2)}) collective-permute-start(f32[4,128,128]{2,1,0:T(8,128)S(1)} %get-tuple-element.33), channel_id=1, source_target_pairs={{0,2},{1,3},{2,0},{3,1},{4,6},{5,7},{6,4},{7,5},{8,10},{9,11},{10,... | collective-permute-start | bytes 786440 | tf_op jit(solution)/shard_map/ppermute | solution.py:21
  51.3 10.0 %collective-permute-done.9 = f32[4,128,128]{2,1,0:T(8,128)S(1)} collective-permute-done((f32[4,128,128]{2,1,0:T(8,128)S(1)}, f32[4,128,128]{2,1,0:T(8,128)S(1)}, u32[]{:S(2)}, u32[]{:S(2)}) %collective-permute-start.9) | collective-permute-done | bytes 262176 | tf_op jit(solution)/shard_map/ppermute | solution.py:21
  61.3 3.0 %collective-permute-done.8 = f32[4,128,128]{2,1,0:T(8,128)S(1)} collective-permute-done((f32[4,128,128]{2,1,0:T(8,128)S(1)}, f32[4,128,128]{2,1,0:T(8,128)S(1)}, u32[]{:S(2)}, u32[]{:S(2)}) %collective-permute-start.8) | collective-permute-done | bytes 262176 | tf_op jit(solution)/shard_map/ppermute | solution.py:21
  64.3 0.2 collective-permute-start.13
  64.5 0.3 fusion.7
  64.8 0.3 convolution_bitcast_fusion.2
  65.1 0.9 %collective-permute-done.10 = f32[4,128,128]{2,1,0:T(8,128)S(1)} collective-permute-done((f32[4,128,128]{2,1,0:T(8,128)S(1)}, f32[4,128,128]{2,1,0:T(8,128)S(1)}, u32[]{:S(2)}, u32[]{:S(2)}) %collective-permute-start.10) | collective-permute-done | bytes 262176 | tf_op jit(solution)/shard_map/ppermute | solution.py:21
  66.1 1.5 %collective-permute-start.11 = (f32[4,128,128]{2,1,0:T(8,128)S(1)}, f32[4,128,128]{2,1,0:T(8,128)S(1)}, u32[]{:S(2)}, u32[]{:S(2)}) collective-permute-start(f32[4,128,128]{2,1,0:T(8,128)S(1)} %add.104), channel_id=1, source_target_pairs={{0,8},{4,12},{8,0},{12,4},{1,9},{5,13},{9,1},{13,5},{2,10},{6,14},... | collective-permute-start | bytes 786440 | tf_op jit(solution)/shard_map/ppermute | solution.py:21
  67.6 7.6 %collective-permute-done.13 = f32[4,128,128]{2,1,0:T(8,128)S(1)} collective-permute-done((f32[4,128,128]{2,1,0:T(8,128)S(1)}, f32[4,128,128]{2,1,0:T(8,128)S(1)}, u32[]{:S(2)}, u32[]{:S(2)}) %collective-permute-start.13) | collective-permute-done | bytes 262176 | tf_op jit(solution)/shard_map/ppermute | solution.py:21
  75.3 1.1 %fusion.21.local_k = f32[8,128,128]{2,1,0:T(8,128)} fusion(bf16[8,128,128]{2,1,0:T(8,128)(2,1)S(1)} %fusion.7, bf16[128,1024]{1,0:T(8,128)(2,1)S(1)} %copy-done), kind=kOutput, calls=%fused_computation.34 | convolution fusion | flops 33554432 | bytes 1048576 | tf_op jit(solution)/shard_map/hts,thi->hsi/dot_general | solution.py:158
  76.4 1.1 %fusion.13.local_v = f32[8,128,128]{2,1,0:T(8,128)} fusion(bf16[8,128,128]{2,1,0:T(8,128)(2,1)S(1)} %fusion.5, bf16[16,8,8,128]{3,2,1,0:T(8,128)(2,1)S(1)} %get-tuple-element.28), kind=kOutput, calls=%fused_computation.26 | convolution fusion | flops 33554432 | bytes 1048576 | tf_op jit(solution)/shard_map/hts,thj->hsj/dot_general | solution.py:159
  77.5 1.5 %collective-permute-start.15 = (f32[4,128,128]{2,1,0:T(8,128)S(1)}, f32[4,128,128]{2,1,0:T(8,128)S(1)}, u32[]{:S(2)}, u32[]{:S(2)}) collective-permute-start(f32[4,128,128]{2,1,0:T(8,128)S(1)} %add.111), channel_id=1, source_target_pairs={{0,8},{4,12},{8,0},{12,4},{1,9},{5,13},{9,1},{13,5},{2,10},{6,14},... | collective-permute-start | bytes 786440 | tf_op jit(solution)/shard_map/ppermute | solution.py:21
  79.1 0.8 add_select_fusion
  79.9 0.3 fusion.6
  80.2 0.9 copy.27
  81.0 5.3 %collective-permute-done.15 = f32[4,128,128]{2,1,0:T(8,128)S(1)} collective-permute-done((f32[4,128,128]{2,1,0:T(8,128)S(1)}, f32[4,128,128]{2,1,0:T(8,128)S(1)}, u32[]{:S(2)}, u32[]{:S(2)}) %collective-permute-start.15) | collective-permute-done | bytes 262176 | tf_op jit(solution)/shard_map/ppermute | solution.py:21
  86.3 0.8 select_add_fusion.upper_later
  87.1 1.2 %collective-permute-done.12.lower_got = f32[4,128,128]{2,1,0:T(8,128)S(1)} collective-permute-done((f32[4,128,128]{2,1,0:T(8,128)S(1)}, f32[4,128,128]{2,1,0:T(8,128)S(1)}, u32[]{:S(2)}, u32[]{:S(2)}) %collective-permute-start.12) | collective-permute-done | bytes 262176 | tf_op jit(solution)/shard_map/ppermute | solution.py:21
  88.3 0.7 copy-done.3
  89.0 2.7 %shard_map.75 = (bf16[128,1024]{1,0:T(8,128)(2,1)}, bf16[128,1024]{1,0:T(8,128)(2,1)}) custom-call(f32[4,128,128]{2,1,0:T(8,128)} %get-tuple-element.25.lower_known, f32[4,128,128]{2,1,0:T(8,128)} %copy-done.3, f32[4,128,128]{2,1,0:T(8,128)} %select_add_fusion.upper_later, f32[8,128,128]{2,1,0:T(8,128)} %fusion.21.local_k, f32[8,128,128]{2,1,0:T(8,128)} %fusion.13.local_v, ...), custom_call_target="tpu_custom_call" | custom-call | flops 67108864 | bytes 6291456 | tf_op jit(solution)/shard_map/pallas_call | solution.py:108
  (26 shorter events, 0.6 us)
Async XLA Ops:
  0.6 38.7 %copy-start = (bf16[128,1024]{1,0:T(8,128)(2,1)S(1)}, bf16[128,1024]{1,0:T(8,128)(2,1)}, u32[]{:S(2)}) copy-start(bf16[128,1024]{1,0:T(8,128)(2,1)} %param.4) | copy-start | bytes 786436
  0.6 1.2 %copy-start.1 = (bf16[128,1024]{1,0:T(8,128)(2,1)S(1)}, bf16[128,1024]{1,0:T(8,128)(2,1)}, u32[]{:S(2)}) copy-start(bf16[128,1024]{1,0:T(8,128)(2,1)} %value.1) | copy-start | bytes 786436
  2.1 14.9 %collective-permute-start = (f32[4,128,128]{2,1,0:T(8,128)S(1)}, f32[4,128,128]{2,1,0:T(8,128)S(1)}, u32[]{:S(2)}, u32[]{:S(2)}) collective-permute-start(f32[4,128,128]{2,1,0:T(8,128)S(1)} %get-tuple-element.36), channel_id=1, source_target_pairs={{0,1},{1,0},{2,3},{3,2},{4,5},{5,4},{6,7},{7,6},{8,9},{9,8},{10,11... | collective-permute-start | bytes 786440 | tf_op jit(solution)/shard_map/ppermute | solution.py:21
  5.2 14.3 %collective-permute-start.1 = (f32[4,128,128]{2,1,0:T(8,128)S(1)}, f32[4,128,128]{2,1,0:T(8,128)S(1)}, u32[]{:S(2)}, u32[]{:S(2)}) collective-permute-start(f32[4,128,128]{2,1,0:T(8,128)S(1)} %get-tuple-element.37), channel_id=1, source_target_pairs={{0,2},{1,3},{2,0},{3,1},{4,6},{5,7},{6,4},{7,5},{8,10},{9,11},{10,... | collective-permute-start | bytes 786440 | tf_op jit(solution)/shard_map/ppermute | solution.py:21
  19.7 1.6 %collective-permute-start.2 = (f32[4,128,128]{2,1,0:T(8,128)S(1)}, f32[4,128,128]{2,1,0:T(8,128)S(1)}, u32[]{:S(2)}, u32[]{:S(2)}) collective-permute-start(f32[4,128,128]{2,1,0:T(8,128)S(1)} %get-tuple-element.12), channel_id=1, source_target_pairs={{0,4},{4,0},{8,12},{12,8},{1,5},{5,1},{9,13},{13,9},{2,6},{6,2},{1... | collective-permute-start | bytes 786440 | tf_op jit(solution)/shard_map/ppermute | solution.py:21
  21.3 14.8 %collective-permute-start.3 = (f32[4,128,128]{2,1,0:T(8,128)S(1)}, f32[4,128,128]{2,1,0:T(8,128)S(1)}, u32[]{:S(2)}, u32[]{:S(2)}) collective-permute-start(f32[4,128,128]{2,1,0:T(8,128)S(1)} %get-tuple-element.14), channel_id=1, source_target_pairs={{0,2},{1,3},{2,0},{3,1},{4,6},{5,7},{6,4},{7,5},{8,10},{9,11},{10,... | collective-permute-start | bytes 786440 | tf_op jit(solution)/shard_map/ppermute | solution.py:21
  21.7 14.6 %collective-permute-start.6 = (f32[4,128,128]{2,1,0:T(8,128)S(1)}, f32[4,128,128]{2,1,0:T(8,128)S(1)}, u32[]{:S(2)}, u32[]{:S(2)}) collective-permute-start(f32[4,128,128]{2,1,0:T(8,128)S(1)} %add.88), channel_id=1, source_target_pairs={{0,8},{4,12},{8,0},{12,4},{1,9},{5,13},{9,1},{13,5},{2,10},{6,14},... | collective-permute-start | bytes 786440 | tf_op jit(solution)/shard_map/ppermute | solution.py:21
  36.1 1.6 %collective-permute-start.4 = (f32[4,128,128]{2,1,0:T(8,128)S(1)}, f32[4,128,128]{2,1,0:T(8,128)S(1)}, u32[]{:S(2)}, u32[]{:S(2)}) collective-permute-start(f32[4,128,128]{2,1,0:T(8,128)S(1)} %add.90), channel_id=1, source_target_pairs={{0,4},{4,0},{8,12},{12,8},{1,5},{5,1},{9,13},{13,9},{2,6},{6,2},{1... | collective-permute-start | bytes 786440 | tf_op jit(solution)/shard_map/ppermute | solution.py:21
  36.3 8.8 %collective-permute-start.7 = (f32[4,128,128]{2,1,0:T(8,128)S(1)}, f32[4,128,128]{2,1,0:T(8,128)S(1)}, u32[]{:S(2)}, u32[]{:S(2)}) collective-permute-start(f32[4,128,128]{2,1,0:T(8,128)S(1)} %get-tuple-element.26), channel_id=1, source_target_pairs={{0,1},{1,0},{2,3},{3,2},{4,5},{5,4},{6,7},{7,6},{8,9},{9,8},{10,11... | collective-permute-start | bytes 786440 | tf_op jit(solution)/shard_map/ppermute | solution.py:21
  37.8 8.4 %collective-permute-start.5 = (f32[4,128,128]{2,1,0:T(8,128)S(1)}, f32[4,128,128]{2,1,0:T(8,128)S(1)}, u32[]{:S(2)}, u32[]{:S(2)}) collective-permute-start(f32[4,128,128]{2,1,0:T(8,128)S(1)} %add.92), channel_id=1, source_target_pairs={{0,8},{4,12},{8,0},{12,4},{1,9},{5,13},{9,1},{13,5},{2,10},{6,14},... | collective-permute-start | bytes 786440 | tf_op jit(solution)/shard_map/ppermute | solution.py:21
  46.9 1.0 %copy-start.2 = (bf16[128,1024]{1,0:T(8,128)(2,1)S(1)}, bf16[128,1024]{1,0:T(8,128)(2,1)}, u32[]{:S(2)}) copy-start(bf16[128,1024]{1,0:T(8,128)(2,1)} %param.7) | copy-start | bytes 786436
  49.3 11.9 %collective-permute-start.9 = (f32[4,128,128]{2,1,0:T(8,128)S(1)}, f32[4,128,128]{2,1,0:T(8,128)S(1)}, u32[]{:S(2)}, u32[]{:S(2)}) collective-permute-start(f32[4,128,128]{2,1,0:T(8,128)S(1)} %get-tuple-element.32), channel_id=1, source_target_pairs={{0,1},{1,0},{2,3},{3,2},{4,5},{5,4},{6,7},{7,6},{8,9},{9,8},{10,11... | collective-permute-start | bytes 786440 | tf_op jit(solution)/shard_map/ppermute | solution.py:21
  50.2 14.1 %collective-permute-start.8 = (f32[4,128,128]{2,1,0:T(8,128)S(1)}, f32[4,128,128]{2,1,0:T(8,128)S(1)}, u32[]{:S(2)}, u32[]{:S(2)}) collective-permute-start(f32[4,128,128]{2,1,0:T(8,128)S(1)} %get-tuple-element.33), channel_id=1, source_target_pairs={{0,2},{1,3},{2,0},{3,1},{4,6},{5,7},{6,4},{7,5},{8,10},{9,11},{10,... | collective-permute-start | bytes 786440 | tf_op jit(solution)/shard_map/ppermute | solution.py:21
  64.3 10.9 %collective-permute-start.13 = (f32[4,128,128]{2,1,0:T(8,128)S(1)}, f32[4,128,128]{2,1,0:T(8,128)S(1)}, u32[]{:S(2)}, u32[]{:S(2)}) collective-permute-start(f32[4,128,128]{2,1,0:T(8,128)S(1)} %get-tuple-element.30), channel_id=1, source_target_pairs={{0,2},{1,3},{2,0},{3,1},{4,6},{5,7},{6,4},{7,5},{8,10},{9,11},{10,... | collective-permute-start | bytes 786440 | tf_op jit(solution)/shard_map/ppermute | solution.py:21
  64.5 1.5 %collective-permute-start.10 = (f32[4,128,128]{2,1,0:T(8,128)S(1)}, f32[4,128,128]{2,1,0:T(8,128)S(1)}, u32[]{:S(2)}, u32[]{:S(2)}) collective-permute-start(f32[4,128,128]{2,1,0:T(8,128)S(1)} %get-tuple-element.16), channel_id=1, source_target_pairs={{0,4},{4,0},{8,12},{12,8},{1,5},{5,1},{9,13},{13,9},{2,6},{6,2},{1... | collective-permute-start | bytes 786440 | tf_op jit(solution)/shard_map/ppermute | solution.py:21
  66.1 13.0 %collective-permute-start.11 = (f32[4,128,128]{2,1,0:T(8,128)S(1)}, f32[4,128,128]{2,1,0:T(8,128)S(1)}, u32[]{:S(2)}, u32[]{:S(2)}) collective-permute-start(f32[4,128,128]{2,1,0:T(8,128)S(1)} %add.104), channel_id=1, source_target_pairs={{0,8},{4,12},{8,0},{12,4},{1,9},{5,13},{9,1},{13,5},{2,10},{6,14},... | collective-permute-start | bytes 786440 | tf_op jit(solution)/shard_map/ppermute | solution.py:21
  75.3 2.2 %collective-permute-start.14 = (f32[4,128,128]{2,1,0:T(8,128)S(1)}, f32[4,128,128]{2,1,0:T(8,128)S(1)}, u32[]{:S(2)}, u32[]{:S(2)}) collective-permute-start(f32[4,128,128]{2,1,0:T(8,128)S(1)} %add.109), channel_id=1, source_target_pairs={{0,4},{4,0},{8,12},{12,8},{1,5},{5,1},{9,13},{13,9},{2,6},{6,2},{1... | collective-permute-start | bytes 786440 | tf_op jit(solution)/shard_map/ppermute | solution.py:21
  77.5 8.8 %collective-permute-start.15 = (f32[4,128,128]{2,1,0:T(8,128)S(1)}, f32[4,128,128]{2,1,0:T(8,128)S(1)}, u32[]{:S(2)}, u32[]{:S(2)}) collective-permute-start(f32[4,128,128]{2,1,0:T(8,128)S(1)} %add.111), channel_id=1, source_target_pairs={{0,8},{4,12},{8,0},{12,4},{1,9},{5,13},{9,1},{13,5},{2,10},{6,14},... | collective-permute-start | bytes 786440 | tf_op jit(solution)/shard_map/ppermute | solution.py:21
  79.9 8.4 %collective-permute-start.12 = (f32[4,128,128]{2,1,0:T(8,128)S(1)}, f32[4,128,128]{2,1,0:T(8,128)S(1)}, u32[]{:S(2)}, u32[]{:S(2)}) collective-permute-start(f32[4,128,128]{2,1,0:T(8,128)S(1)} %get-tuple-element.24), channel_id=1, source_target_pairs={{0,1},{1,0},{2,3},{3,2},{4,5},{5,4},{6,7},{7,6},{8,9},{9,8},{10,11... | collective-permute-start | bytes 786440 | tf_op jit(solution)/shard_map/ppermute | solution.py:21
  88.3 0.7 copy-start.3

commit v13 on v12

--- a/solution.py
+++ b/solution.py
@@ -83,9 +83,17 @@
     return jnp.concatenate([earlier_a, known + got_b], axis=0)
 
 
-def tail_kernel(
-    scaling, lower_known, lower_got, upper_later, local_k, local_v, value, key, out_k, out_v
-):
+def tail_kernel(scaling, *refs):
+    sources, (out_k, out_v), held, semaphores = refs[:7], refs[7:9], refs[9:16], refs[16]
+    copies = [
+        pltpu.make_async_copy(source, target, semaphores.at[i])
+        for i, (source, target) in enumerate(zip(sources, held))
+    ]
+    for copy in copies:
+        copy.start()
+    for copy in copies:
+        copy.wait()
+    lower_known, lower_got, upper_later, local_k, local_v, value, key = held
     half = HEADS // 2
     for h in range(HEADS):
         later = lower_known[h] + lower_got[h] if h < half else upper_later[h - half]
@@ -101,19 +109,22 @@
         out_v[:, cols] = (local_v[h] + scaling * from_later_v).astype(out_v.dtype)
 
 
-def tail(lower_known, lower_got, upper_later, local_k, local_v, value, key):
-    rows = value.shape[0]
+def tail(*operands):
+    rows = operands[-1].shape[0]
     vmem = pl.BlockSpec(memory_space=pltpu.VMEM)
+    anywhere = pl.BlockSpec(memory_space=pl.ANY)
     out = jax.ShapeDtypeStruct((rows, HEADS * HEAD), jnp.bfloat16)
     return pl.pallas_call(
         functools.partial(tail_kernel, HEAD ** (-0.5)),
         out_shape=(out, out),
-        in_specs=[vmem] * 7,
+        in_specs=[anywhere] * len(operands),
         out_specs=(vmem, vmem),
+        scratch_shapes=[pltpu.VMEM(x.shape, x.dtype) for x in operands]
+        + [pltpu.SemaphoreType.DMA((len(operands),))],
         cost_estimate=pl.CostEstimate(
             flops=4 * HEADS * rows * HEAD * HEAD, transcendentals=0, bytes_accessed=12 * rows * 1024 * 4
         ),
-    )(lower_known, lower_got, upper_later, local_k, local_v, value, key)
+    )(*operands)
 
 
 def per_device(query, key, value, grad_out):

time: 91.9 us -> 92 us (level)
  no operation moved by 1% of the time
where the time goes in v13:
time: 92 us; the launch traced here: 91.8 us
  waiting for transfers between devices  62.1 us (68%)
  starting transfers between devices  14.7 us (16%)
  matrix products  4.42 us (5%)
  local copies, waits for them, and re-layouts  3.73 us (4%)
  other arithmetic  3.18 us (3%)
  Pallas kernels  2.79 us (3%)
    ppermute x16, waiting for transfers between devices, swap(): return lax.ppermute(value, axis, [(i, i ^ bit) for i in range(count)])  62.1 us
    ppermute x16, starting transfers between devices, swap(): return lax.ppermute(value, axis, [(i, i ^ bit) for i in range(count)])  14.7 us
    pallas_call x1, Pallas kernels, tail(): pl.pallas_call(functools.partial(tail_kernel, HEAD ** (-0.5)), out_shape=...  2.79 us
    unnamed x9, local copies, waits for them, and re-layouts  2.29 us
  transfers between devices with their start and end apart: 16, of which 13 were waited for; matrix products, arithmetic and copies ran while one was open for 6% of the time, Pallas kernels for 0%

profile of v13, /device:TPU:0, one launch (start us, length us, event | category | flops | bytes accessed | tf_op | source)
XLA Modules:
  0.0 91.8 jit_solution(7493040111644311208)
XLA Ops:
  0.7 1.2 %copy.32 = bf16[128,1024]{0,1:T(8,128)(2,1)S(1)} copy(bf16[128,1024]{1,0:T(8,128)(2,1)} %refs_6_.1) | data formatting | bytes 524288 | tf_op jit(solution)/shard_map/reshape | solution.py:134
  1.8 0.2 fusion.19
  2.1 3.1 %collective-permute-start = (f32[4,128,128]{2,1,0:T(8,128)S(1)}, f32[4,128,128]{2,1,0:T(8,128)S(1)}, u32[]{:S(2)}, u32[]{:S(2)}) collective-permute-start(f32[4,128,128]{2,1,0:T(8,128)S(1)} %get-tuple-element.36), channel_id=1, source_target_pairs={{0,1},{1,0},{2,3},{3,2},{4,5},{5,4},{6,7},{7,6},{8,9},{9,8},{10,11... | collective-permute-start | bytes 786440 | tf_op jit(solution)/shard_map/ppermute | solution.py:21
  5.2 2.6 %collective-permute-start.1 = (f32[4,128,128]{2,1,0:T(8,128)S(1)}, f32[4,128,128]{2,1,0:T(8,128)S(1)}, u32[]{:S(2)}, u32[]{:S(2)}) collective-permute-start(f32[4,128,128]{2,1,0:T(8,128)S(1)} %get-tuple-element.37), channel_id=1, source_target_pairs={{0,2},{1,3},{2,0},{3,1},{4,6},{5,7},{6,4},{7,5},{8,10},{9,11},{10,... | collective-permute-start | bytes 786440 | tf_op jit(solution)/shard_map/ppermute | solution.py:21
  7.8 9.2 %collective-permute-done = f32[4,128,128]{2,1,0:T(8,128)S(1)} collective-permute-done((f32[4,128,128]{2,1,0:T(8,128)S(1)}, f32[4,128,128]{2,1,0:T(8,128)S(1)}, u32[]{:S(2)}, u32[]{:S(2)}) %collective-permute-start) | collective-permute-done | bytes 262176 | tf_op jit(solution)/shard_map/ppermute | solution.py:21
  17.0 2.5 %collective-permute-done.1 = f32[4,128,128]{2,1,0:T(8,128)S(1)} collective-permute-done((f32[4,128,128]{2,1,0:T(8,128)S(1)}, f32[4,128,128]{2,1,0:T(8,128)S(1)}, u32[]{:S(2)}, u32[]{:S(2)}) %collective-permute-start.1) | collective-permute-done | bytes 262176 | tf_op jit(solution)/shard_map/ppermute | solution.py:21
  19.6 0.1 slice_add_fusion.1
  19.7 0.1 collective-permute-start.2
  19.7 1.5 %collective-permute-done.2 = f32[4,128,128]{2,1,0:T(8,128)S(1)} collective-permute-done((f32[4,128,128]{2,1,0:T(8,128)S(1)}, f32[4,128,128]{2,1,0:T(8,128)S(1)}, u32[]{:S(2)}, u32[]{:S(2)}) %collective-permute-start.2) | collective-permute-done | bytes 262176 | tf_op jit(solution)/shard_map/ppermute | solution.py:21
  21.3 0.4 collective-permute-start.3
  21.7 1.5 %collective-permute-start.6 = (f32[4,128,128]{2,1,0:T(8,128)S(1)}, f32[4,128,128]{2,1,0:T(8,128)S(1)}, u32[]{:S(2)}, u32[]{:S(2)}) collective-permute-start(f32[4,128,128]{2,1,0:T(8,128)S(1)} %add.88), channel_id=1, source_target_pairs={{0,8},{4,12},{8,0},{12,4},{1,9},{5,13},{9,1},{13,5},{2,10},{6,14},... | collective-permute-start | bytes 786440 | tf_op jit(solution)/shard_map/ppermute | solution.py:21
  23.2 12.9 %collective-permute-done.3 = f32[4,128,128]{2,1,0:T(8,128)S(1)} collective-permute-done((f32[4,128,128]{2,1,0:T(8,128)S(1)}, f32[4,128,128]{2,1,0:T(8,128)S(1)}, u32[]{:S(2)}, u32[]{:S(2)}) %collective-permute-start.3) | collective-permute-done | bytes 262176 | tf_op jit(solution)/shard_map/ppermute | solution.py:21
  36.1 0.1 collective-permute-start.4
  36.3 0.1 collective-permute-start.7
  36.4 1.3 %collective-permute-done.4 = f32[4,128,128]{2,1,0:T(8,128)S(1)} collective-permute-done((f32[4,128,128]{2,1,0:T(8,128)S(1)}, f32[4,128,128]{2,1,0:T(8,128)S(1)}, u32[]{:S(2)}, u32[]{:S(2)}) %collective-permute-start.4) | collective-permute-done | bytes 262176 | tf_op jit(solution)/shard_map/ppermute | solution.py:21
  37.8 1.6 %collective-permute-start.5 = (f32[4,128,128]{2,1,0:T(8,128)S(1)}, f32[4,128,128]{2,1,0:T(8,128)S(1)}, u32[]{:S(2)}, u32[]{:S(2)}) collective-permute-start(f32[4,128,128]{2,1,0:T(8,128)S(1)} %add.92), channel_id=1, source_target_pairs={{0,8},{4,12},{8,0},{12,4},{1,9},{5,13},{9,1},{13,5},{2,10},{6,14},... | collective-permute-start | bytes 786440 | tf_op jit(solution)/shard_map/ppermute | solution.py:21
  39.3 0.2 fusion.5
  39.6 5.5 %collective-permute-done.7 = f32[4,128,128]{2,1,0:T(8,128)S(1)} collective-permute-done((f32[4,128,128]{2,1,0:T(8,128)S(1)}, f32[4,128,128]{2,1,0:T(8,128)S(1)}, u32[]{:S(2)}, u32[]{:S(2)}) %collective-permute-start.7) | collective-permute-done | bytes 262176 | tf_op jit(solution)/shard_map/ppermute | solution.py:21
  45.1 1.1 %collective-permute-done.5 = f32[4,128,128]{2,1,0:T(8,128)S(1)} collective-permute-done((f32[4,128,128]{2,1,0:T(8,128)S(1)}, f32[4,128,128]{2,1,0:T(8,128)S(1)}, u32[]{:S(2)}, u32[]{:S(2)}) %collective-permute-start.5) | collective-permute-done | bytes 262176 | tf_op jit(solution)/shard_map/ppermute | solution.py:21
  46.2 0.1 add_convert_fusion.1
  46.3 0.3 fusion.3
  46.6 0.3 multiply_reduce_fusion
  47.0 0.2 copy.15
  47.2 0.7 copy-done.2
  47.9 0.2 fusion.8
  48.1 0.9 fusion.11
  49.0 0.3 convolution_bitcast_fusion
  49.3 0.8 collective-permute-start.9
  50.2 1.2 %collective-permute-start.8 = (f32[4,128,128]{2,1,0:T(8,128)S(1)}, f32[4,128,128]{2,1,0:T(8,128)S(1)}, u32[]{:S(2)}, u32[]{:S(2)}) collective-permute-start(f32[4,128,128]{2,1,0:T(8,128)S(1)} %get-tuple-element.33), channel_id=1, source_target_pairs={{0,2},{1,3},{2,0},{3,1},{4,6},{5,7},{6,4},{7,5},{8,10},{9,11},{10,... | collective-permute-start | bytes 786440 | tf_op jit(solution)/shard_map/ppermute | solution.py:21
  51.3 10.0 %collective-permute-done.9 = f32[4,128,128]{2,1,0:T(8,128)S(1)} collective-permute-done((f32[4,128,128]{2,1,0:T(8,128)S(1)}, f32[4,128,128]{2,1,0:T(8,128)S(1)}, u32[]{:S(2)}, u32[]{:S(2)}) %collective-permute-start.9) | collective-permute-done | bytes 262176 | tf_op jit(solution)/shard_map/ppermute | solution.py:21
  61.3 3.0 %collective-permute-done.8 = f32[4,128,128]{2,1,0:T(8,128)S(1)} collective-permute-done((f32[4,128,128]{2,1,0:T(8,128)S(1)}, f32[4,128,128]{2,1,0:T(8,128)S(1)}, u32[]{:S(2)}, u32[]{:S(2)}) %collective-permute-start.8) | collective-permute-done | bytes 262176 | tf_op jit(solution)/shard_map/ppermute | solution.py:21
  64.3 0.2 collective-permute-start.13
  64.5 0.3 fusion.7
  64.8 0.3 convolution_bitcast_fusion.2
  65.1 0.9 %collective-permute-done.10 = f32[4,128,128]{2,1,0:T(8,128)S(1)} collective-permute-done((f32[4,128,128]{2,1,0:T(8,128)S(1)}, f32[4,128,128]{2,1,0:T(8,128)S(1)}, u32[]{:S(2)}, u32[]{:S(2)}) %collective-permute-start.10) | collective-permute-done | bytes 262176 | tf_op jit(solution)/shard_map/ppermute | solution.py:21
  66.1 1.5 %collective-permute-start.11 = (f32[4,128,128]{2,1,0:T(8,128)S(1)}, f32[4,128,128]{2,1,0:T(8,128)S(1)}, u32[]{:S(2)}, u32[]{:S(2)}) collective-permute-start(f32[4,128,128]{2,1,0:T(8,128)S(1)} %add.104), channel_id=1, source_target_pairs={{0,8},{4,12},{8,0},{12,4},{1,9},{5,13},{9,1},{13,5},{2,10},{6,14},... | collective-permute-start | bytes 786440 | tf_op jit(solution)/shard_map/ppermute | solution.py:21
  67.6 7.6 %collective-permute-done.13 = f32[4,128,128]{2,1,0:T(8,128)S(1)} collective-permute-done((f32[4,128,128]{2,1,0:T(8,128)S(1)}, f32[4,128,128]{2,1,0:T(8,128)S(1)}, u32[]{:S(2)}, u32[]{:S(2)}) %collective-permute-start.13) | collective-permute-done | bytes 262176 | tf_op jit(solution)/shard_map/ppermute | solution.py:21
  75.3 1.1 %fusion.21.refs_3_ = f32[8,128,128]{2,1,0:T(8,128)} fusion(bf16[8,128,128]{2,1,0:T(8,128)(2,1)S(1)} %fusion.7, bf16[128,1024]{1,0:T(8,128)(2,1)S(1)} %copy-done), kind=kOutput, calls=%fused_computation.34 | convolution fusion | flops 33554432 | bytes 1048576 | tf_op jit(solution)/shard_map/hts,thi->hsi/dot_general | solution.py:169
  76.4 1.1 %fusion.13.refs_4_ = f32[8,128,128]{2,1,0:T(8,128)} fusion(bf16[8,128,128]{2,1,0:T(8,128)(2,1)S(1)} %fusion.5, bf16[16,8,8,128]{3,2,1,0:T(8,128)(2,1)S(1)} %get-tuple-element.28), kind=kOutput, calls=%fused_computation.26 | convolution fusion | flops 33554432 | bytes 1048576 | tf_op jit(solution)/shard_map/hts,thj->hsj/dot_general | solution.py:170
  77.5 1.5 %collective-permute-start.15 = (f32[4,128,128]{2,1,0:T(8,128)S(1)}, f32[4,128,128]{2,1,0:T(8,128)S(1)}, u32[]{:S(2)}, u32[]{:S(2)}) collective-permute-start(f32[4,128,128]{2,1,0:T(8,128)S(1)} %add.111), channel_id=1, source_target_pairs={{0,8},{4,12},{8,0},{12,4},{1,9},{5,13},{9,1},{13,5},{2,10},{6,14},... | collective-permute-start | bytes 786440 | tf_op jit(solution)/shard_map/ppermute | solution.py:21
  79.1 0.8 add_select_fusion
  79.9 0.3 fusion.6
  80.2 0.9 copy.27
  81.0 5.3 %collective-permute-done.15 = f32[4,128,128]{2,1,0:T(8,128)S(1)} collective-permute-done((f32[4,128,128]{2,1,0:T(8,128)S(1)}, f32[4,128,128]{2,1,0:T(8,128)S(1)}, u32[]{:S(2)}, u32[]{:S(2)}) %collective-permute-start.15) | collective-permute-done | bytes 262176 | tf_op jit(solution)/shard_map/ppermute | solution.py:21
  86.3 0.8 select_add_fusion.refs_2_
  87.1 1.2 %collective-permute-done.12.refs_1_ = f32[4,128,128]{2,1,0:T(8,128)S(1)} collective-permute-done((f32[4,128,128]{2,1,0:T(8,128)S(1)}, f32[4,128,128]{2,1,0:T(8,128)S(1)}, u32[]{:S(2)}, u32[]{:S(2)}) %collective-permute-start.12) | collective-permute-done | bytes 262176 | tf_op jit(solution)/shard_map/ppermute | solution.py:21
  88.3 0.7 copy-done.3
  89.0 2.8 %shard_map.75 = (bf16[128,1024]{1,0:T(8,128)(2,1)}, bf16[128,1024]{1,0:T(8,128)(2,1)}) custom-call(f32[4,128,128]{2,1,0:T(8,128)} %get-tuple-element.25.refs_0_, f32[4,128,128]{2,1,0:T(8,128)} %copy-done.3, f32[4,128,128]{2,1,0:T(8,128)} %select_add_fusion.refs_2_, f32[8,128,128]{2,1,0:T(8,128)} %fusion.21.refs_3_, f32[8,128,128]{2,1,0:T(8,128)} %fusion.13.refs_4_, ...), custom_call_target="tpu_custom_call" | custom-call | flops 67108864 | bytes 6291456 | tf_op jit(solution)/shard_map/pallas_call | solution.py:117
  (26 shorter events, 0.6 us)
Async XLA Ops:
  0.6 38.7 %copy-start = (bf16[128,1024]{1,0:T(8,128)(2,1)S(1)}, bf16[128,1024]{1,0:T(8,128)(2,1)}, u32[]{:S(2)}) copy-start(bf16[128,1024]{1,0:T(8,128)(2,1)} %param.4) | copy-start | bytes 786436
  0.6 1.2 %copy-start.1 = (bf16[128,1024]{1,0:T(8,128)(2,1)S(1)}, bf16[128,1024]{1,0:T(8,128)(2,1)}, u32[]{:S(2)}) copy-start(bf16[128,1024]{1,0:T(8,128)(2,1)} %refs_5_.1) | copy-start | bytes 786436
  2.1 14.9 %collective-permute-start = (f32[4,128,128]{2,1,0:T(8,128)S(1)}, f32[4,128,128]{2,1,0:T(8,128)S(1)}, u32[]{:S(2)}, u32[]{:S(2)}) collective-permute-start(f32[4,128,128]{2,1,0:T(8,128)S(1)} %get-tuple-element.36), channel_id=1, source_target_pairs={{0,1},{1,0},{2,3},{3,2},{4,5},{5,4},{6,7},{7,6},{8,9},{9,8},{10,11... | collective-permute-start | bytes 786440 | tf_op jit(solution)/shard_map/ppermute | solution.py:21
  5.2 14.3 %collective-permute-start.1 = (f32[4,128,128]{2,1,0:T(8,128)S(1)}, f32[4,128,128]{2,1,0:T(8,128)S(1)}, u32[]{:S(2)}, u32[]{:S(2)}) collective-permute-start(f32[4,128,128]{2,1,0:T(8,128)S(1)} %get-tuple-element.37), channel_id=1, source_target_pairs={{0,2},{1,3},{2,0},{3,1},{4,6},{5,7},{6,4},{7,5},{8,10},{9,11},{10,... | collective-permute-start | bytes 786440 | tf_op jit(solution)/shard_map/ppermute | solution.py:21
  19.7 1.6 %collective-permute-start.2 = (f32[4,128,128]{2,1,0:T(8,128)S(1)}, f32[4,128,128]{2,1,0:T(8,128)S(1)}, u32[]{:S(2)}, u32[]{:S(2)}) collective-permute-start(f32[4,128,128]{2,1,0:T(8,128)S(1)} %get-tuple-element.12), channel_id=1, source_target_pairs={{0,4},{4,0},{8,12},{12,8},{1,5},{5,1},{9,13},{13,9},{2,6},{6,2},{1... | collective-permute-start | bytes 786440 | tf_op jit(solution)/shard_map/ppermute | solution.py:21
  21.3 14.8 %collective-permute-start.3 = (f32[4,128,128]{2,1,0:T(8,128)S(1)}, f32[4,128,128]{2,1,0:T(8,128)S(1)}, u32[]{:S(2)}, u32[]{:S(2)}) collective-permute-start(f32[4,128,128]{2,1,0:T(8,128)S(1)} %get-tuple-element.14), channel_id=1, source_target_pairs={{0,2},{1,3},{2,0},{3,1},{4,6},{5,7},{6,4},{7,5},{8,10},{9,11},{10,... | collective-permute-start | bytes 786440 | tf_op jit(solution)/shard_map/ppermute | solution.py:21
  21.7 14.6 %collective-permute-start.6 = (f32[4,128,128]{2,1,0:T(8,128)S(1)}, f32[4,128,128]{2,1,0:T(8,128)S(1)}, u32[]{:S(2)}, u32[]{:S(2)}) collective-permute-start(f32[4,128,128]{2,1,0:T(8,128)S(1)} %add.88), channel_id=1, source_target_pairs={{0,8},{4,12},{8,0},{12,4},{1,9},{5,13},{9,1},{13,5},{2,10},{6,14},... | collective-permute-start | bytes 786440 | tf_op jit(solution)/shard_map/ppermute | solution.py:21
  36.1 1.6 %collective-permute-start.4 = (f32[4,128,128]{2,1,0:T(8,128)S(1)}, f32[4,128,128]{2,1,0:T(8,128)S(1)}, u32[]{:S(2)}, u32[]{:S(2)}) collective-permute-start(f32[4,128,128]{2,1,0:T(8,128)S(1)} %add.90), channel_id=1, source_target_pairs={{0,4},{4,0},{8,12},{12,8},{1,5},{5,1},{9,13},{13,9},{2,6},{6,2},{1... | collective-permute-start | bytes 786440 | tf_op jit(solution)/shard_map/ppermute | solution.py:21
  36.3 8.8 %collective-permute-start.7 = (f32[4,128,128]{2,1,0:T(8,128)S(1)}, f32[4,128,128]{2,1,0:T(8,128)S(1)}, u32[]{:S(2)}, u32[]{:S(2)}) collective-permute-start(f32[4,128,128]{2,1,0:T(8,128)S(1)} %get-tuple-element.26), channel_id=1, source_target_pairs={{0,1},{1,0},{2,3},{3,2},{4,5},{5,4},{6,7},{7,6},{8,9},{9,8},{10,11... | collective-permute-start | bytes 786440 | tf_op jit(solution)/shard_map/ppermute | solution.py:21
  37.8 8.4 %collective-permute-start.5 = (f32[4,128,128]{2,1,0:T(8,128)S(1)}, f32[4,128,128]{2,1,0:T(8,128)S(1)}, u32[]{:S(2)}, u32[]{:S(2)}) collective-permute-start(f32[4,128,128]{2,1,0:T(8,128)S(1)} %add.92), channel_id=1, source_target_pairs={{0,8},{4,12},{8,0},{12,4},{1,9},{5,13},{9,1},{13,5},{2,10},{6,14},... | collective-permute-start | bytes 786440 | tf_op jit(solution)/shard_map/ppermute | solution.py:21
  46.9 1.0 %copy-start.2 = (bf16[128,1024]{1,0:T(8,128)(2,1)S(1)}, bf16[128,1024]{1,0:T(8,128)(2,1)}, u32[]{:S(2)}) copy-start(bf16[128,1024]{1,0:T(8,128)(2,1)} %param.7) | copy-start | bytes 786436
  49.3 11.9 %collective-permute-start.9 = (f32[4,128,128]{2,1,0:T(8,128)S(1)}, f32[4,128,128]{2,1,0:T(8,128)S(1)}, u32[]{:S(2)}, u32[]{:S(2)}) collective-permute-start(f32[4,128,128]{2,1,0:T(8,128)S(1)} %get-tuple-element.32), channel_id=1, source_target_pairs={{0,1},{1,0},{2,3},{3,2},{4,5},{5,4},{6,7},{7,6},{8,9},{9,8},{10,11... | collective-permute-start | bytes 786440 | tf_op jit(solution)/shard_map/ppermute | solution.py:21
  50.2 14.1 %collective-permute-start.8 = (f32[4,128,128]{2,1,0:T(8,128)S(1)}, f32[4,128,128]{2,1,0:T(8,128)S(1)}, u32[]{:S(2)}, u32[]{:S(2)}) collective-permute-start(f32[4,128,128]{2,1,0:T(8,128)S(1)} %get-tuple-element.33), channel_id=1, source_target_pairs={{0,2},{1,3},{2,0},{3,1},{4,6},{5,7},{6,4},{7,5},{8,10},{9,11},{10,... | collective-permute-start | bytes 786440 | tf_op jit(solution)/shard_map/ppermute | solution.py:21
  64.3 10.9 %collective-permute-start.13 = (f32[4,128,128]{2,1,0:T(8,128)S(1)}, f32[4,128,128]{2,1,0:T(8,128)S(1)}, u32[]{:S(2)}, u32[]{:S(2)}) collective-permute-start(f32[4,128,128]{2,1,0:T(8,128)S(1)} %get-tuple-element.30), channel_id=1, source_target_pairs={{0,2},{1,3},{2,0},{3,1},{4,6},{5,7},{6,4},{7,5},{8,10},{9,11},{10,... | collective-permute-start | bytes 786440 | tf_op jit(solution)/shard_map/ppermute | solution.py:21
  64.5 1.5 %collective-permute-start.10 = (f32[4,128,128]{2,1,0:T(8,128)S(1)}, f32[4,128,128]{2,1,0:T(8,128)S(1)}, u32[]{:S(2)}, u32[]{:S(2)}) collective-permute-start(f32[4,128,128]{2,1,0:T(8,128)S(1)} %get-tuple-element.16), channel_id=1, source_target_pairs={{0,4},{4,0},{8,12},{12,8},{1,5},{5,1},{9,13},{13,9},{2,6},{6,2},{1... | collective-permute-start | bytes 786440 | tf_op jit(solution)/shard_map/ppermute | solution.py:21
  66.1 13.0 %collective-permute-start.11 = (f32[4,128,128]{2,1,0:T(8,128)S(1)}, f32[4,128,128]{2,1,0:T(8,128)S(1)}, u32[]{:S(2)}, u32[]{:S(2)}) collective-permute-start(f32[4,128,128]{2,1,0:T(8,128)S(1)} %add.104), channel_id=1, source_target_pairs={{0,8},{4,12},{8,0},{12,4},{1,9},{5,13},{9,1},{13,5},{2,10},{6,14},... | collective-permute-start | bytes 786440 | tf_op jit(solution)/shard_map/ppermute | solution.py:21
  75.3 2.2 %collective-permute-start.14 = (f32[4,128,128]{2,1,0:T(8,128)S(1)}, f32[4,128,128]{2,1,0:T(8,128)S(1)}, u32[]{:S(2)}, u32[]{:S(2)}) collective-permute-start(f32[4,128,128]{2,1,0:T(8,128)S(1)} %add.109), channel_id=1, source_target_pairs={{0,4},{4,0},{8,12},{12,8},{1,5},{5,1},{9,13},{13,9},{2,6},{6,2},{1... | collective-permute-start | bytes 786440 | tf_op jit(solution)/shard_map/ppermute | solution.py:21
  77.5 8.8 %collective-permute-start.15 = (f32[4,128,128]{2,1,0:T(8,128)S(1)}, f32[4,128,128]{2,1,0:T(8,128)S(1)}, u32[]{:S(2)}, u32[]{:S(2)}) collective-permute-start(f32[4,128,128]{2,1,0:T(8,128)S(1)} %add.111), channel_id=1, source_target_pairs={{0,8},{4,12},{8,0},{12,4},{1,9},{5,13},{9,1},{13,5},{2,10},{6,14},... | collective-permute-start | bytes 786440 | tf_op jit(solution)/shard_map/ppermute | solution.py:21
  79.9 8.4 %collective-permute-start.12 = (f32[4,128,128]{2,1,0:T(8,128)S(1)}, f32[4,128,128]{2,1,0:T(8,128)S(1)}, u32[]{:S(2)}, u32[]{:S(2)}) collective-permute-start(f32[4,128,128]{2,1,0:T(8,128)S(1)} %get-tuple-element.24), channel_id=1, source_target_pairs={{0,1},{1,0},{2,3},{3,2},{4,5},{5,4},{6,7},{7,6},{8,9},{9,8},{10,11... | collective-permute-start | bytes 786440 | tf_op jit(solution)/shard_map/ppermute | solution.py:21
  88.3 0.7 copy-start.3

commit v14 on v12

--- a/solution.py
+++ b/solution.py
@@ -116,6 +116,27 @@
     )(lower_known, lower_got, upper_later, local_k, local_v, value, key)
 
 
+def state_kernel(key, value, out):
+    for h in range(HEADS):
+        cols = slice(h * HEAD, (h + 1) * HEAD)
+        out[h] = lax.dot_general(
+            key[:, cols], value[:, cols], (((0,), (0,)), ((), ())), preferred_element_type=jnp.float32
+        )
+
+
+def key_value_state(key, value):
+    vmem = pl.BlockSpec(memory_space=pltpu.VMEM)
+    return pl.pallas_call(
+        state_kernel,
+        out_shape=jax.ShapeDtypeStruct((HEADS, HEAD, HEAD), jnp.float32),
+        in_specs=[vmem, vmem],
+        out_specs=vmem,
+        cost_estimate=pl.CostEstimate(
+            flops=2 * HEADS * key.shape[0] * HEAD * HEAD, transcendentals=0, bytes_accessed=4 * key.size * 2
+        ),
+    )(key, value)
+
+
 def per_device(query, key, value, grad_out):
     rows_dev = query.shape[0]
     scaling = HEAD ** (-0.5)
@@ -125,7 +146,7 @@
     line = lax.broadcasted_iota(jnp.int32, (rows_dev, rows_dev), 0)
     column = lax.broadcasted_iota(jnp.int32, (rows_dev, rows_dev), 1)
     causal = (line >= column)[None]
-    state = jnp.einsum("thi,thj->hij", key_rows, value_rows, preferred_element_type=jnp.float32)
+    state = key_value_state(key, value)
     prior = chunked_scan(state, False)
     prior_half = prior.astype(jnp.bfloat16)
     scores = (

time: 91.9 us -> 94.6 us (1.029)
  Pallas kernels: 2.73 us -> 4.87 us
  local copies, waits for them, and re-layouts: 3.73 us -> 5.1 us
    pallas_call x0 -> x1, Pallas kernels: none -> 2.14 us  [key_value_state(): pl.pallas_call(state_kernel, out_shape=jax.ShapeDtypeStruct((HEADS, HEAD,...]
    unnamed x9 -> x13, local copies, waits for them, and re-layouts: 2.29 us -> 3.58 us
    slice x2, local copies, waits for them, and re-layouts: 0.07 us -> 1.16 us  [chunked_scan(): group_a, group_b = (value[:half], value[half:])]
    reshape x1, local copies, waits for them, and re-layouts: 1.17 us -> 0.17 us  [per_device(): key_rows = key.reshape(rows_dev, HEADS, HEAD)]
where the time goes in v14:
time: 94.6 us; the launch traced here: 94.3 us
  waiting for transfers between devices  61.4 us (65%)
  starting transfers between devices  14.7 us (16%)
  local copies, waits for them, and re-layouts  5.1 us (5%)
  Pallas kernels  4.87 us (5%)
  matrix products  4.24 us (4%)
  other arithmetic  3.16 us (3%)
    ppermute x16, waiting for transfers between devices, swap(): return lax.ppermute(value, axis, [(i, i ^ bit) for i in range(count)])  61.4 us
    ppermute x16, starting transfers between devices, swap(): return lax.ppermute(value, axis, [(i, i ^ bit) for i in range(count)])  14.7 us
    unnamed x13, local copies, waits for them, and re-layouts  3.58 us
    pallas_call x1, Pallas kernels, tail(): pl.pallas_call(functools.partial(tail_kernel, HEAD ** (-0.5)), out_shape=...  2.73 us
    pallas_call x1, Pallas kernels, key_value_state(): pl.pallas_call(state_kernel, out_shape=jax.ShapeDtypeStruct((HEADS, HEAD,...  2.14 us
  transfers between devices with their start and end apart: 16, of which 13 were waited for; matrix products, arithmetic and copies ran while one was open for 6% of the time, Pallas kernels for 0%

profile of v14, /device:TPU:0, one launch (start us, length us, event | category | flops | bytes accessed | tf_op | source)
XLA Modules:
  0.0 94.3 jit_solution(13412242619228895083)
XLA Ops:
  0.6 2.1 %shard_map.75 = f32[8,128,128]{2,1,0:T(8,128)} custom-call(bf16[128,1024]{1,0:T(8,128)(2,1)} %key.3, bf16[128,1024]{1,0:T(8,128)(2,1)} %value.3), custom_call_target="tpu_custom_call" | custom-call | flops 33554432 | bytes 1048576 | tf_op jit(solution)/shard_map/pallas_call | solution.py:129
  2.8 1.1 %fusion.37 = (f32[4,128,128]{2,1,0:T(8,128)S(1)}, f32[4,128,128]{2,1,0:T(8,128)S(1)}) fusion(f32[8,128,128]{2,1,0:T(8,128)} %shard_map.75), kind=kLoop, calls=%fused_computation.66 | loop fusion | bytes 1048576 | tf_op jit(solution)/shard_map/slice | solution.py:52
  3.9 3.1 %collective-permute-start = (f32[4,128,128]{2,1,0:T(8,128)S(1)}, f32[4,128,128]{2,1,0:T(8,128)S(1)}, u32[]{:S(2)}, u32[]{:S(2)}) collective-permute-start(f32[4,128,128]{2,1,0:T(8,128)S(1)} %get-tuple-element.36), channel_id=1, source_target_pairs={{0,1},{1,0},{2,3},{3,2},{4,5},{5,4},{6,7},{7,6},{8,9},{9,8},{10,11... | collective-permute-start | bytes 786440 | tf_op jit(solution)/shard_map/ppermute | solution.py:21
  7.0 2.6 %collective-permute-start.1 = (f32[4,128,128]{2,1,0:T(8,128)S(1)}, f32[4,128,128]{2,1,0:T(8,128)S(1)}, u32[]{:S(2)}, u32[]{:S(2)}) collective-permute-start(f32[4,128,128]{2,1,0:T(8,128)S(1)} %get-tuple-element.37), channel_id=1, source_target_pairs={{0,2},{1,3},{2,0},{3,1},{4,6},{5,7},{6,4},{7,5},{8,10},{9,11},{10,... | collective-permute-start | bytes 786440 | tf_op jit(solution)/shard_map/ppermute | solution.py:21
  9.6 9.2 %collective-permute-done = f32[4,128,128]{2,1,0:T(8,128)S(1)} collective-permute-done((f32[4,128,128]{2,1,0:T(8,128)S(1)}, f32[4,128,128]{2,1,0:T(8,128)S(1)}, u32[]{:S(2)}, u32[]{:S(2)}) %collective-permute-start) | collective-permute-done | bytes 262176 | tf_op jit(solution)/shard_map/ppermute | solution.py:21
  18.8 2.5 %collective-permute-done.1 = f32[4,128,128]{2,1,0:T(8,128)S(1)} collective-permute-done((f32[4,128,128]{2,1,0:T(8,128)S(1)}, f32[4,128,128]{2,1,0:T(8,128)S(1)}, u32[]{:S(2)}, u32[]{:S(2)}) %collective-permute-start.1) | collective-permute-done | bytes 262176 | tf_op jit(solution)/shard_map/ppermute | solution.py:21
  21.4 0.1 slice_add_fusion.1
  21.5 1.5 %collective-permute-done.2 = f32[4,128,128]{2,1,0:T(8,128)S(1)} collective-permute-done((f32[4,128,128]{2,1,0:T(8,128)S(1)}, f32[4,128,128]{2,1,0:T(8,128)S(1)}, u32[]{:S(2)}, u32[]{:S(2)}) %collective-permute-start.2) | collective-permute-done | bytes 262176 | tf_op jit(solution)/shard_map/ppermute | solution.py:21
  23.1 0.4 collective-permute-start.3
  23.5 1.5 %collective-permute-start.6 = (f32[4,128,128]{2,1,0:T(8,128)S(1)}, f32[4,128,128]{2,1,0:T(8,128)S(1)}, u32[]{:S(2)}, u32[]{:S(2)}) collective-permute-start(f32[4,128,128]{2,1,0:T(8,128)S(1)} %add.88), channel_id=1, source_target_pairs={{0,8},{4,12},{8,0},{12,4},{1,9},{5,13},{9,1},{13,5},{2,10},{6,14},... | collective-permute-start | bytes 786440 | tf_op jit(solution)/shard_map/ppermute | solution.py:21
  25.0 12.9 %collective-permute-done.3 = f32[4,128,128]{2,1,0:T(8,128)S(1)} collective-permute-done((f32[4,128,128]{2,1,0:T(8,128)S(1)}, f32[4,128,128]{2,1,0:T(8,128)S(1)}, u32[]{:S(2)}, u32[]{:S(2)}) %collective-permute-start.3) | collective-permute-done | bytes 262176 | tf_op jit(solution)/shard_map/ppermute | solution.py:21
  37.9 0.1 collective-permute-start.4
  38.2 0.7 copy-done.2
  38.9 0.2 copy.30
  39.1 0.5 collective-permute-done.4
  39.6 1.6 %collective-permute-start.5 = (f32[4,128,128]{2,1,0:T(8,128)S(1)}, f32[4,128,128]{2,1,0:T(8,128)S(1)}, u32[]{:S(2)}, u32[]{:S(2)}) collective-permute-start(f32[4,128,128]{2,1,0:T(8,128)S(1)} %add.92), channel_id=1, source_target_pairs={{0,8},{4,12},{8,0},{12,4},{1,9},{5,13},{9,1},{13,5},{2,10},{6,14},... | collective-permute-start | bytes 786440 | tf_op jit(solution)/shard_map/ppermute | solution.py:21
  41.1 0.2 fusion.5
  41.4 5.5 %collective-permute-done.7 = f32[4,128,128]{2,1,0:T(8,128)S(1)} collective-permute-done((f32[4,128,128]{2,1,0:T(8,128)S(1)}, f32[4,128,128]{2,1,0:T(8,128)S(1)}, u32[]{:S(2)}, u32[]{:S(2)}) %collective-permute-start.7) | collective-permute-done | bytes 262176 | tf_op jit(solution)/shard_map/ppermute | solution.py:21
  46.9 1.1 %collective-permute-done.5 = f32[4,128,128]{2,1,0:T(8,128)S(1)} collective-permute-done((f32[4,128,128]{2,1,0:T(8,128)S(1)}, f32[4,128,128]{2,1,0:T(8,128)S(1)}, u32[]{:S(2)}, u32[]{:S(2)}) %collective-permute-start.5) | collective-permute-done | bytes 262176 | tf_op jit(solution)/shard_map/ppermute | solution.py:21
  48.1 0.3 fusion.3
  48.4 0.6 copy-done.3
  49.0 0.3 multiply_reduce_fusion
  49.4 0.2 copy.13
  49.6 0.7 copy-done.4
  50.3 0.2 fusion.8
  50.5 0.9 fusion.11
  51.4 0.3 convolution_bitcast_fusion
  51.8 1.0 %collective-permute-start.9 = (f32[4,128,128]{2,1,0:T(8,128)S(1)}, f32[4,128,128]{2,1,0:T(8,128)S(1)}, u32[]{:S(2)}, u32[]{:S(2)}) collective-permute-start(f32[4,128,128]{2,1,0:T(8,128)S(1)} %get-tuple-element.32), channel_id=1, source_target_pairs={{0,1},{1,0},{2,3},{3,2},{4,5},{5,4},{6,7},{7,6},{8,9},{9,8},{10,11... | collective-permute-start | bytes 786440 | tf_op jit(solution)/shard_map/ppermute | solution.py:21
  52.8 1.0 %collective-permute-start.8 = (f32[4,128,128]{2,1,0:T(8,128)S(1)}, f32[4,128,128]{2,1,0:T(8,128)S(1)}, u32[]{:S(2)}, u32[]{:S(2)}) collective-permute-start(f32[4,128,128]{2,1,0:T(8,128)S(1)} %get-tuple-element.33), channel_id=1, source_target_pairs={{0,2},{1,3},{2,0},{3,1},{4,6},{5,7},{6,4},{7,5},{8,10},{9,11},{10,... | collective-permute-start | bytes 786440 | tf_op jit(solution)/shard_map/ppermute | solution.py:21
  53.7 10.0 %collective-permute-done.9 = f32[4,128,128]{2,1,0:T(8,128)S(1)} collective-permute-done((f32[4,128,128]{2,1,0:T(8,128)S(1)}, f32[4,128,128]{2,1,0:T(8,128)S(1)}, u32[]{:S(2)}, u32[]{:S(2)}) %collective-permute-start.9) | collective-permute-done | bytes 262176 | tf_op jit(solution)/shard_map/ppermute | solution.py:21
  63.7 3.1 %collective-permute-done.8 = f32[4,128,128]{2,1,0:T(8,128)S(1)} collective-permute-done((f32[4,128,128]{2,1,0:T(8,128)S(1)}, f32[4,128,128]{2,1,0:T(8,128)S(1)}, u32[]{:S(2)}, u32[]{:S(2)}) %collective-permute-start.8) | collective-permute-done | bytes 262176 | tf_op jit(solution)/shard_map/ppermute | solution.py:21
  66.9 0.2 collective-permute-start.13
  67.1 0.3 fusion.7
  67.4 0.3 convolution_bitcast_fusion.2
  67.7 0.9 collective-permute-done.10
  68.6 1.6 %collective-permute-start.11 = (f32[4,128,128]{2,1,0:T(8,128)S(1)}, f32[4,128,128]{2,1,0:T(8,128)S(1)}, u32[]{:S(2)}, u32[]{:S(2)}) collective-permute-start(f32[4,128,128]{2,1,0:T(8,128)S(1)} %add.104), channel_id=1, source_target_pairs={{0,8},{4,12},{8,0},{12,4},{1,9},{5,13},{9,1},{13,5},{2,10},{6,14},... | collective-permute-start | bytes 786440 | tf_op jit(solution)/shard_map/ppermute | solution.py:21
  70.2 7.6 %collective-permute-done.13 = f32[4,128,128]{2,1,0:T(8,128)S(1)} collective-permute-done((f32[4,128,128]{2,1,0:T(8,128)S(1)}, f32[4,128,128]{2,1,0:T(8,128)S(1)}, u32[]{:S(2)}, u32[]{:S(2)}) %collective-permute-start.13) | collective-permute-done | bytes 262176 | tf_op jit(solution)/shard_map/ppermute | solution.py:21
  77.9 1.1 %fusion.19.local_k = f32[8,128,128]{2,1,0:T(8,128)} fusion(bf16[8,128,128]{2,1,0:T(8,128)(2,1)S(1)} %fusion.7, bf16[128,1024]{1,0:T(8,128)(2,1)S(1)} %copy-done), kind=kOutput, calls=%fused_computation.32 | convolution fusion | flops 33554432 | bytes 1048576 | tf_op jit(solution)/shard_map/hts,thi->hsi/dot_general | solution.py:179
  79.0 1.1 %fusion.13.local_v = f32[8,128,128]{2,1,0:T(8,128)} fusion(bf16[8,128,128]{2,1,0:T(8,128)(2,1)S(1)} %fusion.5, bf16[16,8,8,128]{3,2,1,0:T(8,128)(2,1)S(1)} %get-tuple-element.28), kind=kOutput, calls=%fused_computation.26 | convolution fusion | flops 33554432 | bytes 1048576 | tf_op jit(solution)/shard_map/hts,thj->hsj/dot_general | solution.py:180
  80.2 1.6 %collective-permute-start.15 = (f32[4,128,128]{2,1,0:T(8,128)S(1)}, f32[4,128,128]{2,1,0:T(8,128)S(1)}, u32[]{:S(2)}, u32[]{:S(2)}) collective-permute-start(f32[4,128,128]{2,1,0:T(8,128)S(1)} %add.111), channel_id=1, source_target_pairs={{0,8},{4,12},{8,0},{12,4},{1,9},{5,13},{9,1},{13,5},{2,10},{6,14},... | collective-permute-start | bytes 786440 | tf_op jit(solution)/shard_map/ppermute | solution.py:21
  81.7 0.8 add_select_fusion
  82.5 0.3 fusion.6
  82.8 0.9 copy.25
  83.6 5.3 %collective-permute-done.15 = f32[4,128,128]{2,1,0:T(8,128)S(1)} collective-permute-done((f32[4,128,128]{2,1,0:T(8,128)S(1)}, f32[4,128,128]{2,1,0:T(8,128)S(1)}, u32[]{:S(2)}, u32[]{:S(2)}) %collective-permute-start.15) | collective-permute-done | bytes 262176 | tf_op jit(solution)/shard_map/ppermute | solution.py:21
  88.9 0.8 select_add_fusion.upper_later
  89.7 1.2 %collective-permute-done.12.lower_got = f32[4,128,128]{2,1,0:T(8,128)S(1)} collective-permute-done((f32[4,128,128]{2,1,0:T(8,128)S(1)}, f32[4,128,128]{2,1,0:T(8,128)S(1)}, u32[]{:S(2)}, u32[]{:S(2)}) %collective-permute-start.12) | collective-permute-done | bytes 262176 | tf_op jit(solution)/shard_map/ppermute | solution.py:21
  90.9 0.7 copy-done.5
  91.6 2.7 %shard_map.76 = (bf16[128,1024]{1,0:T(8,128)(2,1)}, bf16[128,1024]{1,0:T(8,128)(2,1)}) custom-call(f32[4,128,128]{2,1,0:T(8,128)} %get-tuple-element.25.lower_known, f32[4,128,128]{2,1,0:T(8,128)} %copy-done.5, f32[4,128,128]{2,1,0:T(8,128)} %select_add_fusion.upper_later, f32[8,128,128]{2,1,0:T(8,128)} %fusion.19.local_k, f32[8,128,128]{2,1,0:T(8,128)} %fusion.13.local_v, ...), custom_call_target="tpu_custom_call" | custom-call | flops 67108864 | bytes 6291456 | tf_op jit(solution)/shard_map/pallas_call | solution.py:108
  (30 shorter events, 0.7 us)
Async XLA Ops:
  0.6 40.5 %copy-start = (bf16[128,1024]{1,0:T(8,128)(2,1)S(1)}, bf16[128,1024]{1,0:T(8,128)(2,1)}, u32[]{:S(2)}) copy-start(bf16[128,1024]{1,0:T(8,128)(2,1)} %param.4) | copy-start | bytes 786436
  2.8 18.6 %copy-start.1 = (f32[8,128,128]{2,1,0:T(8,128)S(1)}, f32[8,128,128]{2,1,0:T(8,128)}, u32[]{:S(2)}) copy-start(f32[8,128,128]{2,1,0:T(8,128)} %shard_map.75) | copy-start | bytes 1572868
  3.9 14.9 %collective-permute-start = (f32[4,128,128]{2,1,0:T(8,128)S(1)}, f32[4,128,128]{2,1,0:T(8,128)S(1)}, u32[]{:S(2)}, u32[]{:S(2)}) collective-permute-start(f32[4,128,128]{2,1,0:T(8,128)S(1)} %get-tuple-element.36), channel_id=1, source_target_pairs={{0,1},{1,0},{2,3},{3,2},{4,5},{5,4},{6,7},{7,6},{8,9},{9,8},{10,11... | collective-permute-start | bytes 786440 | tf_op jit(solution)/shard_map/ppermute | solution.py:21
  7.0 14.3 %collective-permute-start.1 = (f32[4,128,128]{2,1,0:T(8,128)S(1)}, f32[4,128,128]{2,1,0:T(8,128)S(1)}, u32[]{:S(2)}, u32[]{:S(2)}) collective-permute-start(f32[4,128,128]{2,1,0:T(8,128)S(1)} %get-tuple-element.37), channel_id=1, source_target_pairs={{0,2},{1,3},{2,0},{3,1},{4,6},{5,7},{6,4},{7,5},{8,10},{9,11},{10,... | collective-permute-start | bytes 786440 | tf_op jit(solution)/shard_map/ppermute | solution.py:21
  21.5 1.6 %collective-permute-start.2 = (f32[4,128,128]{2,1,0:T(8,128)S(1)}, f32[4,128,128]{2,1,0:T(8,128)S(1)}, u32[]{:S(2)}, u32[]{:S(2)}) collective-permute-start(f32[4,128,128]{2,1,0:T(8,128)S(1)} %get-tuple-element.12), channel_id=1, source_target_pairs={{0,4},{4,0},{8,12},{12,8},{1,5},{5,1},{9,13},{13,9},{2,6},{6,2},{1... | collective-permute-start | bytes 786440 | tf_op jit(solution)/shard_map/ppermute | solution.py:21
  23.1 14.8 %collective-permute-start.3 = (f32[4,128,128]{2,1,0:T(8,128)S(1)}, f32[4,128,128]{2,1,0:T(8,128)S(1)}, u32[]{:S(2)}, u32[]{:S(2)}) collective-permute-start(f32[4,128,128]{2,1,0:T(8,128)S(1)} %get-tuple-element.14), channel_id=1, source_target_pairs={{0,2},{1,3},{2,0},{3,1},{4,6},{5,7},{6,4},{7,5},{8,10},{9,11},{10,... | collective-permute-start | bytes 786440 | tf_op jit(solution)/shard_map/ppermute | solution.py:21
  23.5 14.6 %collective-permute-start.6 = (f32[4,128,128]{2,1,0:T(8,128)S(1)}, f32[4,128,128]{2,1,0:T(8,128)S(1)}, u32[]{:S(2)}, u32[]{:S(2)}) collective-permute-start(f32[4,128,128]{2,1,0:T(8,128)S(1)} %add.88), channel_id=1, source_target_pairs={{0,8},{4,12},{8,0},{12,4},{1,9},{5,13},{9,1},{13,5},{2,10},{6,14},... | collective-permute-start | bytes 786440 | tf_op jit(solution)/shard_map/ppermute | solution.py:21
  37.9 1.0 %copy-start.2 = (bf16[128,1024]{1,0:T(8,128)(2,1)S(1)}, bf16[128,1024]{1,0:T(8,128)(2,1)}, u32[]{:S(2)}) copy-start(bf16[128,1024]{1,0:T(8,128)(2,1)} %key.3) | copy-start | bytes 786436
  37.9 1.6 %collective-permute-start.4 = (f32[4,128,128]{2,1,0:T(8,128)S(1)}, f32[4,128,128]{2,1,0:T(8,128)S(1)}, u32[]{:S(2)}, u32[]{:S(2)}) collective-permute-start(f32[4,128,128]{2,1,0:T(8,128)S(1)} %add.90), channel_id=1, source_target_pairs={{0,4},{4,0},{8,12},{12,8},{1,5},{5,1},{9,13},{13,9},{2,6},{6,2},{1... | collective-permute-start | bytes 786440 | tf_op jit(solution)/shard_map/ppermute | solution.py:21
  38.1 8.8 %collective-permute-start.7 = (f32[4,128,128]{2,1,0:T(8,128)S(1)}, f32[4,128,128]{2,1,0:T(8,128)S(1)}, u32[]{:S(2)}, u32[]{:S(2)}) collective-permute-start(f32[4,128,128]{2,1,0:T(8,128)S(1)} %get-tuple-element.26), channel_id=1, source_target_pairs={{0,1},{1,0},{2,3},{3,2},{4,5},{5,4},{6,7},{7,6},{8,9},{9,8},{10,11... | collective-permute-start | bytes 786440 | tf_op jit(solution)/shard_map/ppermute | solution.py:21
  39.6 8.4 %collective-permute-start.5 = (f32[4,128,128]{2,1,0:T(8,128)S(1)}, f32[4,128,128]{2,1,0:T(8,128)S(1)}, u32[]{:S(2)}, u32[]{:S(2)}) collective-permute-start(f32[4,128,128]{2,1,0:T(8,128)S(1)} %add.92), channel_id=1, source_target_pairs={{0,8},{4,12},{8,0},{12,4},{1,9},{5,13},{9,1},{13,5},{2,10},{6,14},... | collective-permute-start | bytes 786440 | tf_op jit(solution)/shard_map/ppermute | solution.py:21
  48.1 1.0 %copy-start.3 = (bf16[128,1024]{1,0:T(8,128)(2,1)S(1)}, bf16[128,1024]{1,0:T(8,128)(2,1)}, u32[]{:S(2)}) copy-start(bf16[128,1024]{1,0:T(8,128)(2,1)} %value.3) | copy-start | bytes 786436
  49.4 1.0 %copy-start.4 = (bf16[128,1024]{1,0:T(8,128)(2,1)S(1)}, bf16[128,1024]{1,0:T(8,128)(2,1)}, u32[]{:S(2)}) copy-start(bf16[128,1024]{1,0:T(8,128)(2,1)} %param.7) | copy-start | bytes 786436
  51.8 11.9 %collective-permute-start.9 = (f32[4,128,128]{2,1,0:T(8,128)S(1)}, f32[4,128,128]{2,1,0:T(8,128)S(1)}, u32[]{:S(2)}, u32[]{:S(2)}) collective-permute-start(f32[4,128,128]{2,1,0:T(8,128)S(1)} %get-tuple-element.32), channel_id=1, source_target_pairs={{0,1},{1,0},{2,3},{3,2},{4,5},{5,4},{6,7},{7,6},{8,9},{9,8},{10,11... | collective-permute-start | bytes 786440 | tf_op jit(solution)/shard_map/ppermute | solution.py:21
  52.8 14.1 %collective-permute-start.8 = (f32[4,128,128]{2,1,0:T(8,128)S(1)}, f32[4,128,128]{2,1,0:T(8,128)S(1)}, u32[]{:S(2)}, u32[]{:S(2)}) collective-permute-start(f32[4,128,128]{2,1,0:T(8,128)S(1)} %get-tuple-element.33), channel_id=1, source_target_pairs={{0,2},{1,3},{2,0},{3,1},{4,6},{5,7},{6,4},{7,5},{8,10},{9,11},{10,... | collective-permute-start | bytes 786440 | tf_op jit(solution)/shard_map/ppermute | solution.py:21
  66.9 10.9 %collective-permute-start.13 = (f32[4,128,128]{2,1,0:T(8,128)S(1)}, f32[4,128,128]{2,1,0:T(8,128)S(1)}, u32[]{:S(2)}, u32[]{:S(2)}) collective-permute-start(f32[4,128,128]{2,1,0:T(8,128)S(1)} %get-tuple-element.30), channel_id=1, source_target_pairs={{0,2},{1,3},{2,0},{3,1},{4,6},{5,7},{6,4},{7,5},{8,10},{9,11},{10,... | collective-permute-start | bytes 786440 | tf_op jit(solution)/shard_map/ppermute | solution.py:21
  67.1 1.5 %collective-permute-start.10 = (f32[4,128,128]{2,1,0:T(8,128)S(1)}, f32[4,128,128]{2,1,0:T(8,128)S(1)}, u32[]{:S(2)}, u32[]{:S(2)}) collective-permute-start(f32[4,128,128]{2,1,0:T(8,128)S(1)} %get-tuple-element.16), channel_id=1, source_target_pairs={{0,4},{4,0},{8,12},{12,8},{1,5},{5,1},{9,13},{13,9},{2,6},{6,2},{1... | collective-permute-start | bytes 786440 | tf_op jit(solution)/shard_map/ppermute | solution.py:21
  68.6 13.1 %collective-permute-start.11 = (f32[4,128,128]{2,1,0:T(8,128)S(1)}, f32[4,128,128]{2,1,0:T(8,128)S(1)}, u32[]{:S(2)}, u32[]{:S(2)}) collective-permute-start(f32[4,128,128]{2,1,0:T(8,128)S(1)} %add.104), channel_id=1, source_target_pairs={{0,8},{4,12},{8,0},{12,4},{1,9},{5,13},{9,1},{13,5},{2,10},{6,14},... | collective-permute-start | bytes 786440 | tf_op jit(solution)/shard_map/ppermute | solution.py:21
  77.9 2.3 %collective-permute-start.14 = (f32[4,128,128]{2,1,0:T(8,128)S(1)}, f32[4,128,128]{2,1,0:T(8,128)S(1)}, u32[]{:S(2)}, u32[]{:S(2)}) collective-permute-start(f32[4,128,128]{2,1,0:T(8,128)S(1)} %add.109), channel_id=1, source_target_pairs={{0,4},{4,0},{8,12},{12,8},{1,5},{5,1},{9,13},{13,9},{2,6},{6,2},{1... | collective-permute-start | bytes 786440 | tf_op jit(solution)/shard_map/ppermute | solution.py:21
  80.2 8.8 %collective-permute-start.15 = (f32[4,128,128]{2,1,0:T(8,128)S(1)}, f32[4,128,128]{2,1,0:T(8,128)S(1)}, u32[]{:S(2)}, u32[]{:S(2)}) collective-permute-start(f32[4,128,128]{2,1,0:T(8,128)S(1)} %add.111), channel_id=1, source_target_pairs={{0,8},{4,12},{8,0},{12,4},{1,9},{5,13},{9,1},{13,5},{2,10},{6,14},... | collective-permute-start | bytes 786440 | tf_op jit(solution)/shard_map/ppermute | solution.py:21
  82.5 8.4 %collective-permute-start.12 = (f32[4,128,128]{2,1,0:T(8,128)S(1)}, f32[4,128,128]{2,1,0:T(8,128)S(1)}, u32[]{:S(2)}, u32[]{:S(2)}) collective-permute-start(f32[4,128,128]{2,1,0:T(8,128)S(1)} %get-tuple-element.24), channel_id=1, source_target_pairs={{0,1},{1,0},{2,3},{3,2},{4,5},{5,4},{6,7},{7,6},{8,9},{9,8},{10,11... | collective-permute-start | bytes 786440 | tf_op jit(solution)/shard_map/ppermute | solution.py:21
  90.9 0.7 copy-start.5

commit v15 on v12

--- a/solution.py
+++ b/solution.py
@@ -50,13 +50,11 @@
 def chunked_scan(value, backward):
     half = value.shape[0] // 2
     group_a, group_b = value[:half], value[half:]
-    if backward:
-        group_a, group_b = group_b, group_a
     inner_bits, outer_bits = axis_bits("inner"), axis_bits("outer")
     if not inner_bits:
         result = scan_inner_first(value, backward)
         if backward:
-            return result[:half], jnp.zeros_like(result[:half]), result[half:]
+            return result[:half], result[half:], jnp.zeros_like(result[half:])
         return result
     earlier_a, total_a = subcube_step([], group_a, "inner", inner_bits[0], backward)
     earlier_b, total_b = [], group_b
@@ -79,16 +77,16 @@
     earlier_a = added(earlier_a, group_a)
     got_b = swap(sent, "inner", low)
     if backward:
-        return known, got_b, earlier_a
+        return earlier_a, known, got_b
     return jnp.concatenate([earlier_a, known + got_b], axis=0)
 
 
 def tail_kernel(
-    scaling, lower_known, lower_got, upper_later, local_k, local_v, value, key, out_k, out_v
+    scaling, lower_later, upper_known, upper_got, local_k, local_v, value, key, out_k, out_v
 ):
     half = HEADS // 2
     for h in range(HEADS):
-        later = lower_known[h] + lower_got[h] if h < half else upper_later[h - half]
+        later = lower_later[h] if h < half else upper_known[h - half] + upper_got[h - half]
         later_half = later.astype(jnp.bfloat16)
         cols = slice(h * HEAD, (h + 1) * HEAD)
         from_later_k = lax.dot_general(
@@ -101,7 +99,7 @@
         out_v[:, cols] = (local_v[h] + scaling * from_later_v).astype(out_v.dtype)
 
 
-def tail(lower_known, lower_got, upper_later, local_k, local_v, value, key):
+def tail(lower_later, upper_known, upper_got, local_k, local_v, value, key):
     rows = value.shape[0]
     vmem = pl.BlockSpec(memory_space=pltpu.VMEM)
     out = jax.ShapeDtypeStruct((rows, HEADS * HEAD), jnp.bfloat16)
@@ -113,7 +111,7 @@
         cost_estimate=pl.CostEstimate(
             flops=4 * HEADS * rows * HEAD * HEAD, transcendentals=0, bytes_accessed=12 * rows * 1024 * 4
         ),
-    )(lower_known, lower_got, upper_later, local_k, local_v, value, key)
+    )(lower_later, upper_known, upper_got, local_k, local_v, value, key)
 
 
 def per_device(query, key, value, grad_out):
@@ -154,10 +152,10 @@
         + jnp.einsum("thj,hij->thi", grad_half, prior_half, preferred_element_type=jnp.float32)
     )
     grad_state = jnp.einsum("thi,thj->hij", queries, grad_half, preferred_element_type=jnp.float32)
-    lower_known, lower_got, upper_later = chunked_scan(grad_state, True)
+    lower_later, upper_known, upper_got = chunked_scan(grad_state, True)
     local_k = jnp.einsum("hts,thi->hsi", dscore_half, queries, preferred_element_type=jnp.float32)
     local_v = jnp.einsum("hts,thj->hsj", score_half, grad_half, preferred_element_type=jnp.float32)
-    grad_k, grad_v = tail(lower_known, lower_got, upper_later, local_k, local_v, value, key)
+    grad_k, grad_v = tail(lower_later, upper_known, upper_got, local_k, local_v, value, key)
     width = HEADS * HEAD
     return (
         normed.astype(jnp.bfloat16),

time: 91.9 us -> 92.8 us (level)
  no operation moved by 1% of the time
where the time goes in v15:
time: 92.8 us; the launch traced here: 92.6 us
  waiting for transfers between devices  62.2 us (67%)
  starting transfers between devices  15.5 us (17%)
  matrix products  4.44 us (5%)
  local copies, waits for them, and re-layouts  3.74 us (4%)
  other arithmetic  3.17 us (3%)
  Pallas kernels  2.73 us (3%)
    ppermute x16, waiting for transfers between devices, swap(): return lax.ppermute(value, axis, [(i, i ^ bit) for i in range(count)])  62.2 us
    ppermute x16, starting transfers between devices, swap(): return lax.ppermute(value, axis, [(i, i ^ bit) for i in range(count)])  15.5 us
    pallas_call x1, Pallas kernels, tail(): pl.pallas_call(functools.partial(tail_kernel, HEAD ** (-0.5)), out_shape=...  2.73 us
    unnamed x9, local copies, waits for them, and re-layouts  2.3 us
  transfers between devices with their start and end apart: 16, of which 13 were waited for; matrix products, arithmetic and copies ran while one was open for 6% of the time, Pallas kernels for 0%

profile of v15, /device:TPU:0, one launch (start us, length us, event | category | flops | bytes accessed | tf_op | source)
XLA Modules:
  0.0 92.6 jit_solution(12651067172530626710)
XLA Ops:
  0.7 1.2 %copy.32 = bf16[128,1024]{0,1:T(8,128)(2,1)S(1)} copy(bf16[128,1024]{1,0:T(8,128)(2,1)} %key.1) | data formatting | bytes 524288 | tf_op jit(solution)/shard_map/reshape | solution.py:121
  1.8 0.2 fusion.19
  2.1 3.1 %collective-permute-start = (f32[4,128,128]{2,1,0:T(8,128)S(1)}, f32[4,128,128]{2,1,0:T(8,128)S(1)}, u32[]{:S(2)}, u32[]{:S(2)}) collective-permute-start(f32[4,128,128]{2,1,0:T(8,128)S(1)} %get-tuple-element.36), channel_id=1, source_target_pairs={{0,1},{1,0},{2,3},{3,2},{4,5},{5,4},{6,7},{7,6},{8,9},{9,8},{10,11... | collective-permute-start | bytes 786440 | tf_op jit(solution)/shard_map/ppermute | solution.py:21
  5.2 2.6 %collective-permute-start.1 = (f32[4,128,128]{2,1,0:T(8,128)S(1)}, f32[4,128,128]{2,1,0:T(8,128)S(1)}, u32[]{:S(2)}, u32[]{:S(2)}) collective-permute-start(f32[4,128,128]{2,1,0:T(8,128)S(1)} %get-tuple-element.37), channel_id=1, source_target_pairs={{0,2},{1,3},{2,0},{3,1},{4,6},{5,7},{6,4},{7,5},{8,10},{9,11},{10,... | collective-permute-start | bytes 786440 | tf_op jit(solution)/shard_map/ppermute | solution.py:21
  7.8 9.2 %collective-permute-done = f32[4,128,128]{2,1,0:T(8,128)S(1)} collective-permute-done((f32[4,128,128]{2,1,0:T(8,128)S(1)}, f32[4,128,128]{2,1,0:T(8,128)S(1)}, u32[]{:S(2)}, u32[]{:S(2)}) %collective-permute-start) | collective-permute-done | bytes 262176 | tf_op jit(solution)/shard_map/ppermute | solution.py:21
  17.0 2.5 %collective-permute-done.1 = f32[4,128,128]{2,1,0:T(8,128)S(1)} collective-permute-done((f32[4,128,128]{2,1,0:T(8,128)S(1)}, f32[4,128,128]{2,1,0:T(8,128)S(1)}, u32[]{:S(2)}, u32[]{:S(2)}) %collective-permute-start.1) | collective-permute-done | bytes 262176 | tf_op jit(solution)/shard_map/ppermute | solution.py:21
  19.6 0.1 slice_add_fusion.1
  19.7 0.1 collective-permute-start.2
  19.7 1.5 %collective-permute-done.2 = f32[4,128,128]{2,1,0:T(8,128)S(1)} collective-permute-done((f32[4,128,128]{2,1,0:T(8,128)S(1)}, f32[4,128,128]{2,1,0:T(8,128)S(1)}, u32[]{:S(2)}, u32[]{:S(2)}) %collective-permute-start.2) | collective-permute-done | bytes 262176 | tf_op jit(solution)/shard_map/ppermute | solution.py:21
  21.3 0.4 collective-permute-start.3
  21.7 1.5 %collective-permute-start.6 = (f32[4,128,128]{2,1,0:T(8,128)S(1)}, f32[4,128,128]{2,1,0:T(8,128)S(1)}, u32[]{:S(2)}, u32[]{:S(2)}) collective-permute-start(f32[4,128,128]{2,1,0:T(8,128)S(1)} %add.88), channel_id=1, source_target_pairs={{0,8},{4,12},{8,0},{12,4},{1,9},{5,13},{9,1},{13,5},{2,10},{6,14},... | collective-permute-start | bytes 786440 | tf_op jit(solution)/shard_map/ppermute | solution.py:21
  23.2 12.9 %collective-permute-done.3 = f32[4,128,128]{2,1,0:T(8,128)S(1)} collective-permute-done((f32[4,128,128]{2,1,0:T(8,128)S(1)}, f32[4,128,128]{2,1,0:T(8,128)S(1)}, u32[]{:S(2)}, u32[]{:S(2)}) %collective-permute-start.3) | collective-permute-done | bytes 262176 | tf_op jit(solution)/shard_map/ppermute | solution.py:21
  36.1 0.1 collective-permute-start.4
  36.4 1.3 %collective-permute-done.4 = f32[4,128,128]{2,1,0:T(8,128)S(1)} collective-permute-done((f32[4,128,128]{2,1,0:T(8,128)S(1)}, f32[4,128,128]{2,1,0:T(8,128)S(1)}, u32[]{:S(2)}, u32[]{:S(2)}) %collective-permute-start.4) | collective-permute-done | bytes 262176 | tf_op jit(solution)/shard_map/ppermute | solution.py:21
  37.8 1.6 %collective-permute-start.5 = (f32[4,128,128]{2,1,0:T(8,128)S(1)}, f32[4,128,128]{2,1,0:T(8,128)S(1)}, u32[]{:S(2)}, u32[]{:S(2)}) collective-permute-start(f32[4,128,128]{2,1,0:T(8,128)S(1)} %add.92), channel_id=1, source_target_pairs={{0,8},{4,12},{8,0},{12,4},{1,9},{5,13},{9,1},{13,5},{2,10},{6,14},... | collective-permute-start | bytes 786440 | tf_op jit(solution)/shard_map/ppermute | solution.py:21
  39.3 0.2 fusion.5
  39.6 5.5 %collective-permute-done.7 = f32[4,128,128]{2,1,0:T(8,128)S(1)} collective-permute-done((f32[4,128,128]{2,1,0:T(8,128)S(1)}, f32[4,128,128]{2,1,0:T(8,128)S(1)}, u32[]{:S(2)}, u32[]{:S(2)}) %collective-permute-start.7) | collective-permute-done | bytes 262176 | tf_op jit(solution)/shard_map/ppermute | solution.py:21
  45.1 1.1 %collective-permute-done.5 = f32[4,128,128]{2,1,0:T(8,128)S(1)} collective-permute-done((f32[4,128,128]{2,1,0:T(8,128)S(1)}, f32[4,128,128]{2,1,0:T(8,128)S(1)}, u32[]{:S(2)}, u32[]{:S(2)}) %collective-permute-start.5) | collective-permute-done | bytes 262176 | tf_op jit(solution)/shard_map/ppermute | solution.py:21
  46.2 0.1 add_convert_fusion.1
  46.3 0.3 fusion.3
  46.6 0.3 multiply_reduce_fusion
  47.0 0.2 copy.15
  47.2 0.7 copy-done.2
  47.9 0.2 fusion.8
  48.1 0.9 fusion.11
  49.0 0.3 convolution_bitcast_fusion
  49.3 0.7 collective-permute-start.12
  50.1 1.3 %collective-permute-start.8 = (f32[4,128,128]{2,1,0:T(8,128)S(1)}, f32[4,128,128]{2,1,0:T(8,128)S(1)}, u32[]{:S(2)}, u32[]{:S(2)}) collective-permute-start(f32[4,128,128]{2,1,0:T(8,128)S(1)} %get-tuple-element.33), channel_id=1, source_target_pairs={{0,1},{1,0},{2,3},{3,2},{4,5},{5,4},{6,7},{7,6},{8,9},{9,8},{10,11... | collective-permute-start | bytes 786440 | tf_op jit(solution)/shard_map/ppermute | solution.py:21
  51.3 12.1 %collective-permute-done.12 = f32[4,128,128]{2,1,0:T(8,128)S(1)} collective-permute-done((f32[4,128,128]{2,1,0:T(8,128)S(1)}, f32[4,128,128]{2,1,0:T(8,128)S(1)}, u32[]{:S(2)}, u32[]{:S(2)}) %collective-permute-start.12) | collective-permute-done | bytes 262176 | tf_op jit(solution)/shard_map/ppermute | solution.py:21
  63.5 0.9 collective-permute-start.9
  64.4 0.3 fusion.7
  64.7 1.1 %fusion.13.local_v = f32[8,128,128]{2,1,0:T(8,128)} fusion(bf16[8,128,128]{2,1,0:T(8,128)(2,1)S(1)} %fusion.5, bf16[16,8,8,128]{3,2,1,0:T(8,128)(2,1)S(1)} %get-tuple-element.28), kind=kOutput, calls=%fused_computation.26 | convolution fusion | flops 33554432 | bytes 1048576 | tf_op jit(solution)/shard_map/hts,thj->hsj/dot_general | solution.py:157
  65.8 0.2 collective-permute-done.13
  66.0 1.6 %collective-permute-start.14 = (f32[4,128,128]{2,1,0:T(8,128)S(1)}, f32[4,128,128]{2,1,0:T(8,128)S(1)}, u32[]{:S(2)}, u32[]{:S(2)}) collective-permute-start(f32[4,128,128]{2,1,0:T(8,128)S(1)} %add.109), channel_id=1, source_target_pairs={{0,8},{4,12},{8,0},{12,4},{1,9},{5,13},{9,1},{13,5},{2,10},{6,14},... | collective-permute-start | bytes 786440 | tf_op jit(solution)/shard_map/ppermute | solution.py:21
  67.5 9.3 %collective-permute-done.9 = f32[4,128,128]{2,1,0:T(8,128)S(1)} collective-permute-done((f32[4,128,128]{2,1,0:T(8,128)S(1)}, f32[4,128,128]{2,1,0:T(8,128)S(1)}, u32[]{:S(2)}, u32[]{:S(2)}) %collective-permute-start.9) | collective-permute-done | bytes 262176 | tf_op jit(solution)/shard_map/ppermute | solution.py:21
  76.8 0.1 collective-permute-start.10
  76.9 1.1 %fusion.21.local_k = f32[8,128,128]{2,1,0:T(8,128)} fusion(bf16[8,128,128]{2,1,0:T(8,128)(2,1)S(1)} %fusion.7, bf16[128,1024]{1,0:T(8,128)(2,1)S(1)} %copy-done), kind=kOutput, calls=%fused_computation.34 | convolution fusion | flops 33554432 | bytes 1048576 | tf_op jit(solution)/shard_map/hts,thi->hsi/dot_general | solution.py:156
  78.0 0.3 convolution_bitcast_fusion.2
  78.3 0.1 collective-permute-done.10
  78.5 1.6 %collective-permute-start.11 = (f32[4,128,128]{2,1,0:T(8,128)S(1)}, f32[4,128,128]{2,1,0:T(8,128)S(1)}, u32[]{:S(2)}, u32[]{:S(2)}) collective-permute-start(f32[4,128,128]{2,1,0:T(8,128)S(1)} %add.106), channel_id=1, source_target_pairs={{0,8},{4,12},{8,0},{12,4},{1,9},{5,13},{9,1},{13,5},{2,10},{6,14},... | collective-permute-start | bytes 786440 | tf_op jit(solution)/shard_map/ppermute | solution.py:21
  80.1 0.8 add_select_fusion
  80.8 0.3 fusion.6
  81.1 0.9 copy.27
  82.0 5.2 %collective-permute-done.11 = f32[4,128,128]{2,1,0:T(8,128)S(1)} collective-permute-done((f32[4,128,128]{2,1,0:T(8,128)S(1)}, f32[4,128,128]{2,1,0:T(8,128)S(1)}, u32[]{:S(2)}, u32[]{:S(2)}) %collective-permute-start.11) | collective-permute-done | bytes 262176 | tf_op jit(solution)/shard_map/ppermute | solution.py:21
  87.1 0.8 select_add_fusion.lower_later
  87.9 1.2 %collective-permute-done.15.upper_got = f32[4,128,128]{2,1,0:T(8,128)S(1)} collective-permute-done((f32[4,128,128]{2,1,0:T(8,128)S(1)}, f32[4,128,128]{2,1,0:T(8,128)S(1)}, u32[]{:S(2)}, u32[]{:S(2)}) %collective-permute-start.15) | collective-permute-done | bytes 262176 | tf_op jit(solution)/shard_map/ppermute | solution.py:21
  89.1 0.7 copy-done.3
  89.8 2.7 %shard_map.75 = (bf16[128,1024]{1,0:T(8,128)(2,1)}, bf16[128,1024]{1,0:T(8,128)(2,1)}) custom-call(f32[4,128,128]{2,1,0:T(8,128)} %select_add_fusion.lower_later, f32[4,128,128]{2,1,0:T(8,128)} %get-tuple-element.25.upper_known, f32[4,128,128]{2,1,0:T(8,128)} %copy-done.3, f32[8,128,128]{2,1,0:T(8,128)} %fusion.21.local_k, f32[8,128,128]{2,1,0:T(8,128)} %fusion.13.local_v, ...), custom_call_target="tpu_custom_call" | custom-call | flops 67108864 | bytes 6291456 | tf_op jit(solution)/shard_map/pallas_call | solution.py:106
  (26 shorter events, 0.6 us)
Async XLA Ops:
  0.6 38.7 %copy-start = (bf16[128,1024]{1,0:T(8,128)(2,1)S(1)}, bf16[128,1024]{1,0:T(8,128)(2,1)}, u32[]{:S(2)}) copy-start(bf16[128,1024]{1,0:T(8,128)(2,1)} %param.4) | copy-start | bytes 786436
  0.6 1.2 %copy-start.1 = (bf16[128,1024]{1,0:T(8,128)(2,1)S(1)}, bf16[128,1024]{1,0:T(8,128)(2,1)}, u32[]{:S(2)}) copy-start(bf16[128,1024]{1,0:T(8,128)(2,1)} %value.1) | copy-start | bytes 786436
  2.1 14.9 %collective-permute-start = (f32[4,128,128]{2,1,0:T(8,128)S(1)}, f32[4,128,128]{2,1,0:T(8,128)S(1)}, u32[]{:S(2)}, u32[]{:S(2)}) collective-permute-start(f32[4,128,128]{2,1,0:T(8,128)S(1)} %get-tuple-element.36), channel_id=1, source_target_pairs={{0,1},{1,0},{2,3},{3,2},{4,5},{5,4},{6,7},{7,6},{8,9},{9,8},{10,11... | collective-permute-start | bytes 786440 | tf_op jit(solution)/shard_map/ppermute | solution.py:21
  5.2 14.3 %collective-permute-start.1 = (f32[4,128,128]{2,1,0:T(8,128)S(1)}, f32[4,128,128]{2,1,0:T(8,128)S(1)}, u32[]{:S(2)}, u32[]{:S(2)}) collective-permute-start(f32[4,128,128]{2,1,0:T(8,128)S(1)} %get-tuple-element.37), channel_id=1, source_target_pairs={{0,2},{1,3},{2,0},{3,1},{4,6},{5,7},{6,4},{7,5},{8,10},{9,11},{10,... | collective-permute-start | bytes 786440 | tf_op jit(solution)/shard_map/ppermute | solution.py:21
  19.7 1.6 %collective-permute-start.2 = (f32[4,128,128]{2,1,0:T(8,128)S(1)}, f32[4,128,128]{2,1,0:T(8,128)S(1)}, u32[]{:S(2)}, u32[]{:S(2)}) collective-permute-start(f32[4,128,128]{2,1,0:T(8,128)S(1)} %get-tuple-element.12), channel_id=1, source_target_pairs={{0,4},{4,0},{8,12},{12,8},{1,5},{5,1},{9,13},{13,9},{2,6},{6,2},{1... | collective-permute-start | bytes 786440 | tf_op jit(solution)/shard_map/ppermute | solution.py:21
  21.3 14.8 %collective-permute-start.3 = (f32[4,128,128]{2,1,0:T(8,128)S(1)}, f32[4,128,128]{2,1,0:T(8,128)S(1)}, u32[]{:S(2)}, u32[]{:S(2)}) collective-permute-start(f32[4,128,128]{2,1,0:T(8,128)S(1)} %get-tuple-element.14), channel_id=1, source_target_pairs={{0,2},{1,3},{2,0},{3,1},{4,6},{5,7},{6,4},{7,5},{8,10},{9,11},{10,... | collective-permute-start | bytes 786440 | tf_op jit(solution)/shard_map/ppermute | solution.py:21
  21.7 14.6 %collective-permute-start.6 = (f32[4,128,128]{2,1,0:T(8,128)S(1)}, f32[4,128,128]{2,1,0:T(8,128)S(1)}, u32[]{:S(2)}, u32[]{:S(2)}) collective-permute-start(f32[4,128,128]{2,1,0:T(8,128)S(1)} %add.88), channel_id=1, source_target_pairs={{0,8},{4,12},{8,0},{12,4},{1,9},{5,13},{9,1},{13,5},{2,10},{6,14},... | collective-permute-start | bytes 786440 | tf_op jit(solution)/shard_map/ppermute | solution.py:21
  36.1 1.6 %collective-permute-start.4 = (f32[4,128,128]{2,1,0:T(8,128)S(1)}, f32[4,128,128]{2,1,0:T(8,128)S(1)}, u32[]{:S(2)}, u32[]{:S(2)}) collective-permute-start(f32[4,128,128]{2,1,0:T(8,128)S(1)} %add.90), channel_id=1, source_target_pairs={{0,4},{4,0},{8,12},{12,8},{1,5},{5,1},{9,13},{13,9},{2,6},{6,2},{1... | collective-permute-start | bytes 786440 | tf_op jit(solution)/shard_map/ppermute | solution.py:21
  36.3 8.8 %collective-permute-start.7 = (f32[4,128,128]{2,1,0:T(8,128)S(1)}, f32[4,128,128]{2,1,0:T(8,128)S(1)}, u32[]{:S(2)}, u32[]{:S(2)}) collective-permute-start(f32[4,128,128]{2,1,0:T(8,128)S(1)} %get-tuple-element.26), channel_id=1, source_target_pairs={{0,1},{1,0},{2,3},{3,2},{4,5},{5,4},{6,7},{7,6},{8,9},{9,8},{10,11... | collective-permute-start | bytes 786440 | tf_op jit(solution)/shard_map/ppermute | solution.py:21
  37.8 8.4 %collective-permute-start.5 = (f32[4,128,128]{2,1,0:T(8,128)S(1)}, f32[4,128,128]{2,1,0:T(8,128)S(1)}, u32[]{:S(2)}, u32[]{:S(2)}) collective-permute-start(f32[4,128,128]{2,1,0:T(8,128)S(1)} %add.92), channel_id=1, source_target_pairs={{0,8},{4,12},{8,0},{12,4},{1,9},{5,13},{9,1},{13,5},{2,10},{6,14},... | collective-permute-start | bytes 786440 | tf_op jit(solution)/shard_map/ppermute | solution.py:21
  46.9 1.0 %copy-start.2 = (bf16[128,1024]{1,0:T(8,128)(2,1)S(1)}, bf16[128,1024]{1,0:T(8,128)(2,1)}, u32[]{:S(2)}) copy-start(bf16[128,1024]{1,0:T(8,128)(2,1)} %param.7) | copy-start | bytes 786436
  49.3 14.1 %collective-permute-start.12 = (f32[4,128,128]{2,1,0:T(8,128)S(1)}, f32[4,128,128]{2,1,0:T(8,128)S(1)}, u32[]{:S(2)}, u32[]{:S(2)}) collective-permute-start(f32[4,128,128]{2,1,0:T(8,128)S(1)} %get-tuple-element.32), channel_id=1, source_target_pairs={{0,2},{1,3},{2,0},{3,1},{4,6},{5,7},{6,4},{7,5},{8,10},{9,11},{10,... | collective-permute-start | bytes 786440 | tf_op jit(solution)/shard_map/ppermute | solution.py:21
  50.1 13.4 %collective-permute-start.8 = (f32[4,128,128]{2,1,0:T(8,128)S(1)}, f32[4,128,128]{2,1,0:T(8,128)S(1)}, u32[]{:S(2)}, u32[]{:S(2)}) collective-permute-start(f32[4,128,128]{2,1,0:T(8,128)S(1)} %get-tuple-element.33), channel_id=1, source_target_pairs={{0,1},{1,0},{2,3},{3,2},{4,5},{5,4},{6,7},{7,6},{8,9},{9,8},{10,11... | collective-permute-start | bytes 786440 | tf_op jit(solution)/shard_map/ppermute | solution.py:21
  63.5 13.3 %collective-permute-start.9 = (f32[4,128,128]{2,1,0:T(8,128)S(1)}, f32[4,128,128]{2,1,0:T(8,128)S(1)}, u32[]{:S(2)}, u32[]{:S(2)}) collective-permute-start(f32[4,128,128]{2,1,0:T(8,128)S(1)} %get-tuple-element.31), channel_id=1, source_target_pairs={{0,2},{1,3},{2,0},{3,1},{4,6},{5,7},{6,4},{7,5},{8,10},{9,11},{10,... | collective-permute-start | bytes 786440 | tf_op jit(solution)/shard_map/ppermute | solution.py:21
  64.4 1.5 %collective-permute-start.13 = (f32[4,128,128]{2,1,0:T(8,128)S(1)}, f32[4,128,128]{2,1,0:T(8,128)S(1)}, u32[]{:S(2)}, u32[]{:S(2)}) collective-permute-start(f32[4,128,128]{2,1,0:T(8,128)S(1)} %get-tuple-element.16), channel_id=1, source_target_pairs={{0,4},{4,0},{8,12},{12,8},{1,5},{5,1},{9,13},{13,9},{2,6},{6,2},{1... | collective-permute-start | bytes 786440 | tf_op jit(solution)/shard_map/ppermute | solution.py:21
  66.0 14.1 %collective-permute-start.14 = (f32[4,128,128]{2,1,0:T(8,128)S(1)}, f32[4,128,128]{2,1,0:T(8,128)S(1)}, u32[]{:S(2)}, u32[]{:S(2)}) collective-permute-start(f32[4,128,128]{2,1,0:T(8,128)S(1)} %add.109), channel_id=1, source_target_pairs={{0,8},{4,12},{8,0},{12,4},{1,9},{5,13},{9,1},{13,5},{2,10},{6,14},... | collective-permute-start | bytes 786440 | tf_op jit(solution)/shard_map/ppermute | solution.py:21
  76.8 1.6 %collective-permute-start.10 = (f32[4,128,128]{2,1,0:T(8,128)S(1)}, f32[4,128,128]{2,1,0:T(8,128)S(1)}, u32[]{:S(2)}, u32[]{:S(2)}) collective-permute-start(f32[4,128,128]{2,1,0:T(8,128)S(1)} %add.104), channel_id=1, source_target_pairs={{0,4},{4,0},{8,12},{12,8},{1,5},{5,1},{9,13},{13,9},{2,6},{6,2},{1... | collective-permute-start | bytes 786440 | tf_op jit(solution)/shard_map/ppermute | solution.py:21
  78.5 8.7 %collective-permute-start.11 = (f32[4,128,128]{2,1,0:T(8,128)S(1)}, f32[4,128,128]{2,1,0:T(8,128)S(1)}, u32[]{:S(2)}, u32[]{:S(2)}) collective-permute-start(f32[4,128,128]{2,1,0:T(8,128)S(1)} %add.106), channel_id=1, source_target_pairs={{0,8},{4,12},{8,0},{12,4},{1,9},{5,13},{9,1},{13,5},{2,10},{6,14},... | collective-permute-start | bytes 786440 | tf_op jit(solution)/shard_map/ppermute | solution.py:21
  80.8 8.3 %collective-permute-start.15 = (f32[4,128,128]{2,1,0:T(8,128)S(1)}, f32[4,128,128]{2,1,0:T(8,128)S(1)}, u32[]{:S(2)}, u32[]{:S(2)}) collective-permute-start(f32[4,128,128]{2,1,0:T(8,128)S(1)} %get-tuple-element.24), channel_id=1, source_target_pairs={{0,1},{1,0},{2,3},{3,2},{4,5},{5,4},{6,7},{7,6},{8,9},{9,8},{10,11... | collective-permute-start | bytes 786440 | tf_op jit(solution)/shard_map/ppermute | solution.py:21
  89.1 0.7 copy-start.3

commit v16 on v12

--- a/solution.py
+++ b/solution.py
@@ -47,7 +47,7 @@
     return added(earlier, value)
 
 
-def chunked_scan(value, backward):
+def chunked_scan(value, backward, passenger=None):
     half = value.shape[0] // 2
     group_a, group_b = value[:half], value[half:]
     if backward:
@@ -57,7 +57,7 @@
         result = scan_inner_first(value, backward)
         if backward:
             return result[:half], jnp.zeros_like(result[:half]), result[half:]
-        return result
+        return result, passenger
     earlier_a, total_a = subcube_step([], group_a, "inner", inner_bits[0], backward)
     earlier_b, total_b = [], group_b
     for bit in inner_bits[1:]:
@@ -67,7 +67,9 @@
     for index, bit in enumerate(outer_bits):
         rows_before, rows_total = subcube_step(rows_before, rows_total, "outer", bit, backward)
         if index == 0 and not backward:
-            (earlier_a, total_a), _ = lax.optimization_barrier(((earlier_a, total_a), rows_total))
+            (earlier_a, total_a), _, passenger = lax.optimization_barrier(
+                ((earlier_a, total_a), rows_total, passenger)
+            )
     for bit in inner_bits[1:]:
         earlier_a, total_a = subcube_step(earlier_a, total_a, "inner", bit, backward)
     for bit in outer_bits:
@@ -80,7 +82,7 @@
     got_b = swap(sent, "inner", low)
     if backward:
         return known, got_b, earlier_a
-    return jnp.concatenate([earlier_a, known + got_b], axis=0)
+    return jnp.concatenate([earlier_a, known + got_b], axis=0), passenger
 
 
 def tail_kernel(
@@ -126,7 +128,7 @@
     column = lax.broadcasted_iota(jnp.int32, (rows_dev, rows_dev), 1)
     causal = (line >= column)[None]
     state = jnp.einsum("thi,thj->hij", key_rows, value_rows, preferred_element_type=jnp.float32)
-    prior = chunked_scan(state, False)
+    prior, grads_flat = chunked_scan(state, False, grad_out.astype(jnp.float32))
     prior_half = prior.astype(jnp.bfloat16)
     scores = (
         jnp.einsum("thi,shi->hts", queries, key_rows, preferred_element_type=jnp.float32) * scaling
@@ -141,7 +143,6 @@
     flat = attended.reshape(rows_dev, HEADS * HEAD)
     inverse = lax.rsqrt(jnp.mean(flat * flat, axis=-1, keepdims=True) + 1e-05)
     normed = flat * inverse
-    grads_flat = grad_out.astype(jnp.float32)
     grad_pre = inverse * (
         grads_flat - normed * jnp.mean(grads_flat * normed, axis=-1, keepdims=True)
     )

time: 91.9 us -> 92.7 us (level)
  transfers between devices with their start and end apart: 16 -> 16, of which waited for: 13 -> 13; matrix products, arithmetic and copies ran while one was open for 6% -> 7% of each run, Pallas kernels for 0% -> 0%
where the time goes in v16:
time: 92.7 us; the launch traced here: 92.5 us
  waiting for transfers between devices  62.8 us (68%)
  starting transfers between devices  14.8 us (16%)
  matrix products  4.43 us (5%)
  other arithmetic  3.91 us (4%)
  local copies, waits for them, and re-layouts  3.01 us (3%)
  Pallas kernels  2.73 us (3%)
    ppermute x16, waiting for transfers between devices, swap(): return lax.ppermute(value, axis, [(i, i ^ bit) for i in range(count)])  62.8 us
    ppermute x16, starting transfers between devices, swap(): return lax.ppermute(value, axis, [(i, i ^ bit) for i in range(count)])  14.8 us
    pallas_call x1, Pallas kernels, tail(): pl.pallas_call(functools.partial(tail_kernel, HEAD ** (-0.5)), out_shape=...  2.73 us
  transfers between devices with their start and end apart: 16, of which 13 were waited for; matrix products, arithmetic and copies ran while one was open for 7% of the time, Pallas kernels for 0%

profile of v16, /device:TPU:0, one launch (start us, length us, event | category | flops | bytes accessed | tf_op | source)
XLA Modules:
  0.0 92.5 jit_solution(14310318654406678909)
XLA Ops:
  0.7 1.2 %copy.32 = bf16[128,1024]{0,1:T(8,128)(2,1)S(1)} copy(bf16[128,1024]{1,0:T(8,128)(2,1)} %key.1) | data formatting | bytes 524288 | tf_op jit(solution)/shard_map/reshape | solution.py:125
  1.8 0.2 fusion.16
  2.1 3.1 %collective-permute-start = (f32[4,128,128]{2,1,0:T(8,128)S(1)}, f32[4,128,128]{2,1,0:T(8,128)S(1)}, u32[]{:S(2)}, u32[]{:S(2)}) collective-permute-start(f32[4,128,128]{2,1,0:T(8,128)S(1)} %get-tuple-element.38), channel_id=1, source_target_pairs={{0,1},{1,0},{2,3},{3,2},{4,5},{5,4},{6,7},{7,6},{8,9},{9,8},{10,11... | collective-permute-start | bytes 786440 | tf_op jit(solution)/shard_map/ppermute | solution.py:21
  5.2 2.6 %collective-permute-start.1 = (f32[4,128,128]{2,1,0:T(8,128)S(1)}, f32[4,128,128]{2,1,0:T(8,128)S(1)}, u32[]{:S(2)}, u32[]{:S(2)}) collective-permute-start(f32[4,128,128]{2,1,0:T(8,128)S(1)} %get-tuple-element.39), channel_id=1, source_target_pairs={{0,2},{1,3},{2,0},{3,1},{4,6},{5,7},{6,4},{7,5},{8,10},{9,11},{10,... | collective-permute-start | bytes 786440 | tf_op jit(solution)/shard_map/ppermute | solution.py:21
  7.8 9.2 %collective-permute-done = f32[4,128,128]{2,1,0:T(8,128)S(1)} collective-permute-done((f32[4,128,128]{2,1,0:T(8,128)S(1)}, f32[4,128,128]{2,1,0:T(8,128)S(1)}, u32[]{:S(2)}, u32[]{:S(2)}) %collective-permute-start) | collective-permute-done | bytes 262176 | tf_op jit(solution)/shard_map/ppermute | solution.py:21
  17.0 2.5 %collective-permute-done.1 = f32[4,128,128]{2,1,0:T(8,128)S(1)} collective-permute-done((f32[4,128,128]{2,1,0:T(8,128)S(1)}, f32[4,128,128]{2,1,0:T(8,128)S(1)}, u32[]{:S(2)}, u32[]{:S(2)}) %collective-permute-start.1) | collective-permute-done | bytes 262176 | tf_op jit(solution)/shard_map/ppermute | solution.py:21
  19.6 0.1 slice_add_fusion.1
  19.7 0.1 collective-permute-start.2
  19.8 1.5 %collective-permute-done.2 = f32[4,128,128]{2,1,0:T(8,128)S(1)} collective-permute-done((f32[4,128,128]{2,1,0:T(8,128)S(1)}, f32[4,128,128]{2,1,0:T(8,128)S(1)}, u32[]{:S(2)}, u32[]{:S(2)}) %collective-permute-start.2) | collective-permute-done | bytes 262176 | tf_op jit(solution)/shard_map/ppermute | solution.py:21
  21.3 0.4 collective-permute-start.3
  21.7 1.5 %collective-permute-start.6 = (f32[4,128,128]{2,1,0:T(8,128)S(1)}, f32[4,128,128]{2,1,0:T(8,128)}, u32[]{:S(2)}, u32[]{:S(2)}) collective-permute-start(f32[4,128,128]{2,1,0:T(8,128)S(1)} %add.88), channel_id=1, source_target_pairs={{0,8},{4,12},{8,0},{12,4},{1,9},{5,13},{9,1},{13,5},{2,10},{6,14},... | collective-permute-start | bytes 786440 | tf_op jit(solution)/shard_map/ppermute | solution.py:21
  23.2 12.9 %collective-permute-done.3 = f32[4,128,128]{2,1,0:T(8,128)S(1)} collective-permute-done((f32[4,128,128]{2,1,0:T(8,128)S(1)}, f32[4,128,128]{2,1,0:T(8,128)S(1)}, u32[]{:S(2)}, u32[]{:S(2)}) %collective-permute-start.3) | collective-permute-done | bytes 262176 | tf_op jit(solution)/shard_map/ppermute | solution.py:21
  36.1 0.1 collective-permute-start.4
  36.4 1.3 %collective-permute-done.4 = f32[4,128,128]{2,1,0:T(8,128)S(1)} collective-permute-done((f32[4,128,128]{2,1,0:T(8,128)S(1)}, f32[4,128,128]{2,1,0:T(8,128)S(1)}, u32[]{:S(2)}, u32[]{:S(2)}) %collective-permute-start.4) | collective-permute-done | bytes 262176 | tf_op jit(solution)/shard_map/ppermute | solution.py:21
  37.8 1.6 %collective-permute-start.5 = (f32[4,128,128]{2,1,0:T(8,128)S(1)}, f32[4,128,128]{2,1,0:T(8,128)S(1)}, u32[]{:S(2)}, u32[]{:S(2)}) collective-permute-start(f32[4,128,128]{2,1,0:T(8,128)S(1)} %add.92), channel_id=1, source_target_pairs={{0,8},{4,12},{8,0},{12,4},{1,9},{5,13},{9,1},{13,5},{2,10},{6,14},... | collective-permute-start | bytes 786440 | tf_op jit(solution)/shard_map/ppermute | solution.py:21
  39.3 0.2 fusion.5
  39.6 5.5 %collective-permute-done.7 = f32[4,128,128]{2,1,0:T(8,128)S(1)} collective-permute-done((f32[4,128,128]{2,1,0:T(8,128)S(1)}, f32[4,128,128]{2,1,0:T(8,128)S(1)}, u32[]{:S(2)}, u32[]{:S(2)}) %collective-permute-start.7) | collective-permute-done | bytes 262176 | tf_op jit(solution)/shard_map/ppermute | solution.py:21
  45.1 1.1 %collective-permute-done.5 = f32[4,128,128]{2,1,0:T(8,128)S(1)} collective-permute-done((f32[4,128,128]{2,1,0:T(8,128)S(1)}, f32[4,128,128]{2,1,0:T(8,128)S(1)}, u32[]{:S(2)}, u32[]{:S(2)}) %collective-permute-start.5) | collective-permute-done | bytes 262176 | tf_op jit(solution)/shard_map/ppermute | solution.py:21
  46.2 0.1 add_convert_fusion.1
  46.3 0.3 fusion.3
  46.6 0.3 multiply_reduce_fusion.1
  46.9 0.2 copy.15
  47.2 0.2 multiply_reduce_fusion
  47.4 0.9 fusion.8
  48.3 0.3 convolution_bitcast_fusion
  48.6 1.5 %collective-permute-start.9 = (f32[4,128,128]{2,1,0:T(8,128)S(1)}, f32[4,128,128]{2,1,0:T(8,128)S(1)}, u32[]{:S(2)}, u32[]{:S(2)}) collective-permute-start(f32[4,128,128]{2,1,0:T(8,128)S(1)} %get-tuple-element.34), channel_id=1, source_target_pairs={{0,1},{1,0},{2,3},{3,2},{4,5},{5,4},{6,7},{7,6},{8,9},{9,8},{10,11... | collective-permute-start | bytes 786440 | tf_op jit(solution)/shard_map/ppermute | solution.py:21
  50.1 0.5 collective-permute-start.8
  50.6 10.0 %collective-permute-done.9 = f32[4,128,128]{2,1,0:T(8,128)S(1)} collective-permute-done((f32[4,128,128]{2,1,0:T(8,128)S(1)}, f32[4,128,128]{2,1,0:T(8,128)S(1)}, u32[]{:S(2)}, u32[]{:S(2)}) %collective-permute-start.9) | collective-permute-done | bytes 262176 | tf_op jit(solution)/shard_map/ppermute | solution.py:21
  60.6 3.7 %collective-permute-done.8 = f32[4,128,128]{2,1,0:T(8,128)S(1)} collective-permute-done((f32[4,128,128]{2,1,0:T(8,128)S(1)}, f32[4,128,128]{2,1,0:T(8,128)S(1)}, u32[]{:S(2)}, u32[]{:S(2)}) %collective-permute-start.8) | collective-permute-done | bytes 262176 | tf_op jit(solution)/shard_map/ppermute | solution.py:21
  64.3 0.4 collective-permute-start.13
  64.7 0.3 fusion.7
  65.0 0.3 convolution_bitcast_fusion.2
  65.3 0.9 collective-permute-done.10
  66.3 1.5 %collective-permute-start.11 = (f32[4,128,128]{2,1,0:T(8,128)S(1)}, f32[4,128,128]{2,1,0:T(8,128)S(1)}, u32[]{:S(2)}, u32[]{:S(2)}) collective-permute-start(f32[4,128,128]{2,1,0:T(8,128)S(1)} %add.104), channel_id=1, source_target_pairs={{0,8},{4,12},{8,0},{12,4},{1,9},{5,13},{9,1},{13,5},{2,10},{6,14},... | collective-permute-start | bytes 786440 | tf_op jit(solution)/shard_map/ppermute | solution.py:21
  67.8 7.7 %collective-permute-done.13 = f32[4,128,128]{2,1,0:T(8,128)S(1)} collective-permute-done((f32[4,128,128]{2,1,0:T(8,128)S(1)}, f32[4,128,128]{2,1,0:T(8,128)S(1)}, u32[]{:S(2)}, u32[]{:S(2)}) %collective-permute-start.13) | collective-permute-done | bytes 262176 | tf_op jit(solution)/shard_map/ppermute | solution.py:21
  75.5 0.1 collective-permute-start.14
  75.6 1.1 %fusion.18.local_k = f32[8,128,128]{2,1,0:T(8,128)} fusion(bf16[8,128,128]{2,1,0:T(8,128)(2,1)S(1)} %fusion.7, bf16[128,1024]{1,0:T(8,128)(2,1)S(1)} %copy-done), kind=kOutput, calls=%fused_computation.31 | convolution fusion | flops 33554432 | bytes 1048576 | tf_op jit(solution)/shard_map/hts,thi->hsi/dot_general | solution.py:159
  76.7 1.1 %fusion.10.local_v = f32[8,128,128]{2,1,0:T(8,128)} fusion(bf16[8,128,128]{2,1,0:T(8,128)(2,1)S(1)} %fusion.5, bf16[16,8,8,128]{3,2,1,0:T(8,128)(2,1)S(1)} %get-tuple-element.30), kind=kOutput, calls=%fused_computation.23 | convolution fusion | flops 33554432 | bytes 1048576 | tf_op jit(solution)/shard_map/hts,thj->hsj/dot_general | solution.py:160
  77.7 0.7 add.111
  78.5 1.4 %collective-permute-start.15 = (f32[4,128,128]{2,1,0:T(8,128)}, f32[4,128,128]{2,1,0:T(8,128)S(1)}, u32[]{:S(2)}, u32[]{:S(2)}) collective-permute-start(f32[4,128,128]{2,1,0:T(8,128)} %add.111), channel_id=1, source_target_pairs={{0,8},{4,12},{8,0},{12,4},{1,9},{5,13},{9,1},{13,5},{2,10},{6,14},... | collective-permute-start | bytes 786440 | tf_op jit(solution)/shard_map/ppermute | solution.py:21
  79.9 0.8 add_select_fusion
  80.7 0.3 fusion.6
  81.0 0.9 copy.27
  81.8 5.5 %collective-permute-done.15 = f32[4,128,128]{2,1,0:T(8,128)S(1)} collective-permute-done((f32[4,128,128]{2,1,0:T(8,128)}, f32[4,128,128]{2,1,0:T(8,128)S(1)}, u32[]{:S(2)}, u32[]{:S(2)}) %collective-permute-start.15) | collective-permute-done | bytes 262176 | tf_op jit(solution)/shard_map/ppermute | solution.py:21
  87.4 0.8 select_add_fusion.upper_later
  88.2 1.0 %collective-permute-done.12.lower_got = f32[4,128,128]{2,1,0:T(8,128)S(1)} collective-permute-done((f32[4,128,128]{2,1,0:T(8,128)S(1)}, f32[4,128,128]{2,1,0:T(8,128)S(1)}, u32[]{:S(2)}, u32[]{:S(2)}) %collective-permute-start.12) | collective-permute-done | bytes 262176 | tf_op jit(solution)/shard_map/ppermute | solution.py:21
  89.1 0.7 copy-done.3
  89.8 2.7 %shard_map.75 = (bf16[128,1024]{1,0:T(8,128)(2,1)}, bf16[128,1024]{1,0:T(8,128)(2,1)}) custom-call(f32[4,128,128]{2,1,0:T(8,128)} %get-tuple-element.27.lower_known, f32[4,128,128]{2,1,0:T(8,128)} %copy-done.3, f32[4,128,128]{2,1,0:T(8,128)} %select_add_fusion.upper_later, f32[8,128,128]{2,1,0:T(8,128)} %fusion.18.local_k, f32[8,128,128]{2,1,0:T(8,128)} %fusion.10.local_v, ...), custom_call_target="tpu_custom_call" | custom-call | flops 67108864 | bytes 6291456 | tf_op jit(solution)/shard_map/pallas_call | solution.py:110
  (27 shorter events, 0.6 us)
Async XLA Ops:
  0.6 38.7 %copy-start = (bf16[128,1024]{1,0:T(8,128)(2,1)S(1)}, bf16[128,1024]{1,0:T(8,128)(2,1)}, u32[]{:S(2)}) copy-start(bf16[128,1024]{1,0:T(8,128)(2,1)} %param.4) | copy-start | bytes 786436
  0.6 1.2 %copy-start.1 = (bf16[128,1024]{1,0:T(8,128)(2,1)S(1)}, bf16[128,1024]{1,0:T(8,128)(2,1)}, u32[]{:S(2)}) copy-start(bf16[128,1024]{1,0:T(8,128)(2,1)} %value.1) | copy-start | bytes 786436
  2.1 14.9 %collective-permute-start = (f32[4,128,128]{2,1,0:T(8,128)S(1)}, f32[4,128,128]{2,1,0:T(8,128)S(1)}, u32[]{:S(2)}, u32[]{:S(2)}) collective-permute-start(f32[4,128,128]{2,1,0:T(8,128)S(1)} %get-tuple-element.38), channel_id=1, source_target_pairs={{0,1},{1,0},{2,3},{3,2},{4,5},{5,4},{6,7},{7,6},{8,9},{9,8},{10,11... | collective-permute-start | bytes 786440 | tf_op jit(solution)/shard_map/ppermute | solution.py:21
  5.2 14.3 %collective-permute-start.1 = (f32[4,128,128]{2,1,0:T(8,128)S(1)}, f32[4,128,128]{2,1,0:T(8,128)S(1)}, u32[]{:S(2)}, u32[]{:S(2)}) collective-permute-start(f32[4,128,128]{2,1,0:T(8,128)S(1)} %get-tuple-element.39), channel_id=1, source_target_pairs={{0,2},{1,3},{2,0},{3,1},{4,6},{5,7},{6,4},{7,5},{8,10},{9,11},{10,... | collective-permute-start | bytes 786440 | tf_op jit(solution)/shard_map/ppermute | solution.py:21
  7.8 11.9 %copy-start.2 = (bf16[128,1024]{1,0:T(8,128)(2,1)S(1)}, bf16[128,1024]{1,0:T(8,128)(2,1)}, u32[]{:S(2)}) copy-start(bf16[128,1024]{1,0:T(8,128)(2,1)} %param.7) | copy-start | bytes 786436
  19.7 1.6 %collective-permute-start.2 = (f32[4,128,128]{2,1,0:T(8,128)S(1)}, f32[4,128,128]{2,1,0:T(8,128)S(1)}, u32[]{:S(2)}, u32[]{:S(2)}) collective-permute-start(f32[4,128,128]{2,1,0:T(8,128)S(1)} %get-tuple-element.13), channel_id=1, source_target_pairs={{0,4},{4,0},{8,12},{12,8},{1,5},{5,1},{9,13},{13,9},{2,6},{6,2},{1... | collective-permute-start | bytes 786440 | tf_op jit(solution)/shard_map/ppermute | solution.py:21
  21.3 14.8 %collective-permute-start.3 = (f32[4,128,128]{2,1,0:T(8,128)S(1)}, f32[4,128,128]{2,1,0:T(8,128)S(1)}, u32[]{:S(2)}, u32[]{:S(2)}) collective-permute-start(f32[4,128,128]{2,1,0:T(8,128)S(1)} %get-tuple-element.15), channel_id=1, source_target_pairs={{0,2},{1,3},{2,0},{3,1},{4,6},{5,7},{6,4},{7,5},{8,10},{9,11},{10,... | collective-permute-start | bytes 786440 | tf_op jit(solution)/shard_map/ppermute | solution.py:21
  21.7 14.6 %collective-permute-start.6 = (f32[4,128,128]{2,1,0:T(8,128)S(1)}, f32[4,128,128]{2,1,0:T(8,128)}, u32[]{:S(2)}, u32[]{:S(2)}) collective-permute-start(f32[4,128,128]{2,1,0:T(8,128)S(1)} %add.88), channel_id=1, source_target_pairs={{0,8},{4,12},{8,0},{12,4},{1,9},{5,13},{9,1},{13,5},{2,10},{6,14},... | collective-permute-start | bytes 786440 | tf_op jit(solution)/shard_map/ppermute | solution.py:21
  36.1 1.6 %collective-permute-start.4 = (f32[4,128,128]{2,1,0:T(8,128)S(1)}, f32[4,128,128]{2,1,0:T(8,128)S(1)}, u32[]{:S(2)}, u32[]{:S(2)}) collective-permute-start(f32[4,128,128]{2,1,0:T(8,128)S(1)} %add.90), channel_id=1, source_target_pairs={{0,4},{4,0},{8,12},{12,8},{1,5},{5,1},{9,13},{13,9},{2,6},{6,2},{1... | collective-permute-start | bytes 786440 | tf_op jit(solution)/shard_map/ppermute | solution.py:21
  36.3 8.8 %collective-permute-start.7 = (f32[4,128,128]{2,1,0:T(8,128)S(1)}, f32[4,128,128]{2,1,0:T(8,128)S(1)}, u32[]{:S(2)}, u32[]{:S(2)}) collective-permute-start(f32[4,128,128]{2,1,0:T(8,128)S(1)} %get-tuple-element.28), channel_id=1, source_target_pairs={{0,1},{1,0},{2,3},{3,2},{4,5},{5,4},{6,7},{7,6},{8,9},{9,8},{10,11... | collective-permute-start | bytes 786440 | tf_op jit(solution)/shard_map/ppermute | solution.py:21
  37.8 8.4 %collective-permute-start.5 = (f32[4,128,128]{2,1,0:T(8,128)S(1)}, f32[4,128,128]{2,1,0:T(8,128)S(1)}, u32[]{:S(2)}, u32[]{:S(2)}) collective-permute-start(f32[4,128,128]{2,1,0:T(8,128)S(1)} %add.92), channel_id=1, source_target_pairs={{0,8},{4,12},{8,0},{12,4},{1,9},{5,13},{9,1},{13,5},{2,10},{6,14},... | collective-permute-start | bytes 786440 | tf_op jit(solution)/shard_map/ppermute | solution.py:21
  48.6 12.0 %collective-permute-start.9 = (f32[4,128,128]{2,1,0:T(8,128)S(1)}, f32[4,128,128]{2,1,0:T(8,128)S(1)}, u32[]{:S(2)}, u32[]{:S(2)}) collective-permute-start(f32[4,128,128]{2,1,0:T(8,128)S(1)} %get-tuple-element.34), channel_id=1, source_target_pairs={{0,1},{1,0},{2,3},{3,2},{4,5},{5,4},{6,7},{7,6},{8,9},{9,8},{10,11... | collective-permute-start | bytes 786440 | tf_op jit(solution)/shard_map/ppermute | solution.py:21
  50.1 14.1 %collective-permute-start.8 = (f32[4,128,128]{2,1,0:T(8,128)S(1)}, f32[4,128,128]{2,1,0:T(8,128)S(1)}, u32[]{:S(2)}, u32[]{:S(2)}) collective-permute-start(f32[4,128,128]{2,1,0:T(8,128)S(1)} %get-tuple-element.35), channel_id=1, source_target_pairs={{0,2},{1,3},{2,0},{3,1},{4,6},{5,7},{6,4},{7,5},{8,10},{9,11},{10,... | collective-permute-start | bytes 786440 | tf_op jit(solution)/shard_map/ppermute | solution.py:21
  64.3 11.2 %collective-permute-start.13 = (f32[4,128,128]{2,1,0:T(8,128)S(1)}, f32[4,128,128]{2,1,0:T(8,128)S(1)}, u32[]{:S(2)}, u32[]{:S(2)}) collective-permute-start(f32[4,128,128]{2,1,0:T(8,128)S(1)} %get-tuple-element.32), channel_id=1, source_target_pairs={{0,2},{1,3},{2,0},{3,1},{4,6},{5,7},{6,4},{7,5},{8,10},{9,11},{10,... | collective-permute-start | bytes 786440 | tf_op jit(solution)/shard_map/ppermute | solution.py:21
  64.7 1.5 %collective-permute-start.10 = (f32[4,128,128]{2,1,0:T(8,128)S(1)}, f32[4,128,128]{2,1,0:T(8,128)S(1)}, u32[]{:S(2)}, u32[]{:S(2)}) collective-permute-start(f32[4,128,128]{2,1,0:T(8,128)S(1)} %get-tuple-element.18), channel_id=1, source_target_pairs={{0,4},{4,0},{8,12},{12,8},{1,5},{5,1},{9,13},{13,9},{2,6},{6,2},{1... | collective-permute-start | bytes 786440 | tf_op jit(solution)/shard_map/ppermute | solution.py:21
  66.3 13.7 %collective-permute-start.11 = (f32[4,128,128]{2,1,0:T(8,128)S(1)}, f32[4,128,128]{2,1,0:T(8,128)S(1)}, u32[]{:S(2)}, u32[]{:S(2)}) collective-permute-start(f32[4,128,128]{2,1,0:T(8,128)S(1)} %add.104), channel_id=1, source_target_pairs={{0,8},{4,12},{8,0},{12,4},{1,9},{5,13},{9,1},{13,5},{2,10},{6,14},... | collective-permute-start | bytes 786440 | tf_op jit(solution)/shard_map/ppermute | solution.py:21
  75.5 2.2 %collective-permute-start.14 = (f32[4,128,128]{2,1,0:T(8,128)S(1)}, f32[4,128,128]{2,1,0:T(8,128)S(1)}, u32[]{:S(2)}, u32[]{:S(2)}) collective-permute-start(f32[4,128,128]{2,1,0:T(8,128)S(1)} %add.109), channel_id=1, source_target_pairs={{0,4},{4,0},{8,12},{12,8},{1,5},{5,1},{9,13},{13,9},{2,6},{6,2},{1... | collective-permute-start | bytes 786440 | tf_op jit(solution)/shard_map/ppermute | solution.py:21
  78.5 8.9 %collective-permute-start.15 = (f32[4,128,128]{2,1,0:T(8,128)}, f32[4,128,128]{2,1,0:T(8,128)S(1)}, u32[]{:S(2)}, u32[]{:S(2)}) collective-permute-start(f32[4,128,128]{2,1,0:T(8,128)} %add.111), channel_id=1, source_target_pairs={{0,8},{4,12},{8,0},{12,4},{1,9},{5,13},{9,1},{13,5},{2,10},{6,14},... | collective-permute-start | bytes 786440 | tf_op jit(solution)/shard_map/ppermute | solution.py:21
  80.7 8.4 %collective-permute-start.12 = (f32[4,128,128]{2,1,0:T(8,128)S(1)}, f32[4,128,128]{2,1,0:T(8,128)S(1)}, u32[]{:S(2)}, u32[]{:S(2)}) collective-permute-start(f32[4,128,128]{2,1,0:T(8,128)S(1)} %get-tuple-element.26), channel_id=1, source_target_pairs={{0,1},{1,0},{2,3},{3,2},{4,5},{5,4},{6,7},{7,6},{8,9},{9,8},{10,11... | collective-permute-start | bytes 786440 | tf_op jit(solution)/shard_map/ppermute | solution.py:21
  89.1 0.7 copy-start.3

commit v17 on v12

--- a/solution.py
+++ b/solution.py
@@ -47,7 +47,7 @@
     return added(earlier, value)
 
 
-def chunked_scan(value, backward):
+def chunked_scan(value, backward, passenger=None):
     half = value.shape[0] // 2
     group_a, group_b = value[:half], value[half:]
     if backward:
@@ -56,13 +56,15 @@
     if not inner_bits:
         result = scan_inner_first(value, backward)
         if backward:
-            return result[:half], jnp.zeros_like(result[:half]), result[half:]
+            return result[:half], jnp.zeros_like(result[:half]), result[half:], passenger
         return result
     earlier_a, total_a = subcube_step([], group_a, "inner", inner_bits[0], backward)
     earlier_b, total_b = [], group_b
     for bit in inner_bits[1:]:
         earlier_b, total_b = subcube_step(earlier_b, total_b, "inner", bit, backward)
-    (earlier_b, total_b), _ = lax.optimization_barrier(((earlier_b, total_b), total_a))
+    (earlier_b, total_b), _, passenger = lax.optimization_barrier(
+        ((earlier_b, total_b), total_a, passenger)
+    )
     rows_before, rows_total = [], total_b
     for index, bit in enumerate(outer_bits):
         rows_before, rows_total = subcube_step(rows_before, rows_total, "outer", bit, backward)
@@ -79,7 +81,7 @@
     earlier_a = added(earlier_a, group_a)
     got_b = swap(sent, "inner", low)
     if backward:
-        return known, got_b, earlier_a
+        return known, got_b, earlier_a, passenger
     return jnp.concatenate([earlier_a, known + got_b], axis=0)
 
 
@@ -154,9 +156,9 @@
         + jnp.einsum("thj,hij->thi", grad_half, prior_half, preferred_element_type=jnp.float32)
     )
     grad_state = jnp.einsum("thi,thj->hij", queries, grad_half, preferred_element_type=jnp.float32)
-    lower_known, lower_got, upper_later = chunked_scan(grad_state, True)
     local_k = jnp.einsum("hts,thi->hsi", dscore_half, queries, preferred_element_type=jnp.float32)
     local_v = jnp.einsum("hts,thj->hsj", score_half, grad_half, preferred_element_type=jnp.float32)
+    lower_known, lower_got, upper_later, local_k = chunked_scan(grad_state, True, local_k)
     grad_k, grad_v = tail(lower_known, lower_got, upper_later, local_k, local_v, value, key)
     width = HEADS * HEAD
     return (

time: 91.9 us -> 94.7 us (1.030)
  waiting for transfers between devices: 62.1 us -> 63.8 us
    ppermute x16, waiting for transfers between devices: 62.1 us -> 63.8 us  [swap(): return lax.ppermute(value, axis, [(i, i ^ bit) for i in range(count)])]
    unnamed x9 -> x13, local copies, waits for them, and re-layouts: 2.29 us -> 2.32 us
  transfers between devices with their start and end apart: 16 -> 16, of which waited for: 13 -> 14; matrix products, arithmetic and copies ran while one was open for 6% -> 7% of each run, Pallas kernels for 0% -> 0%
where the time goes in v17:
time: 94.7 us; the launch traced here: 94.5 us
  waiting for transfers between devices  63.8 us (67%)
  starting transfers between devices  15 us (16%)
  matrix products  4.43 us (5%)
  other arithmetic  3.88 us (4%)
  local copies, waits for them, and re-layouts  3.76 us (4%)
  Pallas kernels  2.73 us (3%)
    ppermute x16, waiting for transfers between devices, swap(): return lax.ppermute(value, axis, [(i, i ^ bit) for i in range(count)])  63.8 us
    ppermute x16, starting transfers between devices, swap(): return lax.ppermute(value, axis, [(i, i ^ bit) for i in range(count)])  15 us
    pallas_call x1, Pallas kernels, tail(): pl.pallas_call(functools.partial(tail_kernel, HEAD ** (-0.5)), out_shape=...  2.73 us
    unnamed x13, local copies, waits for them, and re-layouts  2.32 us
  transfers between devices with their start and end apart: 16, of which 14 were waited for; matrix products, arithmetic and copies ran while one was open for 7% of the time, Pallas kernels for 0%

profile of v17, /device:TPU:0, one launch (start us, length us, event | category | flops | bytes accessed | tf_op | source)
XLA Modules:
  0.0 94.5 jit_solution(8286460740205949060)
XLA Ops:
  0.7 1.2 %copy.32 = bf16[128,1024]{0,1:T(8,128)(2,1)S(1)} copy(bf16[128,1024]{1,0:T(8,128)(2,1)} %key.1) | data formatting | bytes 524288 | tf_op jit(solution)/shard_map/reshape | solution.py:125
  1.8 0.2 fusion.19
  2.1 3.1 %collective-permute-start = (f32[4,128,128]{2,1,0:T(8,128)S(1)}, f32[4,128,128]{2,1,0:T(8,128)S(1)}, u32[]{:S(2)}, u32[]{:S(2)}) collective-permute-start(f32[4,128,128]{2,1,0:T(8,128)S(1)} %get-tuple-element.38), channel_id=1, source_target_pairs={{0,1},{1,0},{2,3},{3,2},{4,5},{5,4},{6,7},{7,6},{8,9},{9,8},{10,11... | collective-permute-start | bytes 786440 | tf_op jit(solution)/shard_map/ppermute | solution.py:21
  5.2 2.6 %collective-permute-start.1 = (f32[4,128,128]{2,1,0:T(8,128)S(1)}, f32[4,128,128]{2,1,0:T(8,128)S(1)}, u32[]{:S(2)}, u32[]{:S(2)}) collective-permute-start(f32[4,128,128]{2,1,0:T(8,128)S(1)} %get-tuple-element.39), channel_id=1, source_target_pairs={{0,2},{1,3},{2,0},{3,1},{4,6},{5,7},{6,4},{7,5},{8,10},{9,11},{10,... | collective-permute-start | bytes 786440 | tf_op jit(solution)/shard_map/ppermute | solution.py:21
  7.8 9.2 %collective-permute-done = f32[4,128,128]{2,1,0:T(8,128)S(1)} collective-permute-done((f32[4,128,128]{2,1,0:T(8,128)S(1)}, f32[4,128,128]{2,1,0:T(8,128)S(1)}, u32[]{:S(2)}, u32[]{:S(2)}) %collective-permute-start) | collective-permute-done | bytes 262176 | tf_op jit(solution)/shard_map/ppermute | solution.py:21
  17.0 2.5 %collective-permute-done.1 = f32[4,128,128]{2,1,0:T(8,128)S(1)} collective-permute-done((f32[4,128,128]{2,1,0:T(8,128)S(1)}, f32[4,128,128]{2,1,0:T(8,128)S(1)}, u32[]{:S(2)}, u32[]{:S(2)}) %collective-permute-start.1) | collective-permute-done | bytes 262176 | tf_op jit(solution)/shard_map/ppermute | solution.py:21
  19.6 0.1 slice_add_fusion.1
  19.7 1.5 %collective-permute-done.2 = f32[4,128,128]{2,1,0:T(8,128)S(1)} collective-permute-done((f32[4,128,128]{2,1,0:T(8,128)S(1)}, f32[4,128,128]{2,1,0:T(8,128)S(1)}, u32[]{:S(2)}, u32[]{:S(2)}) %collective-permute-start.2) | collective-permute-done | bytes 262176 | tf_op jit(solution)/shard_map/ppermute | solution.py:21
  21.3 0.4 collective-permute-start.3
  21.7 1.5 %collective-permute-start.6 = (f32[4,128,128]{2,1,0:T(8,128)S(1)}, f32[4,128,128]{2,1,0:T(8,128)S(1)}, u32[]{:S(2)}, u32[]{:S(2)}) collective-permute-start(f32[4,128,128]{2,1,0:T(8,128)S(1)} %add.88), channel_id=1, source_target_pairs={{0,8},{4,12},{8,0},{12,4},{1,9},{5,13},{9,1},{13,5},{2,10},{6,14},... | collective-permute-start | bytes 786440 | tf_op jit(solution)/shard_map/ppermute | solution.py:21
  23.2 12.9 %collective-permute-done.3 = f32[4,128,128]{2,1,0:T(8,128)S(1)} collective-permute-done((f32[4,128,128]{2,1,0:T(8,128)S(1)}, f32[4,128,128]{2,1,0:T(8,128)S(1)}, u32[]{:S(2)}, u32[]{:S(2)}) %collective-permute-start.3) | collective-permute-done | bytes 262176 | tf_op jit(solution)/shard_map/ppermute | solution.py:21
  36.1 0.1 collective-permute-start.4
  36.2 0.8 add_select_fusion.1
  37.0 0.7 collective-permute-done.4
  37.8 1.6 %collective-permute-start.5 = (f32[4,128,128]{2,1,0:T(8,128)S(1)}, f32[4,128,128]{2,1,0:T(8,128)S(1)}, u32[]{:S(2)}, u32[]{:S(2)}) collective-permute-start(f32[4,128,128]{2,1,0:T(8,128)S(1)} %add.92), channel_id=1, source_target_pairs={{0,8},{4,12},{8,0},{12,4},{1,9},{5,13},{9,1},{13,5},{2,10},{6,14},... | collective-permute-start | bytes 786440 | tf_op jit(solution)/shard_map/ppermute | solution.py:21
  39.3 0.2 fusion.5
  39.6 6.3 %collective-permute-done.7 = f32[4,128,128]{2,1,0:T(8,128)S(1)} collective-permute-done((f32[4,128,128]{2,1,0:T(8,128)}, f32[4,128,128]{2,1,0:T(8,128)S(1)}, u32[]{:S(2)}, u32[]{:S(2)}) %collective-permute-start.7) | collective-permute-done | bytes 262176 | tf_op jit(solution)/shard_map/ppermute | solution.py:21
  45.9 0.3 collective-permute-done.5
  46.3 0.3 fusion.3
  46.6 0.4 multiply_reduce_fusion
  47.0 0.2 copy.15
  47.2 0.7 copy-done.2
  47.9 0.2 fusion.8
  48.1 0.9 fusion.11
  49.0 0.3 convolution_bitcast_fusion
  49.4 1.4 %collective-permute-start.9 = (f32[4,128,128]{2,1,0:T(8,128)S(1)}, f32[4,128,128]{2,1,0:T(8,128)S(1)}, u32[]{:S(2)}, u32[]{:S(2)}) collective-permute-start(f32[4,128,128]{2,1,0:T(8,128)S(1)} %get-tuple-element.34), channel_id=1, source_target_pairs={{0,1},{1,0},{2,3},{3,2},{4,5},{5,4},{6,7},{7,6},{8,9},{9,8},{10,11... | collective-permute-start | bytes 786440 | tf_op jit(solution)/shard_map/ppermute | solution.py:21
  50.8 0.5 collective-permute-start.8
  51.3 0.3 fusion.7
  51.6 1.1 %fusion.21.local_k = f32[8,128,128]{2,1,0:T(8,128)} fusion(bf16[8,128,128]{2,1,0:T(8,128)(2,1)S(1)} %fusion.7, bf16[128,1024]{1,0:T(8,128)(2,1)S(1)} %copy-done), kind=kOutput, calls=%fused_computation.34 | convolution fusion | flops 33554432 | bytes 1048576 | tf_op jit(solution)/shard_map/hts,thi->hsi/dot_general | solution.py:159
  52.7 8.7 %collective-permute-done.9 = f32[4,128,128]{2,1,0:T(8,128)S(1)} collective-permute-done((f32[4,128,128]{2,1,0:T(8,128)S(1)}, f32[4,128,128]{2,1,0:T(8,128)S(1)}, u32[]{:S(2)}, u32[]{:S(2)}) %collective-permute-start.9) | collective-permute-done | bytes 262176 | tf_op jit(solution)/shard_map/ppermute | solution.py:21
  61.4 3.3 %collective-permute-done.8 = f32[4,128,128]{2,1,0:T(8,128)S(1)} collective-permute-done((f32[4,128,128]{2,1,0:T(8,128)S(1)}, f32[4,128,128]{2,1,0:T(8,128)S(1)}, u32[]{:S(2)}, u32[]{:S(2)}) %collective-permute-start.8) | collective-permute-done | bytes 262176 | tf_op jit(solution)/shard_map/ppermute | solution.py:21
  64.8 0.4 collective-permute-start.13
  65.2 1.1 %collective-permute-done.10 = f32[4,128,128]{2,1,0:T(8,128)S(1)} collective-permute-done((f32[4,128,128]{2,1,0:T(8,128)S(1)}, f32[4,128,128]{2,1,0:T(8,128)S(1)}, u32[]{:S(2)}, u32[]{:S(2)}) %collective-permute-start.10) | collective-permute-done | bytes 262176 | tf_op jit(solution)/shard_map/ppermute | solution.py:21
  66.3 1.6 %collective-permute-start.11 = (f32[4,128,128]{2,1,0:T(8,128)S(1)}, f32[4,128,128]{2,1,0:T(8,128)S(1)}, u32[]{:S(2)}, u32[]{:S(2)}) collective-permute-start(f32[4,128,128]{2,1,0:T(8,128)S(1)} %add.104), channel_id=1, source_target_pairs={{0,8},{4,12},{8,0},{12,4},{1,9},{5,13},{9,1},{13,5},{2,10},{6,14},... | collective-permute-start | bytes 786440 | tf_op jit(solution)/shard_map/ppermute | solution.py:21
  67.9 10.9 %collective-permute-done.13 = f32[4,128,128]{2,1,0:T(8,128)S(1)} collective-permute-done((f32[4,128,128]{2,1,0:T(8,128)S(1)}, f32[4,128,128]{2,1,0:T(8,128)S(1)}, u32[]{:S(2)}, u32[]{:S(2)}) %collective-permute-start.13) | collective-permute-done | bytes 262176 | tf_op jit(solution)/shard_map/ppermute | solution.py:21
  78.8 0.1 collective-permute-start.14
  78.9 0.3 convolution_bitcast_fusion.2
  79.2 1.1 %fusion.13.local_v = f32[8,128,128]{2,1,0:T(8,128)} fusion(bf16[8,128,128]{2,1,0:T(8,128)(2,1)S(1)} %fusion.5, bf16[16,8,8,128]{3,2,1,0:T(8,128)(2,1)S(1)} %get-tuple-element.30), kind=kOutput, calls=%fused_computation.26 | convolution fusion | flops 33554432 | bytes 1048576 | tf_op jit(solution)/shard_map/hts,thj->hsj/dot_general | solution.py:160
  80.3 0.1 collective-permute-done.14
  80.4 1.6 %collective-permute-start.15 = (f32[4,128,128]{2,1,0:T(8,128)S(1)}, f32[4,128,128]{2,1,0:T(8,128)S(1)}, u32[]{:S(2)}, u32[]{:S(2)}) collective-permute-start(f32[4,128,128]{2,1,0:T(8,128)S(1)} %add.111), channel_id=1, source_target_pairs={{0,8},{4,12},{8,0},{12,4},{1,9},{5,13},{9,1},{13,5},{2,10},{6,14},... | collective-permute-start | bytes 786440 | tf_op jit(solution)/shard_map/ppermute | solution.py:21
  82.0 0.8 add_select_fusion
  82.8 0.3 fusion.6
  83.1 0.9 copy.27
  83.9 5.2 %collective-permute-done.15 = f32[4,128,128]{2,1,0:T(8,128)S(1)} collective-permute-done((f32[4,128,128]{2,1,0:T(8,128)S(1)}, f32[4,128,128]{2,1,0:T(8,128)S(1)}, u32[]{:S(2)}, u32[]{:S(2)}) %collective-permute-start.15) | collective-permute-done | bytes 262176 | tf_op jit(solution)/shard_map/ppermute | solution.py:21
  89.1 0.8 select_add_fusion.upper_later
  89.9 1.2 %collective-permute-done.12.lower_got = f32[4,128,128]{2,1,0:T(8,128)S(1)} collective-permute-done((f32[4,128,128]{2,1,0:T(8,128)S(1)}, f32[4,128,128]{2,1,0:T(8,128)S(1)}, u32[]{:S(2)}, u32[]{:S(2)}) %collective-permute-start.12) | collective-permute-done | bytes 262176 | tf_op jit(solution)/shard_map/ppermute | solution.py:21
  91.1 0.7 copy-done.5
  91.7 2.7 %shard_map.75 = (bf16[128,1024]{1,0:T(8,128)(2,1)}, bf16[128,1024]{1,0:T(8,128)(2,1)}) custom-call(f32[4,128,128]{2,1,0:T(8,128)} %get-tuple-element.27.lower_known, f32[4,128,128]{2,1,0:T(8,128)} %copy-done.5, f32[4,128,128]{2,1,0:T(8,128)} %select_add_fusion.upper_later, f32[8,128,128]{2,1,0:T(8,128)} %fusion.21.local_k, f32[8,128,128]{2,1,0:T(8,128)} %fusion.13.local_v, ...), custom_call_target="tpu_custom_call" | custom-call | flops 67108864 | bytes 6291456 | tf_op jit(solution)/shard_map/pallas_call | solution.py:110
  (30 shorter events, 0.6 us)
Async XLA Ops:
  0.6 38.7 %copy-start = (bf16[128,1024]{1,0:T(8,128)(2,1)S(1)}, bf16[128,1024]{1,0:T(8,128)(2,1)}, u32[]{:S(2)}) copy-start(bf16[128,1024]{1,0:T(8,128)(2,1)} %param.4) | copy-start | bytes 786436
  0.6 1.2 %copy-start.1 = (bf16[128,1024]{1,0:T(8,128)(2,1)S(1)}, bf16[128,1024]{1,0:T(8,128)(2,1)}, u32[]{:S(2)}) copy-start(bf16[128,1024]{1,0:T(8,128)(2,1)} %value.1) | copy-start | bytes 786436
  2.1 14.9 %collective-permute-start = (f32[4,128,128]{2,1,0:T(8,128)S(1)}, f32[4,128,128]{2,1,0:T(8,128)S(1)}, u32[]{:S(2)}, u32[]{:S(2)}) collective-permute-start(f32[4,128,128]{2,1,0:T(8,128)S(1)} %get-tuple-element.38), channel_id=1, source_target_pairs={{0,1},{1,0},{2,3},{3,2},{4,5},{5,4},{6,7},{7,6},{8,9},{9,8},{10,11... | collective-permute-start | bytes 786440 | tf_op jit(solution)/shard_map/ppermute | solution.py:21
  5.2 14.3 %collective-permute-start.1 = (f32[4,128,128]{2,1,0:T(8,128)S(1)}, f32[4,128,128]{2,1,0:T(8,128)S(1)}, u32[]{:S(2)}, u32[]{:S(2)}) collective-permute-start(f32[4,128,128]{2,1,0:T(8,128)S(1)} %get-tuple-element.39), channel_id=1, source_target_pairs={{0,2},{1,3},{2,0},{3,1},{4,6},{5,7},{6,4},{7,5},{8,10},{9,11},{10,... | collective-permute-start | bytes 786440 | tf_op jit(solution)/shard_map/ppermute | solution.py:21
  19.7 1.6 %collective-permute-start.2 = (f32[4,128,128]{2,1,0:T(8,128)S(1)}, f32[4,128,128]{2,1,0:T(8,128)S(1)}, u32[]{:S(2)}, u32[]{:S(2)}) collective-permute-start(f32[4,128,128]{2,1,0:T(8,128)S(1)} %get-tuple-element.13), channel_id=1, source_target_pairs={{0,4},{4,0},{8,12},{12,8},{1,5},{5,1},{9,13},{13,9},{2,6},{6,2},{1... | collective-permute-start | bytes 786440 | tf_op jit(solution)/shard_map/ppermute | solution.py:21
  21.3 14.8 %collective-permute-start.3 = (f32[4,128,128]{2,1,0:T(8,128)S(1)}, f32[4,128,128]{2,1,0:T(8,128)S(1)}, u32[]{:S(2)}, u32[]{:S(2)}) collective-permute-start(f32[4,128,128]{2,1,0:T(8,128)S(1)} %get-tuple-element.15), channel_id=1, source_target_pairs={{0,2},{1,3},{2,0},{3,1},{4,6},{5,7},{6,4},{7,5},{8,10},{9,11},{10,... | collective-permute-start | bytes 786440 | tf_op jit(solution)/shard_map/ppermute | solution.py:21
  21.7 14.6 %collective-permute-start.6 = (f32[4,128,128]{2,1,0:T(8,128)S(1)}, f32[4,128,128]{2,1,0:T(8,128)S(1)}, u32[]{:S(2)}, u32[]{:S(2)}) collective-permute-start(f32[4,128,128]{2,1,0:T(8,128)S(1)} %add.88), channel_id=1, source_target_pairs={{0,8},{4,12},{8,0},{12,4},{1,9},{5,13},{9,1},{13,5},{2,10},{6,14},... | collective-permute-start | bytes 786440 | tf_op jit(solution)/shard_map/ppermute | solution.py:21
  36.1 1.6 %collective-permute-start.4 = (f32[4,128,128]{2,1,0:T(8,128)S(1)}, f32[4,128,128]{2,1,0:T(8,128)S(1)}, u32[]{:S(2)}, u32[]{:S(2)}) collective-permute-start(f32[4,128,128]{2,1,0:T(8,128)S(1)} %add.90), channel_id=1, source_target_pairs={{0,4},{4,0},{8,12},{12,8},{1,5},{5,1},{9,13},{13,9},{2,6},{6,2},{1... | collective-permute-start | bytes 786440 | tf_op jit(solution)/shard_map/ppermute | solution.py:21
  37.0 8.9 %collective-permute-start.7 = (f32[4,128,128]{2,1,0:T(8,128)}, f32[4,128,128]{2,1,0:T(8,128)S(1)}, u32[]{:S(2)}, u32[]{:S(2)}) collective-permute-start(f32[4,128,128]{2,1,0:T(8,128)} %get-tuple-element.28), channel_id=1, source_target_pairs={{0,1},{1,0},{2,3},{3,2},{4,5},{5,4},{6,7},{7,6},{8,9},{9,8},{10,11... | collective-permute-start | bytes 786440 | tf_op jit(solution)/shard_map/ppermute | solution.py:21
  37.8 8.4 %collective-permute-start.5 = (f32[4,128,128]{2,1,0:T(8,128)S(1)}, f32[4,128,128]{2,1,0:T(8,128)S(1)}, u32[]{:S(2)}, u32[]{:S(2)}) collective-permute-start(f32[4,128,128]{2,1,0:T(8,128)S(1)} %add.92), channel_id=1, source_target_pairs={{0,8},{4,12},{8,0},{12,4},{1,9},{5,13},{9,1},{13,5},{2,10},{6,14},... | collective-permute-start | bytes 786440 | tf_op jit(solution)/shard_map/ppermute | solution.py:21
  47.0 1.0 %copy-start.2 = (bf16[128,1024]{1,0:T(8,128)(2,1)S(1)}, bf16[128,1024]{1,0:T(8,128)(2,1)}, u32[]{:S(2)}) copy-start(bf16[128,1024]{1,0:T(8,128)(2,1)} %param.7) | copy-start | bytes 786436
  49.4 12.0 %collective-permute-start.9 = (f32[4,128,128]{2,1,0:T(8,128)S(1)}, f32[4,128,128]{2,1,0:T(8,128)S(1)}, u32[]{:S(2)}, u32[]{:S(2)}) collective-permute-start(f32[4,128,128]{2,1,0:T(8,128)S(1)} %get-tuple-element.34), channel_id=1, source_target_pairs={{0,1},{1,0},{2,3},{3,2},{4,5},{5,4},{6,7},{7,6},{8,9},{9,8},{10,11... | collective-permute-start | bytes 786440 | tf_op jit(solution)/shard_map/ppermute | solution.py:21
  50.8 13.8 %collective-permute-start.8 = (f32[4,128,128]{2,1,0:T(8,128)S(1)}, f32[4,128,128]{2,1,0:T(8,128)S(1)}, u32[]{:S(2)}, u32[]{:S(2)}) collective-permute-start(f32[4,128,128]{2,1,0:T(8,128)S(1)} %get-tuple-element.35), channel_id=1, source_target_pairs={{0,2},{1,3},{2,0},{3,1},{4,6},{5,7},{6,4},{7,5},{8,10},{9,11},{10,... | collective-permute-start | bytes 786440 | tf_op jit(solution)/shard_map/ppermute | solution.py:21
  51.6 1.1 %copy-start.3 = (bf16[8,128,128]{2,1,0:T(8,128)(2,1)}, bf16[8,128,128]{2,1,0:T(8,128)(2,1)S(1)}, u32[]{:S(2)}) copy-start(bf16[8,128,128]{2,1,0:T(8,128)(2,1)S(1)} %fusion.7) | copy-start | bytes 786436
  64.7 1.6 %collective-permute-start.10 = (f32[4,128,128]{2,1,0:T(8,128)S(1)}, f32[4,128,128]{2,1,0:T(8,128)S(1)}, u32[]{:S(2)}, u32[]{:S(2)}) collective-permute-start(f32[4,128,128]{2,1,0:T(8,128)S(1)} %get-tuple-element.17), channel_id=1, source_target_pairs={{0,4},{4,0},{8,12},{12,8},{1,5},{5,1},{9,13},{13,9},{2,6},{6,2},{1... | collective-permute-start | bytes 786440 | tf_op jit(solution)/shard_map/ppermute | solution.py:21
  64.8 14.0 %collective-permute-start.13 = (f32[4,128,128]{2,1,0:T(8,128)S(1)}, f32[4,128,128]{2,1,0:T(8,128)S(1)}, u32[]{:S(2)}, u32[]{:S(2)}) collective-permute-start(f32[4,128,128]{2,1,0:T(8,128)S(1)} %get-tuple-element.32), channel_id=1, source_target_pairs={{0,2},{1,3},{2,0},{3,1},{4,6},{5,7},{6,4},{7,5},{8,10},{9,11},{10,... | collective-permute-start | bytes 786440 | tf_op jit(solution)/shard_map/ppermute | solution.py:21
  66.3 12.6 %copy-start.4 = (bf16[8,128,128]{2,1,0:T(8,128)(2,1)S(1)}, bf16[8,128,128]{2,1,0:T(8,128)(2,1)}, u32[]{:S(2)}) copy-start(bf16[8,128,128]{2,1,0:T(8,128)(2,1)} %copy-done.3) | copy-start | bytes 786436
  66.3 15.7 %collective-permute-start.11 = (f32[4,128,128]{2,1,0:T(8,128)S(1)}, f32[4,128,128]{2,1,0:T(8,128)S(1)}, u32[]{:S(2)}, u32[]{:S(2)}) collective-permute-start(f32[4,128,128]{2,1,0:T(8,128)S(1)} %add.104), channel_id=1, source_target_pairs={{0,8},{4,12},{8,0},{12,4},{1,9},{5,13},{9,1},{13,5},{2,10},{6,14},... | collective-permute-start | bytes 786440 | tf_op jit(solution)/shard_map/ppermute | solution.py:21
  78.8 1.6 %collective-permute-start.14 = (f32[4,128,128]{2,1,0:T(8,128)S(1)}, f32[4,128,128]{2,1,0:T(8,128)S(1)}, u32[]{:S(2)}, u32[]{:S(2)}) collective-permute-start(f32[4,128,128]{2,1,0:T(8,128)S(1)} %add.109), channel_id=1, source_target_pairs={{0,4},{4,0},{8,12},{12,8},{1,5},{5,1},{9,13},{13,9},{2,6},{6,2},{1... | collective-permute-start | bytes 786440 | tf_op jit(solution)/shard_map/ppermute | solution.py:21
  80.4 8.6 %collective-permute-start.15 = (f32[4,128,128]{2,1,0:T(8,128)S(1)}, f32[4,128,128]{2,1,0:T(8,128)S(1)}, u32[]{:S(2)}, u32[]{:S(2)}) collective-permute-start(f32[4,128,128]{2,1,0:T(8,128)S(1)} %add.111), channel_id=1, source_target_pairs={{0,8},{4,12},{8,0},{12,4},{1,9},{5,13},{9,1},{13,5},{2,10},{6,14},... | collective-permute-start | bytes 786440 | tf_op jit(solution)/shard_map/ppermute | solution.py:21
  82.8 8.3 %collective-permute-start.12 = (f32[4,128,128]{2,1,0:T(8,128)S(1)}, f32[4,128,128]{2,1,0:T(8,128)S(1)}, u32[]{:S(2)}, u32[]{:S(2)}) collective-permute-start(f32[4,128,128]{2,1,0:T(8,128)S(1)} %get-tuple-element.26), channel_id=1, source_target_pairs={{0,1},{1,0},{2,3},{3,2},{4,5},{5,4},{6,7},{7,6},{8,9},{9,8},{10,11... | collective-permute-start | bytes 786440 | tf_op jit(solution)/shard_map/ppermute | solution.py:21
  91.1 0.7 copy-start.5

commit v18 on v12

--- a/solution.py
+++ b/solution.py
@@ -84,7 +84,7 @@
 
 
 def tail_kernel(
-    scaling, lower_known, lower_got, upper_later, local_k, local_v, value, key, out_k, out_v
+    scaling, lower_known, lower_got, upper_later, dscore, score, query, grad, value, key, out_k, out_v
 ):
     half = HEADS // 2
     for h in range(HEADS):
@@ -94,26 +94,32 @@
         from_later_k = lax.dot_general(
             value[:, cols], later_half, (((1,), (1,)), ((), ())), preferred_element_type=jnp.float32
         )
-        out_k[:, cols] = (scaling * (local_k[h] + from_later_k)).astype(out_k.dtype)
+        local_k = lax.dot_general(
+            dscore[h], query[:, cols], (((0,), (0,)), ((), ())), preferred_element_type=jnp.float32
+        )
+        out_k[:, cols] = (scaling * (local_k + from_later_k)).astype(out_k.dtype)
         from_later_v = lax.dot_general(
             key[:, cols], later_half, (((1,), (0,)), ((), ())), preferred_element_type=jnp.float32
         )
-        out_v[:, cols] = (local_v[h] + scaling * from_later_v).astype(out_v.dtype)
+        local_v = lax.dot_general(
+            score[h], grad[:, cols], (((0,), (0,)), ((), ())), preferred_element_type=jnp.float32
+        )
+        out_v[:, cols] = (local_v + scaling * from_later_v).astype(out_v.dtype)
 
 
-def tail(lower_known, lower_got, upper_later, local_k, local_v, value, key):
+def tail(lower_known, lower_got, upper_later, dscore, score, query, grad, value, key):
     rows = value.shape[0]
     vmem = pl.BlockSpec(memory_space=pltpu.VMEM)
     out = jax.ShapeDtypeStruct((rows, HEADS * HEAD), jnp.bfloat16)
     return pl.pallas_call(
         functools.partial(tail_kernel, HEAD ** (-0.5)),
         out_shape=(out, out),
-        in_specs=[vmem] * 7,
+        in_specs=[vmem] * 9,
         out_specs=(vmem, vmem),
         cost_estimate=pl.CostEstimate(
-            flops=4 * HEADS * rows * HEAD * HEAD, transcendentals=0, bytes_accessed=12 * rows * 1024 * 4
+            flops=8 * HEADS * rows * HEAD * HEAD, transcendentals=0, bytes_accessed=12 * rows * 1024 * 4
         ),
-    )(lower_known, lower_got, upper_later, local_k, local_v, value, key)
+    )(lower_known, lower_got, upper_later, dscore, score, query, grad, value, key)
 
 
 def per_device(query, key, value, grad_out):
@@ -155,9 +161,17 @@
     )
     grad_state = jnp.einsum("thi,thj->hij", queries, grad_half, preferred_element_type=jnp.float32)
     lower_known, lower_got, upper_later = chunked_scan(grad_state, True)
-    local_k = jnp.einsum("hts,thi->hsi", dscore_half, queries, preferred_element_type=jnp.float32)
-    local_v = jnp.einsum("hts,thj->hsj", score_half, grad_half, preferred_element_type=jnp.float32)
-    grad_k, grad_v = tail(lower_known, lower_got, upper_later, local_k, local_v, value, key)
+    grad_k, grad_v = tail(
+        lower_known,
+        lower_got,
+        upper_later,
+        dscore_half,
+        score_half,
+        query,
+        grad_half.reshape(rows_dev, HEADS * HEAD),
+        value,
+        key,
+    )
     width = HEADS * HEAD
     return (
         normed.astype(jnp.bfloat16),

time: 91.9 us -> 95.7 us (1.041)
  waiting for transfers between devices: 62.1 us -> 65.7 us
  matrix products: 4.42 us -> 2.29 us
  local copies, waits for them, and re-layouts: 3.73 us -> 4.84 us
    ppermute x16, waiting for transfers between devices: 62.1 us -> 65.7 us  [swap(): return lax.ppermute(value, axis, [(i, i ^ bit) for i in range(count)])]
    dot_general x2 -> x0, matrix products: 2.16 us -> none  [the longest x1 1.09 us: per_device(): jnp.einsum('hts,thi->hsi', dscore_half, queries, preferred_element_type=j...]
    unnamed x9 -> x15, local copies, waits for them, and re-layouts: 2.29 us -> 3.25 us
  transfers between devices with their start and end apart: 16 -> 16, of which waited for: 13 -> 14; matrix products, arithmetic and copies ran while one was open for 6% -> 5% of each run, Pallas kernels for 0% -> 0%
where the time goes in v18:
time: 95.7 us; the launch traced here: 95.5 us
  waiting for transfers between devices  65.7 us (69%)
  starting transfers between devices  15 us (16%)
  local copies, waits for them, and re-layouts  4.84 us (5%)
  other arithmetic  3.96 us (4%)
  Pallas kernels  2.9 us (3%)
  matrix products  2.29 us (2%)
    ppermute x16, waiting for transfers between devices, swap(): return lax.ppermute(value, axis, [(i, i ^ bit) for i in range(count)])  65.7 us
    ppermute x16, starting transfers between devices, swap(): return lax.ppermute(value, axis, [(i, i ^ bit) for i in range(count)])  15 us
    unnamed x15, local copies, waits for them, and re-layouts  3.25 us
    pallas_call x1, Pallas kernels, tail(): pl.pallas_call(functools.partial(tail_kernel, HEAD ** (-0.5)), out_shape=...  2.9 us
  transfers between devices with their start and end apart: 16, of which 14 were waited for; matrix products, arithmetic and copies ran while one was open for 5% of the time, Pallas kernels for 0%

profile of v18, /device:TPU:0, one launch (start us, length us, event | category | flops | bytes accessed | tf_op | source)
XLA Modules:
  0.0 95.5 jit_solution(5043337658554671791)
XLA Ops:
  0.6 1.2 %copy.27 = bf16[128,1024]{0,1:T(8,128)(2,1)S(1)} copy(bf16[128,1024]{1,0:T(8,128)(2,1)} %key.1) | data formatting | bytes 524288 | tf_op jit(solution)/shard_map/reshape | solution.py:129
  1.8 0.2 fusion.13
  2.1 3.1 %collective-permute-start = (f32[4,128,128]{2,1,0:T(8,128)S(1)}, f32[4,128,128]{2,1,0:T(8,128)S(1)}, u32[]{:S(2)}, u32[]{:S(2)}) collective-permute-start(f32[4,128,128]{2,1,0:T(8,128)S(1)} %get-tuple-element.36), channel_id=1, source_target_pairs={{0,1},{1,0},{2,3},{3,2},{4,5},{5,4},{6,7},{7,6},{8,9},{9,8},{10,11... | collective-permute-start | bytes 786440 | tf_op jit(solution)/shard_map/ppermute | solution.py:21
  5.2 2.6 %collective-permute-start.1 = (f32[4,128,128]{2,1,0:T(8,128)S(1)}, f32[4,128,128]{2,1,0:T(8,128)S(1)}, u32[]{:S(2)}, u32[]{:S(2)}) collective-permute-start(f32[4,128,128]{2,1,0:T(8,128)S(1)} %get-tuple-element.37), channel_id=1, source_target_pairs={{0,2},{1,3},{2,0},{3,1},{4,6},{5,7},{6,4},{7,5},{8,10},{9,11},{10,... | collective-permute-start | bytes 786440 | tf_op jit(solution)/shard_map/ppermute | solution.py:21
  7.8 9.2 %collective-permute-done = f32[4,128,128]{2,1,0:T(8,128)S(1)} collective-permute-done((f32[4,128,128]{2,1,0:T(8,128)S(1)}, f32[4,128,128]{2,1,0:T(8,128)S(1)}, u32[]{:S(2)}, u32[]{:S(2)}) %collective-permute-start) | collective-permute-done | bytes 262176 | tf_op jit(solution)/shard_map/ppermute | solution.py:21
  17.0 2.5 %collective-permute-done.1 = f32[4,128,128]{2,1,0:T(8,128)S(1)} collective-permute-done((f32[4,128,128]{2,1,0:T(8,128)S(1)}, f32[4,128,128]{2,1,0:T(8,128)S(1)}, u32[]{:S(2)}, u32[]{:S(2)}) %collective-permute-start.1) | collective-permute-done | bytes 262176 | tf_op jit(solution)/shard_map/ppermute | solution.py:21
  19.7 1.5 %collective-permute-done.2 = f32[4,128,128]{2,1,0:T(8,128)S(1)} collective-permute-done((f32[4,128,128]{2,1,0:T(8,128)S(1)}, f32[4,128,128]{2,1,0:T(8,128)S(1)}, u32[]{:S(2)}, u32[]{:S(2)}) %collective-permute-start.2) | collective-permute-done | bytes 262176 | tf_op jit(solution)/shard_map/ppermute | solution.py:21
  21.3 0.4 collective-permute-start.3
  21.7 1.5 %collective-permute-start.6 = (f32[4,128,128]{2,1,0:T(8,128)S(1)}, f32[4,128,128]{2,1,0:T(8,128)S(1)}, u32[]{:S(2)}, u32[]{:S(2)}) collective-permute-start(f32[4,128,128]{2,1,0:T(8,128)S(1)} %add.88), channel_id=1, source_target_pairs={{0,8},{4,12},{8,0},{12,4},{1,9},{5,13},{9,1},{13,5},{2,10},{6,14},... | collective-permute-start | bytes 786440 | tf_op jit(solution)/shard_map/ppermute | solution.py:21
  23.1 12.9 %collective-permute-done.3 = f32[4,128,128]{2,1,0:T(8,128)S(1)} collective-permute-done((f32[4,128,128]{2,1,0:T(8,128)S(1)}, f32[4,128,128]{2,1,0:T(8,128)S(1)}, u32[]{:S(2)}, u32[]{:S(2)}) %collective-permute-start.3) | collective-permute-done | bytes 262176 | tf_op jit(solution)/shard_map/ppermute | solution.py:21
  36.1 0.1 collective-permute-start.4
  36.4 1.3 %collective-permute-done.4 = f32[4,128,128]{2,1,0:T(8,128)S(1)} collective-permute-done((f32[4,128,128]{2,1,0:T(8,128)S(1)}, f32[4,128,128]{2,1,0:T(8,128)S(1)}, u32[]{:S(2)}, u32[]{:S(2)}) %collective-permute-start.4) | collective-permute-done | bytes 262176 | tf_op jit(solution)/shard_map/ppermute | solution.py:21
  37.7 1.6 %collective-permute-start.5 = (f32[4,128,128]{2,1,0:T(8,128)S(1)}, f32[4,128,128]{2,1,0:T(8,128)S(1)}, u32[]{:S(2)}, u32[]{:S(2)}) collective-permute-start(f32[4,128,128]{2,1,0:T(8,128)S(1)} %add.92), channel_id=1, source_target_pairs={{0,8},{4,12},{8,0},{12,4},{1,9},{5,13},{9,1},{13,5},{2,10},{6,14},... | collective-permute-start | bytes 786440 | tf_op jit(solution)/shard_map/ppermute | solution.py:21
  39.3 0.2 fusion.5.score
  39.5 5.5 %collective-permute-done.7 = f32[4,128,128]{2,1,0:T(8,128)S(1)} collective-permute-done((f32[4,128,128]{2,1,0:T(8,128)S(1)}, f32[4,128,128]{2,1,0:T(8,128)S(1)}, u32[]{:S(2)}, u32[]{:S(2)}) %collective-permute-start.7) | collective-permute-done | bytes 262176 | tf_op jit(solution)/shard_map/ppermute | solution.py:21
  45.1 1.1 %collective-permute-done.5 = f32[4,128,128]{2,1,0:T(8,128)S(1)} collective-permute-done((f32[4,128,128]{2,1,0:T(8,128)S(1)}, f32[4,128,128]{2,1,0:T(8,128)S(1)}, u32[]{:S(2)}, u32[]{:S(2)}) %collective-permute-start.5) | collective-permute-done | bytes 262176 | tf_op jit(solution)/shard_map/ppermute | solution.py:21
  46.2 0.3 fusion.3
  46.6 0.3 multiply_reduce_fusion
  47.0 0.2 copy.26
  47.2 0.7 copy-done.5
  47.9 0.2 fusion.8
  48.1 0.9 fusion.10
  49.0 0.2 copy.28
  49.2 0.5 copy-done
  49.7 0.3 convolution_bitcast_fusion
  50.1 0.8 collective-permute-start.9
  50.9 1.1 %collective-permute-start.8 = (f32[4,128,128]{2,1,0:T(8,128)S(1)}, f32[4,128,128]{2,1,0:T(8,128)S(1)}, u32[]{:S(2)}, u32[]{:S(2)}) collective-permute-start(f32[4,128,128]{2,1,0:T(8,128)S(1)} %get-tuple-element.33), channel_id=1, source_target_pairs={{0,2},{1,3},{2,0},{3,1},{4,6},{5,7},{6,4},{7,5},{8,10},{9,11},{10,... | collective-permute-start | bytes 786440 | tf_op jit(solution)/shard_map/ppermute | solution.py:21
  52.1 10.0 %collective-permute-done.9 = f32[4,128,128]{2,1,0:T(8,128)S(1)} collective-permute-done((f32[4,128,128]{2,1,0:T(8,128)S(1)}, f32[4,128,128]{2,1,0:T(8,128)S(1)}, u32[]{:S(2)}, u32[]{:S(2)}) %collective-permute-start.9) | collective-permute-done | bytes 262176 | tf_op jit(solution)/shard_map/ppermute | solution.py:21
  62.0 2.7 %collective-permute-done.8 = f32[4,128,128]{2,1,0:T(8,128)S(1)} collective-permute-done((f32[4,128,128]{2,1,0:T(8,128)S(1)}, f32[4,128,128]{2,1,0:T(8,128)S(1)}, u32[]{:S(2)}, u32[]{:S(2)}) %collective-permute-start.8) | collective-permute-done | bytes 262176 | tf_op jit(solution)/shard_map/ppermute | solution.py:21
  64.9 0.4 collective-permute-start.13
  65.3 1.1 %collective-permute-done.10 = f32[4,128,128]{2,1,0:T(8,128)S(1)} collective-permute-done((f32[4,128,128]{2,1,0:T(8,128)S(1)}, f32[4,128,128]{2,1,0:T(8,128)S(1)}, u32[]{:S(2)}, u32[]{:S(2)}) %collective-permute-start.10) | collective-permute-done | bytes 262176 | tf_op jit(solution)/shard_map/ppermute | solution.py:21
  66.4 1.6 %collective-permute-start.11 = (f32[4,128,128]{2,1,0:T(8,128)S(1)}, f32[4,128,128]{2,1,0:T(8,128)S(1)}, u32[]{:S(2)}, u32[]{:S(2)}) collective-permute-start(f32[4,128,128]{2,1,0:T(8,128)S(1)} %add.104), channel_id=1, source_target_pairs={{0,8},{4,12},{8,0},{12,4},{1,9},{5,13},{9,1},{13,5},{2,10},{6,14},... | collective-permute-start | bytes 786440 | tf_op jit(solution)/shard_map/ppermute | solution.py:21
  68.0 10.9 %collective-permute-done.13 = f32[4,128,128]{2,1,0:T(8,128)S(1)} collective-permute-done((f32[4,128,128]{2,1,0:T(8,128)S(1)}, f32[4,128,128]{2,1,0:T(8,128)S(1)}, u32[]{:S(2)}, u32[]{:S(2)}) %collective-permute-start.13) | collective-permute-done | bytes 262176 | tf_op jit(solution)/shard_map/ppermute | solution.py:21
  78.9 0.1 collective-permute-start.14
  79.0 0.3 fusion.7.dscore
  79.4 0.3 convolution_bitcast_fusion.2
  79.7 0.4 copy-done.4
  80.1 0.4 collective-permute-done.14
  80.5 0.7 add.111
  81.3 1.5 %collective-permute-start.15 = (f32[4,128,128]{2,1,0:T(8,128)}, f32[4,128,128]{2,1,0:T(8,128)S(1)}, u32[]{:S(2)}, u32[]{:S(2)}) collective-permute-start(f32[4,128,128]{2,1,0:T(8,128)} %add.111), channel_id=1, source_target_pairs={{0,8},{4,12},{8,0},{12,4},{1,9},{5,13},{9,1},{13,5},{2,10},{6,14},... | collective-permute-start | bytes 786440 | tf_op jit(solution)/shard_map/ppermute | solution.py:21
  82.7 0.9 add_select_fusion
  83.6 0.2 fusion.6
  83.8 0.9 copy.23
  84.7 5.1 %collective-permute-done.15 = f32[4,128,128]{2,1,0:T(8,128)S(1)} collective-permute-done((f32[4,128,128]{2,1,0:T(8,128)}, f32[4,128,128]{2,1,0:T(8,128)S(1)}, u32[]{:S(2)}, u32[]{:S(2)}) %collective-permute-start.15) | collective-permute-done | bytes 262176 | tf_op jit(solution)/shard_map/ppermute | solution.py:21
  89.8 0.8 select_add_fusion.upper_later
  90.6 1.3 %collective-permute-done.12.lower_got = f32[4,128,128]{2,1,0:T(8,128)S(1)} collective-permute-done((f32[4,128,128]{2,1,0:T(8,128)}, f32[4,128,128]{2,1,0:T(8,128)S(1)}, u32[]{:S(2)}, u32[]{:S(2)}) %collective-permute-start.12) | collective-permute-done | bytes 262176 | tf_op jit(solution)/shard_map/ppermute | solution.py:21
  91.9 0.7 copy-done.6
  92.6 2.9 %shard_map.75 = (bf16[128,1024]{1,0:T(8,128)(2,1)}, bf16[128,1024]{1,0:T(8,128)(2,1)}) custom-call(f32[4,128,128]{2,1,0:T(8,128)} %get-tuple-element.25.lower_known, f32[4,128,128]{2,1,0:T(8,128)} %copy-done.6, f32[4,128,128]{2,1,0:T(8,128)} %select_add_fusion.upper_later, bf16[8,128,128]{2,1,0:T(8,128)(2,1)} %copy-done.4, bf16[8,128,128]{2,1,0:T(8,128)(2,1)} %copy-done.3, ...), custom_call_target="tpu_custom_call" | custom-call | flops 134217728 | bytes 6291456 | tf_op jit(solution)/shard_map/pallas_call | solution.py:114
  (31 shorter events, 0.8 us)
Async XLA Ops:
  0.6 1.2 %copy-start.1 = (bf16[128,1024]{1,0:T(8,128)(2,1)S(1)}, bf16[128,1024]{1,0:T(8,128)(2,1)}, u32[]{:S(2)}) copy-start(bf16[128,1024]{1,0:T(8,128)(2,1)} %value.1) | copy-start | bytes 786436
  2.1 14.9 %collective-permute-start = (f32[4,128,128]{2,1,0:T(8,128)S(1)}, f32[4,128,128]{2,1,0:T(8,128)S(1)}, u32[]{:S(2)}, u32[]{:S(2)}) collective-permute-start(f32[4,128,128]{2,1,0:T(8,128)S(1)} %get-tuple-element.36), channel_id=1, source_target_pairs={{0,1},{1,0},{2,3},{3,2},{4,5},{5,4},{6,7},{7,6},{8,9},{9,8},{10,11... | collective-permute-start | bytes 786440 | tf_op jit(solution)/shard_map/ppermute | solution.py:21
  5.2 14.3 %collective-permute-start.1 = (f32[4,128,128]{2,1,0:T(8,128)S(1)}, f32[4,128,128]{2,1,0:T(8,128)S(1)}, u32[]{:S(2)}, u32[]{:S(2)}) collective-permute-start(f32[4,128,128]{2,1,0:T(8,128)S(1)} %get-tuple-element.37), channel_id=1, source_target_pairs={{0,2},{1,3},{2,0},{3,1},{4,6},{5,7},{6,4},{7,5},{8,10},{9,11},{10,... | collective-permute-start | bytes 786440 | tf_op jit(solution)/shard_map/ppermute | solution.py:21
  19.6 1.6 %collective-permute-start.2 = (f32[4,128,128]{2,1,0:T(8,128)S(1)}, f32[4,128,128]{2,1,0:T(8,128)S(1)}, u32[]{:S(2)}, u32[]{:S(2)}) collective-permute-start(f32[4,128,128]{2,1,0:T(8,128)S(1)} %get-tuple-element.12), channel_id=1, source_target_pairs={{0,4},{4,0},{8,12},{12,8},{1,5},{5,1},{9,13},{13,9},{2,6},{6,2},{1... | collective-permute-start | bytes 786440 | tf_op jit(solution)/shard_map/ppermute | solution.py:21
  21.3 14.8 %collective-permute-start.3 = (f32[4,128,128]{2,1,0:T(8,128)S(1)}, f32[4,128,128]{2,1,0:T(8,128)S(1)}, u32[]{:S(2)}, u32[]{:S(2)}) collective-permute-start(f32[4,128,128]{2,1,0:T(8,128)S(1)} %get-tuple-element.14), channel_id=1, source_target_pairs={{0,2},{1,3},{2,0},{3,1},{4,6},{5,7},{6,4},{7,5},{8,10},{9,11},{10,... | collective-permute-start | bytes 786440 | tf_op jit(solution)/shard_map/ppermute | solution.py:21
  21.7 14.6 %collective-permute-start.6 = (f32[4,128,128]{2,1,0:T(8,128)S(1)}, f32[4,128,128]{2,1,0:T(8,128)S(1)}, u32[]{:S(2)}, u32[]{:S(2)}) collective-permute-start(f32[4,128,128]{2,1,0:T(8,128)S(1)} %add.88), channel_id=1, source_target_pairs={{0,8},{4,12},{8,0},{12,4},{1,9},{5,13},{9,1},{13,5},{2,10},{6,14},... | collective-permute-start | bytes 786440 | tf_op jit(solution)/shard_map/ppermute | solution.py:21
  36.1 1.6 %collective-permute-start.4 = (f32[4,128,128]{2,1,0:T(8,128)S(1)}, f32[4,128,128]{2,1,0:T(8,128)S(1)}, u32[]{:S(2)}, u32[]{:S(2)}) collective-permute-start(f32[4,128,128]{2,1,0:T(8,128)S(1)} %add.90), channel_id=1, source_target_pairs={{0,4},{4,0},{8,12},{12,8},{1,5},{5,1},{9,13},{13,9},{2,6},{6,2},{1... | collective-permute-start | bytes 786440 | tf_op jit(solution)/shard_map/ppermute | solution.py:21
  36.3 8.8 %collective-permute-start.7 = (f32[4,128,128]{2,1,0:T(8,128)S(1)}, f32[4,128,128]{2,1,0:T(8,128)S(1)}, u32[]{:S(2)}, u32[]{:S(2)}) collective-permute-start(f32[4,128,128]{2,1,0:T(8,128)S(1)} %get-tuple-element.26), channel_id=1, source_target_pairs={{0,1},{1,0},{2,3},{3,2},{4,5},{5,4},{6,7},{7,6},{8,9},{9,8},{10,11... | collective-permute-start | bytes 786440 | tf_op jit(solution)/shard_map/ppermute | solution.py:21
  36.4 2.9 %copy-start.2 = (bf16[128,1024]{1,0:T(8,128)(2,1)S(1)}, bf16[128,1024]{1,0:T(8,128)(2,1)}, u32[]{:S(2)}) copy-start(bf16[128,1024]{1,0:T(8,128)(2,1)} %query.1) | copy-start | bytes 786436
  37.7 8.4 %collective-permute-start.5 = (f32[4,128,128]{2,1,0:T(8,128)S(1)}, f32[4,128,128]{2,1,0:T(8,128)S(1)}, u32[]{:S(2)}, u32[]{:S(2)}) collective-permute-start(f32[4,128,128]{2,1,0:T(8,128)S(1)} %add.92), channel_id=1, source_target_pairs={{0,8},{4,12},{8,0},{12,4},{1,9},{5,13},{9,1},{13,5},{2,10},{6,14},... | collective-permute-start | bytes 786440 | tf_op jit(solution)/shard_map/ppermute | solution.py:21
  39.5 7.1 %copy-start.3 = (bf16[8,128,128]{2,1,0:T(8,128)(2,1)}, bf16[8,128,128]{2,1,0:T(8,128)(2,1)S(1)}, u32[]{:S(2)}) copy-start(bf16[8,128,128]{2,1,0:T(8,128)(2,1)S(1)} %fusion.5.score) | copy-start | bytes 786436
  46.9 1.0 %copy-start.5 = (bf16[128,1024]{1,0:T(8,128)(2,1)S(1)}, bf16[128,1024]{1,0:T(8,128)(2,1)}, u32[]{:S(2)}) copy-start(bf16[128,1024]{1,0:T(8,128)(2,1)} %param.7) | copy-start | bytes 786436
  49.0 0.7 copy-start
  50.1 11.9 %collective-permute-start.9 = (f32[4,128,128]{2,1,0:T(8,128)S(1)}, f32[4,128,128]{2,1,0:T(8,128)S(1)}, u32[]{:S(2)}, u32[]{:S(2)}) collective-permute-start(f32[4,128,128]{2,1,0:T(8,128)S(1)} %get-tuple-element.32), channel_id=1, source_target_pairs={{0,1},{1,0},{2,3},{3,2},{4,5},{5,4},{6,7},{7,6},{8,9},{9,8},{10,11... | collective-permute-start | bytes 786440 | tf_op jit(solution)/shard_map/ppermute | solution.py:21
  50.9 13.8 %collective-permute-start.8 = (f32[4,128,128]{2,1,0:T(8,128)S(1)}, f32[4,128,128]{2,1,0:T(8,128)S(1)}, u32[]{:S(2)}, u32[]{:S(2)}) collective-permute-start(f32[4,128,128]{2,1,0:T(8,128)S(1)} %get-tuple-element.33), channel_id=1, source_target_pairs={{0,2},{1,3},{2,0},{3,1},{4,6},{5,7},{6,4},{7,5},{8,10},{9,11},{10,... | collective-permute-start | bytes 786440 | tf_op jit(solution)/shard_map/ppermute | solution.py:21
  64.8 1.6 %collective-permute-start.10 = (f32[4,128,128]{2,1,0:T(8,128)S(1)}, f32[4,128,128]{2,1,0:T(8,128)S(1)}, u32[]{:S(2)}, u32[]{:S(2)}) collective-permute-start(f32[4,128,128]{2,1,0:T(8,128)S(1)} %get-tuple-element.16), channel_id=1, source_target_pairs={{0,4},{4,0},{8,12},{12,8},{1,5},{5,1},{9,13},{13,9},{2,6},{6,2},{1... | collective-permute-start | bytes 786440 | tf_op jit(solution)/shard_map/ppermute | solution.py:21
  64.9 14.0 %collective-permute-start.13 = (f32[4,128,128]{2,1,0:T(8,128)S(1)}, f32[4,128,128]{2,1,0:T(8,128)S(1)}, u32[]{:S(2)}, u32[]{:S(2)}) collective-permute-start(f32[4,128,128]{2,1,0:T(8,128)S(1)} %get-tuple-element.30), channel_id=1, source_target_pairs={{0,2},{1,3},{2,0},{3,1},{4,6},{5,7},{6,4},{7,5},{8,10},{9,11},{10,... | collective-permute-start | bytes 786440 | tf_op jit(solution)/shard_map/ppermute | solution.py:21
  66.4 16.3 %collective-permute-start.11 = (f32[4,128,128]{2,1,0:T(8,128)S(1)}, f32[4,128,128]{2,1,0:T(8,128)S(1)}, u32[]{:S(2)}, u32[]{:S(2)}) collective-permute-start(f32[4,128,128]{2,1,0:T(8,128)S(1)} %add.104), channel_id=1, source_target_pairs={{0,8},{4,12},{8,0},{12,4},{1,9},{5,13},{9,1},{13,5},{2,10},{6,14},... | collective-permute-start | bytes 786440 | tf_op jit(solution)/shard_map/ppermute | solution.py:21
  78.9 1.6 %collective-permute-start.14 = (f32[4,128,128]{2,1,0:T(8,128)S(1)}, f32[4,128,128]{2,1,0:T(8,128)S(1)}, u32[]{:S(2)}, u32[]{:S(2)}) collective-permute-start(f32[4,128,128]{2,1,0:T(8,128)S(1)} %add.109), channel_id=1, source_target_pairs={{0,4},{4,0},{8,12},{12,8},{1,5},{5,1},{9,13},{13,9},{2,6},{6,2},{1... | collective-permute-start | bytes 786440 | tf_op jit(solution)/shard_map/ppermute | solution.py:21
  79.4 0.7 copy-start.4
  81.3 8.6 %collective-permute-start.15 = (f32[4,128,128]{2,1,0:T(8,128)}, f32[4,128,128]{2,1,0:T(8,128)S(1)}, u32[]{:S(2)}, u32[]{:S(2)}) collective-permute-start(f32[4,128,128]{2,1,0:T(8,128)} %add.111), channel_id=1, source_target_pairs={{0,8},{4,12},{8,0},{12,4},{1,9},{5,13},{9,1},{13,5},{2,10},{6,14},... | collective-permute-start | bytes 786440 | tf_op jit(solution)/shard_map/ppermute | solution.py:21
  83.6 8.3 %collective-permute-start.12 = (f32[4,128,128]{2,1,0:T(8,128)}, f32[4,128,128]{2,1,0:T(8,128)S(1)}, u32[]{:S(2)}, u32[]{:S(2)}) collective-permute-start(f32[4,128,128]{2,1,0:T(8,128)} %get-tuple-element.24), channel_id=1, source_target_pairs={{0,1},{1,0},{2,3},{3,2},{4,5},{5,4},{6,7},{7,6},{8,9},{9,8},{10,11... | collective-permute-start | bytes 786440 | tf_op jit(solution)/shard_map/ppermute | solution.py:21
  91.9 0.7 copy-start.6

commit v19 on v12

--- a/solution.py
+++ b/solution.py
@@ -83,12 +83,10 @@
     return jnp.concatenate([earlier_a, known + got_b], axis=0)
 
 
-def tail_kernel(
-    scaling, lower_known, lower_got, upper_later, local_k, local_v, value, key, out_k, out_v
-):
+def tail_kernel(scaling, lower_later, upper_later, local_k, local_v, value, key, out_k, out_v):
     half = HEADS // 2
     for h in range(HEADS):
-        later = lower_known[h] + lower_got[h] if h < half else upper_later[h - half]
+        later = lower_later[h] if h < half else upper_later[h - half]
         later_half = later.astype(jnp.bfloat16)
         cols = slice(h * HEAD, (h + 1) * HEAD)
         from_later_k = lax.dot_general(
@@ -101,19 +99,19 @@
         out_v[:, cols] = (local_v[h] + scaling * from_later_v).astype(out_v.dtype)
 
 
-def tail(lower_known, lower_got, upper_later, local_k, local_v, value, key):
+def tail(lower_later, upper_later, local_k, local_v, value, key):
     rows = value.shape[0]
     vmem = pl.BlockSpec(memory_space=pltpu.VMEM)
     out = jax.ShapeDtypeStruct((rows, HEADS * HEAD), jnp.bfloat16)
     return pl.pallas_call(
         functools.partial(tail_kernel, HEAD ** (-0.5)),
         out_shape=(out, out),
-        in_specs=[vmem] * 7,
+        in_specs=[vmem] * 6,
         out_specs=(vmem, vmem),
         cost_estimate=pl.CostEstimate(
             flops=4 * HEADS * rows * HEAD * HEAD, transcendentals=0, bytes_accessed=12 * rows * 1024 * 4
         ),
-    )(lower_known, lower_got, upper_later, local_k, local_v, value, key)
+    )(lower_later, upper_later, local_k, local_v, value, key)
 
 
 def per_device(query, key, value, grad_out):
@@ -157,7 +155,7 @@
     lower_known, lower_got, upper_later = chunked_scan(grad_state, True)
     local_k = jnp.einsum("hts,thi->hsi", dscore_half, queries, preferred_element_type=jnp.float32)
     local_v = jnp.einsum("hts,thj->hsj", score_half, grad_half, preferred_element_type=jnp.float32)
-    grad_k, grad_v = tail(lower_known, lower_got, upper_later, local_k, local_v, value, key)
+    grad_k, grad_v = tail(lower_known + lower_got, upper_later, local_k, local_v, value, key)
     width = HEADS * HEAD
     return (
         normed.astype(jnp.bfloat16),

time: 91.9 us -> 91.2 us (level)
    unnamed x9 -> x7, local copies, waits for them, and re-layouts: 2.29 us -> 1.6 us
where the time goes in v19:
time: 91.2 us; the launch traced here: 91.1 us
  waiting for transfers between devices  62.1 us (68%)
  starting transfers between devices  14.8 us (16%)
  matrix products  4.44 us (5%)
  other arithmetic  3.21 us (4%)
  local copies, waits for them, and re-layouts  3.04 us (3%)
  Pallas kernels  2.65 us (3%)
    ppermute x16, waiting for transfers between devices, swap(): return lax.ppermute(value, axis, [(i, i ^ bit) for i in range(count)])  62.1 us
    ppermute x16, starting transfers between devices, swap(): return lax.ppermute(value, axis, [(i, i ^ bit) for i in range(count)])  14.8 us
    pallas_call x1, Pallas kernels, tail(): pl.pallas_call(functools.partial(tail_kernel, HEAD ** (-0.5)), out_shape=...  2.65 us
  transfers between devices with their start and end apart: 16, of which 13 were waited for; matrix products, arithmetic and copies ran while one was open for 6% of the time, Pallas kernels for 0%

profile of v19, /device:TPU:0, one launch (start us, length us, event | category | flops | bytes accessed | tf_op | source)
XLA Modules:
  0.0 91.1 jit_solution(17055227711078366806)
XLA Ops:
  0.7 1.2 %copy.32 = bf16[128,1024]{0,1:T(8,128)(2,1)S(1)} copy(bf16[128,1024]{1,0:T(8,128)(2,1)} %key.1) | data formatting | bytes 524288 | tf_op jit(solution)/shard_map/reshape | solution.py:121
  1.8 0.2 fusion.19
  2.1 3.1 %collective-permute-start = (f32[4,128,128]{2,1,0:T(8,128)S(1)}, f32[4,128,128]{2,1,0:T(8,128)S(1)}, u32[]{:S(2)}, u32[]{:S(2)}) collective-permute-start(f32[4,128,128]{2,1,0:T(8,128)S(1)} %get-tuple-element.36), channel_id=1, source_target_pairs={{0,1},{1,0},{2,3},{3,2},{4,5},{5,4},{6,7},{7,6},{8,9},{9,8},{10,11... | collective-permute-start | bytes 786440 | tf_op jit(solution)/shard_map/ppermute | solution.py:21
  5.2 2.6 %collective-permute-start.1 = (f32[4,128,128]{2,1,0:T(8,128)S(1)}, f32[4,128,128]{2,1,0:T(8,128)S(1)}, u32[]{:S(2)}, u32[]{:S(2)}) collective-permute-start(f32[4,128,128]{2,1,0:T(8,128)S(1)} %get-tuple-element.37), channel_id=1, source_target_pairs={{0,2},{1,3},{2,0},{3,1},{4,6},{5,7},{6,4},{7,5},{8,10},{9,11},{10,... | collective-permute-start | bytes 786440 | tf_op jit(solution)/shard_map/ppermute | solution.py:21
  7.8 9.2 %collective-permute-done = f32[4,128,128]{2,1,0:T(8,128)S(1)} collective-permute-done((f32[4,128,128]{2,1,0:T(8,128)S(1)}, f32[4,128,128]{2,1,0:T(8,128)S(1)}, u32[]{:S(2)}, u32[]{:S(2)}) %collective-permute-start) | collective-permute-done | bytes 262176 | tf_op jit(solution)/shard_map/ppermute | solution.py:21
  17.0 2.5 %collective-permute-done.1 = f32[4,128,128]{2,1,0:T(8,128)S(1)} collective-permute-done((f32[4,128,128]{2,1,0:T(8,128)S(1)}, f32[4,128,128]{2,1,0:T(8,128)S(1)}, u32[]{:S(2)}, u32[]{:S(2)}) %collective-permute-start.1) | collective-permute-done | bytes 262176 | tf_op jit(solution)/shard_map/ppermute | solution.py:21
  19.6 0.1 slice_add_fusion.1
  19.7 0.1 collective-permute-start.2
  19.7 1.5 %collective-permute-done.2 = f32[4,128,128]{2,1,0:T(8,128)S(1)} collective-permute-done((f32[4,128,128]{2,1,0:T(8,128)S(1)}, f32[4,128,128]{2,1,0:T(8,128)S(1)}, u32[]{:S(2)}, u32[]{:S(2)}) %collective-permute-start.2) | collective-permute-done | bytes 262176 | tf_op jit(solution)/shard_map/ppermute | solution.py:21
  21.3 0.4 collective-permute-start.3
  21.7 1.5 %collective-permute-start.6 = (f32[4,128,128]{2,1,0:T(8,128)S(1)}, f32[4,128,128]{2,1,0:T(8,128)S(1)}, u32[]{:S(2)}, u32[]{:S(2)}) collective-permute-start(f32[4,128,128]{2,1,0:T(8,128)S(1)} %add.91), channel_id=1, source_target_pairs={{0,8},{4,12},{8,0},{12,4},{1,9},{5,13},{9,1},{13,5},{2,10},{6,14},... | collective-permute-start | bytes 786440 | tf_op jit(solution)/shard_map/ppermute | solution.py:21
  23.2 12.9 %collective-permute-done.3 = f32[4,128,128]{2,1,0:T(8,128)S(1)} collective-permute-done((f32[4,128,128]{2,1,0:T(8,128)S(1)}, f32[4,128,128]{2,1,0:T(8,128)S(1)}, u32[]{:S(2)}, u32[]{:S(2)}) %collective-permute-start.3) | collective-permute-done | bytes 262176 | tf_op jit(solution)/shard_map/ppermute | solution.py:21
  36.1 0.1 collective-permute-start.4
  36.3 0.1 collective-permute-start.7
  36.4 1.3 %collective-permute-done.4 = f32[4,128,128]{2,1,0:T(8,128)S(1)} collective-permute-done((f32[4,128,128]{2,1,0:T(8,128)S(1)}, f32[4,128,128]{2,1,0:T(8,128)S(1)}, u32[]{:S(2)}, u32[]{:S(2)}) %collective-permute-start.4) | collective-permute-done | bytes 262176 | tf_op jit(solution)/shard_map/ppermute | solution.py:21
  37.8 1.6 %collective-permute-start.5 = (f32[4,128,128]{2,1,0:T(8,128)S(1)}, f32[4,128,128]{2,1,0:T(8,128)S(1)}, u32[]{:S(2)}, u32[]{:S(2)}) collective-permute-start(f32[4,128,128]{2,1,0:T(8,128)S(1)} %add.95), channel_id=1, source_target_pairs={{0,8},{4,12},{8,0},{12,4},{1,9},{5,13},{9,1},{13,5},{2,10},{6,14},... | collective-permute-start | bytes 786440 | tf_op jit(solution)/shard_map/ppermute | solution.py:21
  39.3 0.2 fusion.5
  39.6 5.5 %collective-permute-done.7 = f32[4,128,128]{2,1,0:T(8,128)S(1)} collective-permute-done((f32[4,128,128]{2,1,0:T(8,128)S(1)}, f32[4,128,128]{2,1,0:T(8,128)S(1)}, u32[]{:S(2)}, u32[]{:S(2)}) %collective-permute-start.7) | collective-permute-done | bytes 262176 | tf_op jit(solution)/shard_map/ppermute | solution.py:21
  45.1 1.1 %collective-permute-done.5 = f32[4,128,128]{2,1,0:T(8,128)S(1)} collective-permute-done((f32[4,128,128]{2,1,0:T(8,128)S(1)}, f32[4,128,128]{2,1,0:T(8,128)S(1)}, u32[]{:S(2)}, u32[]{:S(2)}) %collective-permute-start.5) | collective-permute-done | bytes 262176 | tf_op jit(solution)/shard_map/ppermute | solution.py:21
  46.2 0.1 add_convert_fusion.1
  46.3 0.3 fusion.3
  46.6 0.3 multiply_reduce_fusion
  47.0 0.2 copy.15
  47.2 0.7 copy-done.2
  47.9 0.2 fusion.8
  48.1 0.9 fusion.11
  49.0 0.3 convolution_bitcast_fusion
  49.3 0.8 collective-permute-start.9
  50.2 1.2 %collective-permute-start.8 = (f32[4,128,128]{2,1,0:T(8,128)S(1)}, f32[4,128,128]{2,1,0:T(8,128)S(1)}, u32[]{:S(2)}, u32[]{:S(2)}) collective-permute-start(f32[4,128,128]{2,1,0:T(8,128)S(1)} %get-tuple-element.33), channel_id=1, source_target_pairs={{0,2},{1,3},{2,0},{3,1},{4,6},{5,7},{6,4},{7,5},{8,10},{9,11},{10,... | collective-permute-start | bytes 786440 | tf_op jit(solution)/shard_map/ppermute | solution.py:21
  51.3 10.0 %collective-permute-done.9 = f32[4,128,128]{2,1,0:T(8,128)S(1)} collective-permute-done((f32[4,128,128]{2,1,0:T(8,128)S(1)}, f32[4,128,128]{2,1,0:T(8,128)S(1)}, u32[]{:S(2)}, u32[]{:S(2)}) %collective-permute-start.9) | collective-permute-done | bytes 262176 | tf_op jit(solution)/shard_map/ppermute | solution.py:21
  61.3 3.0 %collective-permute-done.8 = f32[4,128,128]{2,1,0:T(8,128)S(1)} collective-permute-done((f32[4,128,128]{2,1,0:T(8,128)S(1)}, f32[4,128,128]{2,1,0:T(8,128)S(1)}, u32[]{:S(2)}, u32[]{:S(2)}) %collective-permute-start.8) | collective-permute-done | bytes 262176 | tf_op jit(solution)/shard_map/ppermute | solution.py:21
  64.3 0.2 collective-permute-start.13
  64.5 0.3 fusion.7
  64.8 0.3 convolution_bitcast_fusion.2
  65.1 0.9 %collective-permute-done.10 = f32[4,128,128]{2,1,0:T(8,128)S(1)} collective-permute-done((f32[4,128,128]{2,1,0:T(8,128)S(1)}, f32[4,128,128]{2,1,0:T(8,128)S(1)}, u32[]{:S(2)}, u32[]{:S(2)}) %collective-permute-start.10) | collective-permute-done | bytes 262176 | tf_op jit(solution)/shard_map/ppermute | solution.py:21
  66.1 1.5 %collective-permute-start.11 = (f32[4,128,128]{2,1,0:T(8,128)S(1)}, f32[4,128,128]{2,1,0:T(8,128)S(1)}, u32[]{:S(2)}, u32[]{:S(2)}) collective-permute-start(f32[4,128,128]{2,1,0:T(8,128)S(1)} %add.107), channel_id=1, source_target_pairs={{0,8},{4,12},{8,0},{12,4},{1,9},{5,13},{9,1},{13,5},{2,10},{6,14},... | collective-permute-start | bytes 786440 | tf_op jit(solution)/shard_map/ppermute | solution.py:21
  67.6 7.6 %collective-permute-done.13 = f32[4,128,128]{2,1,0:T(8,128)S(1)} collective-permute-done((f32[4,128,128]{2,1,0:T(8,128)S(1)}, f32[4,128,128]{2,1,0:T(8,128)S(1)}, u32[]{:S(2)}, u32[]{:S(2)}) %collective-permute-start.13) | collective-permute-done | bytes 262176 | tf_op jit(solution)/shard_map/ppermute | solution.py:21
  75.3 0.1 collective-permute-start.14
  75.3 1.1 %fusion.21.local_k = f32[8,128,128]{2,1,0:T(8,128)} fusion(bf16[8,128,128]{2,1,0:T(8,128)(2,1)S(1)} %fusion.7, bf16[128,1024]{1,0:T(8,128)(2,1)S(1)} %copy-done), kind=kOutput, calls=%fused_computation.34 | convolution fusion | flops 33554432 | bytes 1048576 | tf_op jit(solution)/shard_map/hts,thi->hsi/dot_general | solution.py:156
  76.4 1.1 %fusion.13.local_v = f32[8,128,128]{2,1,0:T(8,128)} fusion(bf16[8,128,128]{2,1,0:T(8,128)(2,1)S(1)} %fusion.5, bf16[16,8,8,128]{3,2,1,0:T(8,128)(2,1)S(1)} %get-tuple-element.28), kind=kOutput, calls=%fused_computation.26 | convolution fusion | flops 33554432 | bytes 1048576 | tf_op jit(solution)/shard_map/hts,thj->hsj/dot_general | solution.py:157
  77.6 1.6 %collective-permute-start.15 = (f32[4,128,128]{2,1,0:T(8,128)S(1)}, f32[4,128,128]{2,1,0:T(8,128)S(1)}, u32[]{:S(2)}, u32[]{:S(2)}) collective-permute-start(f32[4,128,128]{2,1,0:T(8,128)S(1)} %add.115), channel_id=1, source_target_pairs={{0,8},{4,12},{8,0},{12,4},{1,9},{5,13},{9,1},{13,5},{2,10},{6,14},... | collective-permute-start | bytes 786440 | tf_op jit(solution)/shard_map/ppermute | solution.py:21
  79.3 0.3 fusion.6
  79.6 0.9 copy.27
  80.4 5.9 %collective-permute-done.15 = f32[4,128,128]{2,1,0:T(8,128)S(1)} collective-permute-done((f32[4,128,128]{2,1,0:T(8,128)S(1)}, f32[4,128,128]{2,1,0:T(8,128)S(1)}, u32[]{:S(2)}, u32[]{:S(2)}) %collective-permute-start.15) | collective-permute-done | bytes 262176 | tf_op jit(solution)/shard_map/ppermute | solution.py:21
  86.3 0.8 select_add_fusion.upper_later
  87.1 0.6 collective-permute-done.12
  87.7 0.7 add.111.lower_later
  88.4 2.7 %shard_map.75 = (bf16[128,1024]{1,0:T(8,128)(2,1)}, bf16[128,1024]{1,0:T(8,128)(2,1)}) custom-call(f32[4,128,128]{2,1,0:T(8,128)} %add.111.lower_later, f32[4,128,128]{2,1,0:T(8,128)} %select_add_fusion.upper_later, f32[8,128,128]{2,1,0:T(8,128)} %fusion.21.local_k, f32[8,128,128]{2,1,0:T(8,128)} %fusion.13.local_v, bf16[128,1024]{1,0:T(8,128)(2,1)} %value.1, ...), custom_call_target="tpu_custom_call" | custom-call | flops 67108864 | bytes 6291456 | tf_op jit(solution)/shard_map/pallas_call | solution.py:106
  (25 shorter events, 0.6 us)
Async XLA Ops:
  0.6 38.7 %copy-start = (bf16[128,1024]{1,0:T(8,128)(2,1)S(1)}, bf16[128,1024]{1,0:T(8,128)(2,1)}, u32[]{:S(2)}) copy-start(bf16[128,1024]{1,0:T(8,128)(2,1)} %param.4) | copy-start | bytes 786436
  0.6 1.2 %copy-start.1 = (bf16[128,1024]{1,0:T(8,128)(2,1)S(1)}, bf16[128,1024]{1,0:T(8,128)(2,1)}, u32[]{:S(2)}) copy-start(bf16[128,1024]{1,0:T(8,128)(2,1)} %value.1) | copy-start | bytes 786436
  2.1 14.9 %collective-permute-start = (f32[4,128,128]{2,1,0:T(8,128)S(1)}, f32[4,128,128]{2,1,0:T(8,128)S(1)}, u32[]{:S(2)}, u32[]{:S(2)}) collective-permute-start(f32[4,128,128]{2,1,0:T(8,128)S(1)} %get-tuple-element.36), channel_id=1, source_target_pairs={{0,1},{1,0},{2,3},{3,2},{4,5},{5,4},{6,7},{7,6},{8,9},{9,8},{10,11... | collective-permute-start | bytes 786440 | tf_op jit(solution)/shard_map/ppermute | solution.py:21
  5.2 14.3 %collective-permute-start.1 = (f32[4,128,128]{2,1,0:T(8,128)S(1)}, f32[4,128,128]{2,1,0:T(8,128)S(1)}, u32[]{:S(2)}, u32[]{:S(2)}) collective-permute-start(f32[4,128,128]{2,1,0:T(8,128)S(1)} %get-tuple-element.37), channel_id=1, source_target_pairs={{0,2},{1,3},{2,0},{3,1},{4,6},{5,7},{6,4},{7,5},{8,10},{9,11},{10,... | collective-permute-start | bytes 786440 | tf_op jit(solution)/shard_map/ppermute | solution.py:21
  19.7 1.6 %collective-permute-start.2 = (f32[4,128,128]{2,1,0:T(8,128)S(1)}, f32[4,128,128]{2,1,0:T(8,128)S(1)}, u32[]{:S(2)}, u32[]{:S(2)}) collective-permute-start(f32[4,128,128]{2,1,0:T(8,128)S(1)} %get-tuple-element.12), channel_id=1, source_target_pairs={{0,4},{4,0},{8,12},{12,8},{1,5},{5,1},{9,13},{13,9},{2,6},{6,2},{1... | collective-permute-start | bytes 786440 | tf_op jit(solution)/shard_map/ppermute | solution.py:21
  21.3 14.8 %collective-permute-start.3 = (f32[4,128,128]{2,1,0:T(8,128)S(1)}, f32[4,128,128]{2,1,0:T(8,128)S(1)}, u32[]{:S(2)}, u32[]{:S(2)}) collective-permute-start(f32[4,128,128]{2,1,0:T(8,128)S(1)} %get-tuple-element.14), channel_id=1, source_target_pairs={{0,2},{1,3},{2,0},{3,1},{4,6},{5,7},{6,4},{7,5},{8,10},{9,11},{10,... | collective-permute-start | bytes 786440 | tf_op jit(solution)/shard_map/ppermute | solution.py:21
  21.7 14.6 %collective-permute-start.6 = (f32[4,128,128]{2,1,0:T(8,128)S(1)}, f32[4,128,128]{2,1,0:T(8,128)S(1)}, u32[]{:S(2)}, u32[]{:S(2)}) collective-permute-start(f32[4,128,128]{2,1,0:T(8,128)S(1)} %add.91), channel_id=1, source_target_pairs={{0,8},{4,12},{8,0},{12,4},{1,9},{5,13},{9,1},{13,5},{2,10},{6,14},... | collective-permute-start | bytes 786440 | tf_op jit(solution)/shard_map/ppermute | solution.py:21
  36.1 1.6 %collective-permute-start.4 = (f32[4,128,128]{2,1,0:T(8,128)S(1)}, f32[4,128,128]{2,1,0:T(8,128)S(1)}, u32[]{:S(2)}, u32[]{:S(2)}) collective-permute-start(f32[4,128,128]{2,1,0:T(8,128)S(1)} %add.93), channel_id=1, source_target_pairs={{0,4},{4,0},{8,12},{12,8},{1,5},{5,1},{9,13},{13,9},{2,6},{6,2},{1... | collective-permute-start | bytes 786440 | tf_op jit(solution)/shard_map/ppermute | solution.py:21
  36.3 8.8 %collective-permute-start.7 = (f32[4,128,128]{2,1,0:T(8,128)S(1)}, f32[4,128,128]{2,1,0:T(8,128)S(1)}, u32[]{:S(2)}, u32[]{:S(2)}) collective-permute-start(f32[4,128,128]{2,1,0:T(8,128)S(1)} %get-tuple-element.26), channel_id=1, source_target_pairs={{0,1},{1,0},{2,3},{3,2},{4,5},{5,4},{6,7},{7,6},{8,9},{9,8},{10,11... | collective-permute-start | bytes 786440 | tf_op jit(solution)/shard_map/ppermute | solution.py:21
  37.8 8.4 %collective-permute-start.5 = (f32[4,128,128]{2,1,0:T(8,128)S(1)}, f32[4,128,128]{2,1,0:T(8,128)S(1)}, u32[]{:S(2)}, u32[]{:S(2)}) collective-permute-start(f32[4,128,128]{2,1,0:T(8,128)S(1)} %add.95), channel_id=1, source_target_pairs={{0,8},{4,12},{8,0},{12,4},{1,9},{5,13},{9,1},{13,5},{2,10},{6,14},... | collective-permute-start | bytes 786440 | tf_op jit(solution)/shard_map/ppermute | solution.py:21
  46.9 1.0 %copy-start.2 = (bf16[128,1024]{1,0:T(8,128)(2,1)S(1)}, bf16[128,1024]{1,0:T(8,128)(2,1)}, u32[]{:S(2)}) copy-start(bf16[128,1024]{1,0:T(8,128)(2,1)} %param.7) | copy-start | bytes 786436
  49.3 11.9 %collective-permute-start.9 = (f32[4,128,128]{2,1,0:T(8,128)S(1)}, f32[4,128,128]{2,1,0:T(8,128)S(1)}, u32[]{:S(2)}, u32[]{:S(2)}) collective-permute-start(f32[4,128,128]{2,1,0:T(8,128)S(1)} %get-tuple-element.32), channel_id=1, source_target_pairs={{0,1},{1,0},{2,3},{3,2},{4,5},{5,4},{6,7},{7,6},{8,9},{9,8},{10,11... | collective-permute-start | bytes 786440 | tf_op jit(solution)/shard_map/ppermute | solution.py:21
  50.2 14.1 %collective-permute-start.8 = (f32[4,128,128]{2,1,0:T(8,128)S(1)}, f32[4,128,128]{2,1,0:T(8,128)S(1)}, u32[]{:S(2)}, u32[]{:S(2)}) collective-permute-start(f32[4,128,128]{2,1,0:T(8,128)S(1)} %get-tuple-element.33), channel_id=1, source_target_pairs={{0,2},{1,3},{2,0},{3,1},{4,6},{5,7},{6,4},{7,5},{8,10},{9,11},{10,... | collective-permute-start | bytes 786440 | tf_op jit(solution)/shard_map/ppermute | solution.py:21
  64.3 10.9 %collective-permute-start.13 = (f32[4,128,128]{2,1,0:T(8,128)S(1)}, f32[4,128,128]{2,1,0:T(8,128)S(1)}, u32[]{:S(2)}, u32[]{:S(2)}) collective-permute-start(f32[4,128,128]{2,1,0:T(8,128)S(1)} %get-tuple-element.30), channel_id=1, source_target_pairs={{0,2},{1,3},{2,0},{3,1},{4,6},{5,7},{6,4},{7,5},{8,10},{9,11},{10,... | collective-permute-start | bytes 786440 | tf_op jit(solution)/shard_map/ppermute | solution.py:21
  64.5 1.5 %collective-permute-start.10 = (f32[4,128,128]{2,1,0:T(8,128)S(1)}, f32[4,128,128]{2,1,0:T(8,128)S(1)}, u32[]{:S(2)}, u32[]{:S(2)}) collective-permute-start(f32[4,128,128]{2,1,0:T(8,128)S(1)} %get-tuple-element.16), channel_id=1, source_target_pairs={{0,4},{4,0},{8,12},{12,8},{1,5},{5,1},{9,13},{13,9},{2,6},{6,2},{1... | collective-permute-start | bytes 786440 | tf_op jit(solution)/shard_map/ppermute | solution.py:21
  66.1 13.1 %collective-permute-start.11 = (f32[4,128,128]{2,1,0:T(8,128)S(1)}, f32[4,128,128]{2,1,0:T(8,128)S(1)}, u32[]{:S(2)}, u32[]{:S(2)}) collective-permute-start(f32[4,128,128]{2,1,0:T(8,128)S(1)} %add.107), channel_id=1, source_target_pairs={{0,8},{4,12},{8,0},{12,4},{1,9},{5,13},{9,1},{13,5},{2,10},{6,14},... | collective-permute-start | bytes 786440 | tf_op jit(solution)/shard_map/ppermute | solution.py:21
  75.3 2.3 %collective-permute-start.14 = (f32[4,128,128]{2,1,0:T(8,128)S(1)}, f32[4,128,128]{2,1,0:T(8,128)S(1)}, u32[]{:S(2)}, u32[]{:S(2)}) collective-permute-start(f32[4,128,128]{2,1,0:T(8,128)S(1)} %add.113), channel_id=1, source_target_pairs={{0,4},{4,0},{8,12},{12,8},{1,5},{5,1},{9,13},{13,9},{2,6},{6,2},{1... | collective-permute-start | bytes 786440 | tf_op jit(solution)/shard_map/ppermute | solution.py:21
  77.6 8.8 %collective-permute-start.15 = (f32[4,128,128]{2,1,0:T(8,128)S(1)}, f32[4,128,128]{2,1,0:T(8,128)S(1)}, u32[]{:S(2)}, u32[]{:S(2)}) collective-permute-start(f32[4,128,128]{2,1,0:T(8,128)S(1)} %add.115), channel_id=1, source_target_pairs={{0,8},{4,12},{8,0},{12,4},{1,9},{5,13},{9,1},{13,5},{2,10},{6,14},... | collective-permute-start | bytes 786440 | tf_op jit(solution)/shard_map/ppermute | solution.py:21
  79.2 8.5 %collective-permute-start.12 = (f32[4,128,128]{2,1,0:T(8,128)S(1)}, f32[4,128,128]{2,1,0:T(8,128)S(1)}, u32[]{:S(2)}, u32[]{:S(2)}) collective-permute-start(f32[4,128,128]{2,1,0:T(8,128)S(1)} %get-tuple-element.24), channel_id=1, source_target_pairs={{0,1},{1,0},{2,3},{3,2},{4,5},{5,4},{6,7},{7,6},{8,9},{9,8},{10,11... | collective-permute-start | bytes 786440 | tf_op jit(solution)/shard_map/ppermute | solution.py:21

commit v20 on v19

--- a/solution.py
+++ b/solution.py
@@ -64,10 +64,10 @@
         earlier_b, total_b = subcube_step(earlier_b, total_b, "inner", bit, backward)
     (earlier_b, total_b), _ = lax.optimization_barrier(((earlier_b, total_b), total_a))
     rows_before, rows_total = [], total_b
-    for index, bit in enumerate(outer_bits):
+    if not backward:
+        (earlier_a, total_a), _ = lax.optimization_barrier(((earlier_a, total_a), rows_total))
+    for bit in outer_bits:
         rows_before, rows_total = subcube_step(rows_before, rows_total, "outer", bit, backward)
-        if index == 0 and not backward:
-            (earlier_a, total_a), _ = lax.optimization_barrier(((earlier_a, total_a), rows_total))
     for bit in inner_bits[1:]:
         earlier_a, total_a = subcube_step(earlier_a, total_a, "inner", bit, backward)
     for bit in outer_bits:

time: 91.2 us -> 90 us (0.987)
  waiting for transfers between devices: 62.1 us -> 60.7 us
    ppermute x16, waiting for transfers between devices: 62.1 us -> 60.7 us  [swap(): return lax.ppermute(value, axis, [(i, i ^ bit) for i in range(count)])]
where the time goes in v20:
time: 90 us; the launch traced here: 89.8 us
  waiting for transfers between devices  60.7 us (67%)
  starting transfers between devices  14.9 us (17%)
  matrix products  4.46 us (5%)
  other arithmetic  3.21 us (4%)
  local copies, waits for them, and re-layouts  3.04 us (3%)
  Pallas kernels  2.65 us (3%)
    ppermute x16, waiting for transfers between devices, swap(): return lax.ppermute(value, axis, [(i, i ^ bit) for i in range(count)])  60.7 us
    ppermute x16, starting transfers between devices, swap(): return lax.ppermute(value, axis, [(i, i ^ bit) for i in range(count)])  14.9 us
    pallas_call x1, Pallas kernels, tail(): pl.pallas_call(functools.partial(tail_kernel, HEAD ** (-0.5)), out_shape=...  2.65 us
  transfers between devices with their start and end apart: 16, of which 13 were waited for; matrix products, arithmetic and copies ran while one was open for 6% of the time, Pallas kernels for 0%

profile of v20, /device:TPU:0, one launch (start us, length us, event | category | flops | bytes accessed | tf_op | source)
XLA Modules:
  0.0 89.8 jit_solution(15647906201023722219)
XLA Ops:
  0.7 1.2 %copy.32 = bf16[128,1024]{0,1:T(8,128)(2,1)S(1)} copy(bf16[128,1024]{1,0:T(8,128)(2,1)} %key.1) | data formatting | bytes 524288 | tf_op jit(solution)/shard_map/reshape | solution.py:121
  1.8 0.2 fusion.19
  2.1 3.1 %collective-permute-start = (f32[4,128,128]{2,1,0:T(8,128)S(1)}, f32[4,128,128]{2,1,0:T(8,128)S(1)}, u32[]{:S(2)}, u32[]{:S(2)}) collective-permute-start(f32[4,128,128]{2,1,0:T(8,128)S(1)} %get-tuple-element.36), channel_id=1, source_target_pairs={{0,1},{1,0},{2,3},{3,2},{4,5},{5,4},{6,7},{7,6},{8,9},{9,8},{10,11... | collective-permute-start | bytes 786440 | tf_op jit(solution)/shard_map/ppermute | solution.py:21
  5.2 2.6 %collective-permute-start.1 = (f32[4,128,128]{2,1,0:T(8,128)S(1)}, f32[4,128,128]{2,1,0:T(8,128)S(1)}, u32[]{:S(2)}, u32[]{:S(2)}) collective-permute-start(f32[4,128,128]{2,1,0:T(8,128)S(1)} %get-tuple-element.37), channel_id=1, source_target_pairs={{0,2},{1,3},{2,0},{3,1},{4,6},{5,7},{6,4},{7,5},{8,10},{9,11},{10,... | collective-permute-start | bytes 786440 | tf_op jit(solution)/shard_map/ppermute | solution.py:21
  7.8 9.2 %collective-permute-done = f32[4,128,128]{2,1,0:T(8,128)S(1)} collective-permute-done((f32[4,128,128]{2,1,0:T(8,128)S(1)}, f32[4,128,128]{2,1,0:T(8,128)S(1)}, u32[]{:S(2)}, u32[]{:S(2)}) %collective-permute-start) | collective-permute-done | bytes 262176 | tf_op jit(solution)/shard_map/ppermute | solution.py:21
  17.0 2.5 %collective-permute-done.1 = f32[4,128,128]{2,1,0:T(8,128)S(1)} collective-permute-done((f32[4,128,128]{2,1,0:T(8,128)S(1)}, f32[4,128,128]{2,1,0:T(8,128)S(1)}, u32[]{:S(2)}, u32[]{:S(2)}) %collective-permute-start.1) | collective-permute-done | bytes 262176 | tf_op jit(solution)/shard_map/ppermute | solution.py:21
  19.6 0.1 slice_add_fusion.1
  19.7 0.1 collective-permute-start.5
  19.7 0.4 collective-permute-start.2
  20.1 1.1 %collective-permute-done.5 = f32[4,128,128]{2,1,0:T(8,128)S(1)} collective-permute-done((f32[4,128,128]{2,1,0:T(8,128)S(1)}, f32[4,128,128]{2,1,0:T(8,128)S(1)}, u32[]{:S(2)}, u32[]{:S(2)}) %collective-permute-start.5) | collective-permute-done | bytes 262176 | tf_op jit(solution)/shard_map/ppermute | solution.py:21
  21.3 1.6 %collective-permute-start.6 = (f32[4,128,128]{2,1,0:T(8,128)S(1)}, f32[4,128,128]{2,1,0:T(8,128)S(1)}, u32[]{:S(2)}, u32[]{:S(2)}) collective-permute-start(f32[4,128,128]{2,1,0:T(8,128)S(1)} %add.96), channel_id=1, source_target_pairs={{0,8},{4,12},{8,0},{12,4},{1,9},{5,13},{9,1},{13,5},{2,10},{6,14},... | collective-permute-start | bytes 786440 | tf_op jit(solution)/shard_map/ppermute | solution.py:21
  22.8 12.0 %collective-permute-done.2 = f32[4,128,128]{2,1,0:T(8,128)S(1)} collective-permute-done((f32[4,128,128]{2,1,0:T(8,128)S(1)}, f32[4,128,128]{2,1,0:T(8,128)S(1)}, u32[]{:S(2)}, u32[]{:S(2)}) %collective-permute-start.2) | collective-permute-done | bytes 262176 | tf_op jit(solution)/shard_map/ppermute | solution.py:21
  34.9 0.1 collective-permute-start.3
  35.1 0.1 collective-permute-start.7
  35.2 1.3 %collective-permute-done.3 = f32[4,128,128]{2,1,0:T(8,128)S(1)} collective-permute-done((f32[4,128,128]{2,1,0:T(8,128)S(1)}, f32[4,128,128]{2,1,0:T(8,128)S(1)}, u32[]{:S(2)}, u32[]{:S(2)}) %collective-permute-start.3) | collective-permute-done | bytes 262176 | tf_op jit(solution)/shard_map/ppermute | solution.py:21
  36.5 1.6 %collective-permute-start.4 = (f32[4,128,128]{2,1,0:T(8,128)S(1)}, f32[4,128,128]{2,1,0:T(8,128)S(1)}, u32[]{:S(2)}, u32[]{:S(2)}) collective-permute-start(f32[4,128,128]{2,1,0:T(8,128)S(1)} %add.94), channel_id=1, source_target_pairs={{0,8},{4,12},{8,0},{12,4},{1,9},{5,13},{9,1},{13,5},{2,10},{6,14},... | collective-permute-start | bytes 786440 | tf_op jit(solution)/shard_map/ppermute | solution.py:21
  38.1 0.2 fusion.5
  38.3 5.5 %collective-permute-done.7 = f32[4,128,128]{2,1,0:T(8,128)S(1)} collective-permute-done((f32[4,128,128]{2,1,0:T(8,128)S(1)}, f32[4,128,128]{2,1,0:T(8,128)S(1)}, u32[]{:S(2)}, u32[]{:S(2)}) %collective-permute-start.7) | collective-permute-done | bytes 262176 | tf_op jit(solution)/shard_map/ppermute | solution.py:21
  43.8 1.1 %collective-permute-done.4 = f32[4,128,128]{2,1,0:T(8,128)S(1)} collective-permute-done((f32[4,128,128]{2,1,0:T(8,128)S(1)}, f32[4,128,128]{2,1,0:T(8,128)S(1)}, u32[]{:S(2)}, u32[]{:S(2)}) %collective-permute-start.4) | collective-permute-done | bytes 262176 | tf_op jit(solution)/shard_map/ppermute | solution.py:21
  44.9 0.1 add_convert_fusion.1
  45.0 0.3 fusion.3
  45.3 0.4 multiply_reduce_fusion
  45.7 0.2 copy.15
  45.9 0.7 copy-done.2
  46.7 0.2 fusion.8
  46.9 0.9 fusion.11
  47.8 0.3 convolution_bitcast_fusion
  48.1 0.8 collective-permute-start.9
  48.9 1.2 %collective-permute-start.8 = (f32[4,128,128]{2,1,0:T(8,128)S(1)}, f32[4,128,128]{2,1,0:T(8,128)S(1)}, u32[]{:S(2)}, u32[]{:S(2)}) collective-permute-start(f32[4,128,128]{2,1,0:T(8,128)S(1)} %get-tuple-element.33), channel_id=1, source_target_pairs={{0,2},{1,3},{2,0},{3,1},{4,6},{5,7},{6,4},{7,5},{8,10},{9,11},{10,... | collective-permute-start | bytes 786440 | tf_op jit(solution)/shard_map/ppermute | solution.py:21
  50.1 10.0 %collective-permute-done.9 = f32[4,128,128]{2,1,0:T(8,128)S(1)} collective-permute-done((f32[4,128,128]{2,1,0:T(8,128)S(1)}, f32[4,128,128]{2,1,0:T(8,128)S(1)}, u32[]{:S(2)}, u32[]{:S(2)}) %collective-permute-start.9) | collective-permute-done | bytes 262176 | tf_op jit(solution)/shard_map/ppermute | solution.py:21
  60.0 3.0 %collective-permute-done.8 = f32[4,128,128]{2,1,0:T(8,128)S(1)} collective-permute-done((f32[4,128,128]{2,1,0:T(8,128)S(1)}, f32[4,128,128]{2,1,0:T(8,128)S(1)}, u32[]{:S(2)}, u32[]{:S(2)}) %collective-permute-start.8) | collective-permute-done | bytes 262176 | tf_op jit(solution)/shard_map/ppermute | solution.py:21
  63.1 0.1 collective-permute-start.13
  63.2 0.3 fusion.7
  63.5 0.3 convolution_bitcast_fusion.2
  63.8 0.9 %collective-permute-done.10 = f32[4,128,128]{2,1,0:T(8,128)S(1)} collective-permute-done((f32[4,128,128]{2,1,0:T(8,128)S(1)}, f32[4,128,128]{2,1,0:T(8,128)S(1)}, u32[]{:S(2)}, u32[]{:S(2)}) %collective-permute-start.10) | collective-permute-done | bytes 262176 | tf_op jit(solution)/shard_map/ppermute | solution.py:21
  64.8 1.6 %collective-permute-start.11 = (f32[4,128,128]{2,1,0:T(8,128)S(1)}, f32[4,128,128]{2,1,0:T(8,128)S(1)}, u32[]{:S(2)}, u32[]{:S(2)}) collective-permute-start(f32[4,128,128]{2,1,0:T(8,128)S(1)} %add.107), channel_id=1, source_target_pairs={{0,8},{4,12},{8,0},{12,4},{1,9},{5,13},{9,1},{13,5},{2,10},{6,14},... | collective-permute-start | bytes 786440 | tf_op jit(solution)/shard_map/ppermute | solution.py:21
  66.3 7.6 %collective-permute-done.13 = f32[4,128,128]{2,1,0:T(8,128)S(1)} collective-permute-done((f32[4,128,128]{2,1,0:T(8,128)S(1)}, f32[4,128,128]{2,1,0:T(8,128)S(1)}, u32[]{:S(2)}, u32[]{:S(2)}) %collective-permute-start.13) | collective-permute-done | bytes 262176 | tf_op jit(solution)/shard_map/ppermute | solution.py:21
  74.0 0.1 collective-permute-start.14
  74.1 1.1 %fusion.21.local_k = f32[8,128,128]{2,1,0:T(8,128)} fusion(bf16[8,128,128]{2,1,0:T(8,128)(2,1)S(1)} %fusion.7, bf16[128,1024]{1,0:T(8,128)(2,1)S(1)} %copy-done), kind=kOutput, calls=%fused_computation.34 | convolution fusion | flops 33554432 | bytes 1048576 | tf_op jit(solution)/shard_map/hts,thi->hsi/dot_general | solution.py:156
  75.1 1.1 %fusion.13.local_v = f32[8,128,128]{2,1,0:T(8,128)} fusion(bf16[8,128,128]{2,1,0:T(8,128)(2,1)S(1)} %fusion.5, bf16[16,8,8,128]{3,2,1,0:T(8,128)(2,1)S(1)} %get-tuple-element.28), kind=kOutput, calls=%fused_computation.26 | convolution fusion | flops 33554432 | bytes 1048576 | tf_op jit(solution)/shard_map/hts,thj->hsj/dot_general | solution.py:157
  76.3 1.6 %collective-permute-start.15 = (f32[4,128,128]{2,1,0:T(8,128)S(1)}, f32[4,128,128]{2,1,0:T(8,128)S(1)}, u32[]{:S(2)}, u32[]{:S(2)}) collective-permute-start(f32[4,128,128]{2,1,0:T(8,128)S(1)} %add.115), channel_id=1, source_target_pairs={{0,8},{4,12},{8,0},{12,4},{1,9},{5,13},{9,1},{13,5},{2,10},{6,14},... | collective-permute-start | bytes 786440 | tf_op jit(solution)/shard_map/ppermute | solution.py:21
  78.0 0.3 fusion.6
  78.3 0.9 copy.27
  79.1 5.9 %collective-permute-done.15 = f32[4,128,128]{2,1,0:T(8,128)S(1)} collective-permute-done((f32[4,128,128]{2,1,0:T(8,128)S(1)}, f32[4,128,128]{2,1,0:T(8,128)S(1)}, u32[]{:S(2)}, u32[]{:S(2)}) %collective-permute-start.15) | collective-permute-done | bytes 262176 | tf_op jit(solution)/shard_map/ppermute | solution.py:21
  85.0 0.8 select_add_fusion.upper_later
  85.8 0.6 collective-permute-done.12
  86.4 0.7 add.111.lower_later
  87.1 2.7 %shard_map.75 = (bf16[128,1024]{1,0:T(8,128)(2,1)}, bf16[128,1024]{1,0:T(8,128)(2,1)}) custom-call(f32[4,128,128]{2,1,0:T(8,128)} %add.111.lower_later, f32[4,128,128]{2,1,0:T(8,128)} %select_add_fusion.upper_later, f32[8,128,128]{2,1,0:T(8,128)} %fusion.21.local_k, f32[8,128,128]{2,1,0:T(8,128)} %fusion.13.local_v, bf16[128,1024]{1,0:T(8,128)(2,1)} %value.1, ...), custom_call_target="tpu_custom_call" | custom-call | flops 67108864 | bytes 6291456 | tf_op jit(solution)/shard_map/pallas_call | solution.py:106
  (25 shorter events, 0.6 us)
Async XLA Ops:
  0.6 37.4 %copy-start = (bf16[128,1024]{1,0:T(8,128)(2,1)S(1)}, bf16[128,1024]{1,0:T(8,128)(2,1)}, u32[]{:S(2)}) copy-start(bf16[128,1024]{1,0:T(8,128)(2,1)} %param.4) | copy-start | bytes 786436
  0.6 1.2 %copy-start.1 = (bf16[128,1024]{1,0:T(8,128)(2,1)S(1)}, bf16[128,1024]{1,0:T(8,128)(2,1)}, u32[]{:S(2)}) copy-start(bf16[128,1024]{1,0:T(8,128)(2,1)} %value.1) | copy-start | bytes 786436
  2.1 14.9 %collective-permute-start = (f32[4,128,128]{2,1,0:T(8,128)S(1)}, f32[4,128,128]{2,1,0:T(8,128)S(1)}, u32[]{:S(2)}, u32[]{:S(2)}) collective-permute-start(f32[4,128,128]{2,1,0:T(8,128)S(1)} %get-tuple-element.36), channel_id=1, source_target_pairs={{0,1},{1,0},{2,3},{3,2},{4,5},{5,4},{6,7},{7,6},{8,9},{9,8},{10,11... | collective-permute-start | bytes 786440 | tf_op jit(solution)/shard_map/ppermute | solution.py:21
  5.2 14.3 %collective-permute-start.1 = (f32[4,128,128]{2,1,0:T(8,128)S(1)}, f32[4,128,128]{2,1,0:T(8,128)S(1)}, u32[]{:S(2)}, u32[]{:S(2)}) collective-permute-start(f32[4,128,128]{2,1,0:T(8,128)S(1)} %get-tuple-element.37), channel_id=1, source_target_pairs={{0,2},{1,3},{2,0},{3,1},{4,6},{5,7},{6,4},{7,5},{8,10},{9,11},{10,... | collective-permute-start | bytes 786440 | tf_op jit(solution)/shard_map/ppermute | solution.py:21
  19.7 1.6 %collective-permute-start.5 = (f32[4,128,128]{2,1,0:T(8,128)S(1)}, f32[4,128,128]{2,1,0:T(8,128)S(1)}, u32[]{:S(2)}, u32[]{:S(2)}) collective-permute-start(f32[4,128,128]{2,1,0:T(8,128)S(1)} %get-tuple-element.12), channel_id=1, source_target_pairs={{0,4},{4,0},{8,12},{12,8},{1,5},{5,1},{9,13},{13,9},{2,6},{6,2},{1... | collective-permute-start | bytes 786440 | tf_op jit(solution)/shard_map/ppermute | solution.py:21
  19.7 15.1 %collective-permute-start.2 = (f32[4,128,128]{2,1,0:T(8,128)S(1)}, f32[4,128,128]{2,1,0:T(8,128)S(1)}, u32[]{:S(2)}, u32[]{:S(2)}) collective-permute-start(f32[4,128,128]{2,1,0:T(8,128)S(1)} %get-tuple-element.14), channel_id=1, source_target_pairs={{0,2},{1,3},{2,0},{3,1},{4,6},{5,7},{6,4},{7,5},{8,10},{9,11},{10,... | collective-permute-start | bytes 786440 | tf_op jit(solution)/shard_map/ppermute | solution.py:21
  21.3 13.7 %collective-permute-start.6 = (f32[4,128,128]{2,1,0:T(8,128)S(1)}, f32[4,128,128]{2,1,0:T(8,128)S(1)}, u32[]{:S(2)}, u32[]{:S(2)}) collective-permute-start(f32[4,128,128]{2,1,0:T(8,128)S(1)} %add.96), channel_id=1, source_target_pairs={{0,8},{4,12},{8,0},{12,4},{1,9},{5,13},{9,1},{13,5},{2,10},{6,14},... | collective-permute-start | bytes 786440 | tf_op jit(solution)/shard_map/ppermute | solution.py:21
  34.9 1.6 %collective-permute-start.3 = (f32[4,128,128]{2,1,0:T(8,128)S(1)}, f32[4,128,128]{2,1,0:T(8,128)S(1)}, u32[]{:S(2)}, u32[]{:S(2)}) collective-permute-start(f32[4,128,128]{2,1,0:T(8,128)S(1)} %add.92), channel_id=1, source_target_pairs={{0,4},{4,0},{8,12},{12,8},{1,5},{5,1},{9,13},{13,9},{2,6},{6,2},{1... | collective-permute-start | bytes 786440 | tf_op jit(solution)/shard_map/ppermute | solution.py:21
  35.1 8.7 %collective-permute-start.7 = (f32[4,128,128]{2,1,0:T(8,128)S(1)}, f32[4,128,128]{2,1,0:T(8,128)S(1)}, u32[]{:S(2)}, u32[]{:S(2)}) collective-permute-start(f32[4,128,128]{2,1,0:T(8,128)S(1)} %get-tuple-element.26), channel_id=1, source_target_pairs={{0,1},{1,0},{2,3},{3,2},{4,5},{5,4},{6,7},{7,6},{8,9},{9,8},{10,11... | collective-permute-start | bytes 786440 | tf_op jit(solution)/shard_map/ppermute | solution.py:21
  36.5 8.4 %collective-permute-start.4 = (f32[4,128,128]{2,1,0:T(8,128)S(1)}, f32[4,128,128]{2,1,0:T(8,128)S(1)}, u32[]{:S(2)}, u32[]{:S(2)}) collective-permute-start(f32[4,128,128]{2,1,0:T(8,128)S(1)} %add.94), channel_id=1, source_target_pairs={{0,8},{4,12},{8,0},{12,4},{1,9},{5,13},{9,1},{13,5},{2,10},{6,14},... | collective-permute-start | bytes 786440 | tf_op jit(solution)/shard_map/ppermute | solution.py:21
  45.7 1.0 %copy-start.2 = (bf16[128,1024]{1,0:T(8,128)(2,1)S(1)}, bf16[128,1024]{1,0:T(8,128)(2,1)}, u32[]{:S(2)}) copy-start(bf16[128,1024]{1,0:T(8,128)(2,1)} %param.7) | copy-start | bytes 786436
  48.1 11.9 %collective-permute-start.9 = (f32[4,128,128]{2,1,0:T(8,128)S(1)}, f32[4,128,128]{2,1,0:T(8,128)S(1)}, u32[]{:S(2)}, u32[]{:S(2)}) collective-permute-start(f32[4,128,128]{2,1,0:T(8,128)S(1)} %get-tuple-element.32), channel_id=1, source_target_pairs={{0,1},{1,0},{2,3},{3,2},{4,5},{5,4},{6,7},{7,6},{8,9},{9,8},{10,11... | collective-permute-start | bytes 786440 | tf_op jit(solution)/shard_map/ppermute | solution.py:21
  48.9 14.1 %collective-permute-start.8 = (f32[4,128,128]{2,1,0:T(8,128)S(1)}, f32[4,128,128]{2,1,0:T(8,128)S(1)}, u32[]{:S(2)}, u32[]{:S(2)}) collective-permute-start(f32[4,128,128]{2,1,0:T(8,128)S(1)} %get-tuple-element.33), channel_id=1, source_target_pairs={{0,2},{1,3},{2,0},{3,1},{4,6},{5,7},{6,4},{7,5},{8,10},{9,11},{10,... | collective-permute-start | bytes 786440 | tf_op jit(solution)/shard_map/ppermute | solution.py:21
  63.1 10.9 %collective-permute-start.13 = (f32[4,128,128]{2,1,0:T(8,128)S(1)}, f32[4,128,128]{2,1,0:T(8,128)S(1)}, u32[]{:S(2)}, u32[]{:S(2)}) collective-permute-start(f32[4,128,128]{2,1,0:T(8,128)S(1)} %get-tuple-element.30), channel_id=1, source_target_pairs={{0,2},{1,3},{2,0},{3,1},{4,6},{5,7},{6,4},{7,5},{8,10},{9,11},{10,... | collective-permute-start | bytes 786440 | tf_op jit(solution)/shard_map/ppermute | solution.py:21
  63.2 1.6 %collective-permute-start.10 = (f32[4,128,128]{2,1,0:T(8,128)S(1)}, f32[4,128,128]{2,1,0:T(8,128)S(1)}, u32[]{:S(2)}, u32[]{:S(2)}) collective-permute-start(f32[4,128,128]{2,1,0:T(8,128)S(1)} %get-tuple-element.16), channel_id=1, source_target_pairs={{0,4},{4,0},{8,12},{12,8},{1,5},{5,1},{9,13},{13,9},{2,6},{6,2},{1... | collective-permute-start | bytes 786440 | tf_op jit(solution)/shard_map/ppermute | solution.py:21
  64.8 13.0 %collective-permute-start.11 = (f32[4,128,128]{2,1,0:T(8,128)S(1)}, f32[4,128,128]{2,1,0:T(8,128)S(1)}, u32[]{:S(2)}, u32[]{:S(2)}) collective-permute-start(f32[4,128,128]{2,1,0:T(8,128)S(1)} %add.107), channel_id=1, source_target_pairs={{0,8},{4,12},{8,0},{12,4},{1,9},{5,13},{9,1},{13,5},{2,10},{6,14},... | collective-permute-start | bytes 786440 | tf_op jit(solution)/shard_map/ppermute | solution.py:21
  74.0 2.2 %collective-permute-start.14 = (f32[4,128,128]{2,1,0:T(8,128)S(1)}, f32[4,128,128]{2,1,0:T(8,128)S(1)}, u32[]{:S(2)}, u32[]{:S(2)}) collective-permute-start(f32[4,128,128]{2,1,0:T(8,128)S(1)} %add.113), channel_id=1, source_target_pairs={{0,4},{4,0},{8,12},{12,8},{1,5},{5,1},{9,13},{13,9},{2,6},{6,2},{1... | collective-permute-start | bytes 786440 | tf_op jit(solution)/shard_map/ppermute | solution.py:21
  76.3 8.8 %collective-permute-start.15 = (f32[4,128,128]{2,1,0:T(8,128)S(1)}, f32[4,128,128]{2,1,0:T(8,128)S(1)}, u32[]{:S(2)}, u32[]{:S(2)}) collective-permute-start(f32[4,128,128]{2,1,0:T(8,128)S(1)} %add.115), channel_id=1, source_target_pairs={{0,8},{4,12},{8,0},{12,4},{1,9},{5,13},{9,1},{13,5},{2,10},{6,14},... | collective-permute-start | bytes 786440 | tf_op jit(solution)/shard_map/ppermute | solution.py:21
  77.9 8.5 %collective-permute-start.12 = (f32[4,128,128]{2,1,0:T(8,128)S(1)}, f32[4,128,128]{2,1,0:T(8,128)S(1)}, u32[]{:S(2)}, u32[]{:S(2)}) collective-permute-start(f32[4,128,128]{2,1,0:T(8,128)S(1)} %get-tuple-element.24), channel_id=1, source_target_pairs={{0,1},{1,0},{2,3},{3,2},{4,5},{5,4},{6,7},{7,6},{8,9},{9,8},{10,11... | collective-permute-start | bytes 786440 | tf_op jit(solution)/shard_map/ppermute | solution.py:21

commit v21 on v20

--- a/solution.py
+++ b/solution.py
@@ -62,7 +62,8 @@
     earlier_b, total_b = [], group_b
     for bit in inner_bits[1:]:
         earlier_b, total_b = subcube_step(earlier_b, total_b, "inner", bit, backward)
-    (earlier_b, total_b), _ = lax.optimization_barrier(((earlier_b, total_b), total_a))
+    if not backward:
+        (earlier_b, total_b), _ = lax.optimization_barrier(((earlier_b, total_b), total_a))
     rows_before, rows_total = [], total_b
     if not backward:
         (earlier_a, total_a), _ = lax.optimization_barrier(((earlier_a, total_a), rows_total))

time: 90 us -> 92.8 us (1.031)
  waiting for transfers between devices: 60.7 us -> 62.7 us
    ppermute x16, waiting for transfers between devices: 60.7 us -> 62.7 us  [swap(): return lax.ppermute(value, axis, [(i, i ^ bit) for i in range(count)])]
  transfers between devices with their start and end apart: 16 -> 16, of which waited for: 13 -> 11; matrix products, arithmetic and copies ran while one was open for 6% -> 6% of each run, Pallas kernels for 0% -> 0%
where the time goes in v21:
time: 92.8 us; the launch traced here: 92.6 us
  waiting for transfers between devices  62.7 us (68%)
  starting transfers between devices  15.7 us (17%)
  matrix products  4.47 us (5%)
  other arithmetic  3.2 us (3%)
  local copies, waits for them, and re-layouts  3.04 us (3%)
  Pallas kernels  2.65 us (3%)
    ppermute x16, waiting for transfers between devices, swap(): return lax.ppermute(value, axis, [(i, i ^ bit) for i in range(count)])  62.7 us
    ppermute x16, starting transfers between devices, swap(): return lax.ppermute(value, axis, [(i, i ^ bit) for i in range(count)])  15.7 us
    pallas_call x1, Pallas kernels, tail(): pl.pallas_call(functools.partial(tail_kernel, HEAD ** (-0.5)), out_shape=...  2.65 us
  transfers between devices with their start and end apart: 16, of which 11 were waited for; matrix products, arithmetic and copies ran while one was open for 6% of the time, Pallas kernels for 0%

profile of v21, /device:TPU:0, one launch (start us, length us, event | category | flops | bytes accessed | tf_op | source)
XLA Modules:
  0.0 92.6 jit_solution(9951641499710736051)
XLA Ops:
  0.7 1.2 %copy.32 = bf16[128,1024]{0,1:T(8,128)(2,1)S(1)} copy(bf16[128,1024]{1,0:T(8,128)(2,1)} %key.1) | data formatting | bytes 524288 | tf_op jit(solution)/shard_map/reshape | solution.py:122
  1.8 0.2 fusion.19
  2.1 3.1 %collective-permute-start = (f32[4,128,128]{2,1,0:T(8,128)S(1)}, f32[4,128,128]{2,1,0:T(8,128)S(1)}, u32[]{:S(2)}, u32[]{:S(2)}) collective-permute-start(f32[4,128,128]{2,1,0:T(8,128)S(1)} %get-tuple-element.32), channel_id=1, source_target_pairs={{0,1},{1,0},{2,3},{3,2},{4,5},{5,4},{6,7},{7,6},{8,9},{9,8},{10,11... | collective-permute-start | bytes 786440 | tf_op jit(solution)/shard_map/ppermute | solution.py:21
  5.2 2.6 %collective-permute-start.1 = (f32[4,128,128]{2,1,0:T(8,128)S(1)}, f32[4,128,128]{2,1,0:T(8,128)S(1)}, u32[]{:S(2)}, u32[]{:S(2)}) collective-permute-start(f32[4,128,128]{2,1,0:T(8,128)S(1)} %get-tuple-element.33), channel_id=1, source_target_pairs={{0,2},{1,3},{2,0},{3,1},{4,6},{5,7},{6,4},{7,5},{8,10},{9,11},{10,... | collective-permute-start | bytes 786440 | tf_op jit(solution)/shard_map/ppermute | solution.py:21
  7.8 9.2 %collective-permute-done = f32[4,128,128]{2,1,0:T(8,128)S(1)} collective-permute-done((f32[4,128,128]{2,1,0:T(8,128)S(1)}, f32[4,128,128]{2,1,0:T(8,128)S(1)}, u32[]{:S(2)}, u32[]{:S(2)}) %collective-permute-start) | collective-permute-done | bytes 262176 | tf_op jit(solution)/shard_map/ppermute | solution.py:21
  17.0 2.5 %collective-permute-done.1 = f32[4,128,128]{2,1,0:T(8,128)S(1)} collective-permute-done((f32[4,128,128]{2,1,0:T(8,128)S(1)}, f32[4,128,128]{2,1,0:T(8,128)S(1)}, u32[]{:S(2)}, u32[]{:S(2)}) %collective-permute-start.1) | collective-permute-done | bytes 262176 | tf_op jit(solution)/shard_map/ppermute | solution.py:21
  19.6 0.1 slice_add_fusion.1
  19.7 0.1 collective-permute-start.5
  19.7 0.4 collective-permute-start.2
  20.1 1.1 %collective-permute-done.5 = f32[4,128,128]{2,1,0:T(8,128)S(1)} collective-permute-done((f32[4,128,128]{2,1,0:T(8,128)S(1)}, f32[4,128,128]{2,1,0:T(8,128)S(1)}, u32[]{:S(2)}, u32[]{:S(2)}) %collective-permute-start.5) | collective-permute-done | bytes 262176 | tf_op jit(solution)/shard_map/ppermute | solution.py:21
  21.3 1.6 %collective-permute-start.6 = (f32[4,128,128]{2,1,0:T(8,128)S(1)}, f32[4,128,128]{2,1,0:T(8,128)S(1)}, u32[]{:S(2)}, u32[]{:S(2)}) collective-permute-start(f32[4,128,128]{2,1,0:T(8,128)S(1)} %add.96), channel_id=1, source_target_pairs={{0,8},{4,12},{8,0},{12,4},{1,9},{5,13},{9,1},{13,5},{2,10},{6,14},... | collective-permute-start | bytes 786440 | tf_op jit(solution)/shard_map/ppermute | solution.py:21
  22.8 12.0 %collective-permute-done.2 = f32[4,128,128]{2,1,0:T(8,128)S(1)} collective-permute-done((f32[4,128,128]{2,1,0:T(8,128)S(1)}, f32[4,128,128]{2,1,0:T(8,128)S(1)}, u32[]{:S(2)}, u32[]{:S(2)}) %collective-permute-start.2) | collective-permute-done | bytes 262176 | tf_op jit(solution)/shard_map/ppermute | solution.py:21
  34.9 0.1 collective-permute-start.3
  35.1 0.1 collective-permute-start.7
  35.2 1.3 %collective-permute-done.3 = f32[4,128,128]{2,1,0:T(8,128)S(1)} collective-permute-done((f32[4,128,128]{2,1,0:T(8,128)S(1)}, f32[4,128,128]{2,1,0:T(8,128)S(1)}, u32[]{:S(2)}, u32[]{:S(2)}) %collective-permute-start.3) | collective-permute-done | bytes 262176 | tf_op jit(solution)/shard_map/ppermute | solution.py:21
  36.5 1.6 %collective-permute-start.4 = (f32[4,128,128]{2,1,0:T(8,128)S(1)}, f32[4,128,128]{2,1,0:T(8,128)S(1)}, u32[]{:S(2)}, u32[]{:S(2)}) collective-permute-start(f32[4,128,128]{2,1,0:T(8,128)S(1)} %add.94), channel_id=1, source_target_pairs={{0,8},{4,12},{8,0},{12,4},{1,9},{5,13},{9,1},{13,5},{2,10},{6,14},... | collective-permute-start | bytes 786440 | tf_op jit(solution)/shard_map/ppermute | solution.py:21
  38.1 0.2 fusion.5
  38.3 5.5 %collective-permute-done.7 = f32[4,128,128]{2,1,0:T(8,128)S(1)} collective-permute-done((f32[4,128,128]{2,1,0:T(8,128)S(1)}, f32[4,128,128]{2,1,0:T(8,128)S(1)}, u32[]{:S(2)}, u32[]{:S(2)}) %collective-permute-start.7) | collective-permute-done | bytes 262176 | tf_op jit(solution)/shard_map/ppermute | solution.py:21
  43.8 1.1 %collective-permute-done.4 = f32[4,128,128]{2,1,0:T(8,128)S(1)} collective-permute-done((f32[4,128,128]{2,1,0:T(8,128)S(1)}, f32[4,128,128]{2,1,0:T(8,128)S(1)}, u32[]{:S(2)}, u32[]{:S(2)}) %collective-permute-start.4) | collective-permute-done | bytes 262176 | tf_op jit(solution)/shard_map/ppermute | solution.py:21
  44.9 0.1 add_convert_fusion.1
  45.0 0.3 fusion.3
  45.3 0.4 multiply_reduce_fusion
  45.7 0.2 copy.15
  45.9 0.7 copy-done.2
  46.7 0.2 fusion.8
  46.9 0.9 fusion.11
  47.8 0.3 convolution_bitcast_fusion
  48.1 0.7 collective-permute-start.8
  48.8 1.3 %collective-permute-start.12 = (f32[4,128,128]{2,1,0:T(8,128)S(1)}, f32[4,128,128]{2,1,0:T(8,128)S(1)}, u32[]{:S(2)}, u32[]{:S(2)}) collective-permute-start(f32[4,128,128]{2,1,0:T(8,128)S(1)} %get-tuple-element.28), channel_id=1, source_target_pairs={{0,1},{1,0},{2,3},{3,2},{4,5},{5,4},{6,7},{7,6},{8,9},{9,8},{10,11... | collective-permute-start | bytes 786440 | tf_op jit(solution)/shard_map/ppermute | solution.py:21
  50.1 12.1 %collective-permute-done.8 = f32[4,128,128]{2,1,0:T(8,128)S(1)} collective-permute-done((f32[4,128,128]{2,1,0:T(8,128)S(1)}, f32[4,128,128]{2,1,0:T(8,128)S(1)}, u32[]{:S(2)}, u32[]{:S(2)}) %collective-permute-start.8) | collective-permute-done | bytes 262176 | tf_op jit(solution)/shard_map/ppermute | solution.py:21
  62.3 0.9 collective-permute-start.13
  63.2 0.3 fusion.7
  63.5 0.3 convolution_bitcast_fusion.2
  63.9 1.6 %collective-permute-start.10 = (f32[4,128,128]{2,1,0:T(8,128)S(1)}, f32[4,128,128]{2,1,0:T(8,128)S(1)}, u32[]{:S(2)}, u32[]{:S(2)}) collective-permute-start(f32[4,128,128]{2,1,0:T(8,128)S(1)} %add.106), channel_id=1, source_target_pairs={{0,8},{4,12},{8,0},{12,4},{1,9},{5,13},{9,1},{13,5},{2,10},{6,14},... | collective-permute-start | bytes 786440 | tf_op jit(solution)/shard_map/ppermute | solution.py:21
  65.4 11.3 %collective-permute-done.13 = f32[4,128,128]{2,1,0:T(8,128)S(1)} collective-permute-done((f32[4,128,128]{2,1,0:T(8,128)S(1)}, f32[4,128,128]{2,1,0:T(8,128)S(1)}, u32[]{:S(2)}, u32[]{:S(2)}) %collective-permute-start.13) | collective-permute-done | bytes 262176 | tf_op jit(solution)/shard_map/ppermute | solution.py:21
  76.8 0.1 collective-permute-start.14
  76.9 1.1 %fusion.21.local_k = f32[8,128,128]{2,1,0:T(8,128)} fusion(bf16[8,128,128]{2,1,0:T(8,128)(2,1)S(1)} %fusion.7, bf16[128,1024]{1,0:T(8,128)(2,1)S(1)} %copy-done), kind=kOutput, calls=%fused_computation.34 | convolution fusion | flops 33554432 | bytes 1048576 | tf_op jit(solution)/shard_map/hts,thi->hsi/dot_general | solution.py:157
  78.0 1.1 %fusion.13.local_v = f32[8,128,128]{2,1,0:T(8,128)} fusion(bf16[8,128,128]{2,1,0:T(8,128)(2,1)S(1)} %fusion.5, bf16[16,8,8,128]{3,2,1,0:T(8,128)(2,1)S(1)} %get-tuple-element.24), kind=kOutput, calls=%fused_computation.26 | convolution fusion | flops 33554432 | bytes 1048576 | tf_op jit(solution)/shard_map/hts,thj->hsj/dot_general | solution.py:158
  79.1 1.6 %collective-permute-start.15 = (f32[4,128,128]{2,1,0:T(8,128)S(1)}, f32[4,128,128]{2,1,0:T(8,128)S(1)}, u32[]{:S(2)}, u32[]{:S(2)}) collective-permute-start(f32[4,128,128]{2,1,0:T(8,128)S(1)} %add.115), channel_id=1, source_target_pairs={{0,8},{4,12},{8,0},{12,4},{1,9},{5,13},{9,1},{13,5},{2,10},{6,14},... | collective-permute-start | bytes 786440 | tf_op jit(solution)/shard_map/ppermute | solution.py:21
  80.7 0.1 add_select_fusion
  80.8 0.1 collective-permute-start.11
  80.9 0.3 fusion.6
  81.2 0.9 copy.27
  82.0 5.8 %collective-permute-done.15 = f32[4,128,128]{2,1,0:T(8,128)S(1)} collective-permute-done((f32[4,128,128]{2,1,0:T(8,128)S(1)}, f32[4,128,128]{2,1,0:T(8,128)S(1)}, u32[]{:S(2)}, u32[]{:S(2)}) %collective-permute-start.15) | collective-permute-done | bytes 262176 | tf_op jit(solution)/shard_map/ppermute | solution.py:21
  87.9 0.8 select_add_fusion.upper_later
  88.6 0.6 collective-permute-done.11
  89.2 0.7 add.110.lower_later
  89.9 2.7 %shard_map.75 = (bf16[128,1024]{1,0:T(8,128)(2,1)}, bf16[128,1024]{1,0:T(8,128)(2,1)}) custom-call(f32[4,128,128]{2,1,0:T(8,128)} %add.110.lower_later, f32[4,128,128]{2,1,0:T(8,128)} %select_add_fusion.upper_later, f32[8,128,128]{2,1,0:T(8,128)} %fusion.21.local_k, f32[8,128,128]{2,1,0:T(8,128)} %fusion.13.local_v, bf16[128,1024]{1,0:T(8,128)(2,1)} %value.1, ...), custom_call_target="tpu_custom_call" | custom-call | flops 67108864 | bytes 6291456 | tf_op jit(solution)/shard_map/pallas_call | solution.py:107
  (25 shorter events, 0.6 us)
Async XLA Ops:
  0.6 37.4 %copy-start = (bf16[128,1024]{1,0:T(8,128)(2,1)S(1)}, bf16[128,1024]{1,0:T(8,128)(2,1)}, u32[]{:S(2)}) copy-start(bf16[128,1024]{1,0:T(8,128)(2,1)} %param.4) | copy-start | bytes 786436
  0.6 1.2 %copy-start.1 = (bf16[128,1024]{1,0:T(8,128)(2,1)S(1)}, bf16[128,1024]{1,0:T(8,128)(2,1)}, u32[]{:S(2)}) copy-start(bf16[128,1024]{1,0:T(8,128)(2,1)} %value.1) | copy-start | bytes 786436
  2.1 14.9 %collective-permute-start = (f32[4,128,128]{2,1,0:T(8,128)S(1)}, f32[4,128,128]{2,1,0:T(8,128)S(1)}, u32[]{:S(2)}, u32[]{:S(2)}) collective-permute-start(f32[4,128,128]{2,1,0:T(8,128)S(1)} %get-tuple-element.32), channel_id=1, source_target_pairs={{0,1},{1,0},{2,3},{3,2},{4,5},{5,4},{6,7},{7,6},{8,9},{9,8},{10,11... | collective-permute-start | bytes 786440 | tf_op jit(solution)/shard_map/ppermute | solution.py:21
  5.2 14.3 %collective-permute-start.1 = (f32[4,128,128]{2,1,0:T(8,128)S(1)}, f32[4,128,128]{2,1,0:T(8,128)S(1)}, u32[]{:S(2)}, u32[]{:S(2)}) collective-permute-start(f32[4,128,128]{2,1,0:T(8,128)S(1)} %get-tuple-element.33), channel_id=1, source_target_pairs={{0,2},{1,3},{2,0},{3,1},{4,6},{5,7},{6,4},{7,5},{8,10},{9,11},{10,... | collective-permute-start | bytes 786440 | tf_op jit(solution)/shard_map/ppermute | solution.py:21
  19.7 1.6 %collective-permute-start.5 = (f32[4,128,128]{2,1,0:T(8,128)S(1)}, f32[4,128,128]{2,1,0:T(8,128)S(1)}, u32[]{:S(2)}, u32[]{:S(2)}) collective-permute-start(f32[4,128,128]{2,1,0:T(8,128)S(1)} %get-tuple-element.10), channel_id=1, source_target_pairs={{0,4},{4,0},{8,12},{12,8},{1,5},{5,1},{9,13},{13,9},{2,6},{6,2},{1... | collective-permute-start | bytes 786440 | tf_op jit(solution)/shard_map/ppermute | solution.py:21
  19.7 15.1 %collective-permute-start.2 = (f32[4,128,128]{2,1,0:T(8,128)S(1)}, f32[4,128,128]{2,1,0:T(8,128)S(1)}, u32[]{:S(2)}, u32[]{:S(2)}) collective-permute-start(f32[4,128,128]{2,1,0:T(8,128)S(1)} %get-tuple-element.12), channel_id=1, source_target_pairs={{0,2},{1,3},{2,0},{3,1},{4,6},{5,7},{6,4},{7,5},{8,10},{9,11},{10,... | collective-permute-start | bytes 786440 | tf_op jit(solution)/shard_map/ppermute | solution.py:21
  21.3 13.7 %collective-permute-start.6 = (f32[4,128,128]{2,1,0:T(8,128)S(1)}, f32[4,128,128]{2,1,0:T(8,128)S(1)}, u32[]{:S(2)}, u32[]{:S(2)}) collective-permute-start(f32[4,128,128]{2,1,0:T(8,128)S(1)} %add.96), channel_id=1, source_target_pairs={{0,8},{4,12},{8,0},{12,4},{1,9},{5,13},{9,1},{13,5},{2,10},{6,14},... | collective-permute-start | bytes 786440 | tf_op jit(solution)/shard_map/ppermute | solution.py:21
  34.9 1.6 %collective-permute-start.3 = (f32[4,128,128]{2,1,0:T(8,128)S(1)}, f32[4,128,128]{2,1,0:T(8,128)S(1)}, u32[]{:S(2)}, u32[]{:S(2)}) collective-permute-start(f32[4,128,128]{2,1,0:T(8,128)S(1)} %add.92), channel_id=1, source_target_pairs={{0,4},{4,0},{8,12},{12,8},{1,5},{5,1},{9,13},{13,9},{2,6},{6,2},{1... | collective-permute-start | bytes 786440 | tf_op jit(solution)/shard_map/ppermute | solution.py:21
  35.1 8.7 %collective-permute-start.7 = (f32[4,128,128]{2,1,0:T(8,128)S(1)}, f32[4,128,128]{2,1,0:T(8,128)S(1)}, u32[]{:S(2)}, u32[]{:S(2)}) collective-permute-start(f32[4,128,128]{2,1,0:T(8,128)S(1)} %get-tuple-element.22), channel_id=1, source_target_pairs={{0,1},{1,0},{2,3},{3,2},{4,5},{5,4},{6,7},{7,6},{8,9},{9,8},{10,11... | collective-permute-start | bytes 786440 | tf_op jit(solution)/shard_map/ppermute | solution.py:21
  36.5 8.4 %collective-permute-start.4 = (f32[4,128,128]{2,1,0:T(8,128)S(1)}, f32[4,128,128]{2,1,0:T(8,128)S(1)}, u32[]{:S(2)}, u32[]{:S(2)}) collective-permute-start(f32[4,128,128]{2,1,0:T(8,128)S(1)} %add.94), channel_id=1, source_target_pairs={{0,8},{4,12},{8,0},{12,4},{1,9},{5,13},{9,1},{13,5},{2,10},{6,14},... | collective-permute-start | bytes 786440 | tf_op jit(solution)/shard_map/ppermute | solution.py:21
  45.7 1.0 %copy-start.2 = (bf16[128,1024]{1,0:T(8,128)(2,1)S(1)}, bf16[128,1024]{1,0:T(8,128)(2,1)}, u32[]{:S(2)}) copy-start(bf16[128,1024]{1,0:T(8,128)(2,1)} %param.7) | copy-start | bytes 786436
  48.1 14.1 %collective-permute-start.8 = (f32[4,128,128]{2,1,0:T(8,128)S(1)}, f32[4,128,128]{2,1,0:T(8,128)S(1)}, u32[]{:S(2)}, u32[]{:S(2)}) collective-permute-start(f32[4,128,128]{2,1,0:T(8,128)S(1)} %get-tuple-element.29), channel_id=1, source_target_pairs={{0,2},{1,3},{2,0},{3,1},{4,6},{5,7},{6,4},{7,5},{8,10},{9,11},{10,... | collective-permute-start | bytes 786440 | tf_op jit(solution)/shard_map/ppermute | solution.py:21
  48.8 13.4 %collective-permute-start.12 = (f32[4,128,128]{2,1,0:T(8,128)S(1)}, f32[4,128,128]{2,1,0:T(8,128)S(1)}, u32[]{:S(2)}, u32[]{:S(2)}) collective-permute-start(f32[4,128,128]{2,1,0:T(8,128)S(1)} %get-tuple-element.28), channel_id=1, source_target_pairs={{0,1},{1,0},{2,3},{3,2},{4,5},{5,4},{6,7},{7,6},{8,9},{9,8},{10,11... | collective-permute-start | bytes 786440 | tf_op jit(solution)/shard_map/ppermute | solution.py:21
  62.2 1.6 %collective-permute-start.9 = (f32[4,128,128]{2,1,0:T(8,128)S(1)}, f32[4,128,128]{2,1,0:T(8,128)S(1)}, u32[]{:S(2)}, u32[]{:S(2)}) collective-permute-start(f32[4,128,128]{2,1,0:T(8,128)S(1)} %get-tuple-element.27), channel_id=1, source_target_pairs={{0,4},{4,0},{8,12},{12,8},{1,5},{5,1},{9,13},{13,9},{2,6},{6,2},{1... | collective-permute-start | bytes 786440 | tf_op jit(solution)/shard_map/ppermute | solution.py:21
  62.3 14.5 %collective-permute-start.13 = (f32[4,128,128]{2,1,0:T(8,128)S(1)}, f32[4,128,128]{2,1,0:T(8,128)S(1)}, u32[]{:S(2)}, u32[]{:S(2)}) collective-permute-start(f32[4,128,128]{2,1,0:T(8,128)S(1)} %get-tuple-element.26), channel_id=1, source_target_pairs={{0,2},{1,3},{2,0},{3,1},{4,6},{5,7},{6,4},{7,5},{8,10},{9,11},{10,... | collective-permute-start | bytes 786440 | tf_op jit(solution)/shard_map/ppermute | solution.py:21
  63.9 16.8 %collective-permute-start.10 = (f32[4,128,128]{2,1,0:T(8,128)S(1)}, f32[4,128,128]{2,1,0:T(8,128)S(1)}, u32[]{:S(2)}, u32[]{:S(2)}) collective-permute-start(f32[4,128,128]{2,1,0:T(8,128)S(1)} %add.106), channel_id=1, source_target_pairs={{0,8},{4,12},{8,0},{12,4},{1,9},{5,13},{9,1},{13,5},{2,10},{6,14},... | collective-permute-start | bytes 786440 | tf_op jit(solution)/shard_map/ppermute | solution.py:21
  76.8 2.3 %collective-permute-start.14 = (f32[4,128,128]{2,1,0:T(8,128)S(1)}, f32[4,128,128]{2,1,0:T(8,128)S(1)}, u32[]{:S(2)}, u32[]{:S(2)}) collective-permute-start(f32[4,128,128]{2,1,0:T(8,128)S(1)} %add.113), channel_id=1, source_target_pairs={{0,4},{4,0},{8,12},{12,8},{1,5},{5,1},{9,13},{13,9},{2,6},{6,2},{1... | collective-permute-start | bytes 786440 | tf_op jit(solution)/shard_map/ppermute | solution.py:21
  79.1 8.7 %collective-permute-start.15 = (f32[4,128,128]{2,1,0:T(8,128)S(1)}, f32[4,128,128]{2,1,0:T(8,128)S(1)}, u32[]{:S(2)}, u32[]{:S(2)}) collective-permute-start(f32[4,128,128]{2,1,0:T(8,128)S(1)} %add.115), channel_id=1, source_target_pairs={{0,8},{4,12},{8,0},{12,4},{1,9},{5,13},{9,1},{13,5},{2,10},{6,14},... | collective-permute-start | bytes 786440 | tf_op jit(solution)/shard_map/ppermute | solution.py:21
  80.8 8.4 %collective-permute-start.11 = (f32[4,128,128]{2,1,0:T(8,128)S(1)}, f32[4,128,128]{2,1,0:T(8,128)S(1)}, u32[]{:S(2)}, u32[]{:S(2)}) collective-permute-start(f32[4,128,128]{2,1,0:T(8,128)S(1)} %get-tuple-element.20), channel_id=1, source_target_pairs={{0,1},{1,0},{2,3},{3,2},{4,5},{5,4},{6,7},{7,6},{8,9},{9,8},{10,11... | collective-permute-start | bytes 786440 | tf_op jit(solution)/shard_map/ppermute | solution.py:21

commit v22 on v21

--- a/solution.py
+++ b/solution.py
@@ -62,7 +62,7 @@
     earlier_b, total_b = [], group_b
     for bit in inner_bits[1:]:
         earlier_b, total_b = subcube_step(earlier_b, total_b, "inner", bit, backward)
-    if not backward:
+    if backward:
         (earlier_b, total_b), _ = lax.optimization_barrier(((earlier_b, total_b), total_a))
     rows_before, rows_total = [], total_b
     if not backward:

time: 92.8 us -> 89.4 us (0.963)
  waiting for transfers between devices: 62.7 us -> 57.8 us
  starting transfers between devices: 15.7 us -> 17.2 us
    ppermute x16, waiting for transfers between devices: 62.7 us -> 57.8 us  [swap(): return lax.ppermute(value, axis, [(i, i ^ bit) for i in range(count)])]
    ppermute x16, starting transfers between devices: 15.7 us -> 17.2 us  [swap(): return lax.ppermute(value, axis, [(i, i ^ bit) for i in range(count)])]
  transfers between devices with their start and end apart: 16 -> 16, of which waited for: 11 -> 13; matrix products, arithmetic and copies ran while one was open for 6% -> 6% of each run, Pallas kernels for 0% -> 0%
where the time goes in v22:
time: 89.4 us; the launch traced here: 89.2 us
  waiting for transfers between devices  57.8 us (65%)
  starting transfers between devices  17.2 us (19%)
  matrix products  4.48 us (5%)
  other arithmetic  3.2 us (4%)
  local copies, waits for them, and re-layouts  3.04 us (3%)
  Pallas kernels  2.65 us (3%)
    ppermute x16, waiting for transfers between devices, swap(): return lax.ppermute(value, axis, [(i, i ^ bit) for i in range(count)])  57.8 us
    ppermute x16, starting transfers between devices, swap(): return lax.ppermute(value, axis, [(i, i ^ bit) for i in range(count)])  17.2 us
    pallas_call x1, Pallas kernels, tail(): pl.pallas_call(functools.partial(tail_kernel, HEAD ** (-0.5)), out_shape=...  2.65 us
  transfers between devices with their start and end apart: 16, of which 13 were waited for; matrix products, arithmetic and copies ran while one was open for 6% of the time, Pallas kernels for 0%

profile of v22, /device:TPU:0, one launch (start us, length us, event | category | flops | bytes accessed | tf_op | source)
XLA Modules:
  0.0 89.2 jit_solution(7572907550117843115)
XLA Ops:
  0.7 1.2 %copy.32 = bf16[128,1024]{0,1:T(8,128)(2,1)S(1)} copy(bf16[128,1024]{1,0:T(8,128)(2,1)} %key.1) | data formatting | bytes 524288 | tf_op jit(solution)/shard_map/reshape | solution.py:122
  1.8 0.2 fusion.19
  2.1 4.1 %collective-permute-start.1 = (f32[4,128,128]{2,1,0:T(8,128)S(1)}, f32[4,128,128]{2,1,0:T(8,128)S(1)}, u32[]{:S(2)}, u32[]{:S(2)}) collective-permute-start(f32[4,128,128]{2,1,0:T(8,128)S(1)} %get-tuple-element.33), channel_id=1, source_target_pairs={{0,2},{1,3},{2,0},{3,1},{4,6},{5,7},{6,4},{7,5},{8,10},{9,11},{10,... | collective-permute-start | bytes 786440 | tf_op jit(solution)/shard_map/ppermute | solution.py:21
  6.2 1.6 %collective-permute-start = (f32[4,128,128]{2,1,0:T(8,128)S(1)}, f32[4,128,128]{2,1,0:T(8,128)S(1)}, u32[]{:S(2)}, u32[]{:S(2)}) collective-permute-start(f32[4,128,128]{2,1,0:T(8,128)S(1)} %get-tuple-element.32), channel_id=1, source_target_pairs={{0,1},{1,0},{2,3},{3,2},{4,5},{5,4},{6,7},{7,6},{8,9},{9,8},{10,11... | collective-permute-start | bytes 786440 | tf_op jit(solution)/shard_map/ppermute | solution.py:21
  7.8 10.4 %collective-permute-done.1 = f32[4,128,128]{2,1,0:T(8,128)S(1)} collective-permute-done((f32[4,128,128]{2,1,0:T(8,128)S(1)}, f32[4,128,128]{2,1,0:T(8,128)S(1)}, u32[]{:S(2)}, u32[]{:S(2)}) %collective-permute-start.1) | collective-permute-done | bytes 262176 | tf_op jit(solution)/shard_map/ppermute | solution.py:21
  18.3 0.2 collective-permute-done
  18.5 0.1 collective-permute-start.5
  18.6 1.4 %collective-permute-start.2 = (f32[4,128,128]{2,1,0:T(8,128)S(1)}, f32[4,128,128]{2,1,0:T(8,128)S(1)}, u32[]{:S(2)}, u32[]{:S(2)}) collective-permute-start(f32[4,128,128]{2,1,0:T(8,128)S(1)} %get-tuple-element.11), channel_id=1, source_target_pairs={{0,2},{1,3},{2,0},{3,1},{4,6},{5,7},{6,4},{7,5},{8,10},{9,11},{10,... | collective-permute-start | bytes 786440 | tf_op jit(solution)/shard_map/ppermute | solution.py:21
  20.0 0.1 collective-permute-done.5
  20.2 1.6 %collective-permute-start.6 = (f32[4,128,128]{2,1,0:T(8,128)S(1)}, f32[4,128,128]{2,1,0:T(8,128)S(1)}, u32[]{:S(2)}, u32[]{:S(2)}) collective-permute-start(f32[4,128,128]{2,1,0:T(8,128)S(1)} %add.96), channel_id=1, source_target_pairs={{0,8},{4,12},{8,0},{12,4},{1,9},{5,13},{9,1},{13,5},{2,10},{6,14},... | collective-permute-start | bytes 786440 | tf_op jit(solution)/shard_map/ppermute | solution.py:21
  21.8 12.1 %collective-permute-done.2 = f32[4,128,128]{2,1,0:T(8,128)S(1)} collective-permute-done((f32[4,128,128]{2,1,0:T(8,128)S(1)}, f32[4,128,128]{2,1,0:T(8,128)S(1)}, u32[]{:S(2)}, u32[]{:S(2)}) %collective-permute-start.2) | collective-permute-done | bytes 262176 | tf_op jit(solution)/shard_map/ppermute | solution.py:21
  33.9 0.1 collective-permute-start.3
  34.0 0.1 collective-permute-start.7
  34.1 1.3 %collective-permute-done.3 = f32[4,128,128]{2,1,0:T(8,128)S(1)} collective-permute-done((f32[4,128,128]{2,1,0:T(8,128)S(1)}, f32[4,128,128]{2,1,0:T(8,128)S(1)}, u32[]{:S(2)}, u32[]{:S(2)}) %collective-permute-start.3) | collective-permute-done | bytes 262176 | tf_op jit(solution)/shard_map/ppermute | solution.py:21
  35.5 1.6 %collective-permute-start.4 = (f32[4,128,128]{2,1,0:T(8,128)S(1)}, f32[4,128,128]{2,1,0:T(8,128)S(1)}, u32[]{:S(2)}, u32[]{:S(2)}) collective-permute-start(f32[4,128,128]{2,1,0:T(8,128)S(1)} %add.94), channel_id=1, source_target_pairs={{0,8},{4,12},{8,0},{12,4},{1,9},{5,13},{9,1},{13,5},{2,10},{6,14},... | collective-permute-start | bytes 786440 | tf_op jit(solution)/shard_map/ppermute | solution.py:21
  37.1 0.2 fusion.5
  37.3 5.4 %collective-permute-done.7 = f32[4,128,128]{2,1,0:T(8,128)S(1)} collective-permute-done((f32[4,128,128]{2,1,0:T(8,128)S(1)}, f32[4,128,128]{2,1,0:T(8,128)S(1)}, u32[]{:S(2)}, u32[]{:S(2)}) %collective-permute-start.7) | collective-permute-done | bytes 262176 | tf_op jit(solution)/shard_map/ppermute | solution.py:21
  42.8 1.1 %collective-permute-done.4 = f32[4,128,128]{2,1,0:T(8,128)S(1)} collective-permute-done((f32[4,128,128]{2,1,0:T(8,128)S(1)}, f32[4,128,128]{2,1,0:T(8,128)S(1)}, u32[]{:S(2)}, u32[]{:S(2)}) %collective-permute-start.4) | collective-permute-done | bytes 262176 | tf_op jit(solution)/shard_map/ppermute | solution.py:21
  43.9 0.1 add_convert_fusion.1
  44.0 0.3 fusion.3
  44.3 0.4 multiply_reduce_fusion
  44.7 0.2 copy.15
  44.9 0.7 copy-done.2
  45.6 0.2 fusion.8
  45.9 0.9 %fusion.11 = (bf16[16,8,8,128]{3,2,1,0:T(8,128)(2,1)S(1)}, bf16[128,1024]{1,0:T(8,128)(2,1)}) fusion(f32[128,1024]{1,0:T(8,128)S(1)} %copy.15, bf16[128,1024]{1,0:T(8,128)(2,1)S(1)} %copy-done.2, f32[128]{0:T(128)S(1)} %broadcast_multiply_fusion, f32[128]{0:T(128)S(1)} %add_rsqrt_fusion), kind=kLoop, calls=%fused_computation.24 | loop fusion | flops 917504 | bytes 1311744
  46.8 0.3 convolution_bitcast_fusion
  47.1 0.8 collective-permute-start.9
  47.9 2.1 %collective-permute-start.8 = (f32[4,128,128]{2,1,0:T(8,128)S(1)}, f32[4,128,128]{2,1,0:T(8,128)S(1)}, u32[]{:S(2)}, u32[]{:S(2)}) collective-permute-start(f32[4,128,128]{2,1,0:T(8,128)S(1)} %get-tuple-element.29), channel_id=1, source_target_pairs={{0,2},{1,3},{2,0},{3,1},{4,6},{5,7},{6,4},{7,5},{8,10},{9,11},{10,... | collective-permute-start | bytes 786440 | tf_op jit(solution)/shard_map/ppermute | solution.py:21
  50.0 9.9 %collective-permute-done.9 = f32[4,128,128]{2,1,0:T(8,128)S(1)} collective-permute-done((f32[4,128,128]{2,1,0:T(8,128)S(1)}, f32[4,128,128]{2,1,0:T(8,128)S(1)}, u32[]{:S(2)}, u32[]{:S(2)}) %collective-permute-start.9) | collective-permute-done | bytes 262176 | tf_op jit(solution)/shard_map/ppermute | solution.py:21
  59.9 1.9 %collective-permute-done.8 = f32[4,128,128]{2,1,0:T(8,128)S(1)} collective-permute-done((f32[4,128,128]{2,1,0:T(8,128)S(1)}, f32[4,128,128]{2,1,0:T(8,128)S(1)}, u32[]{:S(2)}, u32[]{:S(2)}) %collective-permute-start.8) | collective-permute-done | bytes 262176 | tf_op jit(solution)/shard_map/ppermute | solution.py:21
  61.8 0.4 collective-permute-start.13
  62.2 0.3 fusion.7
  62.5 0.3 convolution_bitcast_fusion.2
  62.8 0.9 %collective-permute-done.10 = f32[4,128,128]{2,1,0:T(8,128)S(1)} collective-permute-done((f32[4,128,128]{2,1,0:T(8,128)S(1)}, f32[4,128,128]{2,1,0:T(8,128)S(1)}, u32[]{:S(2)}, u32[]{:S(2)}) %collective-permute-start.10) | collective-permute-done | bytes 262176 | tf_op jit(solution)/shard_map/ppermute | solution.py:21
  63.8 1.6 %collective-permute-start.11 = (f32[4,128,128]{2,1,0:T(8,128)S(1)}, f32[4,128,128]{2,1,0:T(8,128)S(1)}, u32[]{:S(2)}, u32[]{:S(2)}) collective-permute-start(f32[4,128,128]{2,1,0:T(8,128)S(1)} %add.107), channel_id=1, source_target_pairs={{0,8},{4,12},{8,0},{12,4},{1,9},{5,13},{9,1},{13,5},{2,10},{6,14},... | collective-permute-start | bytes 786440 | tf_op jit(solution)/shard_map/ppermute | solution.py:21
  65.4 7.9 %collective-permute-done.13 = f32[4,128,128]{2,1,0:T(8,128)S(1)} collective-permute-done((f32[4,128,128]{2,1,0:T(8,128)S(1)}, f32[4,128,128]{2,1,0:T(8,128)S(1)}, u32[]{:S(2)}, u32[]{:S(2)}) %collective-permute-start.13) | collective-permute-done | bytes 262176 | tf_op jit(solution)/shard_map/ppermute | solution.py:21
  73.4 0.1 collective-permute-start.14
  73.4 1.1 %fusion.21.local_k = f32[8,128,128]{2,1,0:T(8,128)} fusion(bf16[8,128,128]{2,1,0:T(8,128)(2,1)S(1)} %fusion.7, bf16[128,1024]{1,0:T(8,128)(2,1)S(1)} %copy-done), kind=kOutput, calls=%fused_computation.34 | convolution fusion | flops 33554432 | bytes 1048576 | tf_op jit(solution)/shard_map/hts,thi->hsi/dot_general | solution.py:157
  74.5 1.1 %fusion.13.local_v = f32[8,128,128]{2,1,0:T(8,128)} fusion(bf16[8,128,128]{2,1,0:T(8,128)(2,1)S(1)} %fusion.5, bf16[16,8,8,128]{3,2,1,0:T(8,128)(2,1)S(1)} %get-tuple-element.24), kind=kOutput, calls=%fused_computation.26 | convolution fusion | flops 33554432 | bytes 1048576 | tf_op jit(solution)/shard_map/hts,thj->hsj/dot_general | solution.py:158
  75.7 1.6 %collective-permute-start.15 = (f32[4,128,128]{2,1,0:T(8,128)S(1)}, f32[4,128,128]{2,1,0:T(8,128)S(1)}, u32[]{:S(2)}, u32[]{:S(2)}) collective-permute-start(f32[4,128,128]{2,1,0:T(8,128)S(1)} %add.115), channel_id=1, source_target_pairs={{0,8},{4,12},{8,0},{12,4},{1,9},{5,13},{9,1},{13,5},{2,10},{6,14},... | collective-permute-start | bytes 786440 | tf_op jit(solution)/shard_map/ppermute | solution.py:21
  77.3 0.1 collective-permute-start.12
  77.4 0.3 fusion.6
  77.7 0.9 copy.27
  78.5 5.9 %collective-permute-done.15 = f32[4,128,128]{2,1,0:T(8,128)S(1)} collective-permute-done((f32[4,128,128]{2,1,0:T(8,128)S(1)}, f32[4,128,128]{2,1,0:T(8,128)S(1)}, u32[]{:S(2)}, u32[]{:S(2)}) %collective-permute-start.15) | collective-permute-done | bytes 262176 | tf_op jit(solution)/shard_map/ppermute | solution.py:21
  84.4 0.8 select_add_fusion.upper_later
  85.2 0.6 collective-permute-done.12
  85.8 0.7 add.111.lower_later
  86.5 2.7 %shard_map.75 = (bf16[128,1024]{1,0:T(8,128)(2,1)}, bf16[128,1024]{1,0:T(8,128)(2,1)}) custom-call(f32[4,128,128]{2,1,0:T(8,128)} %add.111.lower_later, f32[4,128,128]{2,1,0:T(8,128)} %select_add_fusion.upper_later, f32[8,128,128]{2,1,0:T(8,128)} %fusion.21.local_k, f32[8,128,128]{2,1,0:T(8,128)} %fusion.13.local_v, bf16[128,1024]{1,0:T(8,128)(2,1)} %value.1, ...), custom_call_target="tpu_custom_call" | custom-call | flops 67108864 | bytes 6291456 | tf_op jit(solution)/shard_map/pallas_call | solution.py:107
  (25 shorter events, 0.6 us)
Async XLA Ops:
  0.6 36.5 %copy-start = (bf16[128,1024]{1,0:T(8,128)(2,1)S(1)}, bf16[128,1024]{1,0:T(8,128)(2,1)}, u32[]{:S(2)}) copy-start(bf16[128,1024]{1,0:T(8,128)(2,1)} %param.4) | copy-start | bytes 786436
  0.6 1.2 %copy-start.1 = (bf16[128,1024]{1,0:T(8,128)(2,1)S(1)}, bf16[128,1024]{1,0:T(8,128)(2,1)}, u32[]{:S(2)}) copy-start(bf16[128,1024]{1,0:T(8,128)(2,1)} %value.1) | copy-start | bytes 786436
  2.1 16.2 %collective-permute-start.1 = (f32[4,128,128]{2,1,0:T(8,128)S(1)}, f32[4,128,128]{2,1,0:T(8,128)S(1)}, u32[]{:S(2)}, u32[]{:S(2)}) collective-permute-start(f32[4,128,128]{2,1,0:T(8,128)S(1)} %get-tuple-element.33), channel_id=1, source_target_pairs={{0,2},{1,3},{2,0},{3,1},{4,6},{5,7},{6,4},{7,5},{8,10},{9,11},{10,... | collective-permute-start | bytes 786440 | tf_op jit(solution)/shard_map/ppermute | solution.py:21
  6.2 12.2 %collective-permute-start = (f32[4,128,128]{2,1,0:T(8,128)S(1)}, f32[4,128,128]{2,1,0:T(8,128)S(1)}, u32[]{:S(2)}, u32[]{:S(2)}) collective-permute-start(f32[4,128,128]{2,1,0:T(8,128)S(1)} %get-tuple-element.32), channel_id=1, source_target_pairs={{0,1},{1,0},{2,3},{3,2},{4,5},{5,4},{6,7},{7,6},{8,9},{9,8},{10,11... | collective-permute-start | bytes 786440 | tf_op jit(solution)/shard_map/ppermute | solution.py:21
  18.5 1.6 %collective-permute-start.5 = (f32[4,128,128]{2,1,0:T(8,128)S(1)}, f32[4,128,128]{2,1,0:T(8,128)S(1)}, u32[]{:S(2)}, u32[]{:S(2)}) collective-permute-start(f32[4,128,128]{2,1,0:T(8,128)S(1)} %get-tuple-element.31), channel_id=1, source_target_pairs={{0,4},{4,0},{8,12},{12,8},{1,5},{5,1},{9,13},{13,9},{2,6},{6,2},{1... | collective-permute-start | bytes 786440 | tf_op jit(solution)/shard_map/ppermute | solution.py:21
  18.6 15.2 %collective-permute-start.2 = (f32[4,128,128]{2,1,0:T(8,128)S(1)}, f32[4,128,128]{2,1,0:T(8,128)S(1)}, u32[]{:S(2)}, u32[]{:S(2)}) collective-permute-start(f32[4,128,128]{2,1,0:T(8,128)S(1)} %get-tuple-element.11), channel_id=1, source_target_pairs={{0,2},{1,3},{2,0},{3,1},{4,6},{5,7},{6,4},{7,5},{8,10},{9,11},{10,... | collective-permute-start | bytes 786440 | tf_op jit(solution)/shard_map/ppermute | solution.py:21
  20.2 13.8 %collective-permute-start.6 = (f32[4,128,128]{2,1,0:T(8,128)S(1)}, f32[4,128,128]{2,1,0:T(8,128)S(1)}, u32[]{:S(2)}, u32[]{:S(2)}) collective-permute-start(f32[4,128,128]{2,1,0:T(8,128)S(1)} %add.96), channel_id=1, source_target_pairs={{0,8},{4,12},{8,0},{12,4},{1,9},{5,13},{9,1},{13,5},{2,10},{6,14},... | collective-permute-start | bytes 786440 | tf_op jit(solution)/shard_map/ppermute | solution.py:21
  33.9 1.6 %collective-permute-start.3 = (f32[4,128,128]{2,1,0:T(8,128)S(1)}, f32[4,128,128]{2,1,0:T(8,128)S(1)}, u32[]{:S(2)}, u32[]{:S(2)}) collective-permute-start(f32[4,128,128]{2,1,0:T(8,128)S(1)} %add.92), channel_id=1, source_target_pairs={{0,4},{4,0},{8,12},{12,8},{1,5},{5,1},{9,13},{13,9},{2,6},{6,2},{1... | collective-permute-start | bytes 786440 | tf_op jit(solution)/shard_map/ppermute | solution.py:21
  34.0 8.8 %collective-permute-start.7 = (f32[4,128,128]{2,1,0:T(8,128)S(1)}, f32[4,128,128]{2,1,0:T(8,128)S(1)}, u32[]{:S(2)}, u32[]{:S(2)}) collective-permute-start(f32[4,128,128]{2,1,0:T(8,128)S(1)} %get-tuple-element.22), channel_id=1, source_target_pairs={{0,1},{1,0},{2,3},{3,2},{4,5},{5,4},{6,7},{7,6},{8,9},{9,8},{10,11... | collective-permute-start | bytes 786440 | tf_op jit(solution)/shard_map/ppermute | solution.py:21
  35.5 8.4 %collective-permute-start.4 = (f32[4,128,128]{2,1,0:T(8,128)S(1)}, f32[4,128,128]{2,1,0:T(8,128)S(1)}, u32[]{:S(2)}, u32[]{:S(2)}) collective-permute-start(f32[4,128,128]{2,1,0:T(8,128)S(1)} %add.94), channel_id=1, source_target_pairs={{0,8},{4,12},{8,0},{12,4},{1,9},{5,13},{9,1},{13,5},{2,10},{6,14},... | collective-permute-start | bytes 786440 | tf_op jit(solution)/shard_map/ppermute | solution.py:21
  44.7 1.0 %copy-start.2 = (bf16[128,1024]{1,0:T(8,128)(2,1)S(1)}, bf16[128,1024]{1,0:T(8,128)(2,1)}, u32[]{:S(2)}) copy-start(bf16[128,1024]{1,0:T(8,128)(2,1)} %param.7) | copy-start | bytes 786436
  47.1 12.8 %collective-permute-start.9 = (f32[4,128,128]{2,1,0:T(8,128)S(1)}, f32[4,128,128]{2,1,0:T(8,128)S(1)}, u32[]{:S(2)}, u32[]{:S(2)}) collective-permute-start(f32[4,128,128]{2,1,0:T(8,128)S(1)} %get-tuple-element.28), channel_id=1, source_target_pairs={{0,1},{1,0},{2,3},{3,2},{4,5},{5,4},{6,7},{7,6},{8,9},{9,8},{10,11... | collective-permute-start | bytes 786440 | tf_op jit(solution)/shard_map/ppermute | solution.py:21
  47.9 13.8 %collective-permute-start.8 = (f32[4,128,128]{2,1,0:T(8,128)S(1)}, f32[4,128,128]{2,1,0:T(8,128)S(1)}, u32[]{:S(2)}, u32[]{:S(2)}) collective-permute-start(f32[4,128,128]{2,1,0:T(8,128)S(1)} %get-tuple-element.29), channel_id=1, source_target_pairs={{0,2},{1,3},{2,0},{3,1},{4,6},{5,7},{6,4},{7,5},{8,10},{9,11},{10,... | collective-permute-start | bytes 786440 | tf_op jit(solution)/shard_map/ppermute | solution.py:21
  61.8 11.5 %collective-permute-start.13 = (f32[4,128,128]{2,1,0:T(8,128)S(1)}, f32[4,128,128]{2,1,0:T(8,128)S(1)}, u32[]{:S(2)}, u32[]{:S(2)}) collective-permute-start(f32[4,128,128]{2,1,0:T(8,128)S(1)} %get-tuple-element.26), channel_id=1, source_target_pairs={{0,2},{1,3},{2,0},{3,1},{4,6},{5,7},{6,4},{7,5},{8,10},{9,11},{10,... | collective-permute-start | bytes 786440 | tf_op jit(solution)/shard_map/ppermute | solution.py:21
  62.2 1.5 %collective-permute-start.10 = (f32[4,128,128]{2,1,0:T(8,128)S(1)}, f32[4,128,128]{2,1,0:T(8,128)S(1)}, u32[]{:S(2)}, u32[]{:S(2)}) collective-permute-start(f32[4,128,128]{2,1,0:T(8,128)S(1)} %get-tuple-element.12), channel_id=1, source_target_pairs={{0,4},{4,0},{8,12},{12,8},{1,5},{5,1},{9,13},{13,9},{2,6},{6,2},{1... | collective-permute-start | bytes 786440 | tf_op jit(solution)/shard_map/ppermute | solution.py:21
  63.8 13.4 %collective-permute-start.11 = (f32[4,128,128]{2,1,0:T(8,128)S(1)}, f32[4,128,128]{2,1,0:T(8,128)S(1)}, u32[]{:S(2)}, u32[]{:S(2)}) collective-permute-start(f32[4,128,128]{2,1,0:T(8,128)S(1)} %add.107), channel_id=1, source_target_pairs={{0,8},{4,12},{8,0},{12,4},{1,9},{5,13},{9,1},{13,5},{2,10},{6,14},... | collective-permute-start | bytes 786440 | tf_op jit(solution)/shard_map/ppermute | solution.py:21
  73.4 2.3 %collective-permute-start.14 = (f32[4,128,128]{2,1,0:T(8,128)S(1)}, f32[4,128,128]{2,1,0:T(8,128)S(1)}, u32[]{:S(2)}, u32[]{:S(2)}) collective-permute-start(f32[4,128,128]{2,1,0:T(8,128)S(1)} %add.113), channel_id=1, source_target_pairs={{0,4},{4,0},{8,12},{12,8},{1,5},{5,1},{9,13},{13,9},{2,6},{6,2},{1... | collective-permute-start | bytes 786440 | tf_op jit(solution)/shard_map/ppermute | solution.py:21
  75.7 8.8 %collective-permute-start.15 = (f32[4,128,128]{2,1,0:T(8,128)S(1)}, f32[4,128,128]{2,1,0:T(8,128)S(1)}, u32[]{:S(2)}, u32[]{:S(2)}) collective-permute-start(f32[4,128,128]{2,1,0:T(8,128)S(1)} %add.115), channel_id=1, source_target_pairs={{0,8},{4,12},{8,0},{12,4},{1,9},{5,13},{9,1},{13,5},{2,10},{6,14},... | collective-permute-start | bytes 786440 | tf_op jit(solution)/shard_map/ppermute | solution.py:21
  77.3 8.5 %collective-permute-start.12 = (f32[4,128,128]{2,1,0:T(8,128)S(1)}, f32[4,128,128]{2,1,0:T(8,128)S(1)}, u32[]{:S(2)}, u32[]{:S(2)}) collective-permute-start(f32[4,128,128]{2,1,0:T(8,128)S(1)} %get-tuple-element.20), channel_id=1, source_target_pairs={{0,1},{1,0},{2,3},{3,2},{4,5},{5,4},{6,7},{7,6},{8,9},{9,8},{10,11... | collective-permute-start | bytes 786440 | tf_op jit(solution)/shard_map/ppermute | solution.py:21

commit v23 on v22

--- a/solution.py
+++ b/solution.py
@@ -75,8 +75,9 @@
         earlier_a, total_a = subcube_step(earlier_a, total_a, "outer", bit, backward)
     low = inner_bits[0]
     counted = partner_counts("inner", low, backward)
-    known = added(rows_before + earlier_b, group_b)
-    sent = jnp.where(counted, known, known + group_b)
+    ready = lax.optimization_barrier(added(rows_before[:-1] + earlier_b, group_b))
+    known = ready + rows_before[-1]
+    sent = jnp.where(counted, ready, ready + group_b) + rows_before[-1]
     earlier_a = added(earlier_a, group_a)
     got_b = swap(sent, "inner", low)
     if backward:

time: 89.4 us -> 92.6 us (1.036)
  other arithmetic: 3.2 us -> 6.04 us
  waiting for transfers between devices: 57.8 us -> 60.1 us
  starting transfers between devices: 17.2 us -> 15.3 us
    ppermute x16, waiting for transfers between devices: 57.8 us -> 60.1 us  [swap(): return lax.ppermute(value, axis, [(i, i ^ bit) for i in range(count)])]
    add x8, other arithmetic: 0.33 us -> 2.25 us  [subcube_step(): return (earlier + [jnp.where(counted, got, 0.0)], total + got)]
    ppermute x16, starting transfers between devices: 17.2 us -> 15.3 us  [swap(): return lax.ppermute(value, axis, [(i, i ^ bit) for i in range(count)])]
    add x1, other arithmetic: 0.73 us -> 1.69 us  [per_device(): lower_known + lower_got]
  transfers between devices with their start and end apart: 16 -> 16, of which waited for: 13 -> 13; matrix products, arithmetic and copies ran while one was open for 6% -> 8% of each run, Pallas kernels for 0% -> 0%
where the time goes in v23:
time: 92.6 us; the launch traced here: 92.4 us
  waiting for transfers between devices  60.1 us (65%)
  starting transfers between devices  15.3 us (17%)
  other arithmetic  6.04 us (7%)
  matrix products  4.46 us (5%)
  local copies, waits for them, and re-layouts  3.04 us (3%)
  Pallas kernels  2.65 us (3%)
    ppermute x16, waiting for transfers between devices, swap(): return lax.ppermute(value, axis, [(i, i ^ bit) for i in range(count)])  60.1 us
    ppermute x16, starting transfers between devices, swap(): return lax.ppermute(value, axis, [(i, i ^ bit) for i in range(count)])  15.3 us
    pallas_call x1, Pallas kernels, tail(): pl.pallas_call(functools.partial(tail_kernel, HEAD ** (-0.5)), out_shape=...  2.65 us
    add x8, other arithmetic, subcube_step(): return (earlier + [jnp.where(counted, got, 0.0)], total + got)  2.25 us
  transfers between devices with their start and end apart: 16, of which 13 were waited for; matrix products, arithmetic and copies ran while one was open for 8% of the time, Pallas kernels for 0%

profile of v23, /device:TPU:0, one launch (start us, length us, event | category | flops | bytes accessed | tf_op | source)
XLA Modules:
  0.0 92.4 jit_solution(7743477413879612238)
XLA Ops:
  0.7 1.2 %copy.32 = bf16[128,1024]{0,1:T(8,128)(2,1)S(1)} copy(bf16[128,1024]{1,0:T(8,128)(2,1)} %key.1) | data formatting | bytes 524288 | tf_op jit(solution)/shard_map/reshape | solution.py:123
  1.8 0.2 fusion.21
  2.1 3.1 %collective-permute-start = (f32[4,128,128]{2,1,0:T(8,128)S(1)}, f32[4,128,128]{2,1,0:T(8,128)S(1)}, u32[]{:S(2)}, u32[]{:S(2)}) collective-permute-start(f32[4,128,128]{2,1,0:T(8,128)S(1)} %get-tuple-element.28), channel_id=1, source_target_pairs={{0,1},{1,0},{2,3},{3,2},{4,5},{5,4},{6,7},{7,6},{8,9},{9,8},{10,11... | collective-permute-start | bytes 786440 | tf_op jit(solution)/shard_map/ppermute | solution.py:21
  5.2 2.6 %collective-permute-start.1 = (f32[4,128,128]{2,1,0:T(8,128)S(1)}, f32[4,128,128]{2,1,0:T(8,128)S(1)}, u32[]{:S(2)}, u32[]{:S(2)}) collective-permute-start(f32[4,128,128]{2,1,0:T(8,128)S(1)} %get-tuple-element.29), channel_id=1, source_target_pairs={{0,2},{1,3},{2,0},{3,1},{4,6},{5,7},{6,4},{7,5},{8,10},{9,11},{10,... | collective-permute-start | bytes 786440 | tf_op jit(solution)/shard_map/ppermute | solution.py:21
  7.8 9.2 %collective-permute-done = f32[4,128,128]{2,1,0:T(8,128)S(1)} collective-permute-done((f32[4,128,128]{2,1,0:T(8,128)S(1)}, f32[4,128,128]{2,1,0:T(8,128)S(1)}, u32[]{:S(2)}, u32[]{:S(2)}) %collective-permute-start) | collective-permute-done | bytes 262176 | tf_op jit(solution)/shard_map/ppermute | solution.py:21
  17.0 2.5 %collective-permute-done.1 = f32[4,128,128]{2,1,0:T(8,128)S(1)} collective-permute-done((f32[4,128,128]{2,1,0:T(8,128)S(1)}, f32[4,128,128]{2,1,0:T(8,128)S(1)}, u32[]{:S(2)}, u32[]{:S(2)}) %collective-permute-start.1) | collective-permute-done | bytes 262176 | tf_op jit(solution)/shard_map/ppermute | solution.py:21
  19.7 0.4 collective-permute-start.2
  20.1 1.1 %collective-permute-done.5 = f32[4,128,128]{2,1,0:T(8,128)S(1)} collective-permute-done((f32[4,128,128]{2,1,0:T(8,128)S(1)}, f32[4,128,128]{2,1,0:T(8,128)S(1)}, u32[]{:S(2)}, u32[]{:S(2)}) %collective-permute-start.5) | collective-permute-done | bytes 262176 | tf_op jit(solution)/shard_map/ppermute | solution.py:21
  21.3 1.6 %collective-permute-start.6 = (f32[4,128,128]{2,1,0:T(8,128)S(1)}, f32[4,128,128]{2,1,0:T(8,128)S(1)}, u32[]{:S(2)}, u32[]{:S(2)}) collective-permute-start(f32[4,128,128]{2,1,0:T(8,128)S(1)} %get-tuple-element.34), channel_id=1, source_target_pairs={{0,8},{4,12},{8,0},{12,4},{1,9},{5,13},{9,1},{13,5},{2,10},{6,14},... | collective-permute-start | bytes 786440 | tf_op jit(solution)/shard_map/ppermute | solution.py:21
  22.8 12.0 %collective-permute-done.2 = f32[4,128,128]{2,1,0:T(8,128)S(1)} collective-permute-done((f32[4,128,128]{2,1,0:T(8,128)S(1)}, f32[4,128,128]{2,1,0:T(8,128)S(1)}, u32[]{:S(2)}, u32[]{:S(2)}) %collective-permute-start.2) | collective-permute-done | bytes 262176 | tf_op jit(solution)/shard_map/ppermute | solution.py:21
  34.8 0.1 collective-permute-start.3
  35.1 1.3 %collective-permute-done.3 = f32[4,128,128]{2,1,0:T(8,128)S(1)} collective-permute-done((f32[4,128,128]{2,1,0:T(8,128)S(1)}, f32[4,128,128]{2,1,0:T(8,128)S(1)}, u32[]{:S(2)}, u32[]{:S(2)}) %collective-permute-start.3) | collective-permute-done | bytes 262176 | tf_op jit(solution)/shard_map/ppermute | solution.py:21
  36.5 1.6 %collective-permute-start.4 = (f32[4,128,128]{2,1,0:T(8,128)S(1)}, f32[4,128,128]{2,1,0:T(8,128)S(1)}, u32[]{:S(2)}, u32[]{:S(2)}) collective-permute-start(f32[4,128,128]{2,1,0:T(8,128)S(1)} %add.100), channel_id=1, source_target_pairs={{0,8},{4,12},{8,0},{12,4},{1,9},{5,13},{9,1},{13,5},{2,10},{6,14},... | collective-permute-start | bytes 786440 | tf_op jit(solution)/shard_map/ppermute | solution.py:21
  38.0 0.2 fusion.5
  38.3 5.5 %collective-permute-done.7 = f32[4,128,128]{2,1,0:T(8,128)S(1)} collective-permute-done((f32[4,128,128]{2,1,0:T(8,128)S(1)}, f32[4,128,128]{2,1,0:T(8,128)S(1)}, u32[]{:S(2)}, u32[]{:S(2)}) %collective-permute-start.7) | collective-permute-done | bytes 262176 | tf_op jit(solution)/shard_map/ppermute | solution.py:21
  43.8 1.1 %collective-permute-done.4 = f32[4,128,128]{2,1,0:T(8,128)S(1)} collective-permute-done((f32[4,128,128]{2,1,0:T(8,128)S(1)}, f32[4,128,128]{2,1,0:T(8,128)S(1)}, u32[]{:S(2)}, u32[]{:S(2)}) %collective-permute-start.4) | collective-permute-done | bytes 262176 | tf_op jit(solution)/shard_map/ppermute | solution.py:21
  44.9 0.1 add_convert_fusion.1
  45.0 0.3 fusion.3
  45.3 0.4 multiply_reduce_fusion
  45.7 0.2 copy.15
  45.9 0.7 copy-done.2
  46.6 0.2 fusion.8
  46.8 0.9 fusion.13
  47.7 0.3 convolution_bitcast_fusion
  48.1 0.8 collective-permute-start.9
  48.9 1.2 %collective-permute-start.8 = (f32[4,128,128]{2,1,0:T(8,128)S(1)}, f32[4,128,128]{2,1,0:T(8,128)}, u32[]{:S(2)}, u32[]{:S(2)}) collective-permute-start(f32[4,128,128]{2,1,0:T(8,128)S(1)} %get-tuple-element.25), channel_id=1, source_target_pairs={{0,2},{1,3},{2,0},{3,1},{4,6},{5,7},{6,4},{7,5},{8,10},{9,11},{10,... | collective-permute-start | bytes 786440 | tf_op jit(solution)/shard_map/ppermute | solution.py:21
  50.0 10.0 %collective-permute-done.9 = f32[4,128,128]{2,1,0:T(8,128)S(1)} collective-permute-done((f32[4,128,128]{2,1,0:T(8,128)S(1)}, f32[4,128,128]{2,1,0:T(8,128)S(1)}, u32[]{:S(2)}, u32[]{:S(2)}) %collective-permute-start.9) | collective-permute-done | bytes 262176 | tf_op jit(solution)/shard_map/ppermute | solution.py:21
  60.0 2.8 %collective-permute-done.8 = f32[4,128,128]{2,1,0:T(8,128)} collective-permute-done((f32[4,128,128]{2,1,0:T(8,128)S(1)}, f32[4,128,128]{2,1,0:T(8,128)}, u32[]{:S(2)}, u32[]{:S(2)}) %collective-permute-start.8) | collective-permute-done | bytes 262176 | tf_op jit(solution)/shard_map/ppermute | solution.py:21
  62.8 1.0 %slice_add_fusion = (f32[4,128,128]{2,1,0:T(8,128)S(1)}, f32[4,128,128]{2,1,0:T(8,128)S(1)}, f32[4,128,128]{2,1,0:T(8,128)S(1)}) fusion(f32[4,128,128]{2,1,0:T(8,128)S(1)} %collective-permute-done.9, f32[8,128,128]{2,1,0:T(8,128)S(1)} %convolution_bitcast_fusion, f32[4,128,128]{2,1,0:T(8,128)} %collective-permute-done.8, pred[]{:T(512)S(6)} %not.17), kind=kLoop, calls=%fused_computation.66 | loop fusion | flops 196608 | bytes 1835009 | tf_op jit(solution)/shard_map/add | solution.py:32
  63.8 0.1 collective-permute-start.10
  63.9 0.3 fusion.7
  64.2 0.4 collective-permute-start.13
  64.6 0.9 %collective-permute-done.10 = f32[4,128,128]{2,1,0:T(8,128)} collective-permute-done((f32[4,128,128]{2,1,0:T(8,128)S(1)}, f32[4,128,128]{2,1,0:T(8,128)}, u32[]{:S(2)}, u32[]{:S(2)}) %collective-permute-start.10) | collective-permute-done | bytes 262176 | tf_op jit(solution)/shard_map/ppermute | solution.py:21
  65.5 1.0 %fusion.43 = (f32[4,128,128]{2,1,0:T(8,128)S(1)}, f32[4,128,128]{2,1,0:T(8,128)S(1)}) fusion(f32[4,128,128]{2,1,0:T(8,128)S(1)} %get-tuple-element.12, f32[4,128,128]{2,1,0:T(8,128)} %collective-permute-done.10, f32[4,128,128]{2,1,0:T(8,128)S(1)} %get-tuple-element.13, pred[]{:T(512)S(6)} %not.16), kind=kLoop, calls=%fused_computation.72 | loop fusion | flops 196608 | bytes 1310721 | tf_op jit(solution)/shard_map/add | solution.py:32
  66.5 1.6 %collective-permute-start.11 = (f32[4,128,128]{2,1,0:T(8,128)S(1)}, f32[4,128,128]{2,1,0:T(8,128)S(1)}, u32[]{:S(2)}, u32[]{:S(2)}) collective-permute-start(f32[4,128,128]{2,1,0:T(8,128)S(1)} %get-tuple-element.31), channel_id=1, source_target_pairs={{0,8},{4,12},{8,0},{12,4},{1,9},{5,13},{9,1},{13,5},{2,10},{6,14},... | collective-permute-start | bytes 786440 | tf_op jit(solution)/shard_map/ppermute | solution.py:21
  68.1 0.3 convolution_bitcast_fusion.2
  68.4 1.1 %fusion.23.local_k = f32[8,128,128]{2,1,0:T(8,128)} fusion(bf16[8,128,128]{2,1,0:T(8,128)(2,1)S(1)} %fusion.7, bf16[128,1024]{1,0:T(8,128)(2,1)S(1)} %copy-done), kind=kOutput, calls=%fused_computation.36 | convolution fusion | flops 33554432 | bytes 1048576 | tf_op jit(solution)/shard_map/hts,thi->hsi/dot_general | solution.py:158
  69.5 8.7 %collective-permute-done.13 = f32[4,128,128]{2,1,0:T(8,128)S(1)} collective-permute-done((f32[4,128,128]{2,1,0:T(8,128)S(1)}, f32[4,128,128]{2,1,0:T(8,128)S(1)}, u32[]{:S(2)}, u32[]{:S(2)}) %collective-permute-start.13) | collective-permute-done | bytes 262176 | tf_op jit(solution)/shard_map/ppermute | solution.py:21
  78.2 0.1 collective-permute-start.14
  78.5 1.1 %fusion.15.local_v = f32[8,128,128]{2,1,0:T(8,128)} fusion(bf16[8,128,128]{2,1,0:T(8,128)(2,1)S(1)} %fusion.5, bf16[16,8,8,128]{3,2,1,0:T(8,128)(2,1)S(1)} %get-tuple-element.20), kind=kOutput, calls=%fused_computation.28 | convolution fusion | flops 33554432 | bytes 1048576 | tf_op jit(solution)/shard_map/hts,thj->hsj/dot_general | solution.py:159
  79.6 0.3 collective-permute-done.14
  79.9 1.6 %collective-permute-start.15 = (f32[4,128,128]{2,1,0:T(8,128)S(1)}, f32[4,128,128]{2,1,0:T(8,128)S(1)}, u32[]{:S(2)}, u32[]{:S(2)}) collective-permute-start(f32[4,128,128]{2,1,0:T(8,128)S(1)} %add.123), channel_id=1, source_target_pairs={{0,8},{4,12},{8,0},{12,4},{1,9},{5,13},{9,1},{13,5},{2,10},{6,14},... | collective-permute-start | bytes 786440 | tf_op jit(solution)/shard_map/ppermute | solution.py:21
  81.5 0.3 fusion.6
  81.7 0.9 copy.27
  82.6 4.7 %collective-permute-done.12 = f32[4,128,128]{2,1,0:T(8,128)} collective-permute-done((f32[4,128,128]{2,1,0:T(8,128)S(1)}, f32[4,128,128]{2,1,0:T(8,128)}, u32[]{:S(2)}, u32[]{:S(2)}) %collective-permute-start.12) | collective-permute-done | bytes 262176 | tf_op jit(solution)/shard_map/ppermute | solution.py:21
  87.3 1.7 %add_add_fusion.lower_later = f32[4,128,128]{2,1,0:T(8,128)} fusion(f32[4,128,128]{2,1,0:T(8,128)} %collective-permute-done.12, f32[4,128,128]{2,1,0:T(8,128)S(1)} %get-tuple-element.32, f32[4,128,128]{2,1,0:T(8,128)S(1)} %collective-permute-done.11, pred[]{:T(512)S(6)} %not.18), kind=kLoop, calls=%fused_computation.43 | loop fusion | flops 196608 | bytes 1048577 | tf_op jit(solution)/shard_map/add | solution.py:160
  88.9 0.8 select_add_fusion.upper_later
  89.7 2.7 %shard_map.75 = (bf16[128,1024]{1,0:T(8,128)(2,1)}, bf16[128,1024]{1,0:T(8,128)(2,1)}) custom-call(f32[4,128,128]{2,1,0:T(8,128)} %add_add_fusion.lower_later, f32[4,128,128]{2,1,0:T(8,128)} %select_add_fusion.upper_later, f32[8,128,128]{2,1,0:T(8,128)} %fusion.23.local_k, f32[8,128,128]{2,1,0:T(8,128)} %fusion.15.local_v, bf16[128,1024]{1,0:T(8,128)(2,1)} %value.1, ...), custom_call_target="tpu_custom_call" | custom-call | flops 67108864 | bytes 6291456 | tf_op jit(solution)/shard_map/pallas_call | solution.py:108
  (25 shorter events, 0.7 us)
Async XLA Ops:
  0.6 37.4 %copy-start = (bf16[128,1024]{1,0:T(8,128)(2,1)S(1)}, bf16[128,1024]{1,0:T(8,128)(2,1)}, u32[]{:S(2)}) copy-start(bf16[128,1024]{1,0:T(8,128)(2,1)} %param.4) | copy-start | bytes 786436
  0.6 1.2 %copy-start.1 = (bf16[128,1024]{1,0:T(8,128)(2,1)S(1)}, bf16[128,1024]{1,0:T(8,128)(2,1)}, u32[]{:S(2)}) copy-start(bf16[128,1024]{1,0:T(8,128)(2,1)} %value.1) | copy-start | bytes 786436
  2.1 14.9 %collective-permute-start = (f32[4,128,128]{2,1,0:T(8,128)S(1)}, f32[4,128,128]{2,1,0:T(8,128)S(1)}, u32[]{:S(2)}, u32[]{:S(2)}) collective-permute-start(f32[4,128,128]{2,1,0:T(8,128)S(1)} %get-tuple-element.28), channel_id=1, source_target_pairs={{0,1},{1,0},{2,3},{3,2},{4,5},{5,4},{6,7},{7,6},{8,9},{9,8},{10,11... | collective-permute-start | bytes 786440 | tf_op jit(solution)/shard_map/ppermute | solution.py:21
  5.2 14.3 %collective-permute-start.1 = (f32[4,128,128]{2,1,0:T(8,128)S(1)}, f32[4,128,128]{2,1,0:T(8,128)S(1)}, u32[]{:S(2)}, u32[]{:S(2)}) collective-permute-start(f32[4,128,128]{2,1,0:T(8,128)S(1)} %get-tuple-element.29), channel_id=1, source_target_pairs={{0,2},{1,3},{2,0},{3,1},{4,6},{5,7},{6,4},{7,5},{8,10},{9,11},{10,... | collective-permute-start | bytes 786440 | tf_op jit(solution)/shard_map/ppermute | solution.py:21
  19.6 1.6 %collective-permute-start.5 = (f32[4,128,128]{2,1,0:T(8,128)S(1)}, f32[4,128,128]{2,1,0:T(8,128)S(1)}, u32[]{:S(2)}, u32[]{:S(2)}) collective-permute-start(f32[4,128,128]{2,1,0:T(8,128)S(1)} %get-tuple-element.27), channel_id=1, source_target_pairs={{0,4},{4,0},{8,12},{12,8},{1,5},{5,1},{9,13},{13,9},{2,6},{6,2},{1... | collective-permute-start | bytes 786440 | tf_op jit(solution)/shard_map/ppermute | solution.py:21
  19.7 15.1 %collective-permute-start.2 = (f32[4,128,128]{2,1,0:T(8,128)S(1)}, f32[4,128,128]{2,1,0:T(8,128)S(1)}, u32[]{:S(2)}, u32[]{:S(2)}) collective-permute-start(f32[4,128,128]{2,1,0:T(8,128)S(1)} %get-tuple-element.11), channel_id=1, source_target_pairs={{0,2},{1,3},{2,0},{3,1},{4,6},{5,7},{6,4},{7,5},{8,10},{9,11},{10,... | collective-permute-start | bytes 786440 | tf_op jit(solution)/shard_map/ppermute | solution.py:21
  21.3 13.7 %collective-permute-start.6 = (f32[4,128,128]{2,1,0:T(8,128)S(1)}, f32[4,128,128]{2,1,0:T(8,128)S(1)}, u32[]{:S(2)}, u32[]{:S(2)}) collective-permute-start(f32[4,128,128]{2,1,0:T(8,128)S(1)} %get-tuple-element.34), channel_id=1, source_target_pairs={{0,8},{4,12},{8,0},{12,4},{1,9},{5,13},{9,1},{13,5},{2,10},{6,14},... | collective-permute-start | bytes 786440 | tf_op jit(solution)/shard_map/ppermute | solution.py:21
  34.8 1.6 %collective-permute-start.3 = (f32[4,128,128]{2,1,0:T(8,128)S(1)}, f32[4,128,128]{2,1,0:T(8,128)S(1)}, u32[]{:S(2)}, u32[]{:S(2)}) collective-permute-start(f32[4,128,128]{2,1,0:T(8,128)S(1)} %add.98), channel_id=1, source_target_pairs={{0,4},{4,0},{8,12},{12,8},{1,5},{5,1},{9,13},{13,9},{2,6},{6,2},{1... | collective-permute-start | bytes 786440 | tf_op jit(solution)/shard_map/ppermute | solution.py:21
  35.0 8.7 %collective-permute-start.7 = (f32[4,128,128]{2,1,0:T(8,128)S(1)}, f32[4,128,128]{2,1,0:T(8,128)S(1)}, u32[]{:S(2)}, u32[]{:S(2)}) collective-permute-start(f32[4,128,128]{2,1,0:T(8,128)S(1)} %fusion.11), channel_id=1, source_target_pairs={{0,1},{1,0},{2,3},{3,2},{4,5},{5,4},{6,7},{7,6},{8,9},{9,8},{10,11... | collective-permute-start | bytes 786440 | tf_op jit(solution)/shard_map/ppermute | solution.py:21
  36.5 8.4 %collective-permute-start.4 = (f32[4,128,128]{2,1,0:T(8,128)S(1)}, f32[4,128,128]{2,1,0:T(8,128)S(1)}, u32[]{:S(2)}, u32[]{:S(2)}) collective-permute-start(f32[4,128,128]{2,1,0:T(8,128)S(1)} %add.100), channel_id=1, source_target_pairs={{0,8},{4,12},{8,0},{12,4},{1,9},{5,13},{9,1},{13,5},{2,10},{6,14},... | collective-permute-start | bytes 786440 | tf_op jit(solution)/shard_map/ppermute | solution.py:21
  45.7 1.0 %copy-start.2 = (bf16[128,1024]{1,0:T(8,128)(2,1)S(1)}, bf16[128,1024]{1,0:T(8,128)(2,1)}, u32[]{:S(2)}) copy-start(bf16[128,1024]{1,0:T(8,128)(2,1)} %param.7) | copy-start | bytes 786436
  48.1 11.9 %collective-permute-start.9 = (f32[4,128,128]{2,1,0:T(8,128)S(1)}, f32[4,128,128]{2,1,0:T(8,128)S(1)}, u32[]{:S(2)}, u32[]{:S(2)}) collective-permute-start(f32[4,128,128]{2,1,0:T(8,128)S(1)} %get-tuple-element.24), channel_id=1, source_target_pairs={{0,1},{1,0},{2,3},{3,2},{4,5},{5,4},{6,7},{7,6},{8,9},{9,8},{10,11... | collective-permute-start | bytes 786440 | tf_op jit(solution)/shard_map/ppermute | solution.py:21
  48.9 13.9 %collective-permute-start.8 = (f32[4,128,128]{2,1,0:T(8,128)S(1)}, f32[4,128,128]{2,1,0:T(8,128)}, u32[]{:S(2)}, u32[]{:S(2)}) collective-permute-start(f32[4,128,128]{2,1,0:T(8,128)S(1)} %get-tuple-element.25), channel_id=1, source_target_pairs={{0,2},{1,3},{2,0},{3,1},{4,6},{5,7},{6,4},{7,5},{8,10},{9,11},{10,... | collective-permute-start | bytes 786440 | tf_op jit(solution)/shard_map/ppermute | solution.py:21
  63.8 1.7 %collective-permute-start.10 = (f32[4,128,128]{2,1,0:T(8,128)S(1)}, f32[4,128,128]{2,1,0:T(8,128)}, u32[]{:S(2)}, u32[]{:S(2)}) collective-permute-start(f32[4,128,128]{2,1,0:T(8,128)S(1)} %get-tuple-element.12), channel_id=1, source_target_pairs={{0,4},{4,0},{8,12},{12,8},{1,5},{5,1},{9,13},{13,9},{2,6},{6,2},{1... | collective-permute-start | bytes 786440 | tf_op jit(solution)/shard_map/ppermute | solution.py:21
  64.2 14.0 %collective-permute-start.13 = (f32[4,128,128]{2,1,0:T(8,128)S(1)}, f32[4,128,128]{2,1,0:T(8,128)S(1)}, u32[]{:S(2)}, u32[]{:S(2)}) collective-permute-start(f32[4,128,128]{2,1,0:T(8,128)S(1)} %get-tuple-element.22), channel_id=1, source_target_pairs={{0,2},{1,3},{2,0},{3,1},{4,6},{5,7},{6,4},{7,5},{8,10},{9,11},{10,... | collective-permute-start | bytes 786440 | tf_op jit(solution)/shard_map/ppermute | solution.py:21
  66.5 11.9 %collective-permute-start.11 = (f32[4,128,128]{2,1,0:T(8,128)S(1)}, f32[4,128,128]{2,1,0:T(8,128)S(1)}, u32[]{:S(2)}, u32[]{:S(2)}) collective-permute-start(f32[4,128,128]{2,1,0:T(8,128)S(1)} %get-tuple-element.31), channel_id=1, source_target_pairs={{0,8},{4,12},{8,0},{12,4},{1,9},{5,13},{9,1},{13,5},{2,10},{6,14},... | collective-permute-start | bytes 786440 | tf_op jit(solution)/shard_map/ppermute | solution.py:21
  78.2 1.6 %collective-permute-start.14 = (f32[4,128,128]{2,1,0:T(8,128)S(1)}, f32[4,128,128]{2,1,0:T(8,128)S(1)}, u32[]{:S(2)}, u32[]{:S(2)}) collective-permute-start(f32[4,128,128]{2,1,0:T(8,128)S(1)} %add.121), channel_id=1, source_target_pairs={{0,4},{4,0},{8,12},{12,8},{1,5},{5,1},{9,13},{13,9},{2,6},{6,2},{1... | collective-permute-start | bytes 786440 | tf_op jit(solution)/shard_map/ppermute | solution.py:21
  78.4 8.8 %collective-permute-start.12 = (f32[4,128,128]{2,1,0:T(8,128)S(1)}, f32[4,128,128]{2,1,0:T(8,128)}, u32[]{:S(2)}, u32[]{:S(2)}) collective-permute-start(f32[4,128,128]{2,1,0:T(8,128)S(1)} %fusion.12), channel_id=1, source_target_pairs={{0,1},{1,0},{2,3},{3,2},{4,5},{5,4},{6,7},{7,6},{8,9},{9,8},{10,11... | collective-permute-start | bytes 786440 | tf_op jit(solution)/shard_map/ppermute | solution.py:21
  79.9 9.1 %collective-permute-start.15 = (f32[4,128,128]{2,1,0:T(8,128)S(1)}, f32[4,128,128]{2,1,0:T(8,128)S(1)}, u32[]{:S(2)}, u32[]{:S(2)}) collective-permute-start(f32[4,128,128]{2,1,0:T(8,128)S(1)} %add.123), channel_id=1, source_target_pairs={{0,8},{4,12},{8,0},{12,4},{1,9},{5,13},{9,1},{13,5},{2,10},{6,14},... | collective-permute-start | bytes 786440 | tf_op jit(solution)/shard_map/ppermute | solution.py:21
